TPU v7x, 32 devices: a whole 2x2x4 slice. The times are simulated.
32 devices in a mesh: groups: 2 (over x), node: 16 (over z, y, core).
Axes of the slice: x: 2, y: 2, z: 4, core: 2. Of those that a mesh axis runs over, the one named last changes fastest.
Arguments:
- features: bfloat16 [32768, 1024], P(('groups', 'node')), parts along dimension 0, may hold values from -6 to 6
- filter_gate_weight: bfloat16 [64, 64], replicated, may hold values from -0.75 to 0.75
- skip_weight: bfloat16 [32, 256], replicated, may hold values from -1 to 1
- mix_weight: bfloat16 [96, 32], replicated, may hold values from -0.625 to 0.625
- band_weight: bfloat16 [16384, 192], P('node'), may hold values from -0.4375 to 0.4375
- far_weight: bfloat16 [64, 15360], P(None, 'node'), may hold values from -0.75 to 0.75
- far_ptr: int32 [16, 17], P('node'), may hold values from 0 to 15, as said below
- far_col: int32 [16, 15], P('node'), may hold values from 0 to 31, as said below
- export_block: int32 [16, 2], replicated, may hold values from 0 to 15, as said below
Outputs:
- residual_output: bfloat16 [32768, 512], P(('groups', 'node')), parts along dimension 0
- skip_out: bfloat16 [32768, 4096], P(('groups', 'node')), parts along dimension 0
There are 2 independent parts, one for each index of `groups`. A program takes and returns all parts, laid end to end along the dimension named above; an argument that names none is the same for every part. Nothing has to cross between parts.
Inputs may be any that keep to these rules, and one draw needn't show every extreme that they name: Each row of export_block holds 2 different local block numbers, each below 16. `far_ptr`: each row starts at 0 and never falls; its last entry is the number of used far-block slots of that device, and some device uses all 15. `far_col`: slots below far_ptr[d][16] name blocks of devices other than d, at most one slot for each other device; the other slots hold 0 and belong to no block row. The device that uses all slots reads entry 0 of device 0 and the last entry of the last device.
All inputs are finite; a program needn't handle non-finite values.
Results may differ from a plain program's by a relative error of at most 0.0052.
Values may be sent and summed in bfloat16 or wider, within the bound.
No kernel may reach another device: no remote copies, remote signals or barrier semaphores. Data moves between devices by JAX's collectives and lax.ppermute only.
A program may use at most 128 MiB of HBM per device.

v0:
```python
import jax
import jax.numpy as jnp
from jax import lax
from jax.sharding import PartitionSpec as P

BLK = 64
TOUT = 16
DILATION_STEP = 16
EXPORT = 2
CHANNEL_WIDTH = 32
S = 256
TIN = 32


def padded_2(block, sides, width):
    for axis, dim in sides:
        count = lax.axis_size(axis)
        forward = [(i, i + 1) for i in range(count - 1)]
        backward = [(target, source) for source, target in forward]
        low = lax.ppermute(
            lax.slice_in_dim(block, block.shape[dim] - width, None, axis=dim), axis, forward
        )
        high = lax.ppermute(lax.slice_in_dim(block, 0, width, axis=dim), axis, backward)
        block = jnp.concatenate([low, block, high], axis=dim)
    return block


def local(
    features,
    filter_gate_weight,
    skip_weight,
    mix_weight,
    band_weight,
    far_weight,
    far_ptr,
    far_col,
    export_block,
):
    node_rows = features.shape[0]
    blocks = node_rows // BLK
    far_cap = far_col.shape[1]
    peer_count = far_cap + 1
    series_input = features.reshape(node_rows, TIN, CHANNEL_WIDTH)
    preact = jnp.einsum(
        "myv,vi->myi",
        series_input[:, :TOUT],
        filter_gate_weight[:CHANNEL_WIDTH],
        preferred_element_type=jnp.float32,
    )
    preact = preact + jnp.einsum(
        "myv,vi->myi",
        series_input[:, DILATION_STEP:],
        filter_gate_weight[CHANNEL_WIDTH:],
        preferred_element_type=jnp.float32,
    )
    hidden = (
        jnp.tanh(preact[..., :CHANNEL_WIDTH]) * jax.nn.sigmoid(preact[..., CHANNEL_WIDTH:])
    ).astype(jnp.bfloat16)
    skip_out = jnp.einsum(
        "ntc,cs->nts", hidden, skip_weight, preferred_element_type=jnp.float32
    ).astype(jnp.bfloat16)
    skip_out = skip_out.reshape(node_rows, TOUT * S)
    hidden_flat = hidden.reshape(node_rows, TOUT * CHANNEL_WIDTH)
    own_index = lax.axis_index("node")
    own_exports = lax.dynamic_slice_in_dim(export_block, own_index, 1, 0)[0]
    columns = far_col[0]
    sources = columns // EXPORT
    slot_export = columns % EXPORT
    pointers = far_ptr[0]
    slot_ids = jnp.arange(far_cap, dtype=jnp.int32)
    assign = (
        (pointers[:-1, None] <= slot_ids[None, :]) & (slot_ids[None, :] < pointers[1:, None])
    ).astype(jnp.float32)
    weights = far_weight.reshape(BLK, far_cap, BLK).transpose(1, 0, 2)
    band_blocks = band_weight.reshape(blocks, BLK, 3 * BLK)
    in_use = slot_ids < pointers[-1]
    matches = (sources[None, :] == jnp.arange(peer_count, dtype=jnp.int32)[:, None]) & in_use[
        None, :
    ]
    wanted = jnp.sum(jnp.where(matches, slot_export[None, :], 0), axis=1)
    requested = lax.all_to_all(wanted[:, None], "node", split_axis=0, concat_axis=0, tiled=True)[
        :, 0
    ]
    send_rows = own_exports[requested]

    def fetch_far(field_blocks):
        arrived = lax.all_to_all(
            field_blocks[send_rows], "node", split_axis=0, concat_axis=0, tiled=True
        )
        return arrived[sources]

    def diffuse(field_rows):
        padded = padded_2(field_rows, (("node", 0),), BLK)
        padded_blocks = padded.reshape(blocks + 2, BLK, field_rows.shape[1])
        summed = jnp.zeros((blocks, BLK, field_rows.shape[1]), jnp.float32)
        for shift_pos in range(3):
            summed = summed + jnp.einsum(
                "rij,rjm->rim",
                band_blocks[:, :, shift_pos * BLK : (shift_pos + 1) * BLK],
                padded_blocks[shift_pos : shift_pos + blocks],
                preferred_element_type=jnp.float32,
            )
        pieces = fetch_far(field_rows.reshape(blocks, BLK, field_rows.shape[1]))
        products = jnp.einsum("kij,kjm->kim", weights, pieces, preferred_element_type=jnp.float32)
        summed = summed + jnp.einsum(
            "rk,kim->rim", assign, products, precision=lax.Precision.HIGHEST
        )
        return summed.reshape(node_rows, field_rows.shape[1]).astype(jnp.bfloat16)

    hop_one = diffuse(hidden_flat)
    hop_two = diffuse(hop_one)
    joined = jnp.concatenate(
        [
            hidden,
            hop_one.reshape(node_rows, TOUT, CHANNEL_WIDTH),
            hop_two.reshape(node_rows, TOUT, CHANNEL_WIDTH),
        ],
        axis=-1,
    )
    mixed_output = jnp.einsum("myv,vi->myi", joined, mix_weight, preferred_element_type=jnp.float32)
    residual_output = (series_input[:, DILATION_STEP:].astype(jnp.float32) + mixed_output).astype(
        jnp.bfloat16
    )
    return (residual_output.reshape(node_rows, TOUT * CHANNEL_WIDTH), skip_out)


def solution(mesh):
    placed = (
        P(("groups", "node"), None),
        P(),
        P(),
        P(),
        P("node", None),
        P(None, "node"),
        P("node", None),
        P("node", None),
        P(),
    )
    return jax.shard_map(
        local,
        mesh=mesh,
        in_specs=placed,
        out_specs=(P(("groups", "node"), None), P(("groups", "node"), None)),
        check_vma=False,
    )
```

profile of v0, /device:TPU:15, one launch (start us, length us, event | category | flops | bytes accessed | tf_op | source)
XLA Modules:
  0.0 138.1 jit_solution(6040651337936078330)
XLA Ops:
  0.6 1.2 slice.121
  1.9 0.6 iota_compare_fusion.3
  2.5 0.7 fusion.53
  3.3 0.7 copy.73
  4.0 6.6 %all-to-all-start = ((s32[16,1,1]{2,1,0:T(1,128)}), s32[16,1,1]{2,1,0:T(1,128)S(1)}, u32[]{:S(2)}, u32[]{:S(2)}) async-start(s32[16,1,1]{2,1,0:T(1,128)} %copy.73), calls=%async_computation | async-start | bytes 16384 | tf_op jit(solution)/shard_map/all_to_all | solution.py:81
  10.6 0.7 constant_dynamic-slice_fusion
  11.9 2.9 %copy.68 = bf16[1024,1024]{0,1:T(8,128)(2,1)S(1)} copy(bf16[1024,1024]{1,0:T(8,128)(2,1)} %param.9) | data formatting | bytes 4194304 | tf_op args[0]
  14.8 0.8 fusion.37
  16.1 1.2 convolution_add_fusion
  17.3 0.8 fusion.16
  18.2 2.3 %slice.112 = bf16[16,64,512]{1,0,2:T(8,128)(2,1)} reshape(bf16[1024,16,32]{0,2,1:T(8,128)(2,1)S(1)} %fusion.16) | data formatting | bytes 2097152 | tf_op jit(solution)/shard_map/slice | solution.py:100
  20.5 2.5 %copy.71 = bf16[16,64,512]{2,1,0:T(8,128)(2,1)S(1)} copy(bf16[16,64,512]{1,0,2:T(8,128)(2,1)} %slice.112) | data formatting | bytes 2097152 | tf_op jit(solution)/shard_map/slice | solution.py:100
  23.4 1.3 fusion.51
  24.7 1.6 %gather_fusion = bf16[16,64,512]{2,1,0:T(8,128)(2,1)} fusion(bf16[16,64,512]{2,1,0:T(8,128)(2,1)S(1)} %copy.71, s32[1024]{0:T(1024)S(1)} %pad_clamp_fusion.1), kind=kCustom, calls=%fused_computation | custom fusion | bytes 2097216 | tf_op jit(solution)/shard_map/gather | solution.py:88
  26.3 6.0 %all-to-all-start.1 = ((bf16[16,64,512]{2,1,0:T(8,128)(2,1)}), bf16[16,64,512]{2,1,0:T(8,128)(2,1)}, u32[]{:S(2)}, u32[]{:S(2)}) async-start(bf16[16,64,512]{2,1,0:T(8,128)(2,1)} %gather_fusion), calls=%async_computation.1 | async-start | bytes 2097152 | tf_op jit(solution)/shard_map/all_to_all | solution.py:87
  32.3 0.8 fusion.55
  33.1 3.3 %collective-permute-start = (bf16[64,512]{0,1:T(8,128)(2,1)}, bf16[64,512]{0,1:T(8,128)(2,1)}, u32[]{:S(2)}, u32[]{:S(2)}) collective-permute-start(bf16[64,512]{0,1:T(8,128)(2,1)} %bitcast.3), channel_id=1, source_target_pairs={{0,1},{1,2},{2,3},{3,4},{4,5},{5,6},{6,7},{7,8},{8,9},{9,10},{10,1... | collective-permute-start | bytes 196616 | tf_op jit(solution)/shard_map/ppermute | solution.py:20
  36.4 2.1 %collective-permute-start.1 = (bf16[64,512]{0,1:T(8,128)(2,1)S(1)}, bf16[64,512]{0,1:T(8,128)(2,1)}, u32[]{:S(2)}, u32[]{:S(2)}) collective-permute-start(bf16[64,512]{0,1:T(8,128)(2,1)S(1)} %bitcast.109), channel_id=1, source_target_pairs={{1,0},{2,1},{3,2},{4,3},{5,4},{6,5},{7,6},{8,7},{9,8},{10,9},{11,1... | collective-permute-start | bytes 196616 | tf_op jit(solution)/shard_map/ppermute | solution.py:23
  39.0 0.7 fusion.52
  39.7 0.8 slice_bitcast_fusion.3
  40.5 1.8 %fusion.24 = f32[16,512,64]{1,2,0:T(8,128)} fusion(bf16[16,64,512]{2,1,0:T(8,128)(2,1)S(1)} %copy.71, bf16[16,64,192]{2,1,0:T(8,128)(2,1)S(1)} %bitcast.96), kind=kOutput, calls=%fused_computation.37 | convolution fusion | flops 67108864 | bytes 3407872 | tf_op jit(solution)/shard_map/rij,rjm->rim/dot_general | solution.py:97
  42.3 14.7 %collective-permute-done = bf16[64,512]{0,1:T(8,128)(2,1)} collective-permute-done((bf16[64,512]{0,1:T(8,128)(2,1)}, bf16[64,512]{0,1:T(8,128)(2,1)}, u32[]{:S(2)}, u32[]{:S(2)}) %collective-permute-start) | collective-permute-done | bytes 65568 | tf_op jit(solution)/shard_map/ppermute | solution.py:20
  57.0 1.6 %collective-permute-done.1 = bf16[64,512]{0,1:T(8,128)(2,1)} collective-permute-done((bf16[64,512]{0,1:T(8,128)(2,1)S(1)}, bf16[64,512]{0,1:T(8,128)(2,1)}, u32[]{:S(2)}, u32[]{:S(2)}) %collective-permute-start.1) | collective-permute-done | bytes 65568 | tf_op jit(solution)/shard_map/ppermute | solution.py:23
  58.7 3.0 %pad_maximum_fusion.2 = (bf16[1024,512]{0,1:T(8,128)(2,1)}, bf16[1024,512]{0,1:T(8,128)(2,1)S(1)}) fusion(bf16[64,512]{0,1:T(8,128)(2,1)} %collective-permute-done.1, bf16[1024,512]{0,1:T(8,128)(2,1)S(1)} %bitcast.92, bf16[64,512]{0,1:T(8,128)(2,1)} %collective-permute-done), kind=kLoop, calls=%fused_computation.32 | loop fusion | flops 4194304 | bytes 3276800 | tf_op jit(solution)/shard_map/concatenate | solution.py:24
  61.7 2.3 %copy.72 = bf16[1024,512]{1,0:T(8,128)(2,1)} copy(bf16[1024,512]{0,1:T(8,128)(2,1)} %get-tuple-element.16) | data formatting | bytes 2097152 | tf_op jit(solution)/shard_map/slice | solution.py:100
  63.9 1.3 copy.69
  65.3 3.0 %fusion.28 = f32[16,512,64]{1,2,0:T(8,128)} fusion(bf16[16,64,512]{2,1,0:T(8,128)(2,1)} %bitcast.105, bf16[16,64,192]{2,1,0:T(8,128)(2,1)S(1)} %bitcast.97), kind=kOutput, calls=%fused_computation.41 | convolution fusion | flops 67108864 | bytes 3407872 | tf_op jit(solution)/shard_map/rij,rjm->rim/dot_general | solution.py:97
  68.2 1.8 %gather_fusion.1 = bf16[15,64,512]{2,1,0:T(8,128)(2,1)S(1)} fusion(bf16[16,64,512]{2,1,0:T(8,128)(2,1)} %all-to-all-done.1, s32[1024]{0:T(1024)S(1)} %pad_clamp_fusion), kind=kCustom, calls=%fused_computation.1 | custom fusion | bytes 1966140 | tf_op jit(solution)/shard_map/gather | solution.py:90
  70.5 2.2 %fusion.14 = f32[16,64,512]{2,0,1:T(8,128)S(1)} fusion(f32[15,64,512]{2,1,0:T(8,128)S(1)} %convolution_bitcast_fusion.1, s32[16]{0:T(128)S(1)} %get-tuple-element.23, s32[16]{0:T(128)S(1)} %get-tuple-element.22), kind=kOutput, calls=%fused_computation.24 | convolution fusion | flops 94372560 | bytes 4063360 | tf_op jit(solution)/shard_map/rk,kim->rim/dot_general | solution.py:105
  72.8 1.4 %fusion.11 = bf16[16,64,512]{2,1,0:T(8,128)(2,1)S(1)} fusion(f32[16,64,512]{2,0,1:T(8,128)S(1)} %fusion.14, f32[16,512,64]{1,2,0:T(8,128)S(1)} %copy-done.6, f32[16,512,64]{1,2,0:T(8,128)S(1)} %copy-done.5, bf16[16,64,512]{2,1,0:T(8,128)(2,1)S(1)} %bitcast.103, bf16[16,64,192]{2,1,0:T(8,128)(2,1)S(1)} %bitcast.98), kind=kOutput, calls=%fused_computation.21 | convolution fusion | flops 69206016 | bytes 8650752 | tf_op jit(solution)/shard_map/rij,rjm->rim/dot_general | solution.py:97
  74.3 1.7 %gather_fusion.2 = bf16[16,64,512]{2,1,0:T(8,128)(2,1)} fusion(bf16[16,64,512]{2,1,0:T(8,128)(2,1)S(1)} %fusion.11, s32[1024]{0:T(1024)} %copy-done.16), kind=kCustom, calls=%fused_computation.2 | custom fusion | bytes 2097216 | tf_op jit(solution)/shard_map/gather | solution.py:88
  76.0 4.5 %all-to-all-start.2 = ((bf16[16,64,512]{2,1,0:T(8,128)(2,1)}), bf16[16,64,512]{2,1,0:T(8,128)(2,1)}, u32[]{:S(2)}, u32[]{:S(2)}) async-start(bf16[16,64,512]{2,1,0:T(8,128)(2,1)} %gather_fusion.2), calls=%async_computation.2 | async-start | bytes 2097152 | tf_op jit(solution)/shard_map/all_to_all | solution.py:87
  80.5 5.9 %convolution_convert_fusion = bf16[1024,16,256]{0,2,1:T(8,128)(2,1)} fusion(bf16[1024,16,32]{0,2,1:T(8,128)(2,1)S(1)} %fusion.16, bf16[32,256]{1,0:T(8,128)(2,1)S(1)} %copy-done), kind=kOutput, calls=%fused_computation.4 | convolution fusion | flops 272629760 | bytes 9453568 | tf_op jit(solution)/shard_map/ntc,cs->nts/dot_general | solution.py:59
  86.4 11.9 %copy.84 = bf16[1024,4096]{1,0:T(8,128)(2,1)} copy(bf16[1024,4096]{0,1:T(8,128)(2,1)} %bitcast.90) | data formatting | bytes 16777216
  98.3 2.3 %collective-permute-start.3 = (bf16[64,512]{1,0:T(8,128)(2,1)S(1)}, bf16[64,512]{1,0:T(8,128)(2,1)S(1)}, u32[]{:S(2)}, u32[]{:S(2)}) collective-permute-start(bf16[64,512]{1,0:T(8,128)(2,1)S(1)} %get-tuple-element.14), channel_id=1, source_target_pairs={{1,0},{2,1},{3,2},{4,3},{5,4},{6,5},{7,6},{8,7},{9,8},{10,9},{11,1... | collective-permute-start | bytes 196616 | tf_op jit(solution)/shard_map/ppermute | solution.py:23
  100.6 4.4 %collective-permute-start.2 = (bf16[64,512]{1,0:T(8,128)(2,1)S(1)}, bf16[64,512]{1,0:T(8,128)(2,1)S(1)}, u32[]{:S(2)}, u32[]{:S(2)}) collective-permute-start(bf16[64,512]{1,0:T(8,128)(2,1)S(1)} %get-tuple-element.15), channel_id=1, source_target_pairs={{0,1},{1,2},{2,3},{3,4},{4,5},{5,6},{6,7},{7,8},{8,9},{9,10},{10,1... | collective-permute-start | bytes 196616 | tf_op jit(solution)/shard_map/ppermute | solution.py:20
  105.0 1.8 %fusion.26 = f32[16,512,64]{1,2,0:T(8,128)} fusion(bf16[16,64,512]{2,1,0:T(8,128)(2,1)S(1)} %fusion.11, bf16[16,64,192]{2,1,0:T(8,128)(2,1)S(1)} %bitcast.99), kind=kOutput, calls=%fused_computation.39 | convolution fusion | flops 67108864 | bytes 3407872 | tf_op jit(solution)/shard_map/rij,rjm->rim/dot_general | solution.py:97
  106.9 2.8 %copy.78 = bf16[16,64,512]{1,0,2:T(8,128)(2,1)} copy(bf16[16,64,512]{2,1,0:T(8,128)(2,1)S(1)} %fusion.11) | data formatting | bytes 2097152 | tf_op jit(solution)/shard_map/convert_element_type | solution.py:108
  109.7 4.1 %convert_element_type.35 = bf16[1024,16,32]{0,2,1:T(8,128)(2,1)} reshape(bf16[16,64,512]{1,0,2:T(8,128)(2,1)} %copy.78) | data formatting | bytes 2097152 | tf_op jit(solution)/shard_map/convert_element_type | solution.py:108
  113.8 1.1 pad_maximum_fusion
  115.4 2.9 %gather_fusion.3 = bf16[15,64,512]{2,1,0:T(8,128)(2,1)} fusion(bf16[16,64,512]{2,1,0:T(8,128)(2,1)} %all-to-all-done.2, s32[1024]{0:T(1024)} %copy-done.15), kind=kCustom, calls=%fused_computation.3 | custom fusion | bytes 1966140 | tf_op jit(solution)/shard_map/gather | solution.py:90
  118.3 1.6 %convolution_bitcast_fusion = f32[15,64,512]{2,1,0:T(8,128)S(1)} fusion(bf16[15,64,512]{2,1,0:T(8,128)(2,1)} %gather_fusion.3, bf16[15,64,64]{2,0,1:T(8,128)(2,1)S(1)} %bitcast.107), kind=kOutput, calls=%fused_computation.28 | convolution fusion | flops 62914560 | bytes 3072000 | tf_op jit(solution)/shard_map/kij,kjm->kim/dot_general | solution.py:104
  119.9 2.2 %fusion.12 = f32[16,64,512]{2,0,1:T(8,128)S(1)} fusion(f32[15,64,512]{2,1,0:T(8,128)S(1)} %convolution_bitcast_fusion, s32[16]{0:T(128)S(1)} %copy-done.20, s32[16]{0:T(128)S(1)} %copy-done.18), kind=kOutput, calls=%fused_computation.22 | convolution fusion | flops 94372560 | bytes 4063360 | tf_op jit(solution)/shard_map/rk,kim->rim/dot_general | solution.py:105
  122.2 2.5 %fusion.10 = bf16[16,64,512]{2,1,0:T(8,128)(2,1)} fusion(f32[16,64,512]{2,0,1:T(8,128)S(1)} %fusion.12, f32[16,512,64]{1,2,0:T(8,128)S(1)} %fusion.30, f32[16,512,64]{1,2,0:T(8,128)S(1)} %copy-done.4, bf16[16,64,512]{2,1,0:T(8,128)(2,1)S(1)} %bitcast.102, bf16[16,64,192]{2,1,0:T(8,128)(2,1)S(1)} %bitcast.101), kind=kOutput, calls=%fused_computation.19 | convolution fusion | flops 69206016 | bytes 8650752 | tf_op jit(solution)/shard_map/rij,rjm->rim/dot_general | solution.py:97
  124.7 3.8 %copy.82 = bf16[16,64,512]{1,0,2:T(8,128)(2,1)} copy(bf16[16,64,512]{2,1,0:T(8,128)(2,1)} %fusion.10) | data formatting | bytes 2097152 | tf_op jit(solution)/shard_map/convert_element_type | solution.py:108
  128.5 4.2 %convert_element_type.38 = bf16[1024,16,32]{0,2,1:T(8,128)(2,1)} reshape(bf16[16,64,512]{1,0,2:T(8,128)(2,1)} %copy.82) | data formatting | bytes 2097152 | tf_op jit(solution)/shard_map/convert_element_type | solution.py:108
  132.8 3.1 %add_convert_fusion = bf16[1024,16,32]{0,2,1:T(8,128)(2,1)} fusion(bf16[1024,16,32]{0,2,1:T(8,128)(2,1)} %convert_element_type.38, bf16[1024,16,32]{0,2,1:T(8,128)(2,1)} %convert_element_type.35, bf16[1024,16,32]{0,2,1:T(8,128)(2,1)S(1)} %fusion.16, bf16[1024,32,32]{0,2,1:T(8,128)(2,1)S(1)} %bitcast.95, bf16[96,32]{0,1:T(8,128)(2,1)S(1)} %copy-done.21), kind=kOutput, calls=%fused_computation.26 | convolution fusion | flops 111673344 | bytes 5249024 | tf_op jit(solution)/shard_map/myv,vi->myi/dot_general | solution.py:120
  135.8 2.3 %copy.83 = bf16[1024,512]{1,0:T(8,128)(2,1)} copy(bf16[1024,512]{0,1:T(8,128)(2,1)} %bitcast.108) | data formatting | bytes 2097152
  (59 shorter events, 3.0 us)
Async XLA Ops:
  0.6 79.9 %copy-start = (bf16[32,256]{1,0:T(8,128)(2,1)S(1)}, bf16[32,256]{1,0:T(8,128)(2,1)}, u32[]{:S(2)}) copy-start(bf16[32,256]{1,0:T(8,128)(2,1)} %param.11) | copy-start | bytes 49156
  4.0 19.0 %all-to-all-start = ((s32[16,1,1]{2,1,0:T(1,128)}), s32[16,1,1]{2,1,0:T(1,128)S(1)}, u32[]{:S(2)}, u32[]{:S(2)}) async-start(s32[16,1,1]{2,1,0:T(1,128)} %copy.73), calls=%async_computation | async-start | bytes 16384 | tf_op jit(solution)/shard_map/all_to_all | solution.py:81
  11.9 2.9 %copy-start.14 = (bf16[64,64]{1,0:T(8,128)(2,1)S(1)}, bf16[64,64]{1,0:T(8,128)(2,1)}, u32[]{:S(2)}) copy-start(bf16[64,64]{1,0:T(8,128)(2,1)} %param.10) | copy-start | bytes 24580
  14.8 1.4 copy-start.2
  24.7 1.6 %copy-start.16 = (s32[1024]{0:T(1024)}, s32[1024]{0:T(1024)S(1)}, u32[]{:S(2)}) copy-start(s32[1024]{0:T(1024)S(1)} %pad_clamp_fusion.1) | copy-start | bytes 12292
  24.7 13.8 %copy-start.13 = (bf16[64,960]{1,0:T(8,128)(2,1)S(1)}, bf16[64,960]{1,0:T(8,128)(2,1)}, u32[]{:S(2)}) copy-start(bf16[64,960]{1,0:T(8,128)(2,1)} %param.14) | copy-start | bytes 368644
  24.7 14.1 %copy-start.12 = (bf16[1024,192]{0,1:T(8,128)(2,1)S(1)}, bf16[1024,192]{0,1:T(8,128)(2,1)}, u32[]{:S(2)}) copy-start(bf16[1024,192]{0,1:T(8,128)(2,1)} %param.13) | copy-start | bytes 1179652
  26.3 41.9 %all-to-all-start.1 = ((bf16[16,64,512]{2,1,0:T(8,128)(2,1)}), bf16[16,64,512]{2,1,0:T(8,128)(2,1)}, u32[]{:S(2)}, u32[]{:S(2)}) async-start(bf16[16,64,512]{2,1,0:T(8,128)(2,1)} %gather_fusion), calls=%async_computation.1 | async-start | bytes 2097152 | tf_op jit(solution)/shard_map/all_to_all | solution.py:87
  33.1 24.0 %collective-permute-start = (bf16[64,512]{0,1:T(8,128)(2,1)}, bf16[64,512]{0,1:T(8,128)(2,1)}, u32[]{:S(2)}, u32[]{:S(2)}) collective-permute-start(bf16[64,512]{0,1:T(8,128)(2,1)} %bitcast.3), channel_id=1, source_target_pairs={{0,1},{1,2},{2,3},{3,4},{4,5},{5,6},{6,7},{7,8},{8,9},{9,10},{10,1... | collective-permute-start | bytes 196616 | tf_op jit(solution)/shard_map/ppermute | solution.py:20
  36.4 22.3 %collective-permute-start.1 = (bf16[64,512]{0,1:T(8,128)(2,1)S(1)}, bf16[64,512]{0,1:T(8,128)(2,1)}, u32[]{:S(2)}, u32[]{:S(2)}) collective-permute-start(bf16[64,512]{0,1:T(8,128)(2,1)S(1)} %bitcast.109), channel_id=1, source_target_pairs={{1,0},{2,1},{3,2},{4,3},{5,4},{6,5},{7,6},{8,7},{9,8},{10,9},{11,1... | collective-permute-start | bytes 196616 | tf_op jit(solution)/shard_map/ppermute | solution.py:23
  39.0 66.0 %copy-start.7 = (bf16[1024,192]{1,0:T(8,128)(2,1)}, bf16[1024,192]{1,0:T(8,128)(2,1)S(1)}, u32[]{:S(2)}) copy-start(bf16[1024,192]{1,0:T(8,128)(2,1)S(1)} %copy.70) | copy-start | bytes 1179652
  40.5 30.0 %copy-start.17 = (s32[16]{0:T(128)}, s32[16]{0:T(128)S(1)}, u32[]{:S(2)}) copy-start(s32[16]{0:T(128)S(1)} %get-tuple-element.22) | copy-start | bytes 196
  40.5 30.0 %copy-start.19 = (s32[16]{0:T(128)}, s32[16]{0:T(128)S(1)}, u32[]{:S(2)}) copy-start(s32[16]{0:T(128)S(1)} %get-tuple-element.23) | copy-start | bytes 196
  42.3 25.9 %copy-start.15 = (s32[1024]{0:T(1024)}, s32[1024]{0:T(1024)S(1)}, u32[]{:S(2)}) copy-start(s32[1024]{0:T(1024)S(1)} %pad_clamp_fusion) | copy-start | bytes 12292
  70.1 2.7 %copy-start.11 = (bf16[1024,512]{1,0:T(8,128)(2,1)S(1)}, bf16[1024,512]{1,0:T(8,128)(2,1)}, u32[]{:S(2)}) copy-start(bf16[1024,512]{1,0:T(8,128)(2,1)} %copy.72) | copy-start | bytes 3145732
  70.5 2.3 %copy-start.5 = (f32[16,512,64]{1,2,0:T(8,128)S(1)}, f32[16,512,64]{1,2,0:T(8,128)}, u32[]{:S(2)}) copy-start(f32[16,512,64]{1,2,0:T(8,128)} %fusion.24) | copy-start | bytes 6291460
  70.5 2.3 %copy-start.6 = (f32[16,512,64]{1,2,0:T(8,128)S(1)}, f32[16,512,64]{1,2,0:T(8,128)}, u32[]{:S(2)}) copy-start(f32[16,512,64]{1,2,0:T(8,128)} %fusion.28) | copy-start | bytes 6291460
  76.0 39.4 %all-to-all-start.2 = ((bf16[16,64,512]{2,1,0:T(8,128)(2,1)}), bf16[16,64,512]{2,1,0:T(8,128)(2,1)}, u32[]{:S(2)}, u32[]{:S(2)}) async-start(bf16[16,64,512]{2,1,0:T(8,128)(2,1)} %gather_fusion.2), calls=%async_computation.2 | async-start | bytes 2097152 | tf_op jit(solution)/shard_map/all_to_all | solution.py:87
  98.3 15.5 %collective-permute-start.3 = (bf16[64,512]{1,0:T(8,128)(2,1)S(1)}, bf16[64,512]{1,0:T(8,128)(2,1)S(1)}, u32[]{:S(2)}, u32[]{:S(2)}) collective-permute-start(bf16[64,512]{1,0:T(8,128)(2,1)S(1)} %get-tuple-element.14), channel_id=1, source_target_pairs={{1,0},{2,1},{3,2},{4,3},{5,4},{6,5},{7,6},{8,7},{9,8},{10,9},{11,1... | collective-permute-start | bytes 196616 | tf_op jit(solution)/shard_map/ppermute | solution.py:23
  100.6 13.2 %collective-permute-start.2 = (bf16[64,512]{1,0:T(8,128)(2,1)S(1)}, bf16[64,512]{1,0:T(8,128)(2,1)S(1)}, u32[]{:S(2)}, u32[]{:S(2)}) collective-permute-start(bf16[64,512]{1,0:T(8,128)(2,1)S(1)} %get-tuple-element.15), channel_id=1, source_target_pairs={{0,1},{1,2},{2,3},{3,4},{4,5},{5,6},{6,7},{7,8},{8,9},{9,10},{10,1... | collective-permute-start | bytes 196616 | tf_op jit(solution)/shard_map/ppermute | solution.py:20
  113.8 1.1 copy-start.8
  115.4 4.5 %copy-start.18 = (s32[16]{0:T(128)S(1)}, s32[16]{0:T(128)}, u32[]{:S(2)}) copy-start(s32[16]{0:T(128)} %copy-done.17) | copy-start | bytes 196
  115.4 4.5 %copy-start.20 = (s32[16]{0:T(128)S(1)}, s32[16]{0:T(128)}, u32[]{:S(2)}) copy-start(s32[16]{0:T(128)} %copy-done.19) | copy-start | bytes 196
  119.9 2.3 %copy-start.4 = (f32[16,512,64]{1,2,0:T(8,128)S(1)}, f32[16,512,64]{1,2,0:T(8,128)}, u32[]{:S(2)}) copy-start(f32[16,512,64]{1,2,0:T(8,128)} %fusion.26) | copy-start | bytes 6291460
  119.9 2.3 %copy-start.9 = (bf16[1024,192]{1,0:T(8,128)(2,1)S(1)}, bf16[1024,192]{1,0:T(8,128)(2,1)}, u32[]{:S(2)}) copy-start(bf16[1024,192]{1,0:T(8,128)(2,1)} %copy-done.7) | copy-start | bytes 1179652
  119.9 2.3 %copy-start.10 = (bf16[1024,512]{1,0:T(8,128)(2,1)S(1)}, bf16[1024,512]{1,0:T(8,128)(2,1)}, u32[]{:S(2)}) copy-start(bf16[1024,512]{1,0:T(8,128)(2,1)} %get-tuple-element.12) | copy-start | bytes 3145732
  128.5 4.2 %copy-start.3 = (bf16[1024,1024]{0,1:T(8,128)(2,1)S(1)}, bf16[1024,1024]{0,1:T(8,128)(2,1)}, u32[]{:S(2)}) copy-start(bf16[1024,1024]{0,1:T(8,128)(2,1)} %copy-done.2) | copy-start | bytes 6291460
  128.5 4.2 %copy-start.21 = (bf16[96,32]{0,1:T(8,128)(2,1)S(1)}, bf16[96,32]{0,1:T(8,128)(2,1)}, u32[]{:S(2)}) copy-start(bf16[96,32]{0,1:T(8,128)(2,1)} %param.12) | copy-start | bytes 18436
  132.8 5.4 %copy-start.1 = (bf16[32,256]{1,0:T(8,128)(2,1)S(1)}, bf16[32,256]{1,0:T(8,128)(2,1)}, u32[]{:S(2)}) copy-start(bf16[32,256]{1,0:T(8,128)(2,1)} %param.11) | copy-start | bytes 49156
where the time goes:
time: 140 us; the launch traced here: 138 us
  local copies, waits for them, and re-layouts  54.4 us (39%)
  starting transfers between devices  29.2 us (21%)
  matrix products  28.4 us (20%)
  waiting for transfers between devices  16.4 us (12%)
  other arithmetic  8.73 us (6%)
    unnamed x48, local copies, waits for them, and re-layouts  17.9 us
    convert_element_type x4, local copies, waits for them, and re-layouts, diffuse(): return summed.reshape(node_rows, field_rows.shape[1]).astype(jnp.bfloat16)  15 us
    ppermute x2, waiting for transfers between devices, padded_2(): lax.ppermute(lax.slice_in_dim(block, block.shape[dim] - width, None, axis...  14.7 us
    dot_general x6, matrix products, diffuse(): jnp.einsum('rij,rjm->rim', band_blocks[:, :, shift_pos * BLK:(shift_pos +...  11 us
    all_to_all x2, starting transfers between devices, fetch_far(): lax.all_to_all(field_blocks[send_rows], 'node', split_axis=0, concat_axis...  10.5 us
    slice x4, local copies, waits for them, and re-layouts, diffuse(): padded_blocks[shift_pos:shift_pos + blocks]  8.43 us
    ppermute x2, starting transfers between devices, padded_2(): lax.ppermute(lax.slice_in_dim(block, block.shape[dim] - width, None, axis...  7.74 us
    all_to_all x1, starting transfers between devices, local(): lax.all_to_all(wanted[:, None], 'node', split_axis=0, concat_axis=0, tile...  6.55 us
  transfers between devices with their start and end apart: 7, of which 2 were waited for; matrix products, arithmetic and copies ran while one was open for 39% of the time, Pallas kernels for 0%

commit v1 on v0

v1 whole, which is shorter than its diff:
```python
import jax
import jax.numpy as jnp
from jax import lax
from jax.experimental import pallas as pl
from jax.experimental.pallas import tpu as pltpu
from jax.sharding import PartitionSpec as P

BLK = 64
TOUT = 16
DILATION_STEP = 16
EXPORT = 2
CHANNEL_WIDTH = 32
S = 256
TIN = 32
CHUNK = 256
ROW_TILE = 256

f32 = jnp.float32
bf16 = jnp.bfloat16


def front_kernel(x_ref, wlo_ref, whi_ref, ws_ref, h_ref, s_ref):
    half = x_ref.shape[1] // 2
    chunks = half // CHUNK
    skip_w = ws_ref.shape[1]
    for j in range(chunks):
        x0 = x_ref[:, j * CHUNK : (j + 1) * CHUNK]
        x1 = x_ref[:, half + j * CHUNK : half + (j + 1) * CHUNK]
        pre = jnp.dot(x0, wlo_ref[...], preferred_element_type=f32)
        pre = pre + jnp.dot(x1, whi_ref[...], preferred_element_type=f32)
        h = (jnp.tanh(pre[:, :CHUNK]) * jax.nn.sigmoid(pre[:, CHUNK:])).astype(bf16)
        h_ref[:, j * CHUNK : (j + 1) * CHUNK] = h
        s_ref[:, j * skip_w : (j + 1) * skip_w] = jnp.dot(
            h, ws_ref[...], preferred_element_type=f32
        ).astype(bf16)


def front(features, wlo, whi, ws):
    rows, cols = features.shape
    half = cols // 2
    skip_cols = ws.shape[1] * (half // CHUNK)
    tile = min(ROW_TILE, rows)
    return pl.pallas_call(
        front_kernel,
        grid=(rows // tile,),
        in_specs=[
            pl.BlockSpec((tile, cols), lambda i: (i, 0)),
            pl.BlockSpec(wlo.shape, lambda i: (0, 0)),
            pl.BlockSpec(whi.shape, lambda i: (0, 0)),
            pl.BlockSpec(ws.shape, lambda i: (0, 0)),
        ],
        out_specs=[
            pl.BlockSpec((tile, half), lambda i: (i, 0)),
            pl.BlockSpec((tile, skip_cols), lambda i: (i, 0)),
        ],
        out_shape=[
            jax.ShapeDtypeStruct((rows, half), bf16),
            jax.ShapeDtypeStruct((rows, skip_cols), bf16),
        ],
        compiler_params=pltpu.CompilerParams(vmem_limit_bytes=48 * 1024 * 1024),
        cost_estimate=pl.CostEstimate(
            flops=2 * rows * CHUNK * (4 * CHUNK + ws.shape[1]) * (half // CHUNK),
            transcendentals=rows * half * 2,
            bytes_accessed=2 * rows * (cols + half + skip_cols),
        ),
    )(features, wlo, whi, ws)


def accumulate(src_ref, row_ref, field_ref, lo_ref, hi_ref, arr_ref, band_ref, farw_ref, acc):
    nblk = field_ref.shape[0] // BLK
    far_cap = farw_ref.shape[0]
    for r in range(nblk):
        prev = lo_ref[...] if r == 0 else field_ref[(r - 1) * BLK : r * BLK, :]
        nxt = hi_ref[...] if r == nblk - 1 else field_ref[(r + 1) * BLK : (r + 2) * BLK, :]
        own = field_ref[r * BLK : (r + 1) * BLK, :]
        v = jnp.dot(band_ref[0, r * BLK : (r + 1) * BLK, :], prev, preferred_element_type=f32)
        v = v + jnp.dot(band_ref[1, r * BLK : (r + 1) * BLK, :], own, preferred_element_type=f32)
        v = v + jnp.dot(band_ref[2, r * BLK : (r + 1) * BLK, :], nxt, preferred_element_type=f32)
        acc[r * BLK : (r + 1) * BLK, :] = v
    acc[nblk * BLK :, :] = jnp.zeros((BLK, acc.shape[1]), f32)

    def slot(k, carry):
        row = row_ref[k]
        piece = arr_ref[src_ref[k]]
        start = pl.multiple_of(row * BLK, BLK)
        acc[pl.ds(start, BLK), :] += jnp.dot(farw_ref[k], piece, preferred_element_type=f32)
        return carry

    lax.fori_loop(0, far_cap, slot, 0)


def hop1_kernel(
    src_ref, row_ref, send_ref, field_ref, lo_ref, hi_ref, arr_ref, band_ref, farw_ref,
    out_ref, out_send_ref, acc,
):
    accumulate(src_ref, row_ref, field_ref, lo_ref, hi_ref, arr_ref, band_ref, farw_ref, acc)
    nrows = field_ref.shape[0]
    out_ref[...] = acc[:nrows, :].astype(bf16)
    for p in range(out_send_ref.shape[0]):
        start = pl.multiple_of(send_ref[p] * BLK, BLK)
        out_send_ref[p] = out_ref[pl.ds(start, BLK), :]


def hop2_kernel(
    src_ref, row_ref, field_ref, lo_ref, hi_ref, arr_ref, band_ref, farw_ref,
    x_ref, h_ref, mix_ref, out_ref, acc,
):
    accumulate(src_ref, row_ref, field_ref, lo_ref, hi_ref, arr_ref, band_ref, farw_ref, acc)
    nrows, width = field_ref.shape
    half = x_ref.shape[1] // 2
    for j in range(width // CHUNK):
        cols = slice(j * CHUNK, (j + 1) * CHUNK)
        two = acc[:nrows, cols].astype(bf16)
        v = x_ref[:, half + j * CHUNK : half + (j + 1) * CHUNK].astype(f32)
        v = v + jnp.dot(h_ref[:, cols], mix_ref[0], preferred_element_type=f32)
        v = v + jnp.dot(field_ref[:, cols], mix_ref[1], preferred_element_type=f32)
        v = v + jnp.dot(two, mix_ref[2], preferred_element_type=f32)
        out_ref[:, cols] = v.astype(bf16)


def vmem():
    return pl.BlockSpec(memory_space=pltpu.VMEM)


def smem():
    return pl.BlockSpec(memory_space=pltpu.SMEM)


def hop1(src, rows, send_rows, field, lo, hi, arrived, band3, farw3):
    nrows, width = field.shape
    return pl.pallas_call(
        hop1_kernel,
        in_specs=[smem(), smem(), smem()] + [vmem()] * 6,
        out_specs=[vmem(), vmem()],
        out_shape=[
            jax.ShapeDtypeStruct((nrows, width), bf16),
            jax.ShapeDtypeStruct(arrived.shape, bf16),
        ],
        scratch_shapes=[pltpu.VMEM((nrows + BLK, width), f32)],
        compiler_params=pltpu.CompilerParams(vmem_limit_bytes=48 * 1024 * 1024),
        cost_estimate=pl.CostEstimate(
            flops=2 * BLK * BLK * width * (3 * nrows // BLK + farw3.shape[0]),
            transcendentals=0,
            bytes_accessed=2 * width * (nrows * 2 + 2 * arrived.shape[0] * BLK),
        ),
    )(src, rows, send_rows, field, lo, hi, arrived, band3, farw3)


def hop2(src, rows, field, lo, hi, arrived, band3, farw3, features, hidden, mix3):
    nrows, width = field.shape
    return pl.pallas_call(
        hop2_kernel,
        in_specs=[smem(), smem()] + [vmem()] * 9,
        out_specs=vmem(),
        out_shape=jax.ShapeDtypeStruct((nrows, width), bf16),
        scratch_shapes=[pltpu.VMEM((nrows + BLK, width), f32)],
        compiler_params=pltpu.CompilerParams(vmem_limit_bytes=48 * 1024 * 1024),
        cost_estimate=pl.CostEstimate(
            flops=2 * BLK * BLK * width * (3 * nrows // BLK + farw3.shape[0])
            + 2 * nrows * width * CHUNK * 3,
            transcendentals=0,
            bytes_accessed=2 * width * (nrows * 6 + arrived.shape[0] * BLK),
        ),
    )(src, rows, field, lo, hi, arrived, band3, farw3, features, hidden, mix3)


def halo(field):
    count = lax.axis_size("node")
    forward = [(i, i + 1) for i in range(count - 1)]
    backward = [(t, s) for s, t in forward]
    lo = lax.ppermute(field[field.shape[0] - BLK :], "node", forward)
    hi = lax.ppermute(field[:BLK], "node", backward)
    return lo, hi


def local(
    features,
    filter_gate_weight,
    skip_weight,
    mix_weight,
    band_weight,
    far_weight,
    far_ptr,
    far_col,
    export_block,
):
    node_rows = features.shape[0]
    blocks = node_rows // BLK
    far_cap = far_col.shape[1]
    peer_count = far_cap + 1
    cw = CHANNEL_WIDTH
    per = CHUNK // cw

    eye = jnp.eye(per, dtype=bf16)
    fgw = filter_gate_weight
    wlo = jnp.concatenate([jnp.kron(eye, fgw[:cw, :cw]), jnp.kron(eye, fgw[:cw, cw:])], axis=1)
    whi = jnp.concatenate([jnp.kron(eye, fgw[cw:, :cw]), jnp.kron(eye, fgw[cw:, cw:])], axis=1)
    ws = jnp.kron(eye, skip_weight)
    mix3 = jnp.stack([jnp.kron(eye, mix_weight[i * cw : (i + 1) * cw]) for i in range(3)])

    hidden, skip_out = front(features, wlo, whi, ws)

    own_index = lax.axis_index("node")
    own_exports = lax.dynamic_slice_in_dim(export_block, own_index, 1, 0)[0]
    columns = far_col[0]
    sources = columns // EXPORT
    slot_export = columns % EXPORT
    pointers = far_ptr[0]
    slot_ids = jnp.arange(far_cap, dtype=jnp.int32)
    slot_rows = jnp.sum(
        (pointers[1:, None] <= slot_ids[None, :]).astype(jnp.int32), axis=0
    ).astype(jnp.int32)
    in_use = slot_ids < pointers[-1]
    matches = (sources[None, :] == jnp.arange(peer_count, dtype=jnp.int32)[:, None]) & in_use[
        None, :
    ]
    wanted = jnp.sum(jnp.where(matches, slot_export[None, :], 0), axis=1)
    requested = lax.all_to_all(wanted[:, None], "node", split_axis=0, concat_axis=0, tiled=True)[
        :, 0
    ]
    send_rows = own_exports[requested].astype(jnp.int32)

    width = hidden.shape[1]
    band3 = band_weight.reshape(node_rows, 3, BLK).transpose(1, 0, 2)
    farw3 = far_weight.reshape(BLK, far_cap, BLK).transpose(1, 0, 2)

    def exchange(send):
        return lax.all_to_all(send, "node", split_axis=0, concat_axis=0, tiled=True)

    send1 = hidden.reshape(blocks, BLK, width)[send_rows]
    arrived1 = exchange(send1)
    lo1, hi1 = halo(hidden)
    hop_one, send2 = hop1(sources, slot_rows, send_rows, hidden, lo1, hi1, arrived1, band3, farw3)
    arrived2 = exchange(send2)
    lo2, hi2 = halo(hop_one)
    residual = hop2(
        sources, slot_rows, hop_one, lo2, hi2, arrived2, band3, farw3, features, hidden, mix3
    )
    return residual, skip_out


def solution(mesh):
    placed = (
        P(("groups", "node"), None),
        P(),
        P(),
        P(),
        P("node", None),
        P(None, "node"),
        P("node", None),
        P("node", None),
        P(),
    )
    return jax.shard_map(
        local,
        mesh=mesh,
        in_specs=placed,
        out_specs=(P(("groups", "node"), None), P(("groups", "node"), None)),
        check_vma=False,
    )
```

time: 140 us -> 111 us (0.79)
  matrix products: 28.4 us -> 0 us
  local copies, waits for them, and re-layouts: 54.4 us -> 28.4 us
  Pallas kernels: 0 us -> 16.6 us
  waiting for transfers between devices: 16.4 us -> 27.1 us
  other arithmetic: 8.73 us -> 6.76 us
    dot_general x14 -> x0, matrix products: 28.4 us -> none  [the longest x6 11 us: diffuse(): jnp.einsum('rij,rjm->rim', band_blocks[:, :, shift_pos * BLK:(shift_pos +...]
    pallas_call x0 -> x3, Pallas kernels: none -> 16.6 us  [the longest x1 6.65 us: hop2(): pl.pallas_call(hop2_kernel, in_specs=[smem(), smem()] + [vmem()] * 9, out...]
    convert_element_type x4 -> x0, local copies, waits for them, and re-layouts: 15 us -> none  [diffuse(): return summed.reshape(node_rows, field_rows.shape[1]).astype(jnp.bfloat16)]
    ppermute x4, waiting for transfers between devices: 16.4 us -> 27.1 us  [the longest x2 27.1 us: halo(): hi = lax.ppermute(field[:BLK], 'node', backward)]
    mul x0 -> x7, local copies, waits for them, and re-layouts: none -> 9.87 us  [the longest x3 6.3 us: local(): jnp.kron(eye, mix_weight[i * cw:(i + 1) * cw])]
    unnamed x48 -> x25, local copies, waits for them, and re-layouts: 17.9 us -> 8.63 us
    gather x5 -> x2, local copies, waits for them, and re-layouts: 8.62 us -> 2.16 us  [the longest x1 1.58 us: local(): send1 = hidden.reshape(blocks, BLK, width)[send_rows]]
    slice x6 -> x7, local copies, waits for them, and re-layouts: 9.2 us -> 2.9 us  [the longest x4 1.14 us: local(): mix_weight[i * cw:(i + 1) * cw]]
  transfers between devices with their start and end apart: 7 -> 7, of which waited for: 2 -> 2; matrix products, arithmetic and copies ran while one was open for 39% -> 19% of each run, Pallas kernels for 0% -> 6%
where the time goes in v1:
time: 111 us; the launch traced here: 110 us
  starting transfers between devices  30 us (27%)
  local copies, waits for them, and re-layouts  28.4 us (26%)
  waiting for transfers between devices  27.1 us (24%)
  Pallas kernels  16.6 us (15%)
  other arithmetic  6.76 us (6%)
    ppermute x2, waiting for transfers between devices, halo(): hi = lax.ppermute(field[:BLK], 'node', backward)  27.1 us
    all_to_all x2, starting transfers between devices, exchange(): return lax.all_to_all(send, 'node', split_axis=0, concat_axis=0, tiled=True)  10.6 us
    unnamed x25, local copies, waits for them, and re-layouts  8.63 us
    ppermute x2, starting transfers between devices, halo(): lo = lax.ppermute(field[field.shape[0] - BLK:], 'node', forward)  8.38 us
    pallas_call x1, Pallas kernels, hop2(): pl.pallas_call(hop2_kernel, in_specs=[smem(), smem()] + [vmem()] * 9, out...  6.65 us
    all_to_all x1, starting transfers between devices, local(): lax.all_to_all(wanted[:, None], 'node', split_axis=0, concat_axis=0, tile...  6.55 us
    mul x3, local copies, waits for them, and re-layouts, local(): jnp.kron(eye, mix_weight[i * cw:(i + 1) * cw])  6.3 us
    pallas_call x1, Pallas kernels, front(): pl.pallas_call(front_kernel, grid=(rows // tile,), in_specs=[pl.BlockSpec...  6.13 us
  transfers between devices with their start and end apart: 7, of which 2 were waited for; matrix products, arithmetic and copies ran while one was open for 19% of the time, Pallas kernels for 6%

profile of v1, /device:TPU:15, one launch (start us, length us, event | category | flops | bytes accessed | tf_op | source)
XLA Modules:
  0.0 109.7 jit_solution(1260088622582267298)
XLA Ops:
  0.7 1.4 %slice.42 = s32[1,1]{1,0:T(1,128)} slice(s32[1,17]{1,0:T(1,128)} %param.15), slice={[0:1], [16:17]} | slice | bytes 8 | tf_op jit(solution)/shard_map/slice | solution.py:213
  2.0 0.6 iota_compare_fusion.3
  2.7 0.7 fusion.4
  3.4 0.1 select_reduce_fusion
  3.5 0.7 copy.31
  4.2 6.6 %all-to-all-start = ((s32[16,1,1]{2,1,0:T(1,128)}), s32[16,1,1]{2,1,0:T(1,128)S(1)}, u32[]{:S(2)}, u32[]{:S(2)}) async-start(s32[16,1,1]{2,1,0:T(1,128)} %copy.31), calls=%async_computation | async-start | bytes 16384 | tf_op jit(solution)/shard_map/all_to_all | solution.py:218
  10.7 0.9 fusion.9
  11.6 0.1 copy.34
  11.7 0.1 copy.36
  11.9 0.9 fusion.8
  12.7 0.9 broadcast_multiply_fusion
  13.6 1.3 %copy.37 = bf16[32,8,8,256]{3,1,2,0:T(8,128)(2,1)} copy(bf16[32,8,8,256]{3,2,1,0:T(8,128)(2,1)S(1)} %bitcast.57) | data formatting | bytes 2097152
  14.9 1.6 %broadcast_multiply_fusion.3 = (bf16[8,32,8,32]{3,2,1,0:T(8,128)(2,1)}, bf16[8,32,8,32]{3,2,1,0:T(8,128)(2,1)}, bf16[8,32,8,32]{3,2,1,0:T(8,128)(2,1)}, bf16[8,3...) fusion(bf16[32,32]{1,0:T(8,128)(2,1)S(1)} %copy.34, ...), kind=kLoop, calls=%fused_computation.7 | loop fusion | flops 458752 | bytes 931968 | tf_op jit(solution)/shard_map/jit(kron)/mul | solution.py:199
  16.5 1.4 %mul.174 = bf16[256,256]{1,0:T(8,128)(2,1)S(1)} reshape(bf16[8,32,8,32]{3,2,1,0:T(8,128)(2,1)} %get-tuple-element.22) | data formatting | bytes 262144 | tf_op jit(solution)/shard_map/jit(kron)/mul | solution.py:196
  17.9 1.4 %mul.177 = bf16[256,256]{1,0:T(8,128)(2,1)S(1)} reshape(bf16[8,32,8,32]{3,2,1,0:T(8,128)(2,1)} %get-tuple-element.23) | data formatting | bytes 262144 | tf_op jit(solution)/shard_map/jit(kron)/mul | solution.py:197
  19.4 0.4 mul.180
  19.7 0.4 mul.171
  20.2 1.2 %copy-done.4 = bf16[32,8,8,256]{3,1,2,0:T(8,128)(2,1)S(1)} copy-done((bf16[32,8,8,256]{3,1,2,0:T(8,128)(2,1)S(1)}, bf16[32,8,8,256]{3,1,2,0:T(8,128)(2,1)}, u32[]{:S(2)}) %copy-start.4) | copy-done | bytes 1048600
  21.4 6.1 %shard_map.104 = (bf16[1024,512]{1,0:T(8,128)(2,1)S(1)}, bf16[1024,4096]{1,0:T(8,128)(2,1)}) custom-call(bf16[1024,1024]{1,0:T(8,128)(2,1)S(1)} %copy-done.1, bf16[256,512]{1,0:T(8,128)(2,1)S(1)} %get-tuple-element.34.wlo_ref, bf16[256,512]{1,0:T(8,128)(2,1)S(1)} %get-tuple-element.35.whi_ref, bf16[256,2048]{1,0:T(8,128)(2,1)S(1)} %bitcast.56), custom_call_target="tpu_custom_call" | custom-call | flops 3221225472 | bytes 11534336 | tf_op jit(solution)/shard_map/pallas_call | solution.py:43
  27.6 0.6 fusion.10
  28.2 0.4 reduce
  28.5 1.3 %fusion.3 = (s32[16]{0:T(128)S(1)}, s32[16]{0:T(128)S(1)}) fusion(s32[]{:T(128)} %bitcast.7, s32[]{:T(128)} %bitcast.6, s32[16]{0:T(128)S(1)} %reduce), kind=kLoop, calls=%fused_computation.34 | loop fusion | flops 128 | bytes 200 | tf_op jit(solution)/shard_map/select_n | solution.py:230
  29.8 1.6 %gather_fusion = bf16[16,64,512]{2,1,0:T(8,128)(2,1)} fusion(bf16[16,64,512]{2,1,0:T(8,128)(2,1)S(1)} %bitcast.51, s32[1024]{0:T(1024)S(1)} %pad_clamp_fusion), kind=kCustom, calls=%fused_computation | custom fusion | bytes 2097216 | tf_op jit(solution)/shard_map/gather | solution.py:230
  31.4 6.0 %all-to-all-start.1 = ((bf16[16,64,512]{2,1,0:T(8,128)(2,1)}), bf16[16,64,512]{2,1,0:T(8,128)(2,1)S(1)}, u32[]{:S(2)}, u32[]{:S(2)}) async-start(bf16[16,64,512]{2,1,0:T(8,128)(2,1)} %gather_fusion), calls=%async_computation.1 | async-start | bytes 2097152 | tf_op jit(solution)/shard_map/all_to_all | solution.py:228
  37.4 2.3 %collective-permute-start.1 = (bf16[64,512]{1,0:T(8,128)(2,1)S(1)}, bf16[64,512]{1,0:T(8,128)(2,1)S(1)}, u32[]{:S(2)}, u32[]{:S(2)}) collective-permute-start(bf16[64,512]{1,0:T(8,128)(2,1)S(1)} %get-tuple-element.12), channel_id=1, source_target_pairs={{1,0},{2,1},{3,2},{4,3},{5,4},{6,5},{7,6},{8,7},{9,8},{10,9},{11,1... | collective-permute-start | bytes 196616 | tf_op jit(solution)/shard_map/ppermute | solution.py:172
  39.7 4.2 %collective-permute-start = (bf16[64,512]{1,0:T(8,128)(2,1)S(1)}, bf16[64,512]{1,0:T(8,128)(2,1)S(1)}, u32[]{:S(2)}, u32[]{:S(2)}) collective-permute-start(bf16[64,512]{1,0:T(8,128)(2,1)S(1)} %get-tuple-element.13), channel_id=1, source_target_pairs={{0,1},{1,2},{2,3},{3,4},{4,5},{5,6},{6,7},{7,8},{8,9},{9,10},{10,1... | collective-permute-start | bytes 196616 | tf_op jit(solution)/shard_map/ppermute | solution.py:171
  43.9 1.1 %reshape.177 = bf16[64,15,64]{2,1,0:T(8,128)(2,1)S(1)} reshape(bf16[64,960]{1,0:T(8,128)(2,1)} %param.14) | data formatting | bytes 245760 | tf_op jit(solution)/shard_map/reshape | solution.py:225
  45.1 1.4 %copy.32 = bf16[1024,3,64]{2,0,1:T(8,128)(2,1)S(1)} copy(bf16[1024,3,64]{0,2,1:T(8,128)(2,1)} %bitcast.58) | data formatting | bytes 786432 | tf_op jit(solution)/shard_map/reshape | solution.py:224
  46.6 0.1 convert_reduce_fusion.row_ref
  46.7 16.3 %collective-permute-done.1.hi_ref = bf16[64,512]{1,0:T(8,128)(2,1)S(1)} collective-permute-done((bf16[64,512]{1,0:T(8,128)(2,1)S(1)}, bf16[64,512]{1,0:T(8,128)(2,1)S(1)}, u32[]{:S(2)}, u32[]{:S(2)}) %collective-permute-start.1) | collective-permute-done | bytes 65568 | tf_op jit(solution)/shard_map/ppermute | solution.py:172
  63.0 3.8 %shard_map.105 = (bf16[1024,512]{1,0:T(8,128)(2,1)S(1)}, bf16[16,64,512]{2,1,0:T(8,128)(2,1)S(1)}) custom-call(s32[15]{0:T(128)S(1)} %and_select_fusion.2.src_ref, s32[15]{0:T(128)S(1)} %convert_reduce_fusion.row_ref, s32[16]{0:T(128)S(1)} %get-tuple-element.31.send_ref, bf16[1024,512]{1,0:T(8,128)(2,1)S(1)} %get-tuple-element.6.field_ref.h_ref, ...), custom_call_target="tpu_custom_call" | custom-call | flops 264241152 | bytes 4194304 | tf_op jit(solution)/shard_map/pallas_call | solution.py:131
  66.8 1.0 copy-done.2
  67.8 1.0 copy-done.5
  68.8 4.5 %all-to-all-start.2 = ((bf16[16,64,512]{2,1,0:T(8,128)(2,1)}), bf16[16,64,512]{2,1,0:T(8,128)(2,1)S(1)}, u32[]{:S(2)}, u32[]{:S(2)}) async-start(bf16[16,64,512]{2,1,0:T(8,128)(2,1)} %copy-done.5), calls=%async_computation.2 | async-start | bytes 2097152 | tf_op jit(solution)/shard_map/all_to_all | solution.py:228
  73.3 2.1 %mul.187 = bf16[1,256,256]{2,1,0:T(8,128)(2,1)} reshape(bf16[8,32,8,32]{3,2,1,0:T(8,128)(2,1)} %get-tuple-element.21) | data formatting | bytes 262144 | tf_op jit(solution)/shard_map/jit(kron)/mul | solution.py:199
  75.4 2.1 %mul.190 = bf16[1,256,256]{2,1,0:T(8,128)(2,1)} reshape(bf16[8,32,8,32]{3,2,1,0:T(8,128)(2,1)} %get-tuple-element.25) | data formatting | bytes 262144 | tf_op jit(solution)/shard_map/jit(kron)/mul | solution.py:199
  77.6 2.1 %mul.193 = bf16[1,256,256]{2,1,0:T(8,128)(2,1)} reshape(bf16[8,32,8,32]{3,2,1,0:T(8,128)(2,1)} %get-tuple-element.26) | data formatting | bytes 262144 | tf_op jit(solution)/shard_map/jit(kron)/mul | solution.py:199
  79.6 0.9 fusion.6
  80.5 2.3 %collective-permute-start.3 = (bf16[64,512]{1,0:T(8,128)(2,1)S(1)}, bf16[64,512]{1,0:T(8,128)(2,1)S(1)}, u32[]{:S(2)}, u32[]{:S(2)}) collective-permute-start(bf16[64,512]{1,0:T(8,128)(2,1)S(1)} %get-tuple-element.10), channel_id=1, source_target_pairs={{1,0},{2,1},{3,2},{4,3},{5,4},{6,5},{7,6},{8,7},{9,8},{10,9},{11,1... | collective-permute-start | bytes 196616 | tf_op jit(solution)/shard_map/ppermute | solution.py:172
  82.8 4.2 %collective-permute-start.2 = (bf16[64,512]{1,0:T(8,128)(2,1)S(1)}, bf16[64,512]{1,0:T(8,128)(2,1)S(1)}, u32[]{:S(2)}, u32[]{:S(2)}) collective-permute-start(bf16[64,512]{1,0:T(8,128)(2,1)S(1)} %get-tuple-element.11), channel_id=1, source_target_pairs={{0,1},{1,2},{2,3},{3,4},{4,5},{5,6},{6,7},{7,8},{8,9},{9,10},{10,1... | collective-permute-start | bytes 196616 | tf_op jit(solution)/shard_map/ppermute | solution.py:171
  87.0 1.1 pad_maximum_fusion.mix_ref
  88.1 10.8 %collective-permute-done.3.hi_ref = bf16[64,512]{1,0:T(8,128)(2,1)S(1)} collective-permute-done((bf16[64,512]{1,0:T(8,128)(2,1)S(1)}, bf16[64,512]{1,0:T(8,128)(2,1)S(1)}, u32[]{:S(2)}, u32[]{:S(2)}) %collective-permute-start.3) | collective-permute-done | bytes 65568 | tf_op jit(solution)/shard_map/ppermute | solution.py:172
  98.9 0.6 copy-done.6
  99.5 0.6 copy-done.8
  100.2 1.2 %copy-done.3 = bf16[1024,512]{1,0:T(8,128)(2,1)S(1)} copy-done((bf16[1024,512]{1,0:T(8,128)(2,1)S(1)}, bf16[1024,512]{1,0:T(8,128)(2,1)}, u32[]{:S(2)}) %copy-start.3) | copy-done | bytes 1048600
  101.4 0.8 copy-done.7
  102.2 0.8 copy-done.9
  103.1 6.6 %shard_map.106 = bf16[1024,512]{1,0:T(8,128)(2,1)} custom-call(s32[15]{0:T(128)S(1)} %and_select_fusion.2.src_ref, s32[15]{0:T(128)S(1)} %convert_reduce_fusion.row_ref, bf16[1024,512]{1,0:T(8,128)(2,1)S(1)} %copy-done.3, bf16[64,512]{1,0:T(8,128)(2,1)S(1)} %copy-done.9, bf16[64,512]{1,0:T(8,128)(2,1)S(1)} %copy-done.7, ...), custom_call_target="tpu_custom_call" | custom-call | flops 1069547520 | bytes 7340032 | tf_op jit(solution)/shard_map/pallas_call | solution.py:151
  (30 shorter events, 0.4 us)
Async XLA Ops:
  0.6 19.4 %copy-start = (s32[16,2]{0,1:T(2,128)S(1)}, s32[16,2]{0,1:T(2,128)}, u32[]{:S(2)}) copy-start(s32[16,2]{0,1:T(2,128)} %param.17) | copy-start | bytes 388
  0.6 19.6 %copy-start.1 = (bf16[1024,1024]{1,0:T(8,128)(2,1)S(1)}, bf16[1024,1024]{1,0:T(8,128)(2,1)}, u32[]{:S(2)}) copy-start(bf16[1024,1024]{1,0:T(8,128)(2,1)} %x_ref.3) | copy-start | bytes 6291460
  4.2 24.0 %all-to-all-start = ((s32[16,1,1]{2,1,0:T(1,128)}), s32[16,1,1]{2,1,0:T(1,128)S(1)}, u32[]{:S(2)}, u32[]{:S(2)}) async-start(s32[16,1,1]{2,1,0:T(1,128)} %copy.31), calls=%async_computation | async-start | bytes 16384 | tf_op jit(solution)/shard_map/all_to_all | solution.py:218
  20.2 1.2 %copy-start.4 = (bf16[32,8,8,256]{3,1,2,0:T(8,128)(2,1)S(1)}, bf16[32,8,8,256]{3,1,2,0:T(8,128)(2,1)}, u32[]{:S(2)}) copy-start(bf16[32,8,8,256]{3,1,2,0:T(8,128)(2,1)} %copy.37) | copy-start | bytes 3145732
  21.4 25.1 %copy-start.10 = (s32[1,15]{1,0:T(1,128)S(1)}, s32[1,15]{1,0:T(1,128)}, u32[]{:S(2)}) copy-start(s32[1,15]{1,0:T(1,128)} %param.16) | copy-start | bytes 184
  21.4 25.1 %copy-start.11 = (s32[1,17]{1,0:T(1,128)S(1)}, s32[1,17]{1,0:T(1,128)}, u32[]{:S(2)}) copy-start(s32[1,17]{1,0:T(1,128)} %param.15) | copy-start | bytes 208
  31.4 31.6 %all-to-all-start.1 = ((bf16[16,64,512]{2,1,0:T(8,128)(2,1)}), bf16[16,64,512]{2,1,0:T(8,128)(2,1)S(1)}, u32[]{:S(2)}, u32[]{:S(2)}) async-start(bf16[16,64,512]{2,1,0:T(8,128)(2,1)} %gather_fusion), calls=%async_computation.1 | async-start | bytes 2097152 | tf_op jit(solution)/shard_map/all_to_all | solution.py:228
  37.4 25.5 %collective-permute-start.1 = (bf16[64,512]{1,0:T(8,128)(2,1)S(1)}, bf16[64,512]{1,0:T(8,128)(2,1)S(1)}, u32[]{:S(2)}, u32[]{:S(2)}) collective-permute-start(bf16[64,512]{1,0:T(8,128)(2,1)S(1)} %get-tuple-element.12), channel_id=1, source_target_pairs={{1,0},{2,1},{3,2},{4,3},{5,4},{6,5},{7,6},{8,7},{9,8},{10,9},{11,1... | collective-permute-start | bytes 196616 | tf_op jit(solution)/shard_map/ppermute | solution.py:172
  39.7 23.3 %collective-permute-start = (bf16[64,512]{1,0:T(8,128)(2,1)S(1)}, bf16[64,512]{1,0:T(8,128)(2,1)S(1)}, u32[]{:S(2)}, u32[]{:S(2)}) collective-permute-start(bf16[64,512]{1,0:T(8,128)(2,1)S(1)} %get-tuple-element.13), channel_id=1, source_target_pairs={{0,1},{1,2},{2,3},{3,4},{4,5},{5,6},{6,7},{7,8},{8,9},{9,10},{10,1... | collective-permute-start | bytes 196616 | tf_op jit(solution)/shard_map/ppermute | solution.py:171
  66.8 1.0 copy-start.2
  67.8 1.0 copy-start.5
  68.8 31.4 %all-to-all-start.2 = ((bf16[16,64,512]{2,1,0:T(8,128)(2,1)}), bf16[16,64,512]{2,1,0:T(8,128)(2,1)S(1)}, u32[]{:S(2)}, u32[]{:S(2)}) async-start(bf16[16,64,512]{2,1,0:T(8,128)(2,1)} %copy-done.5), calls=%async_computation.2 | async-start | bytes 2097152 | tf_op jit(solution)/shard_map/all_to_all | solution.py:228
  80.5 18.4 %collective-permute-start.3 = (bf16[64,512]{1,0:T(8,128)(2,1)S(1)}, bf16[64,512]{1,0:T(8,128)(2,1)S(1)}, u32[]{:S(2)}, u32[]{:S(2)}) collective-permute-start(bf16[64,512]{1,0:T(8,128)(2,1)S(1)} %get-tuple-element.10), channel_id=1, source_target_pairs={{1,0},{2,1},{3,2},{4,3},{5,4},{6,5},{7,6},{8,7},{9,8},{10,9},{11,1... | collective-permute-start | bytes 196616 | tf_op jit(solution)/shard_map/ppermute | solution.py:172
  82.8 16.7 %collective-permute-start.2 = (bf16[64,512]{1,0:T(8,128)(2,1)S(1)}, bf16[64,512]{1,0:T(8,128)(2,1)S(1)}, u32[]{:S(2)}, u32[]{:S(2)}) collective-permute-start(bf16[64,512]{1,0:T(8,128)(2,1)S(1)} %get-tuple-element.11), channel_id=1, source_target_pairs={{0,1},{1,2},{2,3},{3,4},{4,5},{5,6},{6,7},{7,8},{8,9},{9,10},{10,1... | collective-permute-start | bytes 196616 | tf_op jit(solution)/shard_map/ppermute | solution.py:171
  98.9 0.6 copy-start.6
  99.5 0.6 copy-start.8
  100.2 1.2 %copy-start.3 = (bf16[1024,512]{1,0:T(8,128)(2,1)S(1)}, bf16[1024,512]{1,0:T(8,128)(2,1)}, u32[]{:S(2)}) copy-start(bf16[1024,512]{1,0:T(8,128)(2,1)} %copy-done.2) | copy-start | bytes 3145732
  101.4 0.8 copy-start.7
  102.2 0.8 copy-start.9

commit v2 on v1

--- a/solution.py
+++ b/solution.py
@@ -19,51 +19,68 @@
 bf16 = jnp.bfloat16
 
 
-def front_kernel(x_ref, wlo_ref, whi_ref, ws_ref, h_ref, s_ref):
+def hidden_kernel(x_ref, wlo_ref, whi_ref, h_ref):
     half = x_ref.shape[1] // 2
-    chunks = half // CHUNK
-    skip_w = ws_ref.shape[1]
-    for j in range(chunks):
+    for j in range(half // CHUNK):
         x0 = x_ref[:, j * CHUNK : (j + 1) * CHUNK]
         x1 = x_ref[:, half + j * CHUNK : half + (j + 1) * CHUNK]
         pre = jnp.dot(x0, wlo_ref[...], preferred_element_type=f32)
         pre = pre + jnp.dot(x1, whi_ref[...], preferred_element_type=f32)
         h = (jnp.tanh(pre[:, :CHUNK]) * jax.nn.sigmoid(pre[:, CHUNK:])).astype(bf16)
         h_ref[:, j * CHUNK : (j + 1) * CHUNK] = h
+
+
+def skip_kernel(h_ref, ws_ref, s_ref):
+    skip_w = ws_ref.shape[1]
+    for j in range(h_ref.shape[1] // CHUNK):
         s_ref[:, j * skip_w : (j + 1) * skip_w] = jnp.dot(
-            h, ws_ref[...], preferred_element_type=f32
+            h_ref[:, j * CHUNK : (j + 1) * CHUNK], ws_ref[...], preferred_element_type=f32
         ).astype(bf16)
 
 
-def front(features, wlo, whi, ws):
+def front_hidden(features, wlo, whi):
     rows, cols = features.shape
     half = cols // 2
-    skip_cols = ws.shape[1] * (half // CHUNK)
     tile = min(ROW_TILE, rows)
     return pl.pallas_call(
-        front_kernel,
+        hidden_kernel,
         grid=(rows // tile,),
         in_specs=[
             pl.BlockSpec((tile, cols), lambda i: (i, 0)),
             pl.BlockSpec(wlo.shape, lambda i: (0, 0)),
             pl.BlockSpec(whi.shape, lambda i: (0, 0)),
+        ],
+        out_specs=pl.BlockSpec((tile, half), lambda i: (i, 0)),
+        out_shape=jax.ShapeDtypeStruct((rows, half), bf16),
+        compiler_params=pltpu.CompilerParams(vmem_limit_bytes=48 * 1024 * 1024),
+        cost_estimate=pl.CostEstimate(
+            flops=2 * rows * CHUNK * 4 * CHUNK * (half // CHUNK),
+            transcendentals=rows * half * 2,
+            bytes_accessed=2 * rows * (cols + half),
+        ),
+    )(features, wlo, whi)
+
+
+def front_skip(hidden, ws):
+    rows, half = hidden.shape
+    skip_cols = ws.shape[1] * (half // CHUNK)
+    tile = min(ROW_TILE, rows)
+    return pl.pallas_call(
+        skip_kernel,
+        grid=(rows // tile,),
+        in_specs=[
+            pl.BlockSpec((tile, half), lambda i: (i, 0)),
             pl.BlockSpec(ws.shape, lambda i: (0, 0)),
         ],
-        out_specs=[
-            pl.BlockSpec((tile, half), lambda i: (i, 0)),
-            pl.BlockSpec((tile, skip_cols), lambda i: (i, 0)),
-        ],
-        out_shape=[
-            jax.ShapeDtypeStruct((rows, half), bf16),
-            jax.ShapeDtypeStruct((rows, skip_cols), bf16),
-        ],
-        compiler_params=pltpu.CompilerParams(vmem_limit_bytes=48 * 1024 * 1024),
-        cost_estimate=pl.CostEstimate(
-            flops=2 * rows * CHUNK * (4 * CHUNK + ws.shape[1]) * (half // CHUNK),
-            transcendentals=rows * half * 2,
-            bytes_accessed=2 * rows * (cols + half + skip_cols),
-        ),
-    )(features, wlo, whi, ws)
+        out_specs=pl.BlockSpec((tile, skip_cols), lambda i: (i, 0)),
+        out_shape=jax.ShapeDtypeStruct((rows, skip_cols), bf16),
+        compiler_params=pltpu.CompilerParams(vmem_limit_bytes=48 * 1024 * 1024),
+        cost_estimate=pl.CostEstimate(
+            flops=2 * rows * CHUNK * ws.shape[1] * (half // CHUNK),
+            transcendentals=0,
+            bytes_accessed=2 * rows * (half + skip_cols),
+        ),
+    )(hidden, ws)
 
 
 def accumulate(src_ref, row_ref, field_ref, lo_ref, hi_ref, arr_ref, band_ref, farw_ref, acc):
@@ -134,14 +151,14 @@
         out_specs=[vmem(), vmem()],
         out_shape=[
             jax.ShapeDtypeStruct((nrows, width), bf16),
-            jax.ShapeDtypeStruct(arrived.shape, bf16),
+            jax.ShapeDtypeStruct((send_rows.shape[0], BLK, width), bf16),
         ],
         scratch_shapes=[pltpu.VMEM((nrows + BLK, width), f32)],
         compiler_params=pltpu.CompilerParams(vmem_limit_bytes=48 * 1024 * 1024),
         cost_estimate=pl.CostEstimate(
             flops=2 * BLK * BLK * width * (3 * nrows // BLK + farw3.shape[0]),
             transcendentals=0,
-            bytes_accessed=2 * width * (nrows * 2 + 2 * arrived.shape[0] * BLK),
+            bytes_accessed=2 * width * (nrows * 2 + arrived.shape[0] * BLK),
         ),
     )(src, rows, send_rows, field, lo, hi, arrived, band3, farw3)
 
@@ -191,50 +208,47 @@
     cw = CHANNEL_WIDTH
     per = CHUNK // cw
 
-    eye = jnp.eye(per, dtype=bf16)
+    def block_diag(w, reps):
+        r, c = w.shape
+        tiled = jnp.tile(w, (reps, reps))
+        ri = lax.broadcasted_iota(jnp.int32, tiled.shape, 0) // r
+        ci = lax.broadcasted_iota(jnp.int32, tiled.shape, 1) // c
+        return jnp.where(ri == ci, tiled, jnp.zeros_like(tiled))
+
     fgw = filter_gate_weight
-    wlo = jnp.concatenate([jnp.kron(eye, fgw[:cw, :cw]), jnp.kron(eye, fgw[:cw, cw:])], axis=1)
-    whi = jnp.concatenate([jnp.kron(eye, fgw[cw:, :cw]), jnp.kron(eye, fgw[cw:, cw:])], axis=1)
-    ws = jnp.kron(eye, skip_weight)
-    mix3 = jnp.stack([jnp.kron(eye, mix_weight[i * cw : (i + 1) * cw]) for i in range(3)])
-
-    hidden, skip_out = front(features, wlo, whi, ws)
+    wlo = jnp.concatenate([block_diag(fgw[:cw, :cw], per), block_diag(fgw[:cw, cw:], per)], axis=1)
+    whi = jnp.concatenate([block_diag(fgw[cw:, :cw], per), block_diag(fgw[cw:, cw:], per)], axis=1)
+    ws = block_diag(skip_weight, per)
+    mix3 = jnp.stack([block_diag(mix_weight[i * cw : (i + 1) * cw], per) for i in range(3)])
+
+    hidden = front_hidden(features, wlo, whi)
 
     own_index = lax.axis_index("node")
-    own_exports = lax.dynamic_slice_in_dim(export_block, own_index, 1, 0)[0]
-    columns = far_col[0]
-    sources = columns // EXPORT
-    slot_export = columns % EXPORT
+    own_exports = lax.dynamic_slice_in_dim(export_block, own_index, 1, 0)[0].astype(jnp.int32)
+    columns = far_col[0].astype(jnp.int32)
     pointers = far_ptr[0]
     slot_ids = jnp.arange(far_cap, dtype=jnp.int32)
     slot_rows = jnp.sum(
         (pointers[1:, None] <= slot_ids[None, :]).astype(jnp.int32), axis=0
     ).astype(jnp.int32)
-    in_use = slot_ids < pointers[-1]
-    matches = (sources[None, :] == jnp.arange(peer_count, dtype=jnp.int32)[:, None]) & in_use[
-        None, :
-    ]
-    wanted = jnp.sum(jnp.where(matches, slot_export[None, :], 0), axis=1)
-    requested = lax.all_to_all(wanted[:, None], "node", split_axis=0, concat_axis=0, tiled=True)[
-        :, 0
-    ]
-    send_rows = own_exports[requested].astype(jnp.int32)
 
     width = hidden.shape[1]
     band3 = band_weight.reshape(node_rows, 3, BLK).transpose(1, 0, 2)
     farw3 = far_weight.reshape(BLK, far_cap, BLK).transpose(1, 0, 2)
 
     def exchange(send):
-        return lax.all_to_all(send, "node", split_axis=0, concat_axis=0, tiled=True)
-
-    send1 = hidden.reshape(blocks, BLK, width)[send_rows]
+        gathered = lax.all_gather(send, "node", axis=0, tiled=True)
+        return gathered
+
+    send1 = hidden.reshape(blocks, BLK, width)[own_exports]
     arrived1 = exchange(send1)
     lo1, hi1 = halo(hidden)
-    hop_one, send2 = hop1(sources, slot_rows, send_rows, hidden, lo1, hi1, arrived1, band3, farw3)
+    skip_out = front_skip(hidden, ws)
+    hop_one, send2 = hop1(columns, slot_rows, own_exports, hidden, lo1, hi1, arrived1, band3, farw3)
     arrived2 = exchange(send2)
     lo2, hi2 = halo(hop_one)
     residual = hop2(
-        sources, slot_rows, hop_one, lo2, hi2, arrived2, band3, farw3, features, hidden, mix3
+        columns, slot_rows, hop_one, lo2, hi2, arrived2, band3, farw3, features, hidden, mix3
     )
     return residual, skip_out
 

time: 111 us -> 123 us (1.11)
  the two profiles are of different devices: /device:TPU:15 before, /device:TPU:0 now
where the time goes in v2:
time: 123 us; the launch traced here: 122 us
  waiting for transfers between devices  58.9 us (48%)
  local copies, waits for them, and re-layouts  21.3 us (17%)
  Pallas kernels  17.8 us (14%)
  between operations  14.4 us (12%)
  starting transfers between devices  8.73 us (7%)
    all_gather x2, waiting for transfers between devices, exchange(): gathered = lax.all_gather(send, 'node', axis=0, tiled=True)  58.6 us
    another operation x15, local copies, waits for them, and re-layouts, block_diag(): tiled = jnp.tile(w, (reps, reps))  9.42 us
    unnamed x25, local copies, waits for them, and re-layouts  7.56 us
    pallas_call x1, Pallas kernels, hop2(): pl.pallas_call(hop2_kernel, in_specs=[smem(), smem()] + [vmem()] * 9, out...  6.65 us
    ppermute x2, starting transfers between devices, halo(): lo = lax.ppermute(field[field.shape[0] - BLK:], 'node', forward)  6.07 us
    pallas_call x1, Pallas kernels, front_skip(): pl.pallas_call(skip_kernel, grid=(rows // tile,), in_specs=[pl.BlockSpec(...  4.85 us
    pallas_call x1, Pallas kernels, hop1(): pl.pallas_call(hop1_kernel, in_specs=[smem(), smem(), smem()] + [vmem()]...  4.44 us
    ppermute x2, starting transfers between devices, halo(): hi = lax.ppermute(field[:BLK], 'node', backward)  2.58 us
  transfers between devices with their start and end apart: 6, of which 3 were waited for; matrix products, arithmetic and copies ran while one was open for 9% of the time, Pallas kernels for 4%

profile of v2, /device:TPU:0, one launch (start us, length us, event | category | flops | bytes accessed | tf_op | source)
XLA Modules:
  0.0 121.9 jit_solution(16810625266281654627)
XLA Ops:
  7.3 0.6 copy-done
  7.8 0.2 dynamic-slice_reduce_fusion.send_ref
  8.1 0.9 fusion.10
  9.0 0.4 tile.37
  9.3 0.1 tile.34
  9.4 0.4 tile.35
  9.8 0.1 tile.32
  9.9 0.4 tile.33
  10.2 0.1 tile.38
  10.3 0.4 tile.39
  10.7 0.2 broadcast_select_fusion.1
  10.9 0.6 copy-done.1
  11.5 1.8 %shard_map.104.field_ref.h_ref = bf16[1024,512]{1,0:T(8,128)(2,1)S(1)} custom-call(bf16[1024,1024]{1,0:T(8,128)(2,1)S(1)} %copy-done.1, bf16[256,512]{1,0:T(8,128)(2,1)S(1)} %get-tuple-element.24.wlo_ref, bf16[256,512]{1,0:T(8,128)(2,1)S(1)} %get-tuple-element.25.whi_ref), custom_call_target="tpu_custom_call" | custom-call | flops 1073741824 | bytes 3145728 | tf_op jit(solution)/shard_map/pallas_call | solution.py:45
  13.3 1.2 gather_fusion
  14.6 1.3 %collective-permute-start.1 = (bf16[64,512]{1,0:T(8,128)(2,1)S(1)}, bf16[64,512]{1,0:T(8,128)(2,1)S(1)}, u32[]{:S(2)}, u32[]{:S(2)}) collective-permute-start(bf16[64,512]{1,0:T(8,128)(2,1)S(1)} %get-tuple-element.8), channel_id=1, source_target_pairs={{1,0},{2,1},{3,2},{4,3},{5,4},{6,5},{7,6},{8,7},{9,8},{10,9},{11,1... | collective-permute-start | bytes 196616 | tf_op jit(solution)/shard_map/ppermute | solution.py:189
  15.9 3.0 %collective-permute-start = (bf16[64,512]{1,0:T(8,128)(2,1)S(1)}, bf16[64,512]{1,0:T(8,128)(2,1)S(1)}, u32[]{:S(2)}, u32[]{:S(2)}) collective-permute-start(bf16[64,512]{1,0:T(8,128)(2,1)S(1)} %get-tuple-element.9), channel_id=1, source_target_pairs={{0,1},{1,2},{2,3},{3,4},{4,5},{5,6},{6,7},{7,8},{8,9},{9,10},{10,1... | collective-permute-start | bytes 196616 | tf_op jit(solution)/shard_map/ppermute | solution.py:188
  19.0 0.2 reshape.444
  19.3 1.4 %copy.24 = bf16[1024,3,64]{2,0,1:T(8,128)(2,1)S(1)} copy(bf16[1024,3,64]{0,2,1:T(8,128)(2,1)} %bitcast.39) | data formatting | bytes 786432 | tf_op jit(solution)/shard_map/reshape | solution.py:236
  20.7 0.1 slice_bitcast_fusion
  20.7 0.1 convert_reduce_fusion.row_ref
  20.8 38.0 %all-gather.6.cloned.1.call-done.arr_ref = bf16[32,64,512]{2,1,0:T(8,128)(2,1)} async-done(((bf16[2,64,512]{2,1,0:T(8,128)(2,1)}), bf16[32,64,512]{2,1,0:T(8,128)(2,1)}) %all-gather.6.cloned.1.call-update) | async-done | bytes 2097168 | tf_op jit(solution)/shard_map/all_gather | solution.py:240
  58.8 1.6 %copy-done.3 = bf16[32,64,512]{2,1,0:T(8,128)(2,1)S(1)} copy-done((bf16[32,64,512]{2,1,0:T(8,128)(2,1)S(1)}, bf16[32,64,512]{2,1,0:T(8,128)(2,1)}, u32[]{:S(2)}) %copy-start.3) | copy-done | bytes 2097176
  60.4 4.4 %shard_map.105 = (bf16[1024,512]{1,0:T(8,128)(2,1)S(1)}, bf16[2,64,512]{2,1,0:T(8,128)(2,1)}) custom-call(s32[15]{0:T(128)S(1)} %bitcast.35, s32[15]{0:T(128)S(1)} %convert_reduce_fusion.row_ref, s32[2]{0:T(128)S(1)} %dynamic-slice_reduce_fusion.send_ref, bf16[1024,512]{1,0:T(8,128)(2,1)S(1)} %shard_map.104.field_ref.h_ref, ...), custom_call_target="tpu_custom_call" | custom-call | flops 264241152 | bytes 4194304 | tf_op jit(solution)/shard_map/pallas_call | solution.py:148
  64.9 0.1 fusion.11
  64.9 0.1 copy.26
  65.0 0.1 copy.28
  65.1 0.1 copy.27
  65.2 0.9 tile.82
  66.1 1.4 %tile.83 = bf16[1,256,256]{2,1,0:T(8,128)(2,1)S(1)} reshape(bf16[8,32,8,32]{3,2,1,0:T(8,128)(2,1)} %tile.82) | data formatting | bytes 262144 | tf_op jit(solution)/shard_map/tile | solution.py:213
  67.5 0.9 tile.84
  68.4 1.4 %tile.85 = bf16[1,256,256]{2,1,0:T(8,128)(2,1)S(1)} reshape(bf16[8,32,8,32]{3,2,1,0:T(8,128)(2,1)} %tile.84) | data formatting | bytes 262144 | tf_op jit(solution)/shard_map/tile | solution.py:213
  69.8 0.9 tile.80
  70.7 1.4 %tile.81 = bf16[1,256,256]{2,1,0:T(8,128)(2,1)S(1)} reshape(bf16[8,32,8,32]{3,2,1,0:T(8,128)(2,1)} %tile.80) | data formatting | bytes 262144 | tf_op jit(solution)/shard_map/tile | solution.py:213
  72.2 0.8 tile.86
  72.9 0.3 copy.29
  73.3 0.3 fusion.ws_ref
  73.6 4.9 %shard_map.107 = bf16[1024,4096]{1,0:T(8,128)(2,1)} custom-call(bf16[1024,512]{1,0:T(8,128)(2,1)S(1)} %shard_map.104.field_ref.h_ref, bf16[256,2048]{1,0:T(8,128)(2,1)S(1)} %fusion.ws_ref), custom_call_target="tpu_custom_call" | custom-call | flops 2147483648 | bytes 9437184 | tf_op jit(solution)/shard_map/pallas_call | solution.py:68
  78.5 0.2 fusion.3
  78.7 1.3 %collective-permute-start.3 = (bf16[64,512]{1,0:T(8,128)(2,1)S(1)}, bf16[64,512]{1,0:T(8,128)(2,1)S(1)}, u32[]{:S(2)}, u32[]{:S(2)}) collective-permute-start(bf16[64,512]{1,0:T(8,128)(2,1)S(1)} %get-tuple-element.6), channel_id=1, source_target_pairs={{1,0},{2,1},{3,2},{4,3},{5,4},{6,5},{7,6},{8,7},{9,8},{10,9},{11,1... | collective-permute-start | bytes 196616 | tf_op jit(solution)/shard_map/ppermute | solution.py:189
  80.0 3.0 %collective-permute-start.2 = (bf16[64,512]{1,0:T(8,128)(2,1)S(1)}, bf16[64,512]{1,0:T(8,128)(2,1)S(1)}, u32[]{:S(2)}, u32[]{:S(2)}) collective-permute-start(bf16[64,512]{1,0:T(8,128)(2,1)S(1)} %get-tuple-element.7), channel_id=1, source_target_pairs={{0,1},{1,2},{2,3},{3,4},{4,5},{5,6},{6,7},{7,8},{8,9},{9,10},{10,1... | collective-permute-start | bytes 196616 | tf_op jit(solution)/shard_map/ppermute | solution.py:188
  83.1 0.6 copy-done.4
  83.7 0.2 collective-permute-done.2.lo_ref
  83.9 0.6 copy-done.6
  84.5 20.7 %all-gather.4.cloned.1.call-done.arr_ref = bf16[32,64,512]{2,1,0:T(8,128)(2,1)} async-done(((bf16[2,64,512]{2,1,0:T(8,128)(2,1)}), bf16[32,64,512]{2,1,0:T(8,128)(2,1)}) %all-gather.4.cloned.1.call-update) | async-done | bytes 2097168 | tf_op jit(solution)/shard_map/all_gather | solution.py:240
  105.2 1.6 %copy-done.2 = bf16[32,64,512]{2,1,0:T(8,128)(2,1)S(1)} copy-done((bf16[32,64,512]{2,1,0:T(8,128)(2,1)S(1)}, bf16[32,64,512]{2,1,0:T(8,128)(2,1)}, u32[]{:S(2)}) %copy-start.2) | copy-done | bytes 2097176
  106.8 0.8 copy-done.5
  107.6 0.8 copy-done.7
  108.4 6.6 %shard_map.106 = bf16[1024,512]{1,0:T(8,128)(2,1)} custom-call(s32[15]{0:T(128)S(1)} %bitcast.36, s32[15]{0:T(128)S(1)} %convert_reduce_fusion.row_ref, bf16[1024,512]{1,0:T(8,128)(2,1)S(1)} %get-tuple-element.4.field_ref, bf16[64,512]{1,0:T(8,128)(2,1)S(1)} %copy-done.7, bf16[64,512]{1,0:T(8,128)(2,1)S(1)} %copy-done.5, bf16[32,64,512]{2,1,0:T(8,128)(2,1)S(1)} %copy-done.2, ...), custom_call_target="tpu_custom_call" | custom-call | flops 1069547520 | bytes 8388608 | tf_op jit(solution)/shard_map/pallas_call | solution.py:168
  (36 shorter events, 0.4 us)
Async XLA Ops:
  7.2 0.7 copy-start
  7.2 51.6 %all-gather.6.cloned.1.call-start = ((), (), s32[]{:S(2)}) async-start(), calls=%async_computation.1 | async-start | bytes 2228224 | tf_op jit(solution)/shard_map/all_gather | solution.py:240
  9.9 1.6 %copy-start.1 = (bf16[1024,1024]{1,0:T(8,128)(2,1)S(1)}, bf16[1024,1024]{1,0:T(8,128)(2,1)}, u32[]{:S(2)}) copy-start(bf16[1024,1024]{1,0:T(8,128)(2,1)} %x_ref.3) | copy-start | bytes 6291460
  11.5 7.5 %copy-start.9 = (bf16[64,960]{1,0:T(8,128)(2,1)S(1)}, bf16[64,960]{1,0:T(8,128)(2,1)}, u32[]{:S(2)}) copy-start(bf16[64,960]{1,0:T(8,128)(2,1)} %param.14) | copy-start | bytes 368644
  13.3 7.4 %copy-start.11 = (s32[1,17]{1,0:T(1,128)S(1)}, s32[1,17]{1,0:T(1,128)}, u32[]{:S(2)}) copy-start(s32[1,17]{1,0:T(1,128)} %param.15) | copy-start | bytes 208
  13.3 45.5 %copy-start.8 = (s32[1,15]{1,0:T(1,128)S(1)}, s32[1,15]{1,0:T(1,128)}, u32[]{:S(2)}) copy-start(s32[1,15]{1,0:T(1,128)} %param.16) | copy-start | bytes 184
  14.5 90.6 %all-gather.4.cloned.1.call-start = ((), (), s32[]{:S(2)}) async-start(), calls=%async_computation | async-start | bytes 2228224 | tf_op jit(solution)/shard_map/all_gather | solution.py:240
  14.6 6.2 %collective-permute-start.1 = (bf16[64,512]{1,0:T(8,128)(2,1)S(1)}, bf16[64,512]{1,0:T(8,128)(2,1)S(1)}, u32[]{:S(2)}, u32[]{:S(2)}) collective-permute-start(bf16[64,512]{1,0:T(8,128)(2,1)S(1)} %get-tuple-element.8), channel_id=1, source_target_pairs={{1,0},{2,1},{3,2},{4,3},{5,4},{6,5},{7,6},{8,7},{9,8},{10,9},{11,1... | collective-permute-start | bytes 196616 | tf_op jit(solution)/shard_map/ppermute | solution.py:189
  15.9 4.9 %collective-permute-start = (bf16[64,512]{1,0:T(8,128)(2,1)S(1)}, bf16[64,512]{1,0:T(8,128)(2,1)S(1)}, u32[]{:S(2)}, u32[]{:S(2)}) collective-permute-start(bf16[64,512]{1,0:T(8,128)(2,1)S(1)} %get-tuple-element.9), channel_id=1, source_target_pairs={{0,1},{1,2},{2,3},{3,4},{4,5},{5,6},{6,7},{7,8},{8,9},{9,10},{10,1... | collective-permute-start | bytes 196616 | tf_op jit(solution)/shard_map/ppermute | solution.py:188
  58.8 1.6 %copy-start.3 = (bf16[32,64,512]{2,1,0:T(8,128)(2,1)S(1)}, bf16[32,64,512]{2,1,0:T(8,128)(2,1)}, u32[]{:S(2)}) copy-start(bf16[32,64,512]{2,1,0:T(8,128)(2,1)} %all-gather.6.cloned.1.call-done.arr_ref) | copy-start | bytes 6291460
  60.4 4.5 %copy-start.10 = (bf16[96,32]{0,1:T(8,128)(2,1)S(1)}, bf16[96,32]{0,1:T(8,128)(2,1)}, u32[]{:S(2)}) copy-start(bf16[96,32]{0,1:T(8,128)(2,1)} %param.12) | copy-start | bytes 18436
  78.7 4.4 %collective-permute-start.3 = (bf16[64,512]{1,0:T(8,128)(2,1)S(1)}, bf16[64,512]{1,0:T(8,128)(2,1)S(1)}, u32[]{:S(2)}, u32[]{:S(2)}) collective-permute-start(bf16[64,512]{1,0:T(8,128)(2,1)S(1)} %get-tuple-element.6), channel_id=1, source_target_pairs={{1,0},{2,1},{3,2},{4,3},{5,4},{6,5},{7,6},{8,7},{9,8},{10,9},{11,1... | collective-permute-start | bytes 196616 | tf_op jit(solution)/shard_map/ppermute | solution.py:189
  80.0 3.9 %collective-permute-start.2 = (bf16[64,512]{1,0:T(8,128)(2,1)S(1)}, bf16[64,512]{1,0:T(8,128)(2,1)S(1)}, u32[]{:S(2)}, u32[]{:S(2)}) collective-permute-start(bf16[64,512]{1,0:T(8,128)(2,1)S(1)} %get-tuple-element.7), channel_id=1, source_target_pairs={{0,1},{1,2},{2,3},{3,4},{4,5},{5,6},{6,7},{7,8},{8,9},{9,10},{10,1... | collective-permute-start | bytes 196616 | tf_op jit(solution)/shard_map/ppermute | solution.py:188
  83.1 0.6 copy-start.4
  83.9 0.6 copy-start.6
  105.2 1.6 %copy-start.2 = (bf16[32,64,512]{2,1,0:T(8,128)(2,1)S(1)}, bf16[32,64,512]{2,1,0:T(8,128)(2,1)}, u32[]{:S(2)}) copy-start(bf16[32,64,512]{2,1,0:T(8,128)(2,1)} %all-gather.4.cloned.1.call-done.arr_ref) | copy-start | bytes 6291460
  106.8 0.8 copy-start.5
  107.6 0.8 copy-start.7
Sparse Core Ops, SparseCore 0:
  14.7 44.0 all-gather.5
  65.0 40.1 all-gather.3

commit v3 on v2

v3 whole, which is shorter than its diff:
```python
import functools

import jax
import jax.numpy as jnp
from jax import lax
from jax.experimental import pallas as pl
from jax.experimental.pallas import tpu as pltpu
from jax.sharding import PartitionSpec as P

BLK = 64
TOUT = 16
DILATION_STEP = 16
EXPORT = 2
CHANNEL_WIDTH = 32
S = 256
TIN = 32
CHUNK = 256
ROW_TILE = 256

f32 = jnp.float32
bf16 = jnp.bfloat16


def hidden_kernel(x_ref, wlo_ref, whi_ref, h_ref):
    half = x_ref.shape[1] // 2
    for j in range(half // CHUNK):
        x0 = x_ref[:, j * CHUNK : (j + 1) * CHUNK]
        x1 = x_ref[:, half + j * CHUNK : half + (j + 1) * CHUNK]
        pre = jnp.dot(x0, wlo_ref[...], preferred_element_type=f32)
        pre = pre + jnp.dot(x1, whi_ref[...], preferred_element_type=f32)
        h_ref[j] = (jnp.tanh(pre[:, :CHUNK]) * jax.nn.sigmoid(pre[:, CHUNK:])).astype(bf16)


def skip_kernel(h_ref, ws_ref, s_ref):
    skip_w = ws_ref.shape[1]
    for j in range(h_ref.shape[0]):
        s_ref[:, j * skip_w : (j + 1) * skip_w] = jnp.dot(
            h_ref[j], ws_ref[...], preferred_element_type=f32
        ).astype(bf16)


def front_hidden(features, wlo, whi):
    rows, cols = features.shape
    chunks = cols // 2 // CHUNK
    tile = min(ROW_TILE, rows)
    return pl.pallas_call(
        hidden_kernel,
        grid=(rows // tile,),
        in_specs=[
            pl.BlockSpec((tile, cols), lambda i: (i, 0)),
            pl.BlockSpec(wlo.shape, lambda i: (0, 0)),
            pl.BlockSpec(whi.shape, lambda i: (0, 0)),
        ],
        out_specs=pl.BlockSpec((chunks, tile, CHUNK), lambda i: (0, i, 0)),
        out_shape=jax.ShapeDtypeStruct((chunks, rows, CHUNK), bf16),
        compiler_params=pltpu.CompilerParams(vmem_limit_bytes=48 * 1024 * 1024),
        cost_estimate=pl.CostEstimate(
            flops=2 * rows * CHUNK * 4 * CHUNK * chunks,
            transcendentals=rows * CHUNK * chunks * 2,
            bytes_accessed=2 * rows * (cols + CHUNK * chunks),
        ),
    )(features, wlo, whi)


def front_skip(hidden, ws):
    chunks, rows, _ = hidden.shape
    skip_cols = ws.shape[1] * chunks
    tile = min(ROW_TILE, rows)
    return pl.pallas_call(
        skip_kernel,
        grid=(rows // tile,),
        in_specs=[
            pl.BlockSpec((chunks, tile, CHUNK), lambda i: (0, i, 0)),
            pl.BlockSpec(ws.shape, lambda i: (0, 0)),
        ],
        out_specs=pl.BlockSpec((tile, skip_cols), lambda i: (i, 0)),
        out_shape=jax.ShapeDtypeStruct((rows, skip_cols), bf16),
        compiler_params=pltpu.CompilerParams(vmem_limit_bytes=48 * 1024 * 1024),
        cost_estimate=pl.CostEstimate(
            flops=2 * rows * CHUNK * ws.shape[1] * chunks,
            transcendentals=0,
            bytes_accessed=2 * rows * (CHUNK * chunks + skip_cols),
        ),
    )(hidden, ws)


def accumulate(src_ref, row_ref, field, lo_ref, hi_ref, arr_ref, band_ref, farw_ref, acc):
    nblk = field.shape[0] // BLK
    far_cap = farw_ref.shape[0]
    for r in range(nblk):
        prev = lo_ref[...] if r == 0 else field[(r - 1) * BLK : r * BLK, :]
        nxt = hi_ref[...] if r == nblk - 1 else field[(r + 1) * BLK : (r + 2) * BLK, :]
        own = field[r * BLK : (r + 1) * BLK, :]
        v = jnp.dot(band_ref[0, r * BLK : (r + 1) * BLK, :], prev, preferred_element_type=f32)
        v = v + jnp.dot(band_ref[1, r * BLK : (r + 1) * BLK, :], own, preferred_element_type=f32)
        v = v + jnp.dot(band_ref[2, r * BLK : (r + 1) * BLK, :], nxt, preferred_element_type=f32)
        acc[r * BLK : (r + 1) * BLK, :] = v
    acc[nblk * BLK :, :] = jnp.zeros((BLK, acc.shape[1]), f32)

    def slot(k, carry):
        row = row_ref[k]
        piece = arr_ref[src_ref[k]]
        start = pl.multiple_of(row * BLK, BLK)
        acc[pl.ds(start, BLK), :] += jnp.dot(farw_ref[k], piece, preferred_element_type=f32)
        return carry

    lax.fori_loop(0, far_cap, slot, 0)


def hop1_kernel(
    chunk, src_ref, row_ref, send_ref, field_ref, lo_ref, hi_ref, arr_ref, band_ref, farw_ref,
    out_ref, out_send_ref, acc,
):
    field = field_ref.at[chunk]
    accumulate(src_ref, row_ref, field, lo_ref, hi_ref, arr_ref, band_ref, farw_ref, acc)
    nrows = field.shape[0]
    out_ref[...] = acc[:nrows, :].astype(bf16)
    for p in range(out_send_ref.shape[0]):
        start = pl.multiple_of(send_ref[p] * BLK, BLK)
        out_send_ref[p] = out_ref[pl.ds(start, BLK), :]


def hop2_kernel(
    chunk, src_ref, row_ref, field_ref, lo_ref, hi_ref, arr_ref, band_ref, farw_ref,
    x_ref, h_ref, mix_ref, out_ref, acc,
):
    accumulate(src_ref, row_ref, field_ref, lo_ref, hi_ref, arr_ref, band_ref, farw_ref, acc)
    nrows = field_ref.shape[0]
    half = x_ref.shape[1] // 2
    two = acc[:nrows, :].astype(bf16)
    v = x_ref[:, half + chunk * CHUNK : half + (chunk + 1) * CHUNK].astype(f32)
    v = v + jnp.dot(h_ref[chunk], mix_ref[0], preferred_element_type=f32)
    v = v + jnp.dot(field_ref[...], mix_ref[1], preferred_element_type=f32)
    v = v + jnp.dot(two, mix_ref[2], preferred_element_type=f32)
    out_ref[...] = v.astype(bf16)


def vmem():
    return pl.BlockSpec(memory_space=pltpu.VMEM)


def smem():
    return pl.BlockSpec(memory_space=pltpu.SMEM)


def hop1(chunk, src, rows, send_rows, hidden, lo, hi, arrived, band3, farw3):
    _, nrows, width = hidden.shape
    return pl.pallas_call(
        functools.partial(hop1_kernel, chunk),
        in_specs=[smem(), smem(), smem()] + [vmem()] * 6,
        out_specs=[vmem(), vmem()],
        out_shape=[
            jax.ShapeDtypeStruct((nrows, width), bf16),
            jax.ShapeDtypeStruct((send_rows.shape[0], BLK, width), bf16),
        ],
        scratch_shapes=[pltpu.VMEM((nrows + BLK, width), f32)],
        compiler_params=pltpu.CompilerParams(vmem_limit_bytes=48 * 1024 * 1024),
        cost_estimate=pl.CostEstimate(
            flops=2 * BLK * BLK * width * (3 * nrows // BLK + farw3.shape[0]),
            transcendentals=0,
            bytes_accessed=2 * width * (nrows * 2 + 2 * arrived.shape[0] * BLK),
        ),
    )(src, rows, send_rows, hidden, lo, hi, arrived, band3, farw3)


def hop2(chunk, src, rows, field, lo, hi, arrived, band3, farw3, features, hidden, mix3):
    nrows, width = field.shape
    return pl.pallas_call(
        functools.partial(hop2_kernel, chunk),
        in_specs=[smem(), smem()] + [vmem()] * 9,
        out_specs=vmem(),
        out_shape=jax.ShapeDtypeStruct((nrows, width), bf16),
        scratch_shapes=[pltpu.VMEM((nrows + BLK, width), f32)],
        compiler_params=pltpu.CompilerParams(vmem_limit_bytes=48 * 1024 * 1024),
        cost_estimate=pl.CostEstimate(
            flops=2 * BLK * BLK * width * (3 * nrows // BLK + farw3.shape[0])
            + 2 * nrows * width * CHUNK * 3,
            transcendentals=0,
            bytes_accessed=2 * width * (nrows * 5 + arrived.shape[0] * BLK),
        ),
    )(src, rows, field, lo, hi, arrived, band3, farw3, features, hidden, mix3)


def halo(field):
    count = lax.axis_size("node")
    forward = [(i, i + 1) for i in range(count - 1)]
    backward = [(t, s) for s, t in forward]
    lo = lax.ppermute(field[field.shape[0] - BLK :], "node", forward)
    hi = lax.ppermute(field[:BLK], "node", backward)
    return lo, hi


def block_diag(w, reps):
    r, c = w.shape
    shape_r = (reps * r, r)
    rep_r = (
        lax.broadcasted_iota(jnp.int32, shape_r, 0) % r == lax.broadcasted_iota(jnp.int32, shape_r, 1)
    ).astype(bf16)
    shape_c = (c, reps * c)
    rep_c = (
        lax.broadcasted_iota(jnp.int32, shape_c, 1) % c == lax.broadcasted_iota(jnp.int32, shape_c, 0)
    ).astype(bf16)
    rows = jnp.dot(rep_r, w, preferred_element_type=f32).astype(bf16)
    tiled = jnp.dot(rows, rep_c, preferred_element_type=f32)
    shape = tiled.shape
    mask = lax.broadcasted_iota(jnp.int32, shape, 0) // r == lax.broadcasted_iota(jnp.int32, shape, 1) // c
    return jnp.where(mask, tiled, 0.0).astype(bf16)


def local(
    features,
    filter_gate_weight,
    skip_weight,
    mix_weight,
    band_weight,
    far_weight,
    far_ptr,
    far_col,
    export_block,
):
    node_rows = features.shape[0]
    blocks = node_rows // BLK
    far_cap = far_col.shape[1]
    cw = CHANNEL_WIDTH
    per = CHUNK // cw

    fgw = filter_gate_weight
    wlo = jnp.concatenate([block_diag(fgw[:cw, :cw], per), block_diag(fgw[:cw, cw:], per)], axis=1)
    whi = jnp.concatenate([block_diag(fgw[cw:, :cw], per), block_diag(fgw[cw:, cw:], per)], axis=1)
    ws = block_diag(skip_weight, per)
    mix3 = jnp.stack([block_diag(mix_weight[i * cw : (i + 1) * cw], per) for i in range(3)])

    own_index = lax.axis_index("node")
    own_exports = lax.dynamic_slice_in_dim(export_block, own_index, 1, 0)[0].astype(jnp.int32)
    columns = far_col[0].astype(jnp.int32)
    sources = columns // EXPORT
    pointers = far_ptr[0].astype(jnp.int32)
    slot_ids = jnp.arange(far_cap, dtype=jnp.int32)
    slot_rows = jnp.sum(
        (pointers[1:, None] <= slot_ids[None, :]).astype(jnp.int32), axis=0
    ).astype(jnp.int32)
    info = jnp.concatenate([columns, pointers[-1:]])
    info_all = lax.all_gather(info, "node", axis=0)
    cols_all = info_all[:, :far_cap]
    used_all = info_all[:, far_cap]
    hits = (cols_all // EXPORT == own_index) & (slot_ids[None, :] < used_all[:, None])
    requested = jnp.sum(jnp.where(hits, cols_all % EXPORT, 0), axis=1)
    send_rows = own_exports[requested].astype(jnp.int32)

    hidden = front_hidden(features, wlo, whi)
    chunks, _, width = hidden.shape
    band3 = band_weight.reshape(node_rows, 3, BLK).transpose(1, 0, 2)
    farw3 = far_weight.reshape(BLK, far_cap, BLK).transpose(1, 0, 2)

    def exchange(send):
        return lax.all_to_all(send, "node", split_axis=0, concat_axis=0, tiled=True)

    arrived1 = [exchange(hidden[c].reshape(blocks, BLK, width)[send_rows]) for c in range(chunks)]
    halos1 = [halo(hidden[c]) for c in range(chunks)]
    skip_out = front_skip(hidden, ws)
    parts = []
    for c in range(chunks):
        lo1, hi1 = halos1[c]
        hop_one, send2 = hop1(c, sources, slot_rows, send_rows, hidden, lo1, hi1, arrived1[c], band3, farw3)
        arrived2 = exchange(send2)
        lo2, hi2 = halo(hop_one)
        parts.append(
            hop2(c, sources, slot_rows, hop_one, lo2, hi2, arrived2, band3, farw3, features, hidden, mix3)
        )
    residual = jnp.concatenate(parts, axis=1)
    return residual, skip_out


def solution(mesh):
    placed = (
        P(("groups", "node"), None),
        P(),
        P(),
        P(),
        P("node", None),
        P(None, "node"),
        P("node", None),
        P("node", None),
        P(),
    )
    return jax.shard_map(
        local,
        mesh=mesh,
        in_specs=placed,
        out_specs=(P(("groups", "node"), None), P(("groups", "node"), None)),
        check_vma=False,
    )
```

time: 123 us -> 134 us (1.089)
  the two profiles are of different devices: /device:TPU:0 before, /device:TPU:15 now
where the time goes in v3:
time: 134 us; the launch traced here: 132 us
  starting transfers between devices  48.2 us (36%)
  Pallas kernels  20.5 us (15%)
  waiting for transfers between devices  18.9 us (14%)
  local copies, waits for them, and re-layouts  18.8 us (14%)
  matrix products  10.5 us (8%)
  blocking collectives  7.89 us (6%)
  other arithmetic  5.83 us (4%)
  between operations  1.83 us (1%)
    all_to_all x4, starting transfers between devices, exchange(): return lax.all_to_all(send, 'node', split_axis=0, concat_axis=0, tiled=True)  22.4 us
    ppermute x4, starting transfers between devices, halo(): lo = lax.ppermute(field[field.shape[0] - BLK:], 'node', forward)  17.1 us
    all_to_all x4, waiting for transfers between devices, exchange(): return lax.all_to_all(send, 'node', split_axis=0, concat_axis=0, tiled=True)  12.3 us
    unnamed x74, local copies, waits for them, and re-layouts  11.3 us
    dot_general x8, matrix products, block_diag(): tiled = jnp.dot(rows, rep_c, preferred_element_type=f32)  10.5 us
    ppermute x4, starting transfers between devices, halo(): hi = lax.ppermute(field[:BLK], 'node', backward)  8.69 us
    unnamed x1, blocking collectives  7.89 us
    pallas_call x2, Pallas kernels, hop2(): pl.pallas_call(functools.partial(hop2_kernel, chunk), in_specs=[smem(), s...  7.25 us
  transfers between devices with their start and end apart: 12, of which 3 were waited for; matrix products, arithmetic and copies ran while one was open for 10% of the time, Pallas kernels for 11%

profile of v3, /device:TPU:15, one launch (start us, length us, event | category | flops | bytes accessed | tf_op | source)
XLA Modules:
  0.0 132.4 jit_solution(11542553513297857705)
XLA Ops:
  0.8 1.4 %fusion.2 = bf16[256,256]{1,0:T(8,128)(2,1)S(1)} fusion(s32[256]{0:T(256)S(1)} %get-tuple-element.25, s32[256]{0:T(256)S(1)} %get-tuple-element.28, pred[256]{0:T(512)(128)(4,1)S(1)} %get-tuple-element.26, bf16[64,64]{1,0:T(8,128)(2,1)} %param.10, s32[256]{0:T(256)S(1)} %get-tuple-element.24, s32[256]{0:T(256)S(1)} %get-tuple-element.29, ...), kind=kOutput, calls=%fused_computation.14 | convolution fusion | flops 5087232 | bytes 149504 | tf_op jit(solution)/shard_map/dot_general | solution.py:204
  2.2 1.2 fusion.3
  3.5 1.2 fusion.4
  5.3 0.6 slice.86
  7.8 0.8 add_dynamic-update-slice_fusion
  8.6 7.9 %all-reduce = s32[256]{0:T(256)S(1)} all-reduce(s32[256]{0:T(256)S(1)} %add_dynamic-update-slice_fusion), channel_id=2, replica_groups=mesh['groups'=2,'node'=16] {'node'}, use_global_device_ids=true, to_apply=%add | all-reduce | flops 256 | bytes 2048
  17.0 1.3 fusion.110
  18.3 1.9 %shard_map.104.field_ref.h_ref = bf16[2,1024,256]{2,1,0:T(8,128)(2,1)S(1)} custom-call(bf16[1024,1024]{1,0:T(8,128)(2,1)S(1)} %copy-done.1, bf16[256,512]{1,0:T(8,128)(2,1)S(1)} %pad_maximum_fusion.2.wlo_ref, bf16[256,512]{1,0:T(8,128)(2,1)S(1)} %pad_maximum_fusion.3.whi_ref), custom_call_target="tpu_custom_call" | custom-call | flops 1073741824 | bytes 3145728 | tf_op jit(solution)/shard_map/pallas_call | solution.py:46
  20.3 1.4 %gather_fusion = bf16[16,64,256]{2,1,0:T(8,128)(2,1)} fusion(bf16[16,64,256]{2,1,0:T(8,128)(2,1)S(1)} %bitcast.49, s32[1024]{0:T(1024)S(1)} %pad_clamp_fusion), kind=kCustom, calls=%fused_computation | custom fusion | bytes 1048640 | tf_op jit(solution)/shard_map/gather | solution.py:258
  21.7 8.5 %all-to-all-start = ((bf16[16,64,256]{2,1,0:T(8,128)(2,1)}), bf16[16,64,256]{2,1,0:T(8,128)(2,1)S(1)}, u32[]{:S(2)}, u32[]{:S(2)}) async-start(bf16[16,64,256]{2,1,0:T(8,128)(2,1)} %gather_fusion), calls=%async_computation | async-start | bytes 1048576 | tf_op jit(solution)/shard_map/all_to_all | solution.py:256
  30.2 1.4 %gather_fusion.1 = bf16[16,64,256]{2,1,0:T(8,128)(2,1)} fusion(bf16[16,64,256]{2,1,0:T(8,128)(2,1)S(1)} %bitcast.48, s32[1024]{0:T(1024)S(1)} %pad_clamp_fusion), kind=kCustom, calls=%fused_computation.1 | custom fusion | bytes 1048640 | tf_op jit(solution)/shard_map/gather | solution.py:258
  31.6 12.2 %all-to-all-done.arr_ref = bf16[16,64,256]{2,1,0:T(8,128)(2,1)S(1)} async-done(((bf16[16,64,256]{2,1,0:T(8,128)(2,1)}), bf16[16,64,256]{2,1,0:T(8,128)(2,1)S(1)}, u32[]{:S(2)}, u32[]{:S(2)}) %all-to-all-start) | async-done | bytes 524320 | tf_op jit(solution)/shard_map/all_to_all | solution.py:256
  43.8 4.9 %all-to-all-start.2 = ((bf16[16,64,256]{2,1,0:T(8,128)(2,1)}), bf16[16,64,256]{2,1,0:T(8,128)(2,1)S(1)}, u32[]{:S(2)}, u32[]{:S(2)}) async-start(bf16[16,64,256]{2,1,0:T(8,128)(2,1)} %gather_fusion.1), calls=%async_computation.2 | async-start | bytes 1048576 | tf_op jit(solution)/shard_map/all_to_all | solution.py:256
  49.4 2.3 %collective-permute-start.1 = (bf16[64,256]{1,0:T(8,128)(2,1)}, bf16[64,256]{1,0:T(8,128)(2,1)S(1)}, u32[]{:S(2)}, u32[]{:S(2)}) collective-permute-start(bf16[64,256]{1,0:T(8,128)(2,1)} %get-tuple-element.12), channel_id=1, source_target_pairs={{1,0},{2,1},{3,2},{4,3},{5,4},{6,5},{7,6},{8,7},{9,8},{10,9},{11,1... | collective-permute-start | bytes 98312 | tf_op jit(solution)/shard_map/ppermute | solution.py:189
  51.7 4.2 %collective-permute-start = (bf16[64,256]{1,0:T(8,128)(2,1)S(1)}, bf16[64,256]{1,0:T(8,128)(2,1)S(1)}, u32[]{:S(2)}, u32[]{:S(2)}) collective-permute-start(bf16[64,256]{1,0:T(8,128)(2,1)S(1)} %get-tuple-element.15), channel_id=1, source_target_pairs={{0,1},{1,2},{2,3},{3,4},{4,5},{5,6},{6,7},{7,8},{8,9},{9,10},{10,1... | collective-permute-start | bytes 98312 | tf_op jit(solution)/shard_map/ppermute | solution.py:188
  56.3 1.4 %copy.31 = bf16[1024,3,64]{2,0,1:T(8,128)(2,1)S(1)} copy(bf16[1024,3,64]{0,2,1:T(8,128)(2,1)} %bitcast.50) | data formatting | bytes 786432 | tf_op jit(solution)/shard_map/reshape | solution.py:252
  57.8 4.9 %collective-permute-done.1.hi_ref = bf16[64,256]{1,0:T(8,128)(2,1)S(1)} collective-permute-done((bf16[64,256]{1,0:T(8,128)(2,1)}, bf16[64,256]{1,0:T(8,128)(2,1)S(1)}, u32[]{:S(2)}, u32[]{:S(2)}) %collective-permute-start.1) | collective-permute-done | bytes 32800 | tf_op jit(solution)/shard_map/ppermute | solution.py:189
  62.7 3.2 %shard_map.105 = (bf16[1024,256]{1,0:T(8,128)(2,1)S(1)}, bf16[16,64,256]{2,1,0:T(8,128)(2,1)S(1)}) custom-call(s32[15]{0:T(128)S(1)} %and_select_fusion.src_ref, s32[15]{0:T(128)S(1)} %convert_reduce_fusion.row_ref, s32[16]{0:T(128)S(1)} %get-tuple-element.23.send_ref, bf16[2,1024,256]{2,1,0:T(8,128)(2,1)S(1)} %shard_map.104.field_ref.h_ref, ...), custom_call_target="tpu_custom_call" | custom-call | flops 132120576 | bytes 2097152 | tf_op jit(solution)/shard_map/pallas_call | solution.py:148
  65.9 0.8 copy-done.7
  66.7 0.8 copy-done.12
  67.5 4.5 %all-to-all-start.1 = ((bf16[16,64,256]{2,1,0:T(8,128)(2,1)}), bf16[16,64,256]{2,1,0:T(8,128)(2,1)S(1)}, u32[]{:S(2)}, u32[]{:S(2)}) async-start(bf16[16,64,256]{2,1,0:T(8,128)(2,1)} %copy-done.12), calls=%async_computation.1 | async-start | bytes 1048576 | tf_op jit(solution)/shard_map/all_to_all | solution.py:256
  71.9 2.3 %collective-permute-start.5 = (bf16[64,256]{1,0:T(8,128)(2,1)}, bf16[64,256]{1,0:T(8,128)(2,1)}, u32[]{:S(2)}, u32[]{:S(2)}) collective-permute-start(bf16[64,256]{1,0:T(8,128)(2,1)} %get-tuple-element.13), channel_id=1, source_target_pairs={{1,0},{2,1},{3,2},{4,3},{5,4},{6,5},{7,6},{8,7},{9,8},{10,9},{11,1... | collective-permute-start | bytes 98312 | tf_op jit(solution)/shard_map/ppermute | solution.py:189
  74.2 4.2 %collective-permute-start.4 = (bf16[64,256]{1,0:T(8,128)(2,1)}, bf16[64,256]{1,0:T(8,128)(2,1)}, u32[]{:S(2)}, u32[]{:S(2)}) collective-permute-start(bf16[64,256]{1,0:T(8,128)(2,1)} %get-tuple-element.14), channel_id=1, source_target_pairs={{0,1},{1,2},{2,3},{3,4},{4,5},{5,6},{6,7},{7,8},{8,9},{9,10},{10,1... | collective-permute-start | bytes 98312 | tf_op jit(solution)/shard_map/ppermute | solution.py:188
  79.1 1.2 fusion.10
  80.2 1.2 fusion.9
  81.4 1.2 fusion.8
  82.6 1.1 pad_maximum_fusion.1.mix_ref
  84.3 1.7 %collective-permute-done.5.hi_ref = bf16[64,256]{1,0:T(8,128)(2,1)} collective-permute-done((bf16[64,256]{1,0:T(8,128)(2,1)}, bf16[64,256]{1,0:T(8,128)(2,1)}, u32[]{:S(2)}, u32[]{:S(2)}) %collective-permute-start.5) | collective-permute-done | bytes 32800 | tf_op jit(solution)/shard_map/ppermute | solution.py:189
  86.0 3.4 %shard_map.107 = (bf16[1024,256]{1,0:T(8,128)(2,1)S(1)}, bf16[16,64,256]{2,1,0:T(8,128)(2,1)S(1)}) custom-call(s32[15]{0:T(128)S(1)} %and_select_fusion.src_ref, s32[15]{0:T(128)S(1)} %convert_reduce_fusion.row_ref, s32[16]{0:T(128)S(1)} %get-tuple-element.23.send_ref, bf16[2,1024,256]{2,1,0:T(8,128)(2,1)S(1)} %shard_map.104.field_ref.h_ref, ...), custom_call_target="tpu_custom_call" | custom-call | flops 132120576 | bytes 2097152 | tf_op jit(solution)/shard_map/pallas_call | solution.py:148
  89.4 0.8 copy-done.9
  90.2 0.8 copy-done.11
  91.0 4.5 %all-to-all-start.3 = ((bf16[16,64,256]{2,1,0:T(8,128)(2,1)}), bf16[16,64,256]{2,1,0:T(8,128)(2,1)S(1)}, u32[]{:S(2)}, u32[]{:S(2)}) async-start(bf16[16,64,256]{2,1,0:T(8,128)(2,1)} %copy-done.11), calls=%async_computation.3 | async-start | bytes 1048576 | tf_op jit(solution)/shard_map/all_to_all | solution.py:256
  95.5 2.5 %fusion.ws_ref = bf16[256,2048]{1,0:T(8,128)(2,1)} fusion(bf16[32,256]{1,0:T(8,128)(2,1)S(1)} %copy-done, s32[2048]{0:T(1024)} %get-tuple-element.31, s32[2048]{0:T(1024)} %get-tuple-element.32, s32[2048]{0:T(1024)} %get-tuple-element.30, s32[2048]{0:T(1024)} %get-tuple-element.33, s32[256]{0:T(256)} %copy-done.22, s32[256]{0:T(256)} %copy-done.20, ...), kind=kOutput, calls=%fused_computation.3 | convolution fusion | flops 276381696 | bytes 1106432 | tf_op jit(solution)/shard_map/dot_general | solution.py:204
  98.1 1.2 copy-done.6
  99.3 4.9 %shard_map.109 = bf16[1024,4096]{1,0:T(8,128)(2,1)} custom-call(bf16[2,1024,256]{2,1,0:T(8,128)(2,1)S(1)} %shard_map.104.field_ref.h_ref, bf16[256,2048]{1,0:T(8,128)(2,1)S(1)} %copy-done.6), custom_call_target="tpu_custom_call" | custom-call | flops 2147483648 | bytes 9437184 | tf_op jit(solution)/shard_map/pallas_call | solution.py:69
  104.2 2.3 %collective-permute-start.3 = (bf16[64,256]{1,0:T(8,128)(2,1)S(1)}, bf16[64,256]{1,0:T(8,128)(2,1)S(1)}, u32[]{:S(2)}, u32[]{:S(2)}) collective-permute-start(bf16[64,256]{1,0:T(8,128)(2,1)S(1)} %get-tuple-element.16), channel_id=1, source_target_pairs={{1,0},{2,1},{3,2},{4,3},{5,4},{6,5},{7,6},{8,7},{9,8},{10,9},{11,1... | collective-permute-start | bytes 98312 | tf_op jit(solution)/shard_map/ppermute | solution.py:189
  106.4 4.2 %collective-permute-start.2 = (bf16[64,256]{1,0:T(8,128)(2,1)S(1)}, bf16[64,256]{1,0:T(8,128)(2,1)S(1)}, u32[]{:S(2)}, u32[]{:S(2)}) collective-permute-start(bf16[64,256]{1,0:T(8,128)(2,1)S(1)} %get-tuple-element.17), channel_id=1, source_target_pairs={{0,1},{1,2},{2,3},{3,4},{4,5},{5,6},{6,7},{7,8},{8,9},{9,10},{10,1... | collective-permute-start | bytes 98312 | tf_op jit(solution)/shard_map/ppermute | solution.py:188
  110.6 0.8 fusion.114
  111.4 1.9 %collective-permute-start.7 = (bf16[64,256]{1,0:T(8,128)(2,1)S(1)}, bf16[64,256]{1,0:T(8,128)(2,1)S(1)}, u32[]{:S(2)}, u32[]{:S(2)}) collective-permute-start(bf16[64,256]{1,0:T(8,128)(2,1)S(1)} %get-tuple-element.18), channel_id=1, source_target_pairs={{1,0},{2,1},{3,2},{4,3},{5,4},{6,5},{7,6},{8,7},{9,8},{10,9},{11,1... | collective-permute-start | bytes 98312 | tf_op jit(solution)/shard_map/ppermute | solution.py:189
  113.3 4.5 %collective-permute-start.6 = (bf16[64,256]{1,0:T(8,128)(2,1)S(1)}, bf16[64,256]{1,0:T(8,128)(2,1)S(1)}, u32[]{:S(2)}, u32[]{:S(2)}) collective-permute-start(bf16[64,256]{1,0:T(8,128)(2,1)S(1)} %get-tuple-element.19), channel_id=1, source_target_pairs={{0,1},{1,2},{2,3},{3,4},{4,5},{5,6},{6,7},{7,8},{8,9},{9,10},{10,1... | collective-permute-start | bytes 98312 | tf_op jit(solution)/shard_map/ppermute | solution.py:188
  117.9 3.6 %shard_map.106 = bf16[1024,256]{1,0:T(8,128)(2,1)S(1)} custom-call(s32[15]{0:T(128)S(1)} %and_select_fusion.src_ref, s32[15]{0:T(128)S(1)} %convert_reduce_fusion.row_ref, bf16[1024,256]{1,0:T(8,128)(2,1)S(1)} %copy-done.8, bf16[64,256]{1,0:T(8,128)(2,1)S(1)} %collective-permute-done.2.lo_ref, bf16[64,256]{1,0:T(8,128)(2,1)S(1)} %collective-permute-done.3.hi_ref, ...), custom_call_target="tpu_custom_call" | custom-call | flops 534773760 | bytes 3145728 | tf_op jit(solution)/shard_map/pallas_call | solution.py:168
  121.5 0.8 copy-done.4
  123.6 1.6 %copy-done.3 = bf16[1024,1024]{1,0:T(8,128)(2,1)S(1)} copy-done((bf16[1024,1024]{1,0:T(8,128)(2,1)S(1)}, bf16[1024,1024]{1,0:T(8,128)(2,1)}, u32[]{:S(2)}) %copy-start.3) | copy-done | bytes 2097176
  125.2 1.0 copy-done.10
  126.2 0.8 copy-done.14
  127.0 0.8 copy-done.16
  127.7 3.6 %shard_map.108 = bf16[1024,256]{1,0:T(8,128)(2,1)S(1)} custom-call(s32[15]{0:T(128)S(1)} %and_select_fusion.src_ref, s32[15]{0:T(128)S(1)} %convert_reduce_fusion.row_ref, bf16[1024,256]{1,0:T(8,128)(2,1)S(1)} %copy-done.10, bf16[64,256]{1,0:T(8,128)(2,1)S(1)} %copy-done.16, bf16[64,256]{1,0:T(8,128)(2,1)S(1)} %copy-done.14, ...), custom_call_target="tpu_custom_call" | custom-call | flops 534773760 | bytes 3145728 | tf_op jit(solution)/shard_map/pallas_call | solution.py:168
  131.4 1.1 pad_maximum_fusion
  (96 shorter events, 6.0 us)
Async XLA Ops:
  0.6 94.9 %copy-start = (bf16[32,256]{1,0:T(8,128)(2,1)S(1)}, bf16[32,256]{1,0:T(8,128)(2,1)}, u32[]{:S(2)}) copy-start(bf16[32,256]{1,0:T(8,128)(2,1)} %param.11) | copy-start | bytes 49156
  0.6 5.9 %copy-start.31 = (u32[32]{0:T(128)S(1)}, u32[32]{0:T(128)}, u32[]{:S(2)}) copy-start(u32[32]{0:T(128)} %constant.204) | copy-start | bytes 388
  0.7 4.0 %copy-start.27 = (bf16[64,64]{1,0:T(8,128)(2,1)S(1)}, bf16[64,64]{1,0:T(8,128)(2,1)}, u32[]{:S(2)}) copy-start(bf16[64,64]{1,0:T(8,128)(2,1)} %param.10) | copy-start | bytes 24580
  0.7 4.6 %copy-start.29 = (s32[1,17]{1,0:T(1,128)S(1)}, s32[1,17]{1,0:T(1,128)}, u32[]{:S(2)}) copy-start(s32[1,17]{1,0:T(1,128)} %param.15) | copy-start | bytes 208
  0.7 5.2 %copy-start.18 = (s32[16,2]{0,1:T(2,128)S(1)}, s32[16,2]{0,1:T(2,128)}, u32[]{:S(2)}) copy-start(s32[16,2]{0,1:T(2,128)} %param.17) | copy-start | bytes 388
  0.7 7.1 %copy-start.26 = (s32[1,15]{1,0:T(1,128)S(1)}, s32[1,15]{1,0:T(1,128)}, u32[]{:S(2)}) copy-start(s32[1,15]{1,0:T(1,128)} %param.16) | copy-start | bytes 184
  0.7 17.6 %copy-start.1 = (bf16[1024,1024]{1,0:T(8,128)(2,1)S(1)}, bf16[1024,1024]{1,0:T(8,128)(2,1)}, u32[]{:S(2)}) copy-start(bf16[1024,1024]{1,0:T(8,128)(2,1)} %x_ref.5) | copy-start | bytes 6291460
  0.7 19.5 %copy-start.32 = (pred[256]{0:T(512)(128)(4,1)}, pred[256]{0:T(512)(128)(4,1)S(1)}, u32[]{:S(2)}) copy-start(pred[256]{0:T(512)(128)(4,1)S(1)} %get-tuple-element.26) | copy-start | bytes 772
  0.7 19.5 %copy-start.34 = (pred[256]{0:T(512)(128)(4,1)}, pred[256]{0:T(512)(128)(4,1)S(1)}, u32[]{:S(2)}) copy-start(pred[256]{0:T(512)(128)(4,1)S(1)} %get-tuple-element.27) | copy-start | bytes 772
  0.8 5.2 %copy-start.20 = (s32[256]{0:T(256)}, s32[256]{0:T(256)S(1)}, u32[]{:S(2)}) copy-start(s32[256]{0:T(256)S(1)} %get-tuple-element.29) | copy-start | bytes 3076
  0.8 80.7 %copy-start.19 = (s32[256]{0:T(256)}, s32[256]{0:T(256)S(1)}, u32[]{:S(2)}) copy-start(s32[256]{0:T(256)S(1)} %get-tuple-element.28) | copy-start | bytes 3076
  0.8 15.8 %copy-start.22 = (s32[256]{0:T(256)}, s32[256]{0:T(256)S(1)}, u32[]{:S(2)}) copy-start(s32[256]{0:T(256)S(1)} %get-tuple-element.24) | copy-start | bytes 3076
  0.8 16.1 %copy-start.24 = (s32[256]{0:T(256)}, s32[256]{0:T(256)S(1)}, u32[]{:S(2)}) copy-start(s32[256]{0:T(256)S(1)} %get-tuple-element.25) | copy-start | bytes 3076
  20.3 35.6 %copy-start.30 = (s32[1,17]{1,0:T(1,128)S(1)}, s32[1,17]{1,0:T(1,128)}, u32[]{:S(2)}) copy-start(s32[1,17]{1,0:T(1,128)} %param.15) | copy-start | bytes 208
  20.3 35.7 %copy-start.17 = (bf16[64,960]{1,0:T(8,128)(2,1)S(1)}, bf16[64,960]{1,0:T(8,128)(2,1)}, u32[]{:S(2)}) copy-start(bf16[64,960]{1,0:T(8,128)(2,1)} %param.14) | copy-start | bytes 368644
  21.7 22.1 %all-to-all-start = ((bf16[16,64,256]{2,1,0:T(8,128)(2,1)}), bf16[16,64,256]{2,1,0:T(8,128)(2,1)S(1)}, u32[]{:S(2)}, u32[]{:S(2)}) async-start(bf16[16,64,256]{2,1,0:T(8,128)(2,1)} %gather_fusion), calls=%async_computation | async-start | bytes 1048576 | tf_op jit(solution)/shard_map/all_to_all | solution.py:256
  43.8 23.6 %all-to-all-start.2 = ((bf16[16,64,256]{2,1,0:T(8,128)(2,1)}), bf16[16,64,256]{2,1,0:T(8,128)(2,1)S(1)}, u32[]{:S(2)}, u32[]{:S(2)}) async-start(bf16[16,64,256]{2,1,0:T(8,128)(2,1)} %gather_fusion.1), calls=%async_computation.2 | async-start | bytes 1048576 | tf_op jit(solution)/shard_map/all_to_all | solution.py:256
  49.4 13.3 %collective-permute-start.1 = (bf16[64,256]{1,0:T(8,128)(2,1)}, bf16[64,256]{1,0:T(8,128)(2,1)S(1)}, u32[]{:S(2)}, u32[]{:S(2)}) collective-permute-start(bf16[64,256]{1,0:T(8,128)(2,1)} %get-tuple-element.12), channel_id=1, source_target_pairs={{1,0},{2,1},{3,2},{4,3},{5,4},{6,5},{7,6},{8,7},{9,8},{10,9},{11,1... | collective-permute-start | bytes 98312 | tf_op jit(solution)/shard_map/ppermute | solution.py:189
  51.7 11.0 %collective-permute-start = (bf16[64,256]{1,0:T(8,128)(2,1)S(1)}, bf16[64,256]{1,0:T(8,128)(2,1)S(1)}, u32[]{:S(2)}, u32[]{:S(2)}) collective-permute-start(bf16[64,256]{1,0:T(8,128)(2,1)S(1)} %get-tuple-element.15), channel_id=1, source_target_pairs={{0,1},{1,2},{2,3},{3,4},{4,5},{5,6},{6,7},{7,8},{8,9},{9,10},{10,1... | collective-permute-start | bytes 98312 | tf_op jit(solution)/shard_map/ppermute | solution.py:188
  57.7 21.3 %copy-start.21 = (s32[256]{0:T(256)S(1)}, s32[256]{0:T(256)}, u32[]{:S(2)}) copy-start(s32[256]{0:T(256)} %copy-done.20) | copy-start | bytes 3076
  57.7 21.3 %copy-start.23 = (s32[256]{0:T(256)S(1)}, s32[256]{0:T(256)}, u32[]{:S(2)}) copy-start(s32[256]{0:T(256)} %copy-done.22) | copy-start | bytes 3076
  57.7 21.3 %copy-start.25 = (s32[256]{0:T(256)S(1)}, s32[256]{0:T(256)}, u32[]{:S(2)}) copy-start(s32[256]{0:T(256)} %copy-done.24) | copy-start | bytes 3076
  57.7 21.3 %copy-start.28 = (bf16[96,32]{0,1:T(8,128)(2,1)S(1)}, bf16[96,32]{0,1:T(8,128)(2,1)}, u32[]{:S(2)}) copy-start(bf16[96,32]{0,1:T(8,128)(2,1)} %param.12) | copy-start | bytes 18436
  57.8 21.3 %copy-start.33 = (pred[256]{0:T(512)(128)(4,1)S(1)}, pred[256]{0:T(512)(128)(4,1)}, u32[]{:S(2)}) copy-start(pred[256]{0:T(512)(128)(4,1)} %copy-done.32) | copy-start | bytes 772
  57.8 21.3 %copy-start.35 = (pred[256]{0:T(512)(128)(4,1)S(1)}, pred[256]{0:T(512)(128)(4,1)}, u32[]{:S(2)}) copy-start(pred[256]{0:T(512)(128)(4,1)} %copy-done.34) | copy-start | bytes 772
  65.9 0.8 copy-start.7
  66.7 0.8 copy-start.12
  67.5 23.5 %all-to-all-start.1 = ((bf16[16,64,256]{2,1,0:T(8,128)(2,1)}), bf16[16,64,256]{2,1,0:T(8,128)(2,1)S(1)}, u32[]{:S(2)}, u32[]{:S(2)}) async-start(bf16[16,64,256]{2,1,0:T(8,128)(2,1)} %copy-done.12), calls=%async_computation.1 | async-start | bytes 1048576 | tf_op jit(solution)/shard_map/all_to_all | solution.py:256
  71.9 14.0 %collective-permute-start.5 = (bf16[64,256]{1,0:T(8,128)(2,1)}, bf16[64,256]{1,0:T(8,128)(2,1)}, u32[]{:S(2)}, u32[]{:S(2)}) collective-permute-start(bf16[64,256]{1,0:T(8,128)(2,1)} %get-tuple-element.13), channel_id=1, source_target_pairs={{1,0},{2,1},{3,2},{4,3},{5,4},{6,5},{7,6},{8,7},{9,8},{10,9},{11,1... | collective-permute-start | bytes 98312 | tf_op jit(solution)/shard_map/ppermute | solution.py:189
  74.2 11.8 %collective-permute-start.4 = (bf16[64,256]{1,0:T(8,128)(2,1)}, bf16[64,256]{1,0:T(8,128)(2,1)}, u32[]{:S(2)}, u32[]{:S(2)}) collective-permute-start(bf16[64,256]{1,0:T(8,128)(2,1)} %get-tuple-element.14), channel_id=1, source_target_pairs={{0,1},{1,2},{2,3},{3,4},{4,5},{5,6},{6,7},{7,8},{8,9},{9,10},{10,1... | collective-permute-start | bytes 98312 | tf_op jit(solution)/shard_map/ppermute | solution.py:188
  89.4 0.8 copy-start.9
  90.2 0.8 copy-start.11
  91.0 32.6 %all-to-all-start.3 = ((bf16[16,64,256]{2,1,0:T(8,128)(2,1)}), bf16[16,64,256]{2,1,0:T(8,128)(2,1)S(1)}, u32[]{:S(2)}, u32[]{:S(2)}) async-start(bf16[16,64,256]{2,1,0:T(8,128)(2,1)} %copy-done.11), calls=%async_computation.3 | async-start | bytes 1048576 | tf_op jit(solution)/shard_map/all_to_all | solution.py:256
  98.0 1.2 copy-start.6
  99.3 4.9 %copy-start.8 = (bf16[1024,256]{1,0:T(8,128)(2,1)S(1)}, bf16[1024,256]{1,0:T(8,128)(2,1)}, u32[]{:S(2)}) copy-start(bf16[1024,256]{1,0:T(8,128)(2,1)} %copy-done.7) | copy-start | bytes 1572868
  99.3 18.6 %copy-start.2 = (bf16[1024,1024]{1,0:T(8,128)(2,1)S(1)}, bf16[1024,1024]{1,0:T(8,128)(2,1)}, u32[]{:S(2)}) copy-start(bf16[1024,1024]{1,0:T(8,128)(2,1)} %x_ref.5) | copy-start | bytes 6291460
  104.2 13.7 %collective-permute-start.3 = (bf16[64,256]{1,0:T(8,128)(2,1)S(1)}, bf16[64,256]{1,0:T(8,128)(2,1)S(1)}, u32[]{:S(2)}, u32[]{:S(2)}) collective-permute-start(bf16[64,256]{1,0:T(8,128)(2,1)S(1)} %get-tuple-element.16), channel_id=1, source_target_pairs={{1,0},{2,1},{3,2},{4,3},{5,4},{6,5},{7,6},{8,7},{9,8},{10,9},{11,1... | collective-permute-start | bytes 98312 | tf_op jit(solution)/shard_map/ppermute | solution.py:189
  106.4 11.5 %collective-permute-start.2 = (bf16[64,256]{1,0:T(8,128)(2,1)S(1)}, bf16[64,256]{1,0:T(8,128)(2,1)S(1)}, u32[]{:S(2)}, u32[]{:S(2)}) collective-permute-start(bf16[64,256]{1,0:T(8,128)(2,1)S(1)} %get-tuple-element.17), channel_id=1, source_target_pairs={{0,1},{1,2},{2,3},{3,4},{4,5},{5,6},{6,7},{7,8},{8,9},{9,10},{10,1... | collective-permute-start | bytes 98312 | tf_op jit(solution)/shard_map/ppermute | solution.py:188
  111.4 10.9 %collective-permute-start.7 = (bf16[64,256]{1,0:T(8,128)(2,1)S(1)}, bf16[64,256]{1,0:T(8,128)(2,1)S(1)}, u32[]{:S(2)}, u32[]{:S(2)}) collective-permute-start(bf16[64,256]{1,0:T(8,128)(2,1)S(1)} %get-tuple-element.18), channel_id=1, source_target_pairs={{1,0},{2,1},{3,2},{4,3},{5,4},{6,5},{7,6},{8,7},{9,8},{10,9},{11,1... | collective-permute-start | bytes 98312 | tf_op jit(solution)/shard_map/ppermute | solution.py:189
  113.3 9.6 %collective-permute-start.6 = (bf16[64,256]{1,0:T(8,128)(2,1)S(1)}, bf16[64,256]{1,0:T(8,128)(2,1)S(1)}, u32[]{:S(2)}, u32[]{:S(2)}) collective-permute-start(bf16[64,256]{1,0:T(8,128)(2,1)S(1)} %get-tuple-element.19), channel_id=1, source_target_pairs={{0,1},{1,2},{2,3},{3,4},{4,5},{5,6},{6,7},{7,8},{8,9},{9,10},{10,1... | collective-permute-start | bytes 98312 | tf_op jit(solution)/shard_map/ppermute | solution.py:188
  121.5 0.8 copy-start.4
  122.3 0.6 copy-start.13
  123.0 0.6 copy-start.15
  123.6 1.6 %copy-start.3 = (bf16[1024,1024]{1,0:T(8,128)(2,1)S(1)}, bf16[1024,1024]{1,0:T(8,128)(2,1)}, u32[]{:S(2)}) copy-start(bf16[1024,1024]{1,0:T(8,128)(2,1)} %x_ref.5) | copy-start | bytes 6291460
  125.2 1.0 copy-start.10
  126.2 0.8 copy-start.14
  127.0 0.8 copy-start.16
  127.7 3.6 %copy-start.5 = (bf16[1024,256]{1,0:T(8,128)(2,1)S(1)}, bf16[1024,256]{1,0:T(8,128)(2,1)}, u32[]{:S(2)}) copy-start(bf16[1024,256]{1,0:T(8,128)(2,1)} %copy-done.4) | copy-start | bytes 1572868

commit v4 on v2

v4 whole, which is shorter than its diff:
```python
import functools

import jax
import jax.numpy as jnp
from jax import lax
from jax.experimental import pallas as pl
from jax.experimental.pallas import tpu as pltpu
from jax.sharding import PartitionSpec as P

BLK = 64
TOUT = 16
DILATION_STEP = 16
EXPORT = 2
CHANNEL_WIDTH = 32
S = 256
TIN = 32
CHUNK = 256
ROW_TILE = 256

f32 = jnp.float32
bf16 = jnp.bfloat16


def bd_inkernel(w, reps):
    r, c = w.shape
    shape_r = (reps * r, r)
    rep_r = jnp.where(
        lax.broadcasted_iota(jnp.int32, shape_r, 0) % r == lax.broadcasted_iota(jnp.int32, shape_r, 1),
        1.0, 0.0,
    ).astype(bf16)
    shape_c = (c, reps * c)
    rep_c = jnp.where(
        lax.broadcasted_iota(jnp.int32, shape_c, 1) % c == lax.broadcasted_iota(jnp.int32, shape_c, 0),
        1.0, 0.0,
    ).astype(bf16)
    rows = jnp.dot(rep_r, w, preferred_element_type=f32).astype(bf16)
    tiled = jnp.dot(rows, rep_c, preferred_element_type=f32)
    shape = tiled.shape
    mask = lax.broadcasted_iota(jnp.int32, shape, 0) // r == lax.broadcasted_iota(jnp.int32, shape, 1) // c
    return jnp.where(mask, tiled, 0.0).astype(bf16)


def hidden_kernel(x_ref, fgw_ref, h_ref, wlo, whi):
    half = x_ref.shape[1] // 2
    cw = fgw_ref.shape[0] // 2
    per = CHUNK // cw

    @pl.when(pl.program_id(0) == 0)
    def _():
        w = fgw_ref[...]
        wlo[:, :CHUNK] = bd_inkernel(w[:cw, :cw], per)
        wlo[:, CHUNK:] = bd_inkernel(w[:cw, cw:], per)
        whi[:, :CHUNK] = bd_inkernel(w[cw:, :cw], per)
        whi[:, CHUNK:] = bd_inkernel(w[cw:, cw:], per)

    for j in range(half // CHUNK):
        x0 = x_ref[:, j * CHUNK : (j + 1) * CHUNK]
        x1 = x_ref[:, half + j * CHUNK : half + (j + 1) * CHUNK]
        pre = jnp.dot(x0, wlo[...], preferred_element_type=f32)
        pre = pre + jnp.dot(x1, whi[...], preferred_element_type=f32)
        h_ref[:, j * CHUNK : (j + 1) * CHUNK] = (
            jnp.tanh(pre[:, :CHUNK]) * jax.nn.sigmoid(pre[:, CHUNK:])
        ).astype(bf16)


def skip_kernel(h_ref, sw_ref, s_ref, ws):
    cw = sw_ref.shape[0]

    @pl.when(pl.program_id(0) == 0)
    def _():
        ws[...] = bd_inkernel(sw_ref[...], CHUNK // cw)

    skip_w = ws.shape[1]
    for j in range(h_ref.shape[1] // CHUNK):
        s_ref[:, j * skip_w : (j + 1) * skip_w] = jnp.dot(
            h_ref[:, j * CHUNK : (j + 1) * CHUNK], ws[...], preferred_element_type=f32
        ).astype(bf16)


def front_hidden(features, fgw):
    rows, cols = features.shape
    chunks = cols // 2 // CHUNK
    tile = min(ROW_TILE, rows)
    return pl.pallas_call(
        hidden_kernel,
        grid=(rows // tile,),
        in_specs=[
            pl.BlockSpec((tile, cols), lambda i: (i, 0)),
            pl.BlockSpec(fgw.shape, lambda i: (0, 0)),
        ],
        out_specs=pl.BlockSpec((tile, chunks * CHUNK), lambda i: (i, 0)),
        out_shape=jax.ShapeDtypeStruct((rows, chunks * CHUNK), bf16),
        scratch_shapes=[pltpu.VMEM((CHUNK, 2 * CHUNK), bf16), pltpu.VMEM((CHUNK, 2 * CHUNK), bf16)],
        compiler_params=pltpu.CompilerParams(vmem_limit_bytes=48 * 1024 * 1024),
        cost_estimate=pl.CostEstimate(
            flops=2 * rows * CHUNK * 4 * CHUNK * chunks,
            transcendentals=rows * CHUNK * chunks * 2,
            bytes_accessed=2 * rows * (cols + CHUNK * chunks),
        ),
    )(features, fgw)


def front_skip(hidden, skip_weight):
    rows, width = hidden.shape
    chunks = width // CHUNK
    cw, s = skip_weight.shape
    per = CHUNK // cw
    skip_cols = s * per * chunks
    tile = min(ROW_TILE, rows)
    return pl.pallas_call(
        skip_kernel,
        grid=(rows // tile,),
        in_specs=[
            pl.BlockSpec((tile, width), lambda i: (i, 0)),
            pl.BlockSpec(skip_weight.shape, lambda i: (0, 0)),
        ],
        out_specs=pl.BlockSpec((tile, skip_cols), lambda i: (i, 0)),
        out_shape=jax.ShapeDtypeStruct((rows, skip_cols), bf16),
        scratch_shapes=[pltpu.VMEM((CHUNK, s * per), bf16)],
        compiler_params=pltpu.CompilerParams(vmem_limit_bytes=48 * 1024 * 1024),
        cost_estimate=pl.CostEstimate(
            flops=2 * rows * CHUNK * s * per * chunks,
            transcendentals=0,
            bytes_accessed=2 * rows * (CHUNK * chunks + skip_cols),
        ),
    )(hidden, skip_weight)


def accumulate(src_ref, row_ref, field, lo_ref, hi_ref, arr_ref, band_ref, farw_ref, acc):
    nblk = field.shape[0] // BLK
    far_cap = farw_ref.shape[0]
    for r in range(nblk):
        prev = lo_ref[...] if r == 0 else field[(r - 1) * BLK : r * BLK, :]
        nxt = hi_ref[...] if r == nblk - 1 else field[(r + 1) * BLK : (r + 2) * BLK, :]
        own = field[r * BLK : (r + 1) * BLK, :]
        v = jnp.dot(band_ref[0, r * BLK : (r + 1) * BLK, :], prev, preferred_element_type=f32)
        v = v + jnp.dot(band_ref[1, r * BLK : (r + 1) * BLK, :], own, preferred_element_type=f32)
        v = v + jnp.dot(band_ref[2, r * BLK : (r + 1) * BLK, :], nxt, preferred_element_type=f32)
        acc[r * BLK : (r + 1) * BLK, :] = v
    acc[nblk * BLK :, :] = jnp.zeros((BLK, acc.shape[1]), f32)

    def slot(k, carry):
        row = row_ref[k]
        piece = arr_ref[src_ref[k]]
        start = pl.multiple_of(row * BLK, BLK)
        acc[pl.ds(start, BLK), :] += jnp.dot(farw_ref[k], piece, preferred_element_type=f32)
        return carry

    lax.fori_loop(0, far_cap, slot, 0)


def hop1_kernel(
    src_ref, row_ref, send_ref, field_ref, lo_ref, hi_ref, arr_ref, band_ref, farw_ref,
    out_ref, out_send_ref, acc,
):
    accumulate(src_ref, row_ref, field_ref, lo_ref, hi_ref, arr_ref, band_ref, farw_ref, acc)
    nrows = field_ref.shape[0]
    out_ref[...] = acc[:nrows, :].astype(bf16)
    for p in range(out_send_ref.shape[0]):
        start = pl.multiple_of(send_ref[p] * BLK, BLK)
        out_send_ref[p] = out_ref[pl.ds(start, BLK), :]


def hop2_kernel(
    src_ref, row_ref, field_ref, lo_ref, hi_ref, arr_ref, band_ref, farw_ref,
    x_ref, h_ref, mix_ref, out_ref, acc,
):
    accumulate(src_ref, row_ref, field_ref, lo_ref, hi_ref, arr_ref, band_ref, farw_ref, acc)
    nrows, width = field_ref.shape
    half = x_ref.shape[1] // 2
    cw = mix_ref.shape[1]
    per = CHUNK // cw
    mix = mix_ref[...]
    m = [bd_inkernel(mix[i * cw : (i + 1) * cw], per) for i in range(3)]
    for j in range(width // CHUNK):
        cols = slice(j * CHUNK, (j + 1) * CHUNK)
        two = acc[:nrows, cols].astype(bf16)
        v = x_ref[:, half + j * CHUNK : half + (j + 1) * CHUNK].astype(f32)
        v = v + jnp.dot(h_ref[:, cols], m[0], preferred_element_type=f32)
        v = v + jnp.dot(field_ref[:, cols], m[1], preferred_element_type=f32)
        v = v + jnp.dot(two, m[2], preferred_element_type=f32)
        out_ref[:, cols] = v.astype(bf16)


def vmem():
    return pl.BlockSpec(memory_space=pltpu.VMEM)


def smem():
    return pl.BlockSpec(memory_space=pltpu.SMEM)


def hop1(src, rows, send_rows, field, lo, hi, arrived, band3, farw3):
    nrows, width = field.shape
    return pl.pallas_call(
        hop1_kernel,
        in_specs=[smem(), smem(), smem()] + [vmem()] * 6,
        out_specs=[vmem(), vmem()],
        out_shape=[
            jax.ShapeDtypeStruct((nrows, width), bf16),
            jax.ShapeDtypeStruct(arrived.shape, bf16),
        ],
        scratch_shapes=[pltpu.VMEM((nrows + BLK, width), f32)],
        compiler_params=pltpu.CompilerParams(vmem_limit_bytes=48 * 1024 * 1024),
        cost_estimate=pl.CostEstimate(
            flops=2 * BLK * BLK * width * (3 * nrows // BLK + farw3.shape[0]),
            transcendentals=0,
            bytes_accessed=2 * width * (nrows * 2 + 2 * arrived.shape[0] * BLK),
        ),
    )(src, rows, send_rows, field, lo, hi, arrived, band3, farw3)


def hop2(src, rows, field, lo, hi, arrived, band3, farw3, features, hidden, mix):
    nrows, width = field.shape
    return pl.pallas_call(
        hop2_kernel,
        in_specs=[smem(), smem()] + [vmem()] * 9,
        out_specs=vmem(),
        out_shape=jax.ShapeDtypeStruct((nrows, width), bf16),
        scratch_shapes=[pltpu.VMEM((nrows + BLK, width), f32)],
        compiler_params=pltpu.CompilerParams(vmem_limit_bytes=48 * 1024 * 1024),
        cost_estimate=pl.CostEstimate(
            flops=2 * BLK * BLK * width * (3 * nrows // BLK + farw3.shape[0])
            + 2 * nrows * width * CHUNK * 3,
            transcendentals=0,
            bytes_accessed=2 * width * (nrows * 6 + arrived.shape[0] * BLK),
        ),
    )(src, rows, field, lo, hi, arrived, band3, farw3, features, hidden, mix)


def halo(field):
    count = lax.axis_size("node")
    forward = [(i, i + 1) for i in range(count - 1)]
    backward = [(t, s) for s, t in forward]
    lo = lax.ppermute(field[field.shape[0] - BLK :], "node", forward)
    hi = lax.ppermute(field[:BLK], "node", backward)
    return lo, hi


def local(
    features,
    filter_gate_weight,
    skip_weight,
    mix_weight,
    band_weight,
    far_weight,
    far_ptr,
    far_col,
    export_block,
):
    node_rows = features.shape[0]
    blocks = node_rows // BLK
    far_cap = far_col.shape[1]

    own_index = lax.axis_index("node")
    own_exports = lax.dynamic_slice_in_dim(export_block, own_index, 1, 0)[0].astype(jnp.int32)
    columns = far_col[0].astype(jnp.int32)
    sources = columns // EXPORT
    pointers = far_ptr[0].astype(jnp.int32)
    slot_ids = jnp.arange(far_cap, dtype=jnp.int32)
    slot_rows = jnp.sum(
        (pointers[1:, None] <= slot_ids[None, :]).astype(jnp.int32), axis=0
    ).astype(jnp.int32)
    info = jnp.concatenate([columns, pointers[-1:]]).astype(f32)
    info_all = lax.all_gather(info, "node", axis=0).astype(jnp.int32)
    cols_all = info_all[:, :far_cap]
    used_all = info_all[:, far_cap]
    hits = (cols_all // EXPORT == own_index) & (slot_ids[None, :] < used_all[:, None])
    requested = jnp.sum(jnp.where(hits, cols_all % EXPORT, 0), axis=1)
    send_rows = own_exports[requested].astype(jnp.int32)

    hidden = front_hidden(features, filter_gate_weight)
    width = hidden.shape[1]
    band3 = band_weight.reshape(node_rows, 3, BLK).transpose(1, 0, 2)
    farw3 = far_weight.reshape(BLK, far_cap, BLK).transpose(1, 0, 2)

    def exchange(send):
        return lax.all_to_all(send, "node", split_axis=0, concat_axis=0, tiled=True)

    arrived1 = exchange(hidden.reshape(blocks, BLK, width)[send_rows])
    lo1, hi1 = halo(hidden)
    skip_out = front_skip(hidden, skip_weight)
    hop_one, send2 = hop1(sources, slot_rows, send_rows, hidden, lo1, hi1, arrived1, band3, farw3)
    arrived2 = exchange(send2)
    lo2, hi2 = halo(hop_one)
    residual = hop2(
        sources, slot_rows, hop_one, lo2, hi2, arrived2, band3, farw3, features, hidden, mix_weight
    )
    return residual, skip_out


def solution(mesh):
    placed = (
        P(("groups", "node"), None),
        P(),
        P(),
        P(),
        P("node", None),
        P(None, "node"),
        P("node", None),
        P("node", None),
        P(),
    )
    return jax.shard_map(
        local,
        mesh=mesh,
        in_specs=placed,
        out_specs=(P(("groups", "node"), None), P(("groups", "node"), None)),
        check_vma=False,
    )
```

time: 123 us -> 108 us (0.88)
  the two profiles are of different devices: /device:TPU:0 before, /device:TPU:15 now
where the time goes in v4:
time: 108 us; the launch traced here: 107 us
  waiting for transfers between devices  29.8 us (28%)
  starting transfers between devices  27.7 us (26%)
  Pallas kernels  18.7 us (17%)
  blocking collectives  15.5 us (14%)
  local copies, waits for them, and re-layouts  12 us (11%)
  other arithmetic  2.95 us (3%)
    ppermute x2, waiting for transfers between devices, halo(): hi = lax.ppermute(field[:BLK], 'node', backward)  29.7 us
    all_gather x1, blocking collectives, local(): info_all = lax.all_gather(info, 'node', axis=0).astype(jnp.int32)  15.5 us
    all_to_all x2, starting transfers between devices, exchange(): return lax.all_to_all(send, 'node', split_axis=0, concat_axis=0, tiled=True)  14.8 us
    ppermute x2, starting transfers between devices, halo(): lo = lax.ppermute(field[field.shape[0] - BLK:], 'node', forward)  8.38 us
    pallas_call x1, Pallas kernels, hop2(): pl.pallas_call(hop2_kernel, in_specs=[smem(), smem()] + [vmem()] * 9, out...  6.99 us
    unnamed x23, local copies, waits for them, and re-layouts  5.61 us
    pallas_call x1, Pallas kernels, front_skip(): pl.pallas_call(skip_kernel, grid=(rows // tile,), in_specs=[pl.BlockSpec(...  5.44 us
    ppermute x2, starting transfers between devices, halo(): hi = lax.ppermute(field[:BLK], 'node', backward)  4.54 us
  transfers between devices with their start and end apart: 6, of which 2 were waited for; matrix products, arithmetic and copies ran while one was open for 3% of the time, Pallas kernels for 5%

profile of v4, /device:TPU:15, one launch (start us, length us, event | category | flops | bytes accessed | tf_op | source)
XLA Modules:
  0.0 107.4 jit_solution(8636210818705819747)
XLA Ops:
  0.6 0.0 copy-start
  0.6 0.0 copy-start.10
  0.7 0.0 copy-start.9
  0.7 0.0 copy-start.5
  0.7 1.3 %slice.27 = s32[1,1]{1,0:T(1,128)} slice(s32[1,17]{1,0:T(1,128)} %param.15), slice={[0:1], [16:17]} | slice | bytes 8 | tf_op jit(solution)/shard_map/slice | solution.py:264
  2.0 0.0 copy-done
  2.0 0.1 constant_dynamic-slice_fusion
  2.1 0.5 fusion.10
  2.6 1.3 %fusion.6 = f32[1,1,16]{2,1,0:T(1,128)S(1)} fusion(s32[1,1]{1,0:T(1,128)} %slice.27, s32[1,15]{1,0:T(1,128)} %param.16), kind=kLoop, calls=%fused_computation.27 | loop fusion | flops 32 | bytes 128
  4.0 15.5 %all-gather = f32[16,1,16]{2,1,0:T(1,128)S(1)} all-gather(f32[1,1,16]{2,1,0:T(1,128)S(1)} %fusion.6), channel_id=1, replica_groups=mesh['groups'=2,'node'=16] {'node'}, dimensions={0}, use_global_device_ids=true | all-gather | bytes 1088 | tf_op jit(solution)/shard_map/all_gather | solution.py:265
  19.4 0.2 slice_reduce_fusion
  19.6 0.2 fusion.2
  19.8 1.3 %fusion.5 = (s32[16]{0:T(128)S(1)}, s32[16]{0:T(128)S(1)}) fusion(s32[]{:T(128)} %bitcast.6, s32[]{:T(128)} %bitcast.5, s32[16]{0:T(128)S(1)} %fusion.2), kind=kLoop, calls=%fused_computation.25 | loop fusion | flops 128 | bytes 200 | tf_op jit(solution)/shard_map/select_n | solution.py:280
  21.1 0.0 copy-start.1
  21.1 1.6 %copy-done.1 = bf16[1024,1024]{1,0:T(8,128)(2,1)S(1)} copy-done((bf16[1024,1024]{1,0:T(8,128)(2,1)S(1)}, bf16[1024,1024]{1,0:T(8,128)(2,1)}, u32[]{:S(2)}) %copy-start.1) | copy-done | bytes 2097176
  22.7 0.7 copy-done.6
  23.5 2.4 %shard_map.104.field_ref.h_ref = bf16[1024,512]{1,0:T(8,128)(2,1)S(1)} custom-call(bf16[1024,1024]{1,0:T(8,128)(2,1)S(1)} %copy-done.1, bf16[64,64]{1,0:T(8,128)(2,1)S(1)} %copy-done.6), custom_call_target="tpu_custom_call" | custom-call | flops 1073741824 | bytes 3145728 | tf_op jit(solution)/shard_map/pallas_call | solution.py:84
  25.9 1.6 %gather_fusion = bf16[16,64,512]{2,1,0:T(8,128)(2,1)} fusion(bf16[16,64,512]{2,1,0:T(8,128)(2,1)S(1)} %bitcast.31, s32[1024]{0:T(1024)S(1)} %pad_clamp_fusion), kind=kCustom, calls=%fused_computation | custom fusion | bytes 2097216 | tf_op jit(solution)/shard_map/gather | solution.py:280
  27.5 10.2 %all-to-all-start = ((bf16[16,64,512]{2,1,0:T(8,128)(2,1)}), bf16[16,64,512]{2,1,0:T(8,128)(2,1)S(1)}, u32[]{:S(2)}, u32[]{:S(2)}) async-start(bf16[16,64,512]{2,1,0:T(8,128)(2,1)} %gather_fusion), calls=%async_computation | async-start | bytes 2097152 | tf_op jit(solution)/shard_map/all_to_all | solution.py:278
  37.7 2.3 %collective-permute-start.1 = (bf16[64,512]{1,0:T(8,128)(2,1)S(1)}, bf16[64,512]{1,0:T(8,128)(2,1)S(1)}, u32[]{:S(2)}, u32[]{:S(2)}) collective-permute-start(bf16[64,512]{1,0:T(8,128)(2,1)S(1)} %get-tuple-element.8), channel_id=1, source_target_pairs={{1,0},{2,1},{3,2},{4,3},{5,4},{6,5},{7,6},{8,7},{9,8},{10,9},{11,1... | collective-permute-start | bytes 196616 | tf_op jit(solution)/shard_map/ppermute | solution.py:236
  40.0 4.2 %collective-permute-start = (bf16[64,512]{1,0:T(8,128)(2,1)S(1)}, bf16[64,512]{1,0:T(8,128)(2,1)S(1)}, u32[]{:S(2)}, u32[]{:S(2)}) collective-permute-start(bf16[64,512]{1,0:T(8,128)(2,1)S(1)} %get-tuple-element.9), channel_id=1, source_target_pairs={{0,1},{1,2},{2,3},{3,4},{4,5},{5,6},{6,7},{7,8},{8,9},{9,10},{10,1... | collective-permute-start | bytes 196616 | tf_op jit(solution)/shard_map/ppermute | solution.py:235
  44.2 0.0 copy-done.7
  44.2 0.2 reshape.70
  44.4 0.0 copy-start.8
  44.4 0.1 copy.22
  44.5 1.4 %copy.18 = bf16[1024,3,64]{2,0,1:T(8,128)(2,1)S(1)} copy(bf16[1024,3,64]{0,2,1:T(8,128)(2,1)} %bitcast.36) | data formatting | bytes 786432 | tf_op jit(solution)/shard_map/reshape | solution.py:274
  46.0 0.0 copy-done.9
  46.0 0.1 slice_bitcast_fusion
  46.1 0.1 convert_reduce_fusion.row_ref
  46.1 17.1 %collective-permute-done.1.hi_ref = bf16[64,512]{1,0:T(8,128)(2,1)S(1)} collective-permute-done((bf16[64,512]{1,0:T(8,128)(2,1)S(1)}, bf16[64,512]{1,0:T(8,128)(2,1)S(1)}, u32[]{:S(2)}, u32[]{:S(2)}) %collective-permute-start.1) | collective-permute-done | bytes 65568 | tf_op jit(solution)/shard_map/ppermute | solution.py:236
  63.3 0.0 collective-permute-done.lo_ref
  63.3 0.0 all-to-all-done.arr_ref
  63.3 3.8 %shard_map.105 = (bf16[1024,512]{1,0:T(8,128)(2,1)S(1)}, bf16[16,64,512]{2,1,0:T(8,128)(2,1)S(1)}) custom-call(s32[15]{0:T(128)S(1)} %and_select_fusion.src_ref, s32[15]{0:T(128)S(1)} %convert_reduce_fusion.row_ref, s32[16]{0:T(128)S(1)} %get-tuple-element.13.send_ref, bf16[1024,512]{1,0:T(8,128)(2,1)S(1)} %shard_map.104.field_ref.h_ref, ...), custom_call_target="tpu_custom_call" | custom-call | flops 264241152 | bytes 4194304 | tf_op jit(solution)/shard_map/pallas_call | solution.py:195
  67.1 0.0 copy-start.2
  67.1 1.0 copy-done.2
  68.1 1.0 copy-done.4
  69.1 4.5 %all-to-all-start.1 = ((bf16[16,64,512]{2,1,0:T(8,128)(2,1)}), bf16[16,64,512]{2,1,0:T(8,128)(2,1)S(1)}, u32[]{:S(2)}, u32[]{:S(2)}) async-start(bf16[16,64,512]{2,1,0:T(8,128)(2,1)} %copy-done.4), calls=%async_computation.1 | async-start | bytes 2097152 | tf_op jit(solution)/shard_map/all_to_all | solution.py:278
  73.6 0.9 fusion.8
  74.5 2.3 %collective-permute-start.3 = (bf16[64,512]{1,0:T(8,128)(2,1)S(1)}, bf16[64,512]{1,0:T(8,128)(2,1)S(1)}, u32[]{:S(2)}, u32[]{:S(2)}) collective-permute-start(bf16[64,512]{1,0:T(8,128)(2,1)S(1)} %get-tuple-element.6), channel_id=1, source_target_pairs={{1,0},{2,1},{3,2},{4,3},{5,4},{6,5},{7,6},{8,7},{9,8},{10,9},{11,1... | collective-permute-start | bytes 196616 | tf_op jit(solution)/shard_map/ppermute | solution.py:236
  76.7 4.2 %collective-permute-start.2 = (bf16[64,512]{1,0:T(8,128)(2,1)S(1)}, bf16[64,512]{1,0:T(8,128)(2,1)S(1)}, u32[]{:S(2)}, u32[]{:S(2)}) collective-permute-start(bf16[64,512]{1,0:T(8,128)(2,1)S(1)} %get-tuple-element.7), channel_id=1, source_target_pairs={{0,1},{1,2},{2,3},{3,4},{4,5},{5,6},{6,7},{7,8},{8,9},{9,10},{10,1... | collective-permute-start | bytes 196616 | tf_op jit(solution)/shard_map/ppermute | solution.py:235
  81.0 5.4 %shard_map.107 = bf16[1024,4096]{1,0:T(8,128)(2,1)} custom-call(bf16[1024,512]{1,0:T(8,128)(2,1)S(1)} %shard_map.104.field_ref.h_ref, bf16[32,256]{1,0:T(8,128)(2,1)S(1)} %copy-done.5), custom_call_target="tpu_custom_call" | custom-call | flops 2147483648 | bytes 9437184 | tf_op jit(solution)/shard_map/pallas_call | solution.py:110
  86.4 0.0 copy-done.8
  86.4 0.1 copy.20.mix_ref
  86.5 12.6 %collective-permute-done.3.hi_ref = bf16[64,512]{1,0:T(8,128)(2,1)S(1)} collective-permute-done((bf16[64,512]{1,0:T(8,128)(2,1)S(1)}, bf16[64,512]{1,0:T(8,128)(2,1)S(1)}, u32[]{:S(2)}, u32[]{:S(2)}) %collective-permute-start.3) | collective-permute-done | bytes 65568 | tf_op jit(solution)/shard_map/ppermute | solution.py:236
  99.1 0.0 collective-permute-done.2.lo_ref
  99.1 0.0 all-to-all-done.1.arr_ref
  99.2 1.2 %copy-done.3 = bf16[1024,512]{1,0:T(8,128)(2,1)S(1)} copy-done((bf16[1024,512]{1,0:T(8,128)(2,1)S(1)}, bf16[1024,512]{1,0:T(8,128)(2,1)}, u32[]{:S(2)}) %copy-start.3) | copy-done | bytes 1048600
  100.4 7.0 %shard_map.106 = bf16[1024,512]{1,0:T(8,128)(2,1)} custom-call(s32[15]{0:T(128)S(1)} %and_select_fusion.src_ref, s32[15]{0:T(128)S(1)} %convert_reduce_fusion.row_ref, bf16[1024,512]{1,0:T(8,128)(2,1)S(1)} %copy-done.3, bf16[64,512]{1,0:T(8,128)(2,1)S(1)} %collective-permute-done.2.lo_ref, bf16[64,512]{1,0:T(8,128)(2,1)S(1)} %collective-permute-done.3.hi_ref, ...), custom_call_target="tpu_custom_call" | custom-call | flops 1069547520 | bytes 7340032 | tf_op jit(solution)/shard_map/pallas_call | solution.py:215
  (10 shorter events, 0.0 us)
Async XLA Ops:
  0.6 1.4 %copy-start = (s32[16,2]{0,1:T(2,128)S(1)}, s32[16,2]{0,1:T(2,128)}, u32[]{:S(2)}) copy-start(s32[16,2]{0,1:T(2,128)} %param.17) | copy-start | bytes 388
  0.6 45.3 %copy-start.10 = (s32[1,17]{1,0:T(1,128)S(1)}, s32[1,17]{1,0:T(1,128)}, u32[]{:S(2)}) copy-start(s32[1,17]{1,0:T(1,128)} %param.15) | copy-start | bytes 208
  0.7 45.3 %copy-start.9 = (s32[1,15]{1,0:T(1,128)S(1)}, s32[1,15]{1,0:T(1,128)}, u32[]{:S(2)}) copy-start(s32[1,15]{1,0:T(1,128)} %param.16) | copy-start | bytes 184
  0.7 80.3 %copy-start.5 = (bf16[32,256]{1,0:T(8,128)(2,1)S(1)}, bf16[32,256]{1,0:T(8,128)(2,1)}, u32[]{:S(2)}) copy-start(bf16[32,256]{1,0:T(8,128)(2,1)} %sw_ref.1) | copy-start | bytes 49156
  21.1 1.6 %copy-start.1 = (bf16[1024,1024]{1,0:T(8,128)(2,1)S(1)}, bf16[1024,1024]{1,0:T(8,128)(2,1)}, u32[]{:S(2)}) copy-start(bf16[1024,1024]{1,0:T(8,128)(2,1)} %x_ref.3) | copy-start | bytes 6291460
  22.7 0.7 copy-start.6
  23.4 20.7 %copy-start.7 = (bf16[64,960]{1,0:T(8,128)(2,1)S(1)}, bf16[64,960]{1,0:T(8,128)(2,1)}, u32[]{:S(2)}) copy-start(bf16[64,960]{1,0:T(8,128)(2,1)} %param.14) | copy-start | bytes 368644
  27.5 35.8 %all-to-all-start = ((bf16[16,64,512]{2,1,0:T(8,128)(2,1)}), bf16[16,64,512]{2,1,0:T(8,128)(2,1)S(1)}, u32[]{:S(2)}, u32[]{:S(2)}) async-start(bf16[16,64,512]{2,1,0:T(8,128)(2,1)} %gather_fusion), calls=%async_computation | async-start | bytes 2097152 | tf_op jit(solution)/shard_map/all_to_all | solution.py:278
  37.7 25.6 %collective-permute-start.1 = (bf16[64,512]{1,0:T(8,128)(2,1)S(1)}, bf16[64,512]{1,0:T(8,128)(2,1)S(1)}, u32[]{:S(2)}, u32[]{:S(2)}) collective-permute-start(bf16[64,512]{1,0:T(8,128)(2,1)S(1)} %get-tuple-element.8), channel_id=1, source_target_pairs={{1,0},{2,1},{3,2},{4,3},{5,4},{6,5},{7,6},{8,7},{9,8},{10,9},{11,1... | collective-permute-start | bytes 196616 | tf_op jit(solution)/shard_map/ppermute | solution.py:236
  40.0 23.3 %collective-permute-start = (bf16[64,512]{1,0:T(8,128)(2,1)S(1)}, bf16[64,512]{1,0:T(8,128)(2,1)S(1)}, u32[]{:S(2)}, u32[]{:S(2)}) collective-permute-start(bf16[64,512]{1,0:T(8,128)(2,1)S(1)} %get-tuple-element.9), channel_id=1, source_target_pairs={{0,1},{1,2},{2,3},{3,4},{4,5},{5,6},{6,7},{7,8},{8,9},{9,10},{10,1... | collective-permute-start | bytes 196616 | tf_op jit(solution)/shard_map/ppermute | solution.py:235
  44.4 42.0 %copy-start.8 = (bf16[96,32]{0,1:T(8,128)(2,1)S(1)}, bf16[96,32]{0,1:T(8,128)(2,1)}, u32[]{:S(2)}) copy-start(bf16[96,32]{0,1:T(8,128)(2,1)} %param.12) | copy-start | bytes 18436
  67.1 1.0 copy-start.2
  68.1 1.0 copy-start.4
  69.1 30.1 %all-to-all-start.1 = ((bf16[16,64,512]{2,1,0:T(8,128)(2,1)}), bf16[16,64,512]{2,1,0:T(8,128)(2,1)S(1)}, u32[]{:S(2)}, u32[]{:S(2)}) async-start(bf16[16,64,512]{2,1,0:T(8,128)(2,1)} %copy-done.4), calls=%async_computation.1 | async-start | bytes 2097152 | tf_op jit(solution)/shard_map/all_to_all | solution.py:278
  74.5 24.7 %collective-permute-start.3 = (bf16[64,512]{1,0:T(8,128)(2,1)S(1)}, bf16[64,512]{1,0:T(8,128)(2,1)S(1)}, u32[]{:S(2)}, u32[]{:S(2)}) collective-permute-start(bf16[64,512]{1,0:T(8,128)(2,1)S(1)} %get-tuple-element.6), channel_id=1, source_target_pairs={{1,0},{2,1},{3,2},{4,3},{5,4},{6,5},{7,6},{8,7},{9,8},{10,9},{11,1... | collective-permute-start | bytes 196616 | tf_op jit(solution)/shard_map/ppermute | solution.py:236
  76.7 22.4 %collective-permute-start.2 = (bf16[64,512]{1,0:T(8,128)(2,1)S(1)}, bf16[64,512]{1,0:T(8,128)(2,1)S(1)}, u32[]{:S(2)}, u32[]{:S(2)}) collective-permute-start(bf16[64,512]{1,0:T(8,128)(2,1)S(1)} %get-tuple-element.7), channel_id=1, source_target_pairs={{0,1},{1,2},{2,3},{3,4},{4,5},{5,6},{6,7},{7,8},{8,9},{9,10},{10,1... | collective-permute-start | bytes 196616 | tf_op jit(solution)/shard_map/ppermute | solution.py:235
  99.2 1.2 %copy-start.3 = (bf16[1024,512]{1,0:T(8,128)(2,1)S(1)}, bf16[1024,512]{1,0:T(8,128)(2,1)}, u32[]{:S(2)}) copy-start(bf16[1024,512]{1,0:T(8,128)(2,1)} %copy-done.2) | copy-start | bytes 3145732

commit v5 on v4

--- a/solution.py
+++ b/solution.py
@@ -261,12 +261,14 @@
     slot_rows = jnp.sum(
         (pointers[1:, None] <= slot_ids[None, :]).astype(jnp.int32), axis=0
     ).astype(jnp.int32)
-    info = jnp.concatenate([columns, pointers[-1:]]).astype(f32)
-    info_all = lax.all_gather(info, "node", axis=0).astype(jnp.int32)
-    cols_all = info_all[:, :far_cap]
-    used_all = info_all[:, far_cap]
-    hits = (cols_all // EXPORT == own_index) & (slot_ids[None, :] < used_all[:, None])
-    requested = jnp.sum(jnp.where(hits, cols_all % EXPORT, 0), axis=1)
+    slot_export = columns % EXPORT
+    in_use = slot_ids < pointers[-1]
+    peers = jnp.arange(far_col.shape[1] + 1, dtype=jnp.int32)
+    matches = (sources[None, :] == peers[:, None]) & in_use[None, :]
+    wanted = jnp.sum(jnp.where(matches, slot_export[None, :], 0), axis=1)
+    requested = lax.all_to_all(wanted[:, None], "node", split_axis=0, concat_axis=0, tiled=True)[
+        :, 0
+    ]
     send_rows = own_exports[requested].astype(jnp.int32)
 
     hidden = front_hidden(features, filter_gate_weight)

time: 108 us -> 95.8 us (0.89)
  blocking collectives: 15.5 us -> 0 us
  starting transfers between devices: 27.7 us -> 30 us
    all_gather x1 -> x0, blocking collectives: 15.5 us -> none  [local(): info_all = lax.all_gather(info, 'node', axis=0).astype(jnp.int32)]
    all_to_all x0 -> x1, starting transfers between devices: none -> 6.55 us  [local(): lax.all_to_all(wanted[:, None], 'node', split_axis=0, concat_axis=0, tile...]
    all_to_all x2, starting transfers between devices: 14.8 us -> 10.6 us  [exchange(): return lax.all_to_all(send, 'node', split_axis=0, concat_axis=0, tiled=True)]
    unnamed x1 -> x0, other arithmetic: 1.35 us -> none
  transfers between devices with their start and end apart: 6 -> 7, of which waited for: 2 -> 2; matrix products, arithmetic and copies ran while one was open for 3% -> 4% of each run, Pallas kernels for 5% -> 8%
where the time goes in v5:
time: 95.8 us; the launch traced here: 95.1 us
  starting transfers between devices  30 us (31%)
  waiting for transfers between devices  29.8 us (31%)
  Pallas kernels  18.7 us (20%)
  local copies, waits for them, and re-layouts  12.4 us (13%)
  other arithmetic  3.26 us (3%)
    ppermute x2, waiting for transfers between devices, halo(): hi = lax.ppermute(field[:BLK], 'node', backward)  29.8 us
    all_to_all x2, starting transfers between devices, exchange(): return lax.all_to_all(send, 'node', split_axis=0, concat_axis=0, tiled=True)  10.6 us
    ppermute x2, starting transfers between devices, halo(): lo = lax.ppermute(field[field.shape[0] - BLK:], 'node', forward)  8.38 us
    pallas_call x1, Pallas kernels, hop2(): pl.pallas_call(hop2_kernel, in_specs=[smem(), smem()] + [vmem()] * 9, out...  6.98 us
    all_to_all x1, starting transfers between devices, local(): lax.all_to_all(wanted[:, None], 'node', split_axis=0, concat_axis=0, tile...  6.55 us
    unnamed x23, local copies, waits for them, and re-layouts  5.62 us
    pallas_call x1, Pallas kernels, front_skip(): pl.pallas_call(skip_kernel, grid=(rows // tile,), in_specs=[pl.BlockSpec(...  5.45 us
    ppermute x2, starting transfers between devices, halo(): hi = lax.ppermute(field[:BLK], 'node', backward)  4.54 us
  transfers between devices with their start and end apart: 7, of which 2 were waited for; matrix products, arithmetic and copies ran while one was open for 4% of the time, Pallas kernels for 8%

profile of v5, /device:TPU:15, one launch (start us, length us, event | category | flops | bytes accessed | tf_op | source)
XLA Modules:
  0.0 95.1 jit_solution(715237413647677159)
XLA Ops:
  0.6 0.0 copy-start
  0.6 0.0 copy-start.10
  0.7 0.0 copy-start.9
  0.7 0.0 copy-start.5
  0.7 1.3 %slice.21 = s32[1,1]{1,0:T(1,128)} slice(s32[1,17]{1,0:T(1,128)} %param.15), slice={[0:1], [16:17]} | slice | bytes 8 | tf_op jit(solution)/shard_map/slice | solution.py:265
  2.0 0.6 iota_compare_fusion.2
  2.6 0.7 fusion.3
  3.3 0.1 select_reduce_fusion
  3.4 0.7 copy.23
  4.1 6.6 %all-to-all-start = ((s32[16,1,1]{2,1,0:T(1,128)}), s32[16,1,1]{2,1,0:T(1,128)S(1)}, u32[]{:S(2)}, u32[]{:S(2)}) async-start(s32[16,1,1]{2,1,0:T(1,128)} %copy.23), calls=%async_computation | async-start | bytes 16384 | tf_op jit(solution)/shard_map/all_to_all | solution.py:269
  10.6 0.0 copy-done
  10.6 0.1 constant_dynamic-slice_fusion
  10.7 0.6 fusion.7
  11.3 1.6 %copy-done.1 = bf16[1024,1024]{1,0:T(8,128)(2,1)S(1)} copy-done((bf16[1024,1024]{1,0:T(8,128)(2,1)S(1)}, bf16[1024,1024]{1,0:T(8,128)(2,1)}, u32[]{:S(2)}) %copy-start.1) | copy-done | bytes 2097176
  12.9 0.7 copy-done.6
  13.6 2.4 %shard_map.104.field_ref.h_ref = bf16[1024,512]{1,0:T(8,128)(2,1)S(1)} custom-call(bf16[1024,1024]{1,0:T(8,128)(2,1)S(1)} %copy-done.1, bf16[64,64]{1,0:T(8,128)(2,1)S(1)} %copy-done.6), custom_call_target="tpu_custom_call" | custom-call | flops 1073741824 | bytes 3145728 | tf_op jit(solution)/shard_map/pallas_call | solution.py:84
  16.1 0.0 all-to-all-done
  16.1 0.4 reduce
  16.4 1.3 %fusion.2 = (s32[16]{0:T(128)S(1)}, s32[16]{0:T(128)S(1)}) fusion(s32[]{:T(128)} %bitcast.7, s32[]{:T(128)} %bitcast.6, s32[16]{0:T(128)S(1)} %reduce), kind=kLoop, calls=%fused_computation.21 | loop fusion | flops 128 | bytes 200 | tf_op jit(solution)/shard_map/select_n | solution.py:282
  17.8 1.6 %gather_fusion = bf16[16,64,512]{2,1,0:T(8,128)(2,1)} fusion(bf16[16,64,512]{2,1,0:T(8,128)(2,1)S(1)} %bitcast.34, s32[1024]{0:T(1024)S(1)} %pad_clamp_fusion), kind=kCustom, calls=%fused_computation | custom fusion | bytes 2097216 | tf_op jit(solution)/shard_map/gather | solution.py:282
  19.4 6.0 %all-to-all-start.1 = ((bf16[16,64,512]{2,1,0:T(8,128)(2,1)}), bf16[16,64,512]{2,1,0:T(8,128)(2,1)S(1)}, u32[]{:S(2)}, u32[]{:S(2)}) async-start(bf16[16,64,512]{2,1,0:T(8,128)(2,1)} %gather_fusion), calls=%async_computation.1 | async-start | bytes 2097152 | tf_op jit(solution)/shard_map/all_to_all | solution.py:280
  25.4 2.3 %collective-permute-start.1 = (bf16[64,512]{1,0:T(8,128)(2,1)S(1)}, bf16[64,512]{1,0:T(8,128)(2,1)S(1)}, u32[]{:S(2)}, u32[]{:S(2)}) collective-permute-start(bf16[64,512]{1,0:T(8,128)(2,1)S(1)} %get-tuple-element.8), channel_id=1, source_target_pairs={{1,0},{2,1},{3,2},{4,3},{5,4},{6,5},{7,6},{8,7},{9,8},{10,9},{11,1... | collective-permute-start | bytes 196616 | tf_op jit(solution)/shard_map/ppermute | solution.py:236
  27.7 4.2 %collective-permute-start = (bf16[64,512]{1,0:T(8,128)(2,1)S(1)}, bf16[64,512]{1,0:T(8,128)(2,1)S(1)}, u32[]{:S(2)}, u32[]{:S(2)}) collective-permute-start(bf16[64,512]{1,0:T(8,128)(2,1)S(1)} %get-tuple-element.9), channel_id=1, source_target_pairs={{0,1},{1,2},{2,3},{3,4},{4,5},{5,6},{6,7},{7,8},{8,9},{9,10},{10,1... | collective-permute-start | bytes 196616 | tf_op jit(solution)/shard_map/ppermute | solution.py:235
  31.9 0.0 copy-done.7
  31.9 0.2 reshape.67
  32.1 0.0 copy-start.8
  32.1 0.1 copy.28
  32.2 1.4 %copy.24 = bf16[1024,3,64]{2,0,1:T(8,128)(2,1)S(1)} copy(bf16[1024,3,64]{0,2,1:T(8,128)(2,1)} %bitcast.39) | data formatting | bytes 786432 | tf_op jit(solution)/shard_map/reshape | solution.py:276
  33.6 0.1 slice_bitcast_fusion
  33.7 0.1 convert_reduce_fusion.row_ref
  33.8 17.2 %collective-permute-done.1.hi_ref = bf16[64,512]{1,0:T(8,128)(2,1)S(1)} collective-permute-done((bf16[64,512]{1,0:T(8,128)(2,1)S(1)}, bf16[64,512]{1,0:T(8,128)(2,1)S(1)}, u32[]{:S(2)}, u32[]{:S(2)}) %collective-permute-start.1) | collective-permute-done | bytes 65568 | tf_op jit(solution)/shard_map/ppermute | solution.py:236
  51.0 0.0 collective-permute-done.lo_ref
  51.0 0.0 all-to-all-done.1.arr_ref
  51.0 3.8 %shard_map.105 = (bf16[1024,512]{1,0:T(8,128)(2,1)S(1)}, bf16[16,64,512]{2,1,0:T(8,128)(2,1)S(1)}) custom-call(s32[15]{0:T(128)S(1)} %and_select_fusion.2.src_ref, s32[15]{0:T(128)S(1)} %convert_reduce_fusion.row_ref, s32[16]{0:T(128)S(1)} %get-tuple-element.13.send_ref, bf16[1024,512]{1,0:T(8,128)(2,1)S(1)} %shard_map.104.field_ref.h_ref, ...), custom_call_target="tpu_custom_call" | custom-call | flops 264241152 | bytes 4194304 | tf_op jit(solution)/shard_map/pallas_call | solution.py:195
  54.8 0.0 copy-start.2
  54.8 1.0 %copy-done.2 = bf16[1024,512]{1,0:T(8,128)(2,1)} copy-done((bf16[1024,512]{1,0:T(8,128)(2,1)}, bf16[1024,512]{1,0:T(8,128)(2,1)S(1)}, u32[]{:S(2)}) %copy-start.2) | copy-done | bytes 1048600
  55.8 1.0 %copy-done.4 = bf16[16,64,512]{2,1,0:T(8,128)(2,1)} copy-done((bf16[16,64,512]{2,1,0:T(8,128)(2,1)}, bf16[16,64,512]{2,1,0:T(8,128)(2,1)S(1)}, u32[]{:S(2)}) %copy-start.4) | copy-done | bytes 1048600
  56.8 4.6 %all-to-all-start.2 = ((bf16[16,64,512]{2,1,0:T(8,128)(2,1)}), bf16[16,64,512]{2,1,0:T(8,128)(2,1)S(1)}, u32[]{:S(2)}, u32[]{:S(2)}) async-start(bf16[16,64,512]{2,1,0:T(8,128)(2,1)} %copy-done.4), calls=%async_computation.2 | async-start | bytes 2097152 | tf_op jit(solution)/shard_map/all_to_all | solution.py:280
  61.3 0.9 fusion.5
  62.2 2.3 %collective-permute-start.3 = (bf16[64,512]{1,0:T(8,128)(2,1)S(1)}, bf16[64,512]{1,0:T(8,128)(2,1)S(1)}, u32[]{:S(2)}, u32[]{:S(2)}) collective-permute-start(bf16[64,512]{1,0:T(8,128)(2,1)S(1)} %get-tuple-element.6), channel_id=1, source_target_pairs={{1,0},{2,1},{3,2},{4,3},{5,4},{6,5},{7,6},{8,7},{9,8},{10,9},{11,1... | collective-permute-start | bytes 196616 | tf_op jit(solution)/shard_map/ppermute | solution.py:236
  64.5 4.2 %collective-permute-start.2 = (bf16[64,512]{1,0:T(8,128)(2,1)S(1)}, bf16[64,512]{1,0:T(8,128)(2,1)S(1)}, u32[]{:S(2)}, u32[]{:S(2)}) collective-permute-start(bf16[64,512]{1,0:T(8,128)(2,1)S(1)} %get-tuple-element.7), channel_id=1, source_target_pairs={{0,1},{1,2},{2,3},{3,4},{4,5},{5,6},{6,7},{7,8},{8,9},{9,10},{10,1... | collective-permute-start | bytes 196616 | tf_op jit(solution)/shard_map/ppermute | solution.py:235
  68.7 5.4 %shard_map.107 = bf16[1024,4096]{1,0:T(8,128)(2,1)} custom-call(bf16[1024,512]{1,0:T(8,128)(2,1)S(1)} %shard_map.104.field_ref.h_ref, bf16[32,256]{1,0:T(8,128)(2,1)S(1)} %copy-done.5), custom_call_target="tpu_custom_call" | custom-call | flops 2147483648 | bytes 9437184 | tf_op jit(solution)/shard_map/pallas_call | solution.py:110
  74.1 0.1 copy.26.mix_ref
  74.2 12.6 %collective-permute-done.3.hi_ref = bf16[64,512]{1,0:T(8,128)(2,1)S(1)} collective-permute-done((bf16[64,512]{1,0:T(8,128)(2,1)S(1)}, bf16[64,512]{1,0:T(8,128)(2,1)S(1)}, u32[]{:S(2)}, u32[]{:S(2)}) %collective-permute-start.3) | collective-permute-done | bytes 65568 | tf_op jit(solution)/shard_map/ppermute | solution.py:236
  86.9 0.0 collective-permute-done.2.lo_ref
  86.9 0.0 all-to-all-done.2.arr_ref
  86.9 1.2 %copy-done.3 = bf16[1024,512]{1,0:T(8,128)(2,1)S(1)} copy-done((bf16[1024,512]{1,0:T(8,128)(2,1)S(1)}, bf16[1024,512]{1,0:T(8,128)(2,1)}, u32[]{:S(2)}) %copy-start.3) | copy-done | bytes 1048600
  88.1 7.0 %shard_map.106 = bf16[1024,512]{1,0:T(8,128)(2,1)} custom-call(s32[15]{0:T(128)S(1)} %and_select_fusion.2.src_ref, s32[15]{0:T(128)S(1)} %convert_reduce_fusion.row_ref, bf16[1024,512]{1,0:T(8,128)(2,1)S(1)} %copy-done.3, bf16[64,512]{1,0:T(8,128)(2,1)S(1)} %collective-permute-done.2.lo_ref, bf16[64,512]{1,0:T(8,128)(2,1)S(1)} %collective-permute-done.3.hi_ref, ...), custom_call_target="tpu_custom_call" | custom-call | flops 1069547520 | bytes 7340032 | tf_op jit(solution)/shard_map/pallas_call | solution.py:215
  (12 shorter events, 0.0 us)
Async XLA Ops:
  0.6 10.0 %copy-start = (s32[16,2]{0,1:T(2,128)S(1)}, s32[16,2]{0,1:T(2,128)}, u32[]{:S(2)}) copy-start(s32[16,2]{0,1:T(2,128)} %param.17) | copy-start | bytes 388
  0.6 33.0 %copy-start.10 = (s32[1,17]{1,0:T(1,128)S(1)}, s32[1,17]{1,0:T(1,128)}, u32[]{:S(2)}) copy-start(s32[1,17]{1,0:T(1,128)} %param.15) | copy-start | bytes 208
  0.7 32.9 %copy-start.9 = (s32[1,15]{1,0:T(1,128)S(1)}, s32[1,15]{1,0:T(1,128)}, u32[]{:S(2)}) copy-start(s32[1,15]{1,0:T(1,128)} %param.16) | copy-start | bytes 184
  0.7 68.0 %copy-start.5 = (bf16[32,256]{1,0:T(8,128)(2,1)S(1)}, bf16[32,256]{1,0:T(8,128)(2,1)}, u32[]{:S(2)}) copy-start(bf16[32,256]{1,0:T(8,128)(2,1)} %sw_ref.1) | copy-start | bytes 49156
  4.1 12.0 %all-to-all-start = ((s32[16,1,1]{2,1,0:T(1,128)}), s32[16,1,1]{2,1,0:T(1,128)S(1)}, u32[]{:S(2)}, u32[]{:S(2)}) async-start(s32[16,1,1]{2,1,0:T(1,128)} %copy.23), calls=%async_computation | async-start | bytes 16384 | tf_op jit(solution)/shard_map/all_to_all | solution.py:269
  11.3 1.6 %copy-start.1 = (bf16[1024,1024]{1,0:T(8,128)(2,1)S(1)}, bf16[1024,1024]{1,0:T(8,128)(2,1)}, u32[]{:S(2)}) copy-start(bf16[1024,1024]{1,0:T(8,128)(2,1)} %x_ref.3) | copy-start | bytes 6291460
  12.9 0.7 copy-start.6
  13.6 18.3 %copy-start.7 = (bf16[64,960]{1,0:T(8,128)(2,1)S(1)}, bf16[64,960]{1,0:T(8,128)(2,1)}, u32[]{:S(2)}) copy-start(bf16[64,960]{1,0:T(8,128)(2,1)} %param.14) | copy-start | bytes 368644
  19.4 31.6 %all-to-all-start.1 = ((bf16[16,64,512]{2,1,0:T(8,128)(2,1)}), bf16[16,64,512]{2,1,0:T(8,128)(2,1)S(1)}, u32[]{:S(2)}, u32[]{:S(2)}) async-start(bf16[16,64,512]{2,1,0:T(8,128)(2,1)} %gather_fusion), calls=%async_computation.1 | async-start | bytes 2097152 | tf_op jit(solution)/shard_map/all_to_all | solution.py:280
  25.4 25.5 %collective-permute-start.1 = (bf16[64,512]{1,0:T(8,128)(2,1)S(1)}, bf16[64,512]{1,0:T(8,128)(2,1)S(1)}, u32[]{:S(2)}, u32[]{:S(2)}) collective-permute-start(bf16[64,512]{1,0:T(8,128)(2,1)S(1)} %get-tuple-element.8), channel_id=1, source_target_pairs={{1,0},{2,1},{3,2},{4,3},{5,4},{6,5},{7,6},{8,7},{9,8},{10,9},{11,1... | collective-permute-start | bytes 196616 | tf_op jit(solution)/shard_map/ppermute | solution.py:236
  27.7 23.3 %collective-permute-start = (bf16[64,512]{1,0:T(8,128)(2,1)S(1)}, bf16[64,512]{1,0:T(8,128)(2,1)S(1)}, u32[]{:S(2)}, u32[]{:S(2)}) collective-permute-start(bf16[64,512]{1,0:T(8,128)(2,1)S(1)} %get-tuple-element.9), channel_id=1, source_target_pairs={{0,1},{1,2},{2,3},{3,4},{4,5},{5,6},{6,7},{7,8},{8,9},{9,10},{10,1... | collective-permute-start | bytes 196616 | tf_op jit(solution)/shard_map/ppermute | solution.py:235
  32.1 42.0 %copy-start.8 = (bf16[96,32]{0,1:T(8,128)(2,1)S(1)}, bf16[96,32]{0,1:T(8,128)(2,1)}, u32[]{:S(2)}) copy-start(bf16[96,32]{0,1:T(8,128)(2,1)} %param.12) | copy-start | bytes 18436
  54.8 1.0 %copy-start.2 = (bf16[1024,512]{1,0:T(8,128)(2,1)}, bf16[1024,512]{1,0:T(8,128)(2,1)S(1)}, u32[]{:S(2)}) copy-start(bf16[1024,512]{1,0:T(8,128)(2,1)S(1)} %get-tuple-element.4.field_ref) | copy-start | bytes 3145732
  55.8 1.0 %copy-start.4 = (bf16[16,64,512]{2,1,0:T(8,128)(2,1)}, bf16[16,64,512]{2,1,0:T(8,128)(2,1)S(1)}, u32[]{:S(2)}) copy-start(bf16[16,64,512]{2,1,0:T(8,128)(2,1)S(1)} %get-tuple-element.5) | copy-start | bytes 3145732
  56.8 30.1 %all-to-all-start.2 = ((bf16[16,64,512]{2,1,0:T(8,128)(2,1)}), bf16[16,64,512]{2,1,0:T(8,128)(2,1)S(1)}, u32[]{:S(2)}, u32[]{:S(2)}) async-start(bf16[16,64,512]{2,1,0:T(8,128)(2,1)} %copy-done.4), calls=%async_computation.2 | async-start | bytes 2097152 | tf_op jit(solution)/shard_map/all_to_all | solution.py:280
  62.2 24.7 %collective-permute-start.3 = (bf16[64,512]{1,0:T(8,128)(2,1)S(1)}, bf16[64,512]{1,0:T(8,128)(2,1)S(1)}, u32[]{:S(2)}, u32[]{:S(2)}) collective-permute-start(bf16[64,512]{1,0:T(8,128)(2,1)S(1)} %get-tuple-element.6), channel_id=1, source_target_pairs={{1,0},{2,1},{3,2},{4,3},{5,4},{6,5},{7,6},{8,7},{9,8},{10,9},{11,1... | collective-permute-start | bytes 196616 | tf_op jit(solution)/shard_map/ppermute | solution.py:236
  64.5 22.4 %collective-permute-start.2 = (bf16[64,512]{1,0:T(8,128)(2,1)S(1)}, bf16[64,512]{1,0:T(8,128)(2,1)S(1)}, u32[]{:S(2)}, u32[]{:S(2)}) collective-permute-start(bf16[64,512]{1,0:T(8,128)(2,1)S(1)} %get-tuple-element.7), channel_id=1, source_target_pairs={{0,1},{1,2},{2,3},{3,4},{4,5},{5,6},{6,7},{7,8},{8,9},{9,10},{10,1... | collective-permute-start | bytes 196616 | tf_op jit(solution)/shard_map/ppermute | solution.py:235
  86.9 1.2 %copy-start.3 = (bf16[1024,512]{1,0:T(8,128)(2,1)S(1)}, bf16[1024,512]{1,0:T(8,128)(2,1)}, u32[]{:S(2)}) copy-start(bf16[1024,512]{1,0:T(8,128)(2,1)} %copy-done.2) | copy-start | bytes 3145732

commit v6 on v5

--- a/solution.py
+++ b/solution.py
@@ -19,6 +19,14 @@
 
 f32 = jnp.float32
 bf16 = jnp.bfloat16
+
+
+def vmem():
+    return pl.BlockSpec(memory_space=pltpu.VMEM)
+
+
+def smem():
+    return pl.BlockSpec(memory_space=pltpu.SMEM)
 
 
 def bd_inkernel(w, reps):
@@ -40,27 +48,71 @@
     return jnp.where(mask, tiled, 0.0).astype(bf16)
 
 
-def hidden_kernel(x_ref, fgw_ref, h_ref, wlo, whi):
-    half = x_ref.shape[1] // 2
+def send_row(req_ref, exp_ref, p):
+    own = lax.axis_index("node")
+    return exp_ref[own, req_ref[p]]
+
+
+def write_send(req_ref, exp_ref, field_ref, send_ref):
+    def body(p, carry):
+        start = pl.multiple_of(send_row(req_ref, exp_ref, p) * BLK, BLK)
+        send_ref[p] = field_ref[pl.ds(start, BLK), :]
+        return carry
+
+    lax.fori_loop(0, send_ref.shape[0], body, 0)
+
+
+def hidden_kernel(req_ref, exp_ref, x_ref, fgw_ref, h_ref, send_ref):
+    rows, cols = x_ref.shape
+    half = cols // 2
     cw = fgw_ref.shape[0] // 2
     per = CHUNK // cw
-
-    @pl.when(pl.program_id(0) == 0)
-    def _():
-        w = fgw_ref[...]
-        wlo[:, :CHUNK] = bd_inkernel(w[:cw, :cw], per)
-        wlo[:, CHUNK:] = bd_inkernel(w[:cw, cw:], per)
-        whi[:, :CHUNK] = bd_inkernel(w[cw:, :cw], per)
-        whi[:, CHUNK:] = bd_inkernel(w[cw:, cw:], per)
-
-    for j in range(half // CHUNK):
-        x0 = x_ref[:, j * CHUNK : (j + 1) * CHUNK]
-        x1 = x_ref[:, half + j * CHUNK : half + (j + 1) * CHUNK]
-        pre = jnp.dot(x0, wlo[...], preferred_element_type=f32)
-        pre = pre + jnp.dot(x1, whi[...], preferred_element_type=f32)
-        h_ref[:, j * CHUNK : (j + 1) * CHUNK] = (
-            jnp.tanh(pre[:, :CHUNK]) * jax.nn.sigmoid(pre[:, CHUNK:])
-        ).astype(bf16)
+    w = fgw_ref[...]
+    wlo = jnp.concatenate([bd_inkernel(w[:cw, :cw], per), bd_inkernel(w[:cw, cw:], per)], axis=1)
+    whi = jnp.concatenate([bd_inkernel(w[cw:, :cw], per), bd_inkernel(w[cw:, cw:], per)], axis=1)
+    tile = min(ROW_TILE, rows)
+    for t in range(rows // tile):
+        rs = slice(t * tile, (t + 1) * tile)
+        for j in range(half // CHUNK):
+            x0 = x_ref[rs, j * CHUNK : (j + 1) * CHUNK]
+            x1 = x_ref[rs, half + j * CHUNK : half + (j + 1) * CHUNK]
+            pre = jnp.dot(x0, wlo, preferred_element_type=f32)
+            pre = pre + jnp.dot(x1, whi, preferred_element_type=f32)
+            h_ref[rs, j * CHUNK : (j + 1) * CHUNK] = (
+                jnp.tanh(pre[:, :CHUNK]) * jax.nn.sigmoid(pre[:, CHUNK:])
+            ).astype(bf16)
+    write_send(req_ref, exp_ref, h_ref, send_ref)
+
+
+def prep_kernel(col_ref, ptr_ref, out_ref):
+    far_cap = col_ref.shape[1]
+    used = ptr_ref[0, ptr_ref.shape[1] - 1]
+
+    def clear(p, carry):
+        out_ref[p] = 0
+        return carry
+
+    lax.fori_loop(0, out_ref.shape[0], clear, 0)
+
+    def body(k, carry):
+        col = col_ref[0, k]
+
+        @pl.when(k < used)
+        def _():
+            out_ref[col // EXPORT] = col % EXPORT
+
+        return carry
+
+    lax.fori_loop(0, far_cap, body, 0)
+
+
+def prep(far_col, far_ptr):
+    return pl.pallas_call(
+        prep_kernel,
+        in_specs=[smem(), smem()],
+        out_specs=smem(),
+        out_shape=jax.ShapeDtypeStruct((far_col.shape[1] + 1,), jnp.int32),
+    )(far_col, far_ptr)
 
 
 def skip_kernel(h_ref, sw_ref, s_ref, ws):
@@ -77,27 +129,25 @@
         ).astype(bf16)
 
 
-def front_hidden(features, fgw):
+def front_hidden(requested, export_block, features, fgw):
     rows, cols = features.shape
-    chunks = cols // 2 // CHUNK
-    tile = min(ROW_TILE, rows)
+    half = cols // 2
+    peers = requested.shape[0]
     return pl.pallas_call(
         hidden_kernel,
-        grid=(rows // tile,),
-        in_specs=[
-            pl.BlockSpec((tile, cols), lambda i: (i, 0)),
-            pl.BlockSpec(fgw.shape, lambda i: (0, 0)),
+        in_specs=[smem(), smem(), vmem(), vmem()],
+        out_specs=[vmem(), vmem()],
+        out_shape=[
+            jax.ShapeDtypeStruct((rows, half), bf16),
+            jax.ShapeDtypeStruct((peers, BLK, half), bf16),
         ],
-        out_specs=pl.BlockSpec((tile, chunks * CHUNK), lambda i: (i, 0)),
-        out_shape=jax.ShapeDtypeStruct((rows, chunks * CHUNK), bf16),
-        scratch_shapes=[pltpu.VMEM((CHUNK, 2 * CHUNK), bf16), pltpu.VMEM((CHUNK, 2 * CHUNK), bf16)],
         compiler_params=pltpu.CompilerParams(vmem_limit_bytes=48 * 1024 * 1024),
         cost_estimate=pl.CostEstimate(
-            flops=2 * rows * CHUNK * 4 * CHUNK * chunks,
-            transcendentals=rows * CHUNK * chunks * 2,
-            bytes_accessed=2 * rows * (cols + CHUNK * chunks),
+            flops=2 * rows * CHUNK * 4 * CHUNK * (half // CHUNK),
+            transcendentals=rows * half * 2,
+            bytes_accessed=2 * rows * (cols + 2 * half),
         ),
-    )(features, fgw)
+    )(requested, export_block, features, fgw)
 
 
 def front_skip(hidden, skip_weight):
@@ -126,7 +176,7 @@
     )(hidden, skip_weight)
 
 
-def accumulate(src_ref, row_ref, field, lo_ref, hi_ref, arr_ref, band_ref, farw_ref, acc):
+def accumulate(col_ref, ptr_ref, field, lo_ref, hi_ref, arr_ref, band_ref, farw_ref, acc):
     nblk = field.shape[0] // BLK
     far_cap = farw_ref.shape[0]
     for r in range(nblk):
@@ -139,9 +189,13 @@
         acc[r * BLK : (r + 1) * BLK, :] = v
     acc[nblk * BLK :, :] = jnp.zeros((BLK, acc.shape[1]), f32)
 
+    nptr = ptr_ref.shape[1]
+
     def slot(k, carry):
-        row = row_ref[k]
-        piece = arr_ref[src_ref[k]]
+        row = 0
+        for r in range(1, nptr):
+            row = row + jnp.where(ptr_ref[0, r] <= k, 1, 0)
+        piece = arr_ref[col_ref[0, k] // EXPORT]
         start = pl.multiple_of(row * BLK, BLK)
         acc[pl.ds(start, BLK), :] += jnp.dot(farw_ref[k], piece, preferred_element_type=f32)
         return carry
@@ -150,22 +204,20 @@
 
 
 def hop1_kernel(
-    src_ref, row_ref, send_ref, field_ref, lo_ref, hi_ref, arr_ref, band_ref, farw_ref,
+    col_ref, ptr_ref, req_ref, exp_ref, field_ref, lo_ref, hi_ref, arr_ref, band_ref, farw_ref,
     out_ref, out_send_ref, acc,
 ):
-    accumulate(src_ref, row_ref, field_ref, lo_ref, hi_ref, arr_ref, band_ref, farw_ref, acc)
+    accumulate(col_ref, ptr_ref, field_ref, lo_ref, hi_ref, arr_ref, band_ref, farw_ref, acc)
     nrows = field_ref.shape[0]
     out_ref[...] = acc[:nrows, :].astype(bf16)
-    for p in range(out_send_ref.shape[0]):
-        start = pl.multiple_of(send_ref[p] * BLK, BLK)
-        out_send_ref[p] = out_ref[pl.ds(start, BLK), :]
+    write_send(req_ref, exp_ref, out_ref, out_send_ref)
 
 
 def hop2_kernel(
-    src_ref, row_ref, field_ref, lo_ref, hi_ref, arr_ref, band_ref, farw_ref,
+    col_ref, ptr_ref, field_ref, lo_ref, hi_ref, arr_ref, band_ref, farw_ref,
     x_ref, h_ref, mix_ref, out_ref, acc,
 ):
-    accumulate(src_ref, row_ref, field_ref, lo_ref, hi_ref, arr_ref, band_ref, farw_ref, acc)
+    accumulate(col_ref, ptr_ref, field_ref, lo_ref, hi_ref, arr_ref, band_ref, farw_ref, acc)
     nrows, width = field_ref.shape
     half = x_ref.shape[1] // 2
     cw = mix_ref.shape[1]
@@ -182,19 +234,11 @@
         out_ref[:, cols] = v.astype(bf16)
 
 
-def vmem():
-    return pl.BlockSpec(memory_space=pltpu.VMEM)
-
-
-def smem():
-    return pl.BlockSpec(memory_space=pltpu.SMEM)
-
-
-def hop1(src, rows, send_rows, field, lo, hi, arrived, band3, farw3):
+def hop1(far_col, far_ptr, requested, export_block, field, lo, hi, arrived, band3, farw3):
     nrows, width = field.shape
     return pl.pallas_call(
         hop1_kernel,
-        in_specs=[smem(), smem(), smem()] + [vmem()] * 6,
+        in_specs=[smem(), smem(), smem(), smem()] + [vmem()] * 6,
         out_specs=[vmem(), vmem()],
         out_shape=[
             jax.ShapeDtypeStruct((nrows, width), bf16),
@@ -207,10 +251,10 @@
             transcendentals=0,
             bytes_accessed=2 * width * (nrows * 2 + 2 * arrived.shape[0] * BLK),
         ),
-    )(src, rows, send_rows, field, lo, hi, arrived, band3, farw3)
-
-
-def hop2(src, rows, field, lo, hi, arrived, band3, farw3, features, hidden, mix):
+    )(far_col, far_ptr, requested, export_block, field, lo, hi, arrived, band3, farw3)
+
+
+def hop2(far_col, far_ptr, field, lo, hi, arrived, band3, farw3, features, hidden, mix):
     nrows, width = field.shape
     return pl.pallas_call(
         hop2_kernel,
@@ -225,7 +269,7 @@
             transcendentals=0,
             bytes_accessed=2 * width * (nrows * 6 + arrived.shape[0] * BLK),
         ),
-    )(src, rows, field, lo, hi, arrived, band3, farw3, features, hidden, mix)
+    )(far_col, far_ptr, field, lo, hi, arrived, band3, farw3, features, hidden, mix)
 
 
 def halo(field):
@@ -252,26 +296,11 @@
     blocks = node_rows // BLK
     far_cap = far_col.shape[1]
 
-    own_index = lax.axis_index("node")
-    own_exports = lax.dynamic_slice_in_dim(export_block, own_index, 1, 0)[0].astype(jnp.int32)
-    columns = far_col[0].astype(jnp.int32)
-    sources = columns // EXPORT
-    pointers = far_ptr[0].astype(jnp.int32)
-    slot_ids = jnp.arange(far_cap, dtype=jnp.int32)
-    slot_rows = jnp.sum(
-        (pointers[1:, None] <= slot_ids[None, :]).astype(jnp.int32), axis=0
-    ).astype(jnp.int32)
-    slot_export = columns % EXPORT
-    in_use = slot_ids < pointers[-1]
-    peers = jnp.arange(far_col.shape[1] + 1, dtype=jnp.int32)
-    matches = (sources[None, :] == peers[:, None]) & in_use[None, :]
-    wanted = jnp.sum(jnp.where(matches, slot_export[None, :], 0), axis=1)
+    wanted = prep(far_col, far_ptr)
     requested = lax.all_to_all(wanted[:, None], "node", split_axis=0, concat_axis=0, tiled=True)[
         :, 0
     ]
-    send_rows = own_exports[requested].astype(jnp.int32)
-
-    hidden = front_hidden(features, filter_gate_weight)
+    hidden, send1 = front_hidden(requested, export_block, features, filter_gate_weight)
     width = hidden.shape[1]
     band3 = band_weight.reshape(node_rows, 3, BLK).transpose(1, 0, 2)
     farw3 = far_weight.reshape(BLK, far_cap, BLK).transpose(1, 0, 2)
@@ -279,14 +308,14 @@
     def exchange(send):
         return lax.all_to_all(send, "node", split_axis=0, concat_axis=0, tiled=True)
 
-    arrived1 = exchange(hidden.reshape(blocks, BLK, width)[send_rows])
+    arrived1 = exchange(send1)
     lo1, hi1 = halo(hidden)
     skip_out = front_skip(hidden, skip_weight)
-    hop_one, send2 = hop1(sources, slot_rows, send_rows, hidden, lo1, hi1, arrived1, band3, farw3)
+    hop_one, send2 = hop1(far_col, far_ptr, requested, export_block, hidden, lo1, hi1, arrived1, band3, farw3)
     arrived2 = exchange(send2)
     lo2, hi2 = halo(hop_one)
     residual = hop2(
-        sources, slot_rows, hop_one, lo2, hi2, arrived2, band3, farw3, features, hidden, mix_weight
+        far_col, far_ptr, hop_one, lo2, hi2, arrived2, band3, farw3, features, hidden, mix_weight
     )
     return residual, skip_out
 

time: 95.8 us -> 97.4 us (1.017)
  other arithmetic: 3.26 us -> 0.37 us
  waiting for transfers between devices: 29.8 us -> 32.2 us
  Pallas kernels: 18.7 us -> 21 us
    all_to_all x1, waiting for transfers between devices: 0.01 us -> 2.97 us  [local(): lax.all_to_all(wanted[:, None], 'node', split_axis=0, concat_axis=0, tile...]
    pallas_call x2 -> x3, Pallas kernels: 6.24 us -> 8.6 us  [the longest x1 4.25 us: hop1(): pl.pallas_call(hop1_kernel, in_specs=[smem(), smem(), smem(), smem()] + [...]
    gather x2 -> x0, local copies, waits for them, and re-layouts: 2.18 us -> none  [the longest x1 1.58 us: local(): arrived1 = exchange(hidden.reshape(blocks, BLK, width)[send_rows])]
    unnamed x23 -> x22, local copies, waits for them, and re-layouts: 5.62 us -> 7.33 us
    select_n x2 -> x0, other arithmetic: 1.36 us -> none  [the longest x1 1.35 us: local(): arrived1 = exchange(hidden.reshape(blocks, BLK, width)[send_rows])]
    slice x1 -> x0, local copies, waits for them, and re-layouts: 1.28 us -> none  [local(): in_use = slot_ids < pointers[-1]]
  transfers between devices with their start and end apart: 7 -> 7, of which waited for: 2 -> 3; matrix products, arithmetic and copies ran while one was open for 4% -> 4% of each run, Pallas kernels for 8% -> 6%
where the time goes in v6:
time: 97.4 us; the launch traced here: 96.7 us
  waiting for transfers between devices  32.2 us (33%)
  starting transfers between devices  30.2 us (31%)
  Pallas kernels  21 us (22%)
  local copies, waits for them, and re-layouts  12.1 us (12%)
    ppermute x2, waiting for transfers between devices, halo(): hi = lax.ppermute(field[:BLK], 'node', backward)  29.2 us
    all_to_all x2, starting transfers between devices, exchange(): return lax.all_to_all(send, 'node', split_axis=0, concat_axis=0, tiled=True)  10.7 us
    ppermute x2, starting transfers between devices, halo(): lo = lax.ppermute(field[field.shape[0] - BLK:], 'node', forward)  8.38 us
    unnamed x22, local copies, waits for them, and re-layouts  7.33 us
    pallas_call x1, Pallas kernels, hop2(): pl.pallas_call(hop2_kernel, in_specs=[smem(), smem()] + [vmem()] * 9, out...  7.04 us
    all_to_all x1, starting transfers between devices, local(): lax.all_to_all(wanted[:, None], 'node', split_axis=0, concat_axis=0, tile...  6.55 us
    pallas_call x1, Pallas kernels, front_skip(): pl.pallas_call(skip_kernel, grid=(rows // tile,), in_specs=[pl.BlockSpec(...  5.37 us
    ppermute x2, starting transfers between devices, halo(): hi = lax.ppermute(field[:BLK], 'node', backward)  4.54 us
  transfers between devices with their start and end apart: 7, of which 3 were waited for; matrix products, arithmetic and copies ran while one was open for 4% of the time, Pallas kernels for 6%

profile of v6, /device:TPU:15, one launch (start us, length us, event | category | flops | bytes accessed | tf_op | source)
XLA Modules:
  0.0 96.7 jit_solution(3951044096155346306)
XLA Ops:
  0.6 0.0 copy-start.6
  0.6 0.0 copy-start.7
  0.7 0.0 copy-start.9
  0.7 0.0 copy-start.5
  0.7 1.6 %shard_map.104 = s32[16]{0:T(128)} custom-call(s32[1,15]{1,0:T(1,128)} %col_ref.5, s32[1,17]{1,0:T(1,128)} %ptr_ref.5), custom_call_target="tpu_custom_call" | custom-call | tf_op jit(solution)/shard_map/pallas_call | solution.py:110
  2.3 1.3 %copy.25 = s32[16,1,1]{2,1,0:T(1,128)} copy(s32[16,1,1]{0,2,1:T(1,128)} %bitcast.11) | data formatting | bytes 128 | tf_op jit(solution)/shard_map/all_to_all | solution.py:300
  3.6 6.6 %all-to-all-start = ((s32[16,1,1]{2,1,0:T(1,128)}), s32[16,1,1]{2,1,0:T(1,128)S(1)}, u32[]{:S(2)}, u32[]{:S(2)}) async-start(s32[16,1,1]{2,1,0:T(1,128)} %copy.25), calls=%async_computation | async-start | bytes 16384 | tf_op jit(solution)/shard_map/all_to_all | solution.py:300
  10.1 0.8 copy.29.exp_ref
  10.9 3.0 %all-to-all-done = s32[16,1,1]{2,1,0:T(1,128)S(1)} async-done(((s32[16,1,1]{2,1,0:T(1,128)}), s32[16,1,1]{2,1,0:T(1,128)S(1)}, u32[]{:S(2)}, u32[]{:S(2)}) %all-to-all-start) | async-done | bytes 96 | tf_op jit(solution)/shard_map/all_to_all | solution.py:300
  13.9 0.4 reduce.req_ref
  14.3 0.0 copy-start
  14.3 1.6 %copy-done = bf16[1024,1024]{1,0:T(8,128)(2,1)S(1)} copy-done((bf16[1024,1024]{1,0:T(8,128)(2,1)S(1)}, bf16[1024,1024]{1,0:T(8,128)(2,1)}, u32[]{:S(2)}) %copy-start) | copy-done | bytes 2097176
  15.9 0.0 copy-start.8
  15.9 0.7 copy-done.8
  16.6 2.8 %shard_map.105 = (bf16[1024,512]{1,0:T(8,128)(2,1)S(1)}, bf16[16,64,512]{2,1,0:T(8,128)(2,1)S(1)}) custom-call(s32[16]{0:T(128)S(1)} %reduce.req_ref, s32[16,2]{1,0:T(8,128)S(1)} %copy.29.exp_ref, bf16[1024,1024]{1,0:T(8,128)(2,1)S(1)} %copy-done, bf16[64,64]{1,0:T(8,128)(2,1)S(1)} %copy-done.8), custom_call_target="tpu_custom_call" | custom-call | flops 1073741824 | bytes 4194304 | tf_op jit(solution)/shard_map/pallas_call | solution.py:136
  19.3 0.0 copy-start.4
  19.4 1.0 copy-done.4
  20.3 6.2 %all-to-all-start.1 = ((bf16[16,64,512]{2,1,0:T(8,128)(2,1)}), bf16[16,64,512]{2,1,0:T(8,128)(2,1)S(1)}, u32[]{:S(2)}, u32[]{:S(2)}) async-start(bf16[16,64,512]{2,1,0:T(8,128)(2,1)} %copy-done.4), calls=%async_computation.1 | async-start | bytes 2097152 | tf_op jit(solution)/shard_map/all_to_all | solution.py:309
  26.5 2.3 %collective-permute-start.1 = (bf16[64,512]{1,0:T(8,128)(2,1)S(1)}, bf16[64,512]{1,0:T(8,128)(2,1)S(1)}, u32[]{:S(2)}, u32[]{:S(2)}) collective-permute-start(bf16[64,512]{1,0:T(8,128)(2,1)S(1)} %get-tuple-element.12), channel_id=1, source_target_pairs={{1,0},{2,1},{3,2},{4,3},{5,4},{6,5},{7,6},{8,7},{9,8},{10,9},{11,1... | collective-permute-start | bytes 196616 | tf_op jit(solution)/shard_map/ppermute | solution.py:280
  28.8 4.2 %collective-permute-start = (bf16[64,512]{1,0:T(8,128)(2,1)S(1)}, bf16[64,512]{1,0:T(8,128)(2,1)S(1)}, u32[]{:S(2)}, u32[]{:S(2)}) collective-permute-start(bf16[64,512]{1,0:T(8,128)(2,1)S(1)} %get-tuple-element.13), channel_id=1, source_target_pairs={{0,1},{1,2},{2,3},{3,4},{4,5},{5,6},{6,7},{7,8},{8,9},{9,10},{10,1... | collective-permute-start | bytes 196616 | tf_op jit(solution)/shard_map/ppermute | solution.py:279
  33.0 1.1 %reshape.15 = bf16[64,15,64]{2,1,0:T(8,128)(2,1)S(1)} reshape(bf16[64,960]{1,0:T(8,128)(2,1)} %param.14) | data formatting | bytes 245760 | tf_op jit(solution)/shard_map/reshape | solution.py:306
  34.1 0.1 copy.32
  34.2 1.4 %copy.27 = bf16[1024,3,64]{2,0,1:T(8,128)(2,1)S(1)} copy(bf16[1024,3,64]{0,2,1:T(8,128)(2,1)} %bitcast.10) | data formatting | bytes 786432 | tf_op jit(solution)/shard_map/reshape | solution.py:305
  35.6 16.5 %collective-permute-done.1.hi_ref = bf16[64,512]{1,0:T(8,128)(2,1)S(1)} collective-permute-done((bf16[64,512]{1,0:T(8,128)(2,1)S(1)}, bf16[64,512]{1,0:T(8,128)(2,1)S(1)}, u32[]{:S(2)}, u32[]{:S(2)}) %collective-permute-start.1) | collective-permute-done | bytes 65568 | tf_op jit(solution)/shard_map/ppermute | solution.py:280
  52.1 0.0 collective-permute-done.lo_ref
  52.1 0.0 all-to-all-done.1.arr_ref
  52.1 0.0 copy-done.6
  52.1 0.0 copy-done.7
  52.1 4.3 %shard_map.106 = (bf16[1024,512]{1,0:T(8,128)(2,1)S(1)}, bf16[16,64,512]{2,1,0:T(8,128)(2,1)S(1)}) custom-call(s32[1,15]{1,0:T(1,128)S(1)} %copy-done.6, s32[1,17]{1,0:T(1,128)S(1)} %copy-done.7, s32[16]{0:T(128)S(1)} %reduce.req_ref, s32[16,2]{1,0:T(8,128)S(1)} %copy.29.exp_ref, bf16[1024,512]{1,0:T(8,128)(2,1)S(1)} %get-tuple-element.6.field_ref.h_ref, ...), custom_call_target="tpu_custom_call" | custom-call | flops 264241152 | bytes 4194304 | tf_op jit(solution)/shard_map/pallas_call | solution.py:239
  56.3 0.0 copy-start.1
  56.4 1.0 copy-done.1
  57.3 0.0 copy-start.3
  57.3 1.0 %copy-done.3 = bf16[16,64,512]{2,1,0:T(8,128)(2,1)} copy-done((bf16[16,64,512]{2,1,0:T(8,128)(2,1)}, bf16[16,64,512]{2,1,0:T(8,128)(2,1)S(1)}, u32[]{:S(2)}) %copy-start.3) | copy-done | bytes 1048600
  58.3 4.5 %all-to-all-start.2 = ((bf16[16,64,512]{2,1,0:T(8,128)(2,1)}), bf16[16,64,512]{2,1,0:T(8,128)(2,1)S(1)}, u32[]{:S(2)}, u32[]{:S(2)}) async-start(bf16[16,64,512]{2,1,0:T(8,128)(2,1)} %copy-done.3), calls=%async_computation.2 | async-start | bytes 2097152 | tf_op jit(solution)/shard_map/all_to_all | solution.py:309
  62.8 0.0 copy-done.9
  62.8 0.1 copy.30.mix_ref
  63.0 0.9 fusion
  63.8 2.3 %collective-permute-start.3 = (bf16[64,512]{1,0:T(8,128)(2,1)S(1)}, bf16[64,512]{1,0:T(8,128)(2,1)S(1)}, u32[]{:S(2)}, u32[]{:S(2)}) collective-permute-start(bf16[64,512]{1,0:T(8,128)(2,1)S(1)} %get-tuple-element.10), channel_id=1, source_target_pairs={{1,0},{2,1},{3,2},{4,3},{5,4},{6,5},{7,6},{8,7},{9,8},{10,9},{11,1... | collective-permute-start | bytes 196616 | tf_op jit(solution)/shard_map/ppermute | solution.py:280
  66.1 4.2 %collective-permute-start.2 = (bf16[64,512]{1,0:T(8,128)(2,1)S(1)}, bf16[64,512]{1,0:T(8,128)(2,1)S(1)}, u32[]{:S(2)}, u32[]{:S(2)}) collective-permute-start(bf16[64,512]{1,0:T(8,128)(2,1)S(1)} %get-tuple-element.11), channel_id=1, source_target_pairs={{0,1},{1,2},{2,3},{3,4},{4,5},{5,6},{6,7},{7,8},{8,9},{9,10},{10,1... | collective-permute-start | bytes 196616 | tf_op jit(solution)/shard_map/ppermute | solution.py:279
  70.3 0.0 copy-done.5
  70.3 5.4 %shard_map.108 = bf16[1024,4096]{1,0:T(8,128)(2,1)} custom-call(bf16[1024,512]{1,0:T(8,128)(2,1)S(1)} %get-tuple-element.6.field_ref.h_ref, bf16[32,256]{1,0:T(8,128)(2,1)S(1)} %copy-done.5), custom_call_target="tpu_custom_call" | custom-call | flops 2147483648 | bytes 9437184 | tf_op jit(solution)/shard_map/pallas_call | solution.py:160
  75.7 12.7 %collective-permute-done.3.hi_ref = bf16[64,512]{1,0:T(8,128)(2,1)S(1)} collective-permute-done((bf16[64,512]{1,0:T(8,128)(2,1)S(1)}, bf16[64,512]{1,0:T(8,128)(2,1)S(1)}, u32[]{:S(2)}, u32[]{:S(2)}) %collective-permute-start.3) | collective-permute-done | bytes 65568 | tf_op jit(solution)/shard_map/ppermute | solution.py:280
  88.4 0.0 collective-permute-done.2.lo_ref
  88.4 0.0 all-to-all-done.2.arr_ref
  88.4 0.0 copy-start.2
  88.4 1.2 %copy-done.2 = bf16[1024,512]{1,0:T(8,128)(2,1)S(1)} copy-done((bf16[1024,512]{1,0:T(8,128)(2,1)S(1)}, bf16[1024,512]{1,0:T(8,128)(2,1)}, u32[]{:S(2)}) %copy-start.2) | copy-done | bytes 1048600
  89.6 7.0 %shard_map.107 = bf16[1024,512]{1,0:T(8,128)(2,1)} custom-call(s32[1,15]{1,0:T(1,128)S(1)} %copy-done.6, s32[1,17]{1,0:T(1,128)S(1)} %copy-done.7, bf16[1024,512]{1,0:T(8,128)(2,1)S(1)} %copy-done.2, bf16[64,512]{1,0:T(8,128)(2,1)S(1)} %collective-permute-done.2.lo_ref, bf16[64,512]{1,0:T(8,128)(2,1)S(1)} %collective-permute-done.3.hi_ref, ...), custom_call_target="tpu_custom_call" | custom-call | flops 1069547520 | bytes 7340032 | tf_op jit(solution)/shard_map/pallas_call | solution.py:259
  (1 shorter events, 0.0 us)
Async XLA Ops:
  0.6 51.4 %copy-start.6 = (s32[1,15]{1,0:T(1,128)S(1)}, s32[1,15]{1,0:T(1,128)}, u32[]{:S(2)}) copy-start(s32[1,15]{1,0:T(1,128)} %col_ref.5) | copy-start | bytes 184
  0.6 51.4 %copy-start.7 = (s32[1,17]{1,0:T(1,128)S(1)}, s32[1,17]{1,0:T(1,128)}, u32[]{:S(2)}) copy-start(s32[1,17]{1,0:T(1,128)} %ptr_ref.5) | copy-start | bytes 208
  0.7 62.2 %copy-start.9 = (bf16[96,32]{0,1:T(8,128)(2,1)S(1)}, bf16[96,32]{0,1:T(8,128)(2,1)}, u32[]{:S(2)}) copy-start(bf16[96,32]{0,1:T(8,128)(2,1)} %param.12) | copy-start | bytes 18436
  0.7 69.7 %copy-start.5 = (bf16[32,256]{1,0:T(8,128)(2,1)S(1)}, bf16[32,256]{1,0:T(8,128)(2,1)}, u32[]{:S(2)}) copy-start(bf16[32,256]{1,0:T(8,128)(2,1)} %sw_ref.1) | copy-start | bytes 49156
  3.6 10.3 %all-to-all-start = ((s32[16,1,1]{2,1,0:T(1,128)}), s32[16,1,1]{2,1,0:T(1,128)S(1)}, u32[]{:S(2)}, u32[]{:S(2)}) async-start(s32[16,1,1]{2,1,0:T(1,128)} %copy.25), calls=%async_computation | async-start | bytes 16384 | tf_op jit(solution)/shard_map/all_to_all | solution.py:300
  14.3 1.6 %copy-start = (bf16[1024,1024]{1,0:T(8,128)(2,1)S(1)}, bf16[1024,1024]{1,0:T(8,128)(2,1)}, u32[]{:S(2)}) copy-start(bf16[1024,1024]{1,0:T(8,128)(2,1)} %x_ref.3) | copy-start | bytes 6291460
  15.9 0.7 copy-start.8
  19.3 1.0 %copy-start.4 = (bf16[16,64,512]{2,1,0:T(8,128)(2,1)}, bf16[16,64,512]{2,1,0:T(8,128)(2,1)S(1)}, u32[]{:S(2)}) copy-start(bf16[16,64,512]{2,1,0:T(8,128)(2,1)S(1)} %get-tuple-element.7) | copy-start | bytes 3145732
  20.3 31.8 %all-to-all-start.1 = ((bf16[16,64,512]{2,1,0:T(8,128)(2,1)}), bf16[16,64,512]{2,1,0:T(8,128)(2,1)S(1)}, u32[]{:S(2)}, u32[]{:S(2)}) async-start(bf16[16,64,512]{2,1,0:T(8,128)(2,1)} %copy-done.4), calls=%async_computation.1 | async-start | bytes 2097152 | tf_op jit(solution)/shard_map/all_to_all | solution.py:309
  26.5 25.6 %collective-permute-start.1 = (bf16[64,512]{1,0:T(8,128)(2,1)S(1)}, bf16[64,512]{1,0:T(8,128)(2,1)S(1)}, u32[]{:S(2)}, u32[]{:S(2)}) collective-permute-start(bf16[64,512]{1,0:T(8,128)(2,1)S(1)} %get-tuple-element.12), channel_id=1, source_target_pairs={{1,0},{2,1},{3,2},{4,3},{5,4},{6,5},{7,6},{8,7},{9,8},{10,9},{11,1... | collective-permute-start | bytes 196616 | tf_op jit(solution)/shard_map/ppermute | solution.py:280
  28.8 23.3 %collective-permute-start = (bf16[64,512]{1,0:T(8,128)(2,1)S(1)}, bf16[64,512]{1,0:T(8,128)(2,1)S(1)}, u32[]{:S(2)}, u32[]{:S(2)}) collective-permute-start(bf16[64,512]{1,0:T(8,128)(2,1)S(1)} %get-tuple-element.13), channel_id=1, source_target_pairs={{0,1},{1,2},{2,3},{3,4},{4,5},{5,6},{6,7},{7,8},{8,9},{9,10},{10,1... | collective-permute-start | bytes 196616 | tf_op jit(solution)/shard_map/ppermute | solution.py:279
  56.3 1.0 %copy-start.1 = (bf16[1024,512]{1,0:T(8,128)(2,1)}, bf16[1024,512]{1,0:T(8,128)(2,1)S(1)}, u32[]{:S(2)}) copy-start(bf16[1024,512]{1,0:T(8,128)(2,1)S(1)} %get-tuple-element.8.field_ref) | copy-start | bytes 3145732
  57.3 1.0 %copy-start.3 = (bf16[16,64,512]{2,1,0:T(8,128)(2,1)}, bf16[16,64,512]{2,1,0:T(8,128)(2,1)S(1)}, u32[]{:S(2)}) copy-start(bf16[16,64,512]{2,1,0:T(8,128)(2,1)S(1)} %get-tuple-element.9) | copy-start | bytes 3145732
  58.3 30.1 %all-to-all-start.2 = ((bf16[16,64,512]{2,1,0:T(8,128)(2,1)}), bf16[16,64,512]{2,1,0:T(8,128)(2,1)S(1)}, u32[]{:S(2)}, u32[]{:S(2)}) async-start(bf16[16,64,512]{2,1,0:T(8,128)(2,1)} %copy-done.3), calls=%async_computation.2 | async-start | bytes 2097152 | tf_op jit(solution)/shard_map/all_to_all | solution.py:309
  63.8 24.6 %collective-permute-start.3 = (bf16[64,512]{1,0:T(8,128)(2,1)S(1)}, bf16[64,512]{1,0:T(8,128)(2,1)S(1)}, u32[]{:S(2)}, u32[]{:S(2)}) collective-permute-start(bf16[64,512]{1,0:T(8,128)(2,1)S(1)} %get-tuple-element.10), channel_id=1, source_target_pairs={{1,0},{2,1},{3,2},{4,3},{5,4},{6,5},{7,6},{8,7},{9,8},{10,9},{11,1... | collective-permute-start | bytes 196616 | tf_op jit(solution)/shard_map/ppermute | solution.py:280
  66.1 22.3 %collective-permute-start.2 = (bf16[64,512]{1,0:T(8,128)(2,1)S(1)}, bf16[64,512]{1,0:T(8,128)(2,1)S(1)}, u32[]{:S(2)}, u32[]{:S(2)}) collective-permute-start(bf16[64,512]{1,0:T(8,128)(2,1)S(1)} %get-tuple-element.11), channel_id=1, source_target_pairs={{0,1},{1,2},{2,3},{3,4},{4,5},{5,6},{6,7},{7,8},{8,9},{9,10},{10,1... | collective-permute-start | bytes 196616 | tf_op jit(solution)/shard_map/ppermute | solution.py:279
  88.4 1.2 %copy-start.2 = (bf16[1024,512]{1,0:T(8,128)(2,1)S(1)}, bf16[1024,512]{1,0:T(8,128)(2,1)}, u32[]{:S(2)}) copy-start(bf16[1024,512]{1,0:T(8,128)(2,1)} %copy-done.1) | copy-start | bytes 3145732

commit v7 on v6

--- a/solution.py
+++ b/solution.py
@@ -62,7 +62,7 @@
     lax.fori_loop(0, send_ref.shape[0], body, 0)
 
 
-def hidden_kernel(req_ref, exp_ref, x_ref, fgw_ref, h_ref, send_ref):
+def hidden_kernel(x_ref, fgw_ref, h_ref):
     rows, cols = x_ref.shape
     half = cols // 2
     cw = fgw_ref.shape[0] // 2
@@ -81,7 +81,20 @@
             h_ref[rs, j * CHUNK : (j + 1) * CHUNK] = (
                 jnp.tanh(pre[:, :CHUNK]) * jax.nn.sigmoid(pre[:, CHUNK:])
             ).astype(bf16)
-    write_send(req_ref, exp_ref, h_ref, send_ref)
+
+
+def pack_kernel(req_ref, exp_ref, field_ref, send_ref):
+    write_send(req_ref, exp_ref, field_ref, send_ref)
+
+
+def pack(requested, export_block, field):
+    nrows, width = field.shape
+    return pl.pallas_call(
+        pack_kernel,
+        in_specs=[smem(), smem(), vmem()],
+        out_specs=vmem(),
+        out_shape=jax.ShapeDtypeStruct((requested.shape[0], BLK, width), bf16),
+    )(requested, export_block, field)
 
 
 def prep_kernel(col_ref, ptr_ref, out_ref):
@@ -129,25 +142,21 @@
         ).astype(bf16)
 
 
-def front_hidden(requested, export_block, features, fgw):
+def front_hidden(features, fgw):
     rows, cols = features.shape
     half = cols // 2
-    peers = requested.shape[0]
     return pl.pallas_call(
         hidden_kernel,
-        in_specs=[smem(), smem(), vmem(), vmem()],
-        out_specs=[vmem(), vmem()],
-        out_shape=[
-            jax.ShapeDtypeStruct((rows, half), bf16),
-            jax.ShapeDtypeStruct((peers, BLK, half), bf16),
-        ],
+        in_specs=[vmem(), vmem()],
+        out_specs=vmem(),
+        out_shape=jax.ShapeDtypeStruct((rows, half), bf16),
         compiler_params=pltpu.CompilerParams(vmem_limit_bytes=48 * 1024 * 1024),
         cost_estimate=pl.CostEstimate(
             flops=2 * rows * CHUNK * 4 * CHUNK * (half // CHUNK),
             transcendentals=rows * half * 2,
-            bytes_accessed=2 * rows * (cols + 2 * half),
-        ),
-    )(requested, export_block, features, fgw)
+            bytes_accessed=2 * rows * (cols + half),
+        ),
+    )(features, fgw)
 
 
 def front_skip(hidden, skip_weight):
@@ -176,19 +185,21 @@
     )(hidden, skip_weight)
 
 
-def accumulate(col_ref, ptr_ref, field, lo_ref, hi_ref, arr_ref, band_ref, farw_ref, acc):
-    nblk = field.shape[0] // BLK
-    far_cap = farw_ref.shape[0]
+def band_terms(field_ref, lo_ref, hi_ref, band_ref, acc_ref):
+    nblk = field_ref.shape[0] // BLK
     for r in range(nblk):
-        prev = lo_ref[...] if r == 0 else field[(r - 1) * BLK : r * BLK, :]
-        nxt = hi_ref[...] if r == nblk - 1 else field[(r + 1) * BLK : (r + 2) * BLK, :]
-        own = field[r * BLK : (r + 1) * BLK, :]
+        prev = lo_ref[...] if r == 0 else field_ref[(r - 1) * BLK : r * BLK, :]
+        nxt = hi_ref[...] if r == nblk - 1 else field_ref[(r + 1) * BLK : (r + 2) * BLK, :]
+        own = field_ref[r * BLK : (r + 1) * BLK, :]
         v = jnp.dot(band_ref[0, r * BLK : (r + 1) * BLK, :], prev, preferred_element_type=f32)
         v = v + jnp.dot(band_ref[1, r * BLK : (r + 1) * BLK, :], own, preferred_element_type=f32)
         v = v + jnp.dot(band_ref[2, r * BLK : (r + 1) * BLK, :], nxt, preferred_element_type=f32)
-        acc[r * BLK : (r + 1) * BLK, :] = v
-    acc[nblk * BLK :, :] = jnp.zeros((BLK, acc.shape[1]), f32)
-
+        acc_ref[r * BLK : (r + 1) * BLK, :] = v
+    acc_ref[nblk * BLK :, :] = jnp.zeros((BLK, acc_ref.shape[1]), f32)
+
+
+def far_terms(col_ref, ptr_ref, arr_ref, farw_ref, acc):
+    far_cap = farw_ref.shape[0]
     nptr = ptr_ref.shape[1]
 
     def slot(k, carry):
@@ -203,73 +214,119 @@
     lax.fori_loop(0, far_cap, slot, 0)
 
 
-def hop1_kernel(
-    col_ref, ptr_ref, req_ref, exp_ref, field_ref, lo_ref, hi_ref, arr_ref, band_ref, farw_ref,
-    out_ref, out_send_ref, acc,
-):
-    accumulate(col_ref, ptr_ref, field_ref, lo_ref, hi_ref, arr_ref, band_ref, farw_ref, acc)
-    nrows = field_ref.shape[0]
-    out_ref[...] = acc[:nrows, :].astype(bf16)
-    write_send(req_ref, exp_ref, out_ref, out_send_ref)
-
-
-def hop2_kernel(
-    col_ref, ptr_ref, field_ref, lo_ref, hi_ref, arr_ref, band_ref, farw_ref,
-    x_ref, h_ref, mix_ref, out_ref, acc,
-):
-    accumulate(col_ref, ptr_ref, field_ref, lo_ref, hi_ref, arr_ref, band_ref, farw_ref, acc)
-    nrows, width = field_ref.shape
+def band1_kernel(field_ref, lo_ref, hi_ref, band_ref, acc_ref):
+    band_terms(field_ref, lo_ref, hi_ref, band_ref, acc_ref)
+
+
+def band2_kernel(field_ref, lo_ref, hi_ref, band_ref, x_ref, h_ref, mix_ref, acc_ref, part_ref):
+    band_terms(field_ref, lo_ref, hi_ref, band_ref, acc_ref)
+    width = field_ref.shape[1]
     half = x_ref.shape[1] // 2
     cw = mix_ref.shape[1]
     per = CHUNK // cw
     mix = mix_ref[...]
-    m = [bd_inkernel(mix[i * cw : (i + 1) * cw], per) for i in range(3)]
+    m0 = bd_inkernel(mix[:cw], per)
+    m1 = bd_inkernel(mix[cw : 2 * cw], per)
+    for j in range(width // CHUNK):
+        cols = slice(j * CHUNK, (j + 1) * CHUNK)
+        v = x_ref[:, half + j * CHUNK : half + (j + 1) * CHUNK].astype(f32)
+        v = v + jnp.dot(h_ref[:, cols], m0, preferred_element_type=f32)
+        v = v + jnp.dot(field_ref[:, cols], m1, preferred_element_type=f32)
+        part_ref[:, cols] = v
+
+
+def far1_kernel(col_ref, ptr_ref, req_ref, exp_ref, acc_in, arr_ref, farw_ref, out_ref, send_ref, acc):
+    acc[...] = acc_in[...]
+    far_terms(col_ref, ptr_ref, arr_ref, farw_ref, acc)
+    nrows = out_ref.shape[0]
+    out_ref[...] = acc[:nrows, :].astype(bf16)
+    write_send(req_ref, exp_ref, out_ref, send_ref)
+
+
+def far2_kernel(col_ref, ptr_ref, acc_in, arr_ref, farw_ref, part_ref, mix_ref, out_ref, acc):
+    acc[...] = acc_in[...]
+    far_terms(col_ref, ptr_ref, arr_ref, farw_ref, acc)
+    nrows, width = out_ref.shape
+    cw = mix_ref.shape[1]
+    m2 = bd_inkernel(mix_ref[2 * cw :], CHUNK // cw)
     for j in range(width // CHUNK):
         cols = slice(j * CHUNK, (j + 1) * CHUNK)
         two = acc[:nrows, cols].astype(bf16)
-        v = x_ref[:, half + j * CHUNK : half + (j + 1) * CHUNK].astype(f32)
-        v = v + jnp.dot(h_ref[:, cols], m[0], preferred_element_type=f32)
-        v = v + jnp.dot(field_ref[:, cols], m[1], preferred_element_type=f32)
-        v = v + jnp.dot(two, m[2], preferred_element_type=f32)
+        v = part_ref[:, cols] + jnp.dot(two, m2, preferred_element_type=f32)
         out_ref[:, cols] = v.astype(bf16)
 
 
-def hop1(far_col, far_ptr, requested, export_block, field, lo, hi, arrived, band3, farw3):
+BIG_VMEM = pltpu.CompilerParams(vmem_limit_bytes=48 * 1024 * 1024)
+
+
+def band1(field, lo, hi, band3):
     nrows, width = field.shape
     return pl.pallas_call(
-        hop1_kernel,
-        in_specs=[smem(), smem(), smem(), smem()] + [vmem()] * 6,
+        band1_kernel,
+        in_specs=[vmem()] * 4,
+        out_specs=vmem(),
+        out_shape=jax.ShapeDtypeStruct((nrows + BLK, width), f32),
+        compiler_params=BIG_VMEM,
+        cost_estimate=pl.CostEstimate(
+            flops=2 * BLK * width * 3 * nrows, transcendentals=0,
+            bytes_accessed=2 * width * nrows * 3,
+        ),
+    )(field, lo, hi, band3)
+
+
+def band2(field, lo, hi, band3, features, hidden, mix):
+    nrows, width = field.shape
+    return pl.pallas_call(
+        band2_kernel,
+        in_specs=[vmem()] * 7,
+        out_specs=[vmem(), vmem()],
+        out_shape=[
+            jax.ShapeDtypeStruct((nrows + BLK, width), f32),
+            jax.ShapeDtypeStruct((nrows, width), f32),
+        ],
+        compiler_params=BIG_VMEM,
+        cost_estimate=pl.CostEstimate(
+            flops=2 * BLK * width * 3 * nrows + 2 * nrows * width * CHUNK * 2, transcendentals=0,
+            bytes_accessed=2 * width * nrows * 8,
+        ),
+    )(field, lo, hi, band3, features, hidden, mix)
+
+
+def far1(far_col, far_ptr, requested, export_block, acc, arrived, farw3):
+    nrows = acc.shape[0] - BLK
+    width = acc.shape[1]
+    return pl.pallas_call(
+        far1_kernel,
+        in_specs=[smem()] * 4 + [vmem()] * 3,
         out_specs=[vmem(), vmem()],
         out_shape=[
             jax.ShapeDtypeStruct((nrows, width), bf16),
             jax.ShapeDtypeStruct(arrived.shape, bf16),
         ],
-        scratch_shapes=[pltpu.VMEM((nrows + BLK, width), f32)],
-        compiler_params=pltpu.CompilerParams(vmem_limit_bytes=48 * 1024 * 1024),
-        cost_estimate=pl.CostEstimate(
-            flops=2 * BLK * BLK * width * (3 * nrows // BLK + farw3.shape[0]),
-            transcendentals=0,
-            bytes_accessed=2 * width * (nrows * 2 + 2 * arrived.shape[0] * BLK),
-        ),
-    )(far_col, far_ptr, requested, export_block, field, lo, hi, arrived, band3, farw3)
-
-
-def hop2(far_col, far_ptr, field, lo, hi, arrived, band3, farw3, features, hidden, mix):
-    nrows, width = field.shape
-    return pl.pallas_call(
-        hop2_kernel,
-        in_specs=[smem(), smem()] + [vmem()] * 9,
+        scratch_shapes=[pltpu.VMEM(acc.shape, f32)],
+        compiler_params=BIG_VMEM,
+        cost_estimate=pl.CostEstimate(
+            flops=2 * BLK * BLK * width * farw3.shape[0], transcendentals=0,
+            bytes_accessed=2 * width * nrows * 4,
+        ),
+    )(far_col, far_ptr, requested, export_block, acc, arrived, farw3)
+
+
+def far2(far_col, far_ptr, acc, arrived, farw3, part, mix):
+    nrows, width = part.shape
+    return pl.pallas_call(
+        far2_kernel,
+        in_specs=[smem()] * 2 + [vmem()] * 5,
         out_specs=vmem(),
         out_shape=jax.ShapeDtypeStruct((nrows, width), bf16),
-        scratch_shapes=[pltpu.VMEM((nrows + BLK, width), f32)],
-        compiler_params=pltpu.CompilerParams(vmem_limit_bytes=48 * 1024 * 1024),
-        cost_estimate=pl.CostEstimate(
-            flops=2 * BLK * BLK * width * (3 * nrows // BLK + farw3.shape[0])
-            + 2 * nrows * width * CHUNK * 3,
+        scratch_shapes=[pltpu.VMEM(acc.shape, f32)],
+        compiler_params=BIG_VMEM,
+        cost_estimate=pl.CostEstimate(
+            flops=2 * BLK * BLK * width * farw3.shape[0] + 2 * nrows * width * CHUNK,
             transcendentals=0,
-            bytes_accessed=2 * width * (nrows * 6 + arrived.shape[0] * BLK),
-        ),
-    )(far_col, far_ptr, field, lo, hi, arrived, band3, farw3, features, hidden, mix)
+            bytes_accessed=2 * width * nrows * 6,
+        ),
+    )(far_col, far_ptr, acc, arrived, farw3, part, mix)
 
 
 def halo(field):
@@ -293,30 +350,28 @@
     export_block,
 ):
     node_rows = features.shape[0]
-    blocks = node_rows // BLK
     far_cap = far_col.shape[1]
 
     wanted = prep(far_col, far_ptr)
     requested = lax.all_to_all(wanted[:, None], "node", split_axis=0, concat_axis=0, tiled=True)[
         :, 0
     ]
-    hidden, send1 = front_hidden(requested, export_block, features, filter_gate_weight)
-    width = hidden.shape[1]
+    hidden = front_hidden(features, filter_gate_weight)
     band3 = band_weight.reshape(node_rows, 3, BLK).transpose(1, 0, 2)
     farw3 = far_weight.reshape(BLK, far_cap, BLK).transpose(1, 0, 2)
 
     def exchange(send):
         return lax.all_to_all(send, "node", split_axis=0, concat_axis=0, tiled=True)
 
-    arrived1 = exchange(send1)
+    arrived1 = exchange(pack(requested, export_block, hidden))
     lo1, hi1 = halo(hidden)
+    acc1 = band1(hidden, lo1, hi1, band3)
     skip_out = front_skip(hidden, skip_weight)
-    hop_one, send2 = hop1(far_col, far_ptr, requested, export_block, hidden, lo1, hi1, arrived1, band3, farw3)
+    hop_one, send2 = far1(far_col, far_ptr, requested, export_block, acc1, arrived1, farw3)
     arrived2 = exchange(send2)
     lo2, hi2 = halo(hop_one)
-    residual = hop2(
-        far_col, far_ptr, hop_one, lo2, hi2, arrived2, band3, farw3, features, hidden, mix_weight
-    )
+    acc2, part = band2(hop_one, lo2, hi2, band3, features, hidden, mix_weight)
+    residual = far2(far_col, far_ptr, acc2, arrived2, farw3, part, mix_weight)
     return residual, skip_out
 
 

time: 97.4 us -> 107 us (1.099)
  local copies, waits for them, and re-layouts: 12.1 us -> 20.2 us
  Pallas kernels: 21 us -> 24.8 us
  waiting for transfers between devices: 32.2 us -> 30.1 us
    unnamed x22 -> x54, local copies, waits for them, and re-layouts: 7.33 us -> 16.5 us
    pallas_call x3 -> x6, Pallas kernels: 14.1 us -> 17.8 us  [the longest x1 4.6 us: far2(): pl.pallas_call(far2_kernel, in_specs=[smem()] * 2 + [vmem()] * 5, out_spe...]
    all_to_all x1, waiting for transfers between devices: 2.97 us -> 0.01 us  [local(): lax.all_to_all(wanted[:, None], 'node', split_axis=0, concat_axis=0, tile...]
  transfers between devices with their start and end apart: 7 -> 7, of which waited for: 3 -> 2; matrix products, arithmetic and copies ran while one was open for 4% -> 3% of each run, Pallas kernels for 6% -> 11%
where the time goes in v7:
time: 107 us; the launch traced here: 106 us
  waiting for transfers between devices  30.1 us (28%)
  starting transfers between devices  29.6 us (28%)
  Pallas kernels  24.8 us (23%)
  local copies, waits for them, and re-layouts  20.2 us (19%)
    ppermute x2, waiting for transfers between devices, halo(): hi = lax.ppermute(field[:BLK], 'node', backward)  30.1 us
    unnamed x54, local copies, waits for them, and re-layouts  16.5 us
    all_to_all x2, starting transfers between devices, exchange(): return lax.all_to_all(send, 'node', split_axis=0, concat_axis=0, tiled=True)  9.99 us
    ppermute x2, starting transfers between devices, halo(): lo = lax.ppermute(field[field.shape[0] - BLK:], 'node', forward)  8.52 us
    all_to_all x1, starting transfers between devices, local(): lax.all_to_all(wanted[:, None], 'node', split_axis=0, concat_axis=0, tile...  6.55 us
    pallas_call x1, Pallas kernels, front_skip(): pl.pallas_call(skip_kernel, grid=(rows // tile,), in_specs=[pl.BlockSpec(...  5.37 us
    pallas_call x1, Pallas kernels, far2(): pl.pallas_call(far2_kernel, in_specs=[smem()] * 2 + [vmem()] * 5, out_spe...  4.6 us
    ppermute x2, starting transfers between devices, halo(): hi = lax.ppermute(field[:BLK], 'node', backward)  4.54 us
  transfers between devices with their start and end apart: 7, of which 2 were waited for; matrix products, arithmetic and copies ran while one was open for 3% of the time, Pallas kernels for 11%

profile of v7, /device:TPU:15, one launch (start us, length us, event | category | flops | bytes accessed | tf_op | source)
XLA Modules:
  0.0 106.5 jit_solution(8676597059071252782)
XLA Ops:
  0.6 1.6 %shard_map.104 = s32[16]{0:T(128)} custom-call(s32[1,15]{1,0:T(1,128)} %col_ref.5, s32[1,17]{1,0:T(1,128)} %ptr_ref.5), custom_call_target="tpu_custom_call" | custom-call | tf_op jit(solution)/shard_map/pallas_call | solution.py:123
  2.2 1.3 %copy.28 = s32[16,1,1]{2,1,0:T(1,128)} copy(s32[16,1,1]{0,2,1:T(1,128)} %bitcast.11) | data formatting | bytes 128 | tf_op jit(solution)/shard_map/all_to_all | solution.py:356
  3.6 6.6 %all-to-all-start = ((s32[16,1,1]{2,1,0:T(1,128)}), s32[16,1,1]{2,1,0:T(1,128)S(1)}, u32[]{:S(2)}, u32[]{:S(2)}) async-start(s32[16,1,1]{2,1,0:T(1,128)} %copy.28), calls=%async_computation | async-start | bytes 16384 | tf_op jit(solution)/shard_map/all_to_all | solution.py:356
  10.1 1.6 %copy-done.5 = bf16[1024,1024]{1,0:T(8,128)(2,1)S(1)} copy-done((bf16[1024,1024]{1,0:T(8,128)(2,1)S(1)}, bf16[1024,1024]{1,0:T(8,128)(2,1)}, u32[]{:S(2)}) %copy-start.5) | copy-done | bytes 2097176
  11.7 0.7 copy-done.21
  12.4 1.8 %shard_map.105.field_ref.h_ref = bf16[1024,512]{1,0:T(8,128)(2,1)S(1)} custom-call(bf16[1024,1024]{1,0:T(8,128)(2,1)S(1)} %copy-done.5, bf16[64,64]{1,0:T(8,128)(2,1)S(1)} %copy-done.21), custom_call_target="tpu_custom_call" | custom-call | flops 1073741824 | bytes 3145728 | tf_op jit(solution)/shard_map/pallas_call | solution.py:148
  14.2 0.0 copy-start
  14.2 1.0 copy-done
  15.2 0.7 copy.32.exp_ref
  15.9 0.0 all-to-all-done
  15.9 0.9 reduce.req_ref
  16.8 2.6 %shard_map.107 = bf16[16,64,512]{2,1,0:T(8,128)(2,1)} custom-call(s32[16]{0:T(128)} %reduce.req_ref, s32[16,2]{1,0:T(8,128)} %copy.32.exp_ref, bf16[1024,512]{1,0:T(8,128)(2,1)} %copy-done), custom_call_target="tpu_custom_call" | custom-call | tf_op jit(solution)/shard_map/pallas_call | solution.py:92
  19.3 6.0 %all-to-all-start.1 = ((bf16[16,64,512]{2,1,0:T(8,128)(2,1)}), bf16[16,64,512]{2,1,0:T(8,128)(2,1)}, u32[]{:S(2)}, u32[]{:S(2)}) async-start(bf16[16,64,512]{2,1,0:T(8,128)(2,1)} %shard_map.107), calls=%async_computation.1 | async-start | bytes 2097152 | tf_op jit(solution)/shard_map/all_to_all | solution.py:364
  25.4 2.3 %collective-permute-start.1 = (bf16[64,512]{1,0:T(8,128)(2,1)S(1)}, bf16[64,512]{1,0:T(8,128)(2,1)S(1)}, u32[]{:S(2)}, u32[]{:S(2)}) collective-permute-start(bf16[64,512]{1,0:T(8,128)(2,1)S(1)} %get-tuple-element.12), channel_id=1, source_target_pairs={{1,0},{2,1},{3,2},{4,3},{5,4},{6,5},{7,6},{8,7},{9,8},{10,9},{11,1... | collective-permute-start | bytes 196616 | tf_op jit(solution)/shard_map/ppermute | solution.py:337
  27.7 4.2 %collective-permute-start = (bf16[64,512]{1,0:T(8,128)(2,1)S(1)}, bf16[64,512]{1,0:T(8,128)(2,1)S(1)}, u32[]{:S(2)}, u32[]{:S(2)}) collective-permute-start(bf16[64,512]{1,0:T(8,128)(2,1)S(1)} %get-tuple-element.13), channel_id=1, source_target_pairs={{0,1},{1,2},{2,3},{3,4},{4,5},{5,6},{6,7},{7,8},{8,9},{9,10},{10,1... | collective-permute-start | bytes 196616 | tf_op jit(solution)/shard_map/ppermute | solution.py:336
  31.9 0.2 reshape.15
  32.1 0.1 copy.36
  32.2 1.2 %copy.29 = bf16[1024,3,64]{2,0,1:T(8,128)(2,1)} copy(bf16[1024,3,64]{0,2,1:T(8,128)(2,1)S(1)} %bitcast.10) | data formatting | bytes 786432 | tf_op jit(solution)/shard_map/reshape | solution.py:360
  33.4 17.6 %collective-permute-done.1.hi_ref = bf16[64,512]{1,0:T(8,128)(2,1)S(1)} collective-permute-done((bf16[64,512]{1,0:T(8,128)(2,1)S(1)}, bf16[64,512]{1,0:T(8,128)(2,1)S(1)}, u32[]{:S(2)}, u32[]{:S(2)}) %collective-permute-start.1) | collective-permute-done | bytes 65568 | tf_op jit(solution)/shard_map/ppermute | solution.py:337
  50.9 0.6 copy-done.12
  51.5 0.0 collective-permute-done.lo_ref
  51.5 0.6 copy-done.14
  52.2 1.1 %copy-done.2 = bf16[1024,3,64]{2,0,1:T(8,128)(2,1)S(1)} copy-done((bf16[1024,3,64]{2,0,1:T(8,128)(2,1)S(1)}, bf16[1024,3,64]{2,0,1:T(8,128)(2,1)}, u32[]{:S(2)}) %copy-start.2) | copy-done | bytes 393240
  53.3 0.8 copy-done.13
  54.1 0.8 copy-done.15
  55.0 1.0 shard_map.106.acc_in
  56.0 0.0 all-to-all-done.1.arr_ref
  56.0 0.0 copy-start.19
  56.0 0.6 copy-done.19
  56.7 4.0 %shard_map.108 = (bf16[1024,512]{1,0:T(8,128)(2,1)S(1)}, bf16[16,64,512]{2,1,0:T(8,128)(2,1)S(1)}) custom-call(s32[1,15]{1,0:T(1,128)S(1)} %copy-done.18, s32[1,17]{1,0:T(1,128)S(1)} %copy-done.19, s32[16]{0:T(128)S(1)} %copy-done.17, s32[16,2]{1,0:T(8,128)S(1)} %copy-done.11, f32[1088,512]{1,0:T(8,128)S(1)} %shard_map.106.acc_in, ...), custom_call_target="tpu_custom_call" | custom-call | flops 62914560 | bytes 4194304 | tf_op jit(solution)/shard_map/pallas_call | solution.py:298
  60.7 0.0 copy-start.8
  60.7 1.0 copy-done.8
  61.6 1.0 copy-done.10
  62.6 4.0 %all-to-all-start.2 = ((bf16[16,64,512]{2,1,0:T(8,128)(2,1)}), bf16[16,64,512]{2,1,0:T(8,128)(2,1)S(1)}, u32[]{:S(2)}, u32[]{:S(2)}) async-start(bf16[16,64,512]{2,1,0:T(8,128)(2,1)} %copy-done.10), calls=%async_computation.2 | async-start | bytes 2097152 | tf_op jit(solution)/shard_map/all_to_all | solution.py:364
  66.6 0.9 fusion
  67.5 2.3 %collective-permute-start.3 = (bf16[64,512]{1,0:T(8,128)(2,1)S(1)}, bf16[64,512]{1,0:T(8,128)(2,1)S(1)}, u32[]{:S(2)}, u32[]{:S(2)}) collective-permute-start(bf16[64,512]{1,0:T(8,128)(2,1)S(1)} %get-tuple-element.10), channel_id=1, source_target_pairs={{1,0},{2,1},{3,2},{4,3},{5,4},{6,5},{7,6},{8,7},{9,8},{10,9},{11,1... | collective-permute-start | bytes 196616 | tf_op jit(solution)/shard_map/ppermute | solution.py:337
  69.8 0.0 copy-start.24
  69.8 4.3 %collective-permute-start.2 = (bf16[64,512]{1,0:T(8,128)(2,1)S(1)}, bf16[64,512]{1,0:T(8,128)(2,1)S(1)}, u32[]{:S(2)}, u32[]{:S(2)}) collective-permute-start(bf16[64,512]{1,0:T(8,128)(2,1)S(1)} %get-tuple-element.11), channel_id=1, source_target_pairs={{0,1},{1,2},{2,3},{3,4},{4,5},{5,6},{6,7},{7,8},{8,9},{9,10},{10,1... | collective-permute-start | bytes 196616 | tf_op jit(solution)/shard_map/ppermute | solution.py:336
  74.1 5.4 %shard_map.111 = bf16[1024,4096]{1,0:T(8,128)(2,1)} custom-call(bf16[1024,512]{1,0:T(8,128)(2,1)S(1)} %copy-done.1, bf16[32,256]{1,0:T(8,128)(2,1)S(1)} %copy-done.16), custom_call_target="tpu_custom_call" | custom-call | flops 2147483648 | bytes 9437184 | tf_op jit(solution)/shard_map/pallas_call | solution.py:169
  79.5 0.1 copy.33.mix_ref
  79.6 12.6 %collective-permute-done.3.hi_ref = bf16[64,512]{1,0:T(8,128)(2,1)S(1)} collective-permute-done((bf16[64,512]{1,0:T(8,128)(2,1)S(1)}, bf16[64,512]{1,0:T(8,128)(2,1)S(1)}, u32[]{:S(2)}, u32[]{:S(2)}) %collective-permute-start.3) | collective-permute-done | bytes 65568 | tf_op jit(solution)/shard_map/ppermute | solution.py:337
  92.2 0.0 collective-permute-done.2.lo_ref
  92.2 1.2 %copy-done.9 = bf16[1024,512]{1,0:T(8,128)(2,1)S(1)} copy-done((bf16[1024,512]{1,0:T(8,128)(2,1)S(1)}, bf16[1024,512]{1,0:T(8,128)(2,1)}, u32[]{:S(2)}) %copy-start.9) | copy-done | bytes 1048600
  93.4 3.9 %shard_map.109 = (f32[1088,512]{1,0:T(8,128)}, f32[1024,512]{1,0:T(8,128)S(1)}) custom-call(bf16[1024,512]{1,0:T(8,128)(2,1)S(1)} %copy-done.9, bf16[64,512]{1,0:T(8,128)(2,1)S(1)} %collective-permute-done.2.lo_ref, bf16[64,512]{1,0:T(8,128)(2,1)S(1)} %collective-permute-done.3.hi_ref, bf16[3,1024,64]{2,1,0:T(8,128)(2,1)S(1)} %bitcast.7, ...), custom_call_target="tpu_custom_call" | custom-call | flops 738197504 | bytes 8388608 | tf_op jit(solution)/shard_map/pallas_call | solution.py:279
  97.3 1.3 %copy-done.6 = f32[1024,512]{1,0:T(8,128)} copy-done((f32[1024,512]{1,0:T(8,128)}, f32[1024,512]{1,0:T(8,128)S(1)}, u32[]{:S(2)}) %copy-start.6) | copy-done | bytes 2097176
  98.7 1.6 %copy-done.4 = f32[1088,512]{1,0:T(8,128)S(1)} copy-done((f32[1088,512]{1,0:T(8,128)S(1)}, f32[1088,512]{1,0:T(8,128)}, u32[]{:S(2)}) %copy-start.4) | copy-done | bytes 2228248
  100.3 1.6 %copy-done.7 = f32[1024,512]{1,0:T(8,128)S(1)} copy-done((f32[1024,512]{1,0:T(8,128)S(1)}, f32[1024,512]{1,0:T(8,128)}, u32[]{:S(2)}) %copy-start.7) | copy-done | bytes 2097176
  101.9 4.6 %shard_map.110 = bf16[1024,512]{1,0:T(8,128)(2,1)} custom-call(s32[1,15]{1,0:T(1,128)S(1)} %copy-done.18, s32[1,17]{1,0:T(1,128)S(1)} %copy-done.20, f32[1088,512]{1,0:T(8,128)S(1)} %copy-done.4, bf16[16,64,512]{2,1,0:T(8,128)(2,1)S(1)} %all-to-all-done.2.arr_ref, bf16[15,64,64]{2,1,0:T(8,128)(2,1)S(1)} %bitcast.9, f32[1024,512]{1,0:T(8,128)S(1)} %copy-done.7, ...), custom_call_target="tpu_custom_call" | custom-call | flops 331350016 | bytes 6291456 | tf_op jit(solution)/shard_map/pallas_call | solution.py:317
  (35 shorter events, 0.1 us)
Async XLA Ops:
  0.6 14.6 %copy-start.25 = (s32[16,2]{0,1:T(2,128)S(1)}, s32[16,2]{0,1:T(2,128)}, u32[]{:S(2)}) copy-start(s32[16,2]{0,1:T(2,128)} %param.17) | copy-start | bytes 388
  3.6 12.3 %all-to-all-start = ((s32[16,1,1]{2,1,0:T(1,128)}), s32[16,1,1]{2,1,0:T(1,128)S(1)}, u32[]{:S(2)}, u32[]{:S(2)}) async-start(s32[16,1,1]{2,1,0:T(1,128)} %copy.28), calls=%async_computation | async-start | bytes 16384 | tf_op jit(solution)/shard_map/all_to_all | solution.py:356
  10.1 1.6 %copy-start.5 = (bf16[1024,1024]{1,0:T(8,128)(2,1)S(1)}, bf16[1024,1024]{1,0:T(8,128)(2,1)}, u32[]{:S(2)}) copy-start(bf16[1024,1024]{1,0:T(8,128)(2,1)} %x_ref.3) | copy-start | bytes 6291460
  11.7 0.7 copy-start.21
  14.2 1.0 copy-start
  15.9 9.5 %copy-start.1 = (bf16[1024,512]{1,0:T(8,128)(2,1)S(1)}, bf16[1024,512]{1,0:T(8,128)(2,1)}, u32[]{:S(2)}) copy-start(bf16[1024,512]{1,0:T(8,128)(2,1)} %copy-done) | copy-start | bytes 3145732
  16.8 15.1 %copy-start.23 = (bf16[64,960]{1,0:T(8,128)(2,1)S(1)}, bf16[64,960]{1,0:T(8,128)(2,1)}, u32[]{:S(2)}) copy-start(bf16[64,960]{1,0:T(8,128)(2,1)} %param.14) | copy-start | bytes 368644
  16.8 15.4 %copy-start.22 = (bf16[1024,192]{0,1:T(8,128)(2,1)S(1)}, bf16[1024,192]{0,1:T(8,128)(2,1)}, u32[]{:S(2)}) copy-start(bf16[1024,192]{0,1:T(8,128)(2,1)} %param.13) | copy-start | bytes 1179652
  19.3 36.6 %all-to-all-start.1 = ((bf16[16,64,512]{2,1,0:T(8,128)(2,1)}), bf16[16,64,512]{2,1,0:T(8,128)(2,1)}, u32[]{:S(2)}, u32[]{:S(2)}) async-start(bf16[16,64,512]{2,1,0:T(8,128)(2,1)} %shard_map.107), calls=%async_computation.1 | async-start | bytes 2097152 | tf_op jit(solution)/shard_map/all_to_all | solution.py:364
  25.4 25.5 %collective-permute-start.1 = (bf16[64,512]{1,0:T(8,128)(2,1)S(1)}, bf16[64,512]{1,0:T(8,128)(2,1)S(1)}, u32[]{:S(2)}, u32[]{:S(2)}) collective-permute-start(bf16[64,512]{1,0:T(8,128)(2,1)S(1)} %get-tuple-element.12), channel_id=1, source_target_pairs={{1,0},{2,1},{3,2},{4,3},{5,4},{6,5},{7,6},{8,7},{9,8},{10,9},{11,1... | collective-permute-start | bytes 196616 | tf_op jit(solution)/shard_map/ppermute | solution.py:337
  27.7 23.9 %collective-permute-start = (bf16[64,512]{1,0:T(8,128)(2,1)S(1)}, bf16[64,512]{1,0:T(8,128)(2,1)S(1)}, u32[]{:S(2)}, u32[]{:S(2)}) collective-permute-start(bf16[64,512]{1,0:T(8,128)(2,1)S(1)} %get-tuple-element.13), channel_id=1, source_target_pairs={{0,1},{1,2},{2,3},{3,4},{4,5},{5,6},{6,7},{7,8},{8,9},{9,10},{10,1... | collective-permute-start | bytes 196616 | tf_op jit(solution)/shard_map/ppermute | solution.py:336
  32.2 23.8 %copy-start.11 = (s32[16,2]{1,0:T(8,128)S(1)}, s32[16,2]{1,0:T(8,128)}, u32[]{:S(2)}) copy-start(s32[16,2]{1,0:T(8,128)} %copy.32.exp_ref) | copy-start | bytes 388
  33.4 22.6 %copy-start.17 = (s32[16]{0:T(128)S(1)}, s32[16]{0:T(128)}, u32[]{:S(2)}) copy-start(s32[16]{0:T(128)} %reduce.req_ref) | copy-start | bytes 196
  33.4 22.6 %copy-start.18 = (s32[1,15]{1,0:T(1,128)S(1)}, s32[1,15]{1,0:T(1,128)}, u32[]{:S(2)}) copy-start(s32[1,15]{1,0:T(1,128)} %col_ref.5) | copy-start | bytes 184
  50.9 0.6 copy-start.12
  51.5 0.6 copy-start.14
  52.2 1.1 %copy-start.2 = (bf16[1024,3,64]{2,0,1:T(8,128)(2,1)S(1)}, bf16[1024,3,64]{2,0,1:T(8,128)(2,1)}, u32[]{:S(2)}) copy-start(bf16[1024,3,64]{2,0,1:T(8,128)(2,1)} %copy.29) | copy-start | bytes 1179652
  53.3 0.8 copy-start.13
  54.1 0.8 copy-start.15
  56.0 0.7 copy-start.19
  56.6 17.5 %copy-start.16 = (bf16[32,256]{1,0:T(8,128)(2,1)S(1)}, bf16[32,256]{1,0:T(8,128)(2,1)}, u32[]{:S(2)}) copy-start(bf16[32,256]{1,0:T(8,128)(2,1)} %sw_ref.1) | copy-start | bytes 49156
  60.7 1.0 copy-start.8
  61.6 1.0 copy-start.10
  62.6 36.0 %all-to-all-start.2 = ((bf16[16,64,512]{2,1,0:T(8,128)(2,1)}), bf16[16,64,512]{2,1,0:T(8,128)(2,1)S(1)}, u32[]{:S(2)}, u32[]{:S(2)}) async-start(bf16[16,64,512]{2,1,0:T(8,128)(2,1)} %copy-done.10), calls=%async_computation.2 | async-start | bytes 2097152 | tf_op jit(solution)/shard_map/all_to_all | solution.py:364
  67.5 24.7 %collective-permute-start.3 = (bf16[64,512]{1,0:T(8,128)(2,1)S(1)}, bf16[64,512]{1,0:T(8,128)(2,1)S(1)}, u32[]{:S(2)}, u32[]{:S(2)}) collective-permute-start(bf16[64,512]{1,0:T(8,128)(2,1)S(1)} %get-tuple-element.10), channel_id=1, source_target_pairs={{1,0},{2,1},{3,2},{4,3},{5,4},{6,5},{7,6},{8,7},{9,8},{10,9},{11,1... | collective-permute-start | bytes 196616 | tf_op jit(solution)/shard_map/ppermute | solution.py:337
  69.8 9.7 %copy-start.24 = (bf16[96,32]{0,1:T(8,128)(2,1)S(1)}, bf16[96,32]{0,1:T(8,128)(2,1)}, u32[]{:S(2)}) copy-start(bf16[96,32]{0,1:T(8,128)(2,1)} %param.12) | copy-start | bytes 18436
  69.8 22.4 %copy-start.3 = (bf16[1024,3,64]{2,0,1:T(8,128)(2,1)S(1)}, bf16[1024,3,64]{2,0,1:T(8,128)(2,1)}, u32[]{:S(2)}) copy-start(bf16[1024,3,64]{2,0,1:T(8,128)(2,1)} %copy.29) | copy-start | bytes 1179652
  69.8 22.4 %collective-permute-start.2 = (bf16[64,512]{1,0:T(8,128)(2,1)S(1)}, bf16[64,512]{1,0:T(8,128)(2,1)S(1)}, u32[]{:S(2)}, u32[]{:S(2)}) collective-permute-start(bf16[64,512]{1,0:T(8,128)(2,1)S(1)} %get-tuple-element.11), channel_id=1, source_target_pairs={{0,1},{1,2},{2,3},{3,4},{4,5},{5,6},{6,7},{7,8},{8,9},{9,10},{10,1... | collective-permute-start | bytes 196616 | tf_op jit(solution)/shard_map/ppermute | solution.py:336
  79.5 19.2 %copy-start.20 = (s32[1,17]{1,0:T(1,128)S(1)}, s32[1,17]{1,0:T(1,128)}, u32[]{:S(2)}) copy-start(s32[1,17]{1,0:T(1,128)} %ptr_ref.5) | copy-start | bytes 208
  92.2 1.2 %copy-start.9 = (bf16[1024,512]{1,0:T(8,128)(2,1)S(1)}, bf16[1024,512]{1,0:T(8,128)(2,1)}, u32[]{:S(2)}) copy-start(bf16[1024,512]{1,0:T(8,128)(2,1)} %copy-done.8) | copy-start | bytes 3145732
  97.3 1.3 %copy-start.6 = (f32[1024,512]{1,0:T(8,128)}, f32[1024,512]{1,0:T(8,128)S(1)}, u32[]{:S(2)}) copy-start(f32[1024,512]{1,0:T(8,128)S(1)} %get-tuple-element.9.part_ref) | copy-start | bytes 6291460
  98.7 1.6 %copy-start.4 = (f32[1088,512]{1,0:T(8,128)S(1)}, f32[1088,512]{1,0:T(8,128)}, u32[]{:S(2)}) copy-start(f32[1088,512]{1,0:T(8,128)} %get-tuple-element.7.acc_in) | copy-start | bytes 6684676
  100.3 1.6 %copy-start.7 = (f32[1024,512]{1,0:T(8,128)S(1)}, f32[1024,512]{1,0:T(8,128)}, u32[]{:S(2)}) copy-start(f32[1024,512]{1,0:T(8,128)} %copy-done.6) | copy-start | bytes 6291460

commit v8 on v5

--- a/solution.py
+++ b/solution.py
@@ -126,46 +126,83 @@
     )(hidden, skip_weight)
 
 
-def accumulate(src_ref, row_ref, field, lo_ref, hi_ref, arr_ref, band_ref, farw_ref, acc):
-    nblk = field.shape[0] // BLK
+def fill_pad(field_ref, lo_ref, hi_ref, pad):
+    nrows = field_ref.shape[0]
+    pad[:BLK, :] = lo_ref[...]
+    pad[BLK : BLK + nrows, :] = field_ref[...]
+    pad[BLK + nrows :, :] = hi_ref[...]
+
+
+def band_block(band_ref, pad, t):
+    start = pl.multiple_of(t * BLK, BLK)
+    return jnp.dot(
+        band_ref[pl.ds(start, BLK), :], pad[pl.ds(start, 3 * BLK), :], preferred_element_type=f32
+    )
+
+
+def slot_product(col_ref, farw_ref, arr_ref, k):
+    return jnp.dot(farw_ref[k], arr_ref[col_ref[0, k] // EXPORT], preferred_element_type=f32)
+
+
+def accumulate(col_ref, ptr_ref, field_ref, lo_ref, hi_ref, arr_ref, band_ref, farw_ref, acc, pad):
+    nblk = field_ref.shape[0] // BLK
     far_cap = farw_ref.shape[0]
+    nptr = ptr_ref.shape[1]
+    fill_pad(field_ref, lo_ref, hi_ref, pad)
     for r in range(nblk):
-        prev = lo_ref[...] if r == 0 else field[(r - 1) * BLK : r * BLK, :]
-        nxt = hi_ref[...] if r == nblk - 1 else field[(r + 1) * BLK : (r + 2) * BLK, :]
-        own = field[r * BLK : (r + 1) * BLK, :]
-        v = jnp.dot(band_ref[0, r * BLK : (r + 1) * BLK, :], prev, preferred_element_type=f32)
-        v = v + jnp.dot(band_ref[1, r * BLK : (r + 1) * BLK, :], own, preferred_element_type=f32)
-        v = v + jnp.dot(band_ref[2, r * BLK : (r + 1) * BLK, :], nxt, preferred_element_type=f32)
-        acc[r * BLK : (r + 1) * BLK, :] = v
+        acc[r * BLK : (r + 1) * BLK, :] = band_block(band_ref, pad, r)
     acc[nblk * BLK :, :] = jnp.zeros((BLK, acc.shape[1]), f32)
 
     def slot(k, carry):
-        row = row_ref[k]
-        piece = arr_ref[src_ref[k]]
+        row = 0
+        for r in range(1, nptr):
+            row = row + jnp.where(ptr_ref[0, r] <= k, 1, 0)
         start = pl.multiple_of(row * BLK, BLK)
-        acc[pl.ds(start, BLK), :] += jnp.dot(farw_ref[k], piece, preferred_element_type=f32)
+        acc[pl.ds(start, BLK), :] += slot_product(col_ref, farw_ref, arr_ref, k)
         return carry
 
     lax.fori_loop(0, far_cap, slot, 0)
 
 
+def early_kernel(
+    col_ref, ptr_ref, req_ref, exp_ref, field_ref, lo_ref, hi_ref, arr_ref, band_ref, farw_ref,
+    send_ref, edge_ref, pad, blk,
+):
+    nblk = field_ref.shape[0] // BLK
+    own = lax.axis_index("node")
+    fill_pad(field_ref, lo_ref, hi_ref, pad)
+    targets = [exp_ref[own, 0], exp_ref[own, 1], 0, nblk - 1]
+    for i, t in enumerate(targets):
+        v = band_block(band_ref, pad, t)
+
+        def slot(k, acc):
+            return acc + slot_product(col_ref, farw_ref, arr_ref, k)
+
+        v = lax.fori_loop(ptr_ref[0, t], ptr_ref[0, t + 1], slot, v)
+        blk[i] = v.astype(bf16)
+
+    def body(p, carry):
+        send_ref[p] = blk[req_ref[p]]
+        return carry
+
+    lax.fori_loop(0, send_ref.shape[0], body, 0)
+    edge_ref[0] = blk[2]
+    edge_ref[1] = blk[3]
+
+
 def hop1_kernel(
-    src_ref, row_ref, send_ref, field_ref, lo_ref, hi_ref, arr_ref, band_ref, farw_ref,
-    out_ref, out_send_ref, acc,
+    col_ref, ptr_ref, field_ref, lo_ref, hi_ref, arr_ref, band_ref, farw_ref, out_ref, acc, pad,
 ):
-    accumulate(src_ref, row_ref, field_ref, lo_ref, hi_ref, arr_ref, band_ref, farw_ref, acc)
+    accumulate(col_ref, ptr_ref, field_ref, lo_ref, hi_ref, arr_ref, band_ref, farw_ref, acc, pad)
     nrows = field_ref.shape[0]
     out_ref[...] = acc[:nrows, :].astype(bf16)
-    for p in range(out_send_ref.shape[0]):
-        start = pl.multiple_of(send_ref[p] * BLK, BLK)
-        out_send_ref[p] = out_ref[pl.ds(start, BLK), :]
 
 
 def hop2_kernel(
-    src_ref, row_ref, field_ref, lo_ref, hi_ref, arr_ref, band_ref, farw_ref,
-    x_ref, h_ref, mix_ref, out_ref, acc,
+    col_ref, ptr_ref, field_ref, lo_ref, hi_ref, arr_ref, band_ref, farw_ref,
+    x_ref, h_ref, mix_ref, out_ref, acc, pad,
 ):
-    accumulate(src_ref, row_ref, field_ref, lo_ref, hi_ref, arr_ref, band_ref, farw_ref, acc)
+    accumulate(col_ref, ptr_ref, field_ref, lo_ref, hi_ref, arr_ref, band_ref, farw_ref, acc, pad)
     nrows, width = field_ref.shape
     half = x_ref.shape[1] // 2
     cw = mix_ref.shape[1]
@@ -190,50 +227,75 @@
     return pl.BlockSpec(memory_space=pltpu.SMEM)
 
 
-def hop1(src, rows, send_rows, field, lo, hi, arrived, band3, farw3):
+BIG_VMEM = pltpu.CompilerParams(vmem_limit_bytes=48 * 1024 * 1024)
+
+
+def scratch(field):
     nrows, width = field.shape
-    return pl.pallas_call(
-        hop1_kernel,
-        in_specs=[smem(), smem(), smem()] + [vmem()] * 6,
+    return [pltpu.VMEM((nrows + BLK, width), f32), pltpu.VMEM((nrows + 2 * BLK, width), bf16)]
+
+
+def early(far_col, far_ptr, requested, export_block, field, lo, hi, arrived, band, farw3):
+    nrows, width = field.shape
+    return pl.pallas_call(
+        early_kernel,
+        in_specs=[smem()] * 4 + [vmem()] * 6,
         out_specs=[vmem(), vmem()],
         out_shape=[
-            jax.ShapeDtypeStruct((nrows, width), bf16),
             jax.ShapeDtypeStruct(arrived.shape, bf16),
+            jax.ShapeDtypeStruct((2, BLK, width), bf16),
         ],
-        scratch_shapes=[pltpu.VMEM((nrows + BLK, width), f32)],
-        compiler_params=pltpu.CompilerParams(vmem_limit_bytes=48 * 1024 * 1024),
+        scratch_shapes=[pltpu.VMEM((nrows + 2 * BLK, width), bf16), pltpu.VMEM((4, BLK, width), bf16)],
+        compiler_params=BIG_VMEM,
+        cost_estimate=pl.CostEstimate(
+            flops=2 * BLK * BLK * width * (12 + farw3.shape[0]),
+            transcendentals=0,
+            bytes_accessed=2 * width * (nrows + 2 * arrived.shape[0] * BLK),
+        ),
+    )(far_col, far_ptr, requested, export_block, field, lo, hi, arrived, band, farw3)
+
+
+def hop1(far_col, far_ptr, field, lo, hi, arrived, band, farw3):
+    nrows, width = field.shape
+    return pl.pallas_call(
+        hop1_kernel,
+        in_specs=[smem(), smem()] + [vmem()] * 6,
+        out_specs=vmem(),
+        out_shape=jax.ShapeDtypeStruct((nrows, width), bf16),
+        scratch_shapes=scratch(field),
+        compiler_params=BIG_VMEM,
         cost_estimate=pl.CostEstimate(
             flops=2 * BLK * BLK * width * (3 * nrows // BLK + farw3.shape[0]),
             transcendentals=0,
-            bytes_accessed=2 * width * (nrows * 2 + 2 * arrived.shape[0] * BLK),
-        ),
-    )(src, rows, send_rows, field, lo, hi, arrived, band3, farw3)
-
-
-def hop2(src, rows, field, lo, hi, arrived, band3, farw3, features, hidden, mix):
+            bytes_accessed=2 * width * (nrows * 2 + arrived.shape[0] * BLK),
+        ),
+    )(far_col, far_ptr, field, lo, hi, arrived, band, farw3)
+
+
+def hop2(far_col, far_ptr, field, lo, hi, arrived, band, farw3, features, hidden, mix):
     nrows, width = field.shape
     return pl.pallas_call(
         hop2_kernel,
         in_specs=[smem(), smem()] + [vmem()] * 9,
         out_specs=vmem(),
         out_shape=jax.ShapeDtypeStruct((nrows, width), bf16),
-        scratch_shapes=[pltpu.VMEM((nrows + BLK, width), f32)],
-        compiler_params=pltpu.CompilerParams(vmem_limit_bytes=48 * 1024 * 1024),
+        scratch_shapes=scratch(field),
+        compiler_params=BIG_VMEM,
         cost_estimate=pl.CostEstimate(
             flops=2 * BLK * BLK * width * (3 * nrows // BLK + farw3.shape[0])
             + 2 * nrows * width * CHUNK * 3,
             transcendentals=0,
             bytes_accessed=2 * width * (nrows * 6 + arrived.shape[0] * BLK),
         ),
-    )(src, rows, field, lo, hi, arrived, band3, farw3, features, hidden, mix)
-
-
-def halo(field):
+    )(far_col, far_ptr, field, lo, hi, arrived, band, farw3, features, hidden, mix)
+
+
+def halo(first, last):
     count = lax.axis_size("node")
     forward = [(i, i + 1) for i in range(count - 1)]
     backward = [(t, s) for s, t in forward]
-    lo = lax.ppermute(field[field.shape[0] - BLK :], "node", forward)
-    hi = lax.ppermute(field[:BLK], "node", backward)
+    lo = lax.ppermute(last, "node", forward)
+    hi = lax.ppermute(first, "node", backward)
     return lo, hi
 
 
@@ -272,21 +334,24 @@
     send_rows = own_exports[requested].astype(jnp.int32)
 
     hidden = front_hidden(features, filter_gate_weight)
+    blocks = node_rows // BLK
     width = hidden.shape[1]
-    band3 = band_weight.reshape(node_rows, 3, BLK).transpose(1, 0, 2)
     farw3 = far_weight.reshape(BLK, far_cap, BLK).transpose(1, 0, 2)
 
     def exchange(send):
         return lax.all_to_all(send, "node", split_axis=0, concat_axis=0, tiled=True)
 
     arrived1 = exchange(hidden.reshape(blocks, BLK, width)[send_rows])
-    lo1, hi1 = halo(hidden)
+    lo1, hi1 = halo(hidden[:BLK], hidden[node_rows - BLK :])
     skip_out = front_skip(hidden, skip_weight)
-    hop_one, send2 = hop1(sources, slot_rows, send_rows, hidden, lo1, hi1, arrived1, band3, farw3)
+    send2, edge = early(
+        far_col, far_ptr, requested, export_block, hidden, lo1, hi1, arrived1, band_weight, farw3
+    )
     arrived2 = exchange(send2)
-    lo2, hi2 = halo(hop_one)
+    lo2, hi2 = halo(edge[0], edge[1])
+    hop_one = hop1(far_col, far_ptr, hidden, lo1, hi1, arrived1, band_weight, farw3)
     residual = hop2(
-        sources, slot_rows, hop_one, lo2, hi2, arrived2, band3, farw3, features, hidden, mix_weight
+        far_col, far_ptr, hop_one, lo2, hi2, arrived2, band_weight, farw3, features, hidden, mix_weight
     )
     return residual, skip_out
 

time: 95.8 us -> 94.7 us (0.989)
  waiting for transfers between devices: 29.8 us -> 26.8 us
  Pallas kernels: 18.7 us -> 19.8 us
    ppermute x4, waiting for transfers between devices: 29.8 us -> 26.8 us  [the longest x2 26.8 us: halo(): hi = lax.ppermute(first, 'node', backward)]
    pallas_call x1 -> x2, Pallas kernels: 3.82 us -> 5.71 us  [the longest x1 3.56 us: hop1(): pl.pallas_call(hop1_kernel, in_specs=[smem(), smem()] + [vmem()] * 6, out...]
    unnamed x23 -> x29, local copies, waits for them, and re-layouts: 5.62 us -> 7.48 us
    reshape x1 -> x0, local copies, waits for them, and re-layouts: 1.37 us -> none  [local(): band3 = band_weight.reshape(node_rows, 3, BLK).transpose(1, 0, 2)]
  transfers between devices with their start and end apart: 7 -> 7, of which waited for: 2 -> 2; matrix products, arithmetic and copies ran while one was open for 4% -> 3% of each run, Pallas kernels for 8% -> 12%
where the time goes in v8:
time: 94.7 us; the launch traced here: 93.9 us
  starting transfers between devices  30.1 us (32%)
  waiting for transfers between devices  26.8 us (28%)
  Pallas kernels  19.8 us (21%)
  local copies, waits for them, and re-layouts  13.2 us (14%)
  other arithmetic  3.11 us (3%)
    ppermute x2, waiting for transfers between devices, halo(): hi = lax.ppermute(first, 'node', backward)  26.8 us
    all_to_all x2, starting transfers between devices, exchange(): return lax.all_to_all(send, 'node', split_axis=0, concat_axis=0, tiled=True)  10.5 us
    ppermute x2, starting transfers between devices, halo(): lo = lax.ppermute(last, 'node', forward)  8.38 us
    unnamed x29, local copies, waits for them, and re-layouts  7.48 us
    all_to_all x1, starting transfers between devices, local(): lax.all_to_all(wanted[:, None], 'node', split_axis=0, concat_axis=0, tile...  6.55 us
    pallas_call x1, Pallas kernels, hop2(): pl.pallas_call(hop2_kernel, in_specs=[smem(), smem()] + [vmem()] * 9, out...  6.36 us
    pallas_call x1, Pallas kernels, front_skip(): pl.pallas_call(skip_kernel, grid=(rows // tile,), in_specs=[pl.BlockSpec(...  5.35 us
    ppermute x2, starting transfers between devices, halo(): hi = lax.ppermute(first, 'node', backward)  4.66 us
  transfers between devices with their start and end apart: 7, of which 2 were waited for; matrix products, arithmetic and copies ran while one was open for 3% of the time, Pallas kernels for 12%

profile of v8, /device:TPU:15, one launch (start us, length us, event | category | flops | bytes accessed | tf_op | source)
XLA Modules:
  0.0 93.9 jit_solution(10403568209276696673)
XLA Ops:
  0.6 0.0 copy-start.7
  0.6 0.0 copy-start.6
  0.7 0.0 copy-start.12
  0.7 0.0 copy-start.5
  0.7 1.3 %slice.18 = s32[1,1]{1,0:T(1,128)} slice(s32[1,17]{1,0:T(1,128)} %ptr_ref.5), slice={[0:1], [16:17]} | slice | bytes 8 | tf_op jit(solution)/shard_map/slice | solution.py:327
  1.9 0.6 iota_compare_fusion.1
  2.6 0.7 fusion.3
  3.3 0.1 select_reduce_fusion
  3.4 0.7 copy.36
  4.1 6.6 %all-to-all-start = ((s32[16,1,1]{2,1,0:T(1,128)}), s32[16,1,1]{2,1,0:T(1,128)S(1)}, u32[]{:S(2)}, u32[]{:S(2)}) async-start(s32[16,1,1]{2,1,0:T(1,128)} %copy.36), calls=%async_computation | async-start | bytes 16384 | tf_op jit(solution)/shard_map/all_to_all | solution.py:331
  10.6 0.7 constant_dynamic-slice_fusion
  11.4 0.5 fusion.5
  11.9 1.6 %copy-done.2 = bf16[1024,1024]{1,0:T(8,128)(2,1)S(1)} copy-done((bf16[1024,1024]{1,0:T(8,128)(2,1)S(1)}, bf16[1024,1024]{1,0:T(8,128)(2,1)}, u32[]{:S(2)}) %copy-start.2) | copy-done | bytes 2097176
  13.5 0.7 copy-done.8
  14.2 2.4 %shard_map.104.field_ref.h_ref = bf16[1024,512]{1,0:T(8,128)(2,1)S(1)} custom-call(bf16[1024,1024]{1,0:T(8,128)(2,1)S(1)} %copy-done.2, bf16[64,64]{1,0:T(8,128)(2,1)S(1)} %copy-done.8), custom_call_target="tpu_custom_call" | custom-call | flops 1073741824 | bytes 3145728 | tf_op jit(solution)/shard_map/pallas_call | solution.py:84
  16.6 0.0 all-to-all-done
  16.6 0.4 reduce.req_ref
  17.0 1.3 %fusion.2 = s32[16]{0:T(128)S(1)} fusion(s32[16]{0:T(128)S(1)} %reduce.req_ref, s32[]{:T(128)} %bitcast.6, s32[]{:T(128)} %bitcast.5), kind=kLoop, calls=%fused_computation.17 | loop fusion | flops 128 | bytes 136 | tf_op jit(solution)/shard_map/select_n | solution.py:344
  18.3 1.6 %gather_fusion = bf16[16,64,512]{2,1,0:T(8,128)(2,1)} fusion(bf16[16,64,512]{2,1,0:T(8,128)(2,1)S(1)} %bitcast.20, s32[1024]{0:T(1024)S(1)} %pad_clamp_fusion), kind=kCustom, calls=%fused_computation | custom fusion | bytes 2097216 | tf_op jit(solution)/shard_map/gather | solution.py:344
  19.9 6.0 %all-to-all-start.1 = ((bf16[16,64,512]{2,1,0:T(8,128)(2,1)}), bf16[16,64,512]{2,1,0:T(8,128)(2,1)S(1)}, u32[]{:S(2)}, u32[]{:S(2)}) async-start(bf16[16,64,512]{2,1,0:T(8,128)(2,1)} %gather_fusion), calls=%async_computation.1 | async-start | bytes 2097152 | tf_op jit(solution)/shard_map/all_to_all | solution.py:342
  25.9 0.6 fusion.4
  26.6 2.4 %collective-permute-start.1 = (bf16[64,512]{1,0:T(8,128)(2,1)}, bf16[64,512]{1,0:T(8,128)(2,1)S(1)}, u32[]{:S(2)}, u32[]{:S(2)}) collective-permute-start(bf16[64,512]{1,0:T(8,128)(2,1)} %get-tuple-element.6), channel_id=1, source_target_pairs={{1,0},{2,1},{3,2},{4,3},{5,4},{6,5},{7,6},{8,7},{9,8},{10,9},{11,1... | collective-permute-start | bytes 196616 | tf_op jit(solution)/shard_map/ppermute | solution.py:298
  29.0 4.2 %collective-permute-start = (bf16[64,512]{1,0:T(8,128)(2,1)S(1)}, bf16[64,512]{1,0:T(8,128)(2,1)S(1)}, u32[]{:S(2)}, u32[]{:S(2)}) collective-permute-start(bf16[64,512]{1,0:T(8,128)(2,1)S(1)} %get-tuple-element.7), channel_id=1, source_target_pairs={{0,1},{1,2},{2,3},{3,4},{4,5},{5,6},{6,7},{7,8},{8,9},{9,10},{10,1... | collective-permute-start | bytes 196616 | tf_op jit(solution)/shard_map/ppermute | solution.py:297
  33.2 0.1 copy.39.exp_ref
  33.3 0.0 copy-done.10
  33.3 0.2 reshape.61
  33.5 0.1 copy.44
  33.6 0.2 copy.38.band_ref
  33.8 17.7 %collective-permute-done.1.hi_ref = bf16[64,512]{1,0:T(8,128)(2,1)S(1)} collective-permute-done((bf16[64,512]{1,0:T(8,128)(2,1)}, bf16[64,512]{1,0:T(8,128)(2,1)S(1)}, u32[]{:S(2)}, u32[]{:S(2)}) %collective-permute-start.1) | collective-permute-done | bytes 65568 | tf_op jit(solution)/shard_map/ppermute | solution.py:298
  51.5 0.0 collective-permute-done.lo_ref
  51.5 0.0 all-to-all-done.1.arr_ref
  51.5 2.1 %shard_map.106 = (bf16[16,64,512]{2,1,0:T(8,128)(2,1)S(1)}, bf16[2,64,512]{2,1,0:T(8,128)(2,1)S(1)}) custom-call(s32[1,15]{1,0:T(1,128)S(1)} %copy-done.6, s32[1,17]{1,0:T(1,128)S(1)} %copy-done.7, s32[16]{0:T(128)S(1)} %reduce.req_ref, s32[16,2]{1,0:T(8,128)S(1)} %copy.39.exp_ref, bf16[1024,512]{1,0:T(8,128)(2,1)S(1)} %shard_map.104.field_ref.h_ref, ...), custom_call_target="tpu_custom_call" | custom-call | flops 113246208 | bytes 3145728 | tf_op jit(solution)/shard_map/pallas_call | solution.py:240
  53.7 1.0 %copy-done.4 = bf16[16,64,512]{2,1,0:T(8,128)(2,1)} copy-done((bf16[16,64,512]{2,1,0:T(8,128)(2,1)}, bf16[16,64,512]{2,1,0:T(8,128)(2,1)S(1)}, u32[]{:S(2)}) %copy-start.4) | copy-done | bytes 1048600
  54.6 4.5 %all-to-all-start.2 = ((bf16[16,64,512]{2,1,0:T(8,128)(2,1)}), bf16[16,64,512]{2,1,0:T(8,128)(2,1)}, u32[]{:S(2)}, u32[]{:S(2)}) async-start(bf16[16,64,512]{2,1,0:T(8,128)(2,1)} %copy-done.4), calls=%async_computation.2 | async-start | bytes 2097152 | tf_op jit(solution)/shard_map/all_to_all | solution.py:342
  59.2 2.3 %collective-permute-start.3 = (bf16[64,512]{1,0:T(8,128)(2,1)S(1)}, bf16[64,512]{1,0:T(8,128)(2,1)S(1)}, u32[]{:S(2)}, u32[]{:S(2)}) collective-permute-start(bf16[64,512]{1,0:T(8,128)(2,1)S(1)} %get-tuple-element.8), channel_id=1, source_target_pairs={{1,0},{2,1},{3,2},{4,3},{5,4},{6,5},{7,6},{8,7},{9,8},{10,9},{11,1... | collective-permute-start | bytes 196616 | tf_op jit(solution)/shard_map/ppermute | solution.py:298
  61.5 4.2 %collective-permute-start.2 = (bf16[64,512]{1,0:T(8,128)(2,1)S(1)}, bf16[64,512]{1,0:T(8,128)(2,1)S(1)}, u32[]{:S(2)}, u32[]{:S(2)}) collective-permute-start(bf16[64,512]{1,0:T(8,128)(2,1)S(1)} %get-tuple-element.9), channel_id=1, source_target_pairs={{0,1},{1,2},{2,3},{3,4},{4,5},{5,6},{6,7},{7,8},{8,9},{9,10},{10,1... | collective-permute-start | bytes 196616 | tf_op jit(solution)/shard_map/ppermute | solution.py:297
  65.7 5.4 %shard_map.108 = bf16[1024,4096]{1,0:T(8,128)(2,1)} custom-call(bf16[1024,512]{1,0:T(8,128)(2,1)S(1)} %shard_map.104.field_ref.h_ref, bf16[32,256]{1,0:T(8,128)(2,1)S(1)} %copy-done.5), custom_call_target="tpu_custom_call" | custom-call | flops 2147483648 | bytes 9437184 | tf_op jit(solution)/shard_map/pallas_call | solution.py:110
  71.0 0.0 copy-done.11
  71.0 0.1 copy.42.mix_ref
  71.1 3.6 %shard_map.105.field_ref = bf16[1024,512]{1,0:T(8,128)(2,1)S(1)} custom-call(s32[1,15]{1,0:T(1,128)S(1)} %copy-done.6, s32[1,17]{1,0:T(1,128)S(1)} %copy-done.7, bf16[1024,512]{1,0:T(8,128)(2,1)S(1)} %shard_map.104.field_ref.h_ref, bf16[64,512]{1,0:T(8,128)(2,1)S(1)} %collective-permute-done.lo_ref, bf16[64,512]{1,0:T(8,128)(2,1)S(1)} %collective-permute-done.1.hi_ref, ...), custom_call_target="tpu_custom_call" | custom-call | flops 264241152 | bytes 3145728 | tf_op jit(solution)/shard_map/pallas_call | solution.py:260
  74.7 0.0 copy-start
  74.7 1.0 %copy-done = bf16[1024,512]{1,0:T(8,128)(2,1)} copy-done((bf16[1024,512]{1,0:T(8,128)(2,1)}, bf16[1024,512]{1,0:T(8,128)(2,1)S(1)}, u32[]{:S(2)}) %copy-start) | copy-done | bytes 1048600
  75.7 9.1 %collective-permute-done.3.hi_ref = bf16[64,512]{1,0:T(8,128)(2,1)S(1)} collective-permute-done((bf16[64,512]{1,0:T(8,128)(2,1)S(1)}, bf16[64,512]{1,0:T(8,128)(2,1)S(1)}, u32[]{:S(2)}, u32[]{:S(2)}) %collective-permute-start.3) | collective-permute-done | bytes 65568 | tf_op jit(solution)/shard_map/ppermute | solution.py:298
  84.7 0.0 collective-permute-done.2.lo_ref
  84.7 0.0 all-to-all-done.2.arr_ref
  84.7 1.2 %copy-done.1 = bf16[1024,512]{1,0:T(8,128)(2,1)S(1)} copy-done((bf16[1024,512]{1,0:T(8,128)(2,1)S(1)}, bf16[1024,512]{1,0:T(8,128)(2,1)}, u32[]{:S(2)}) %copy-start.1) | copy-done | bytes 1048600
  86.0 1.6 %copy-done.3 = bf16[1024,1024]{1,0:T(8,128)(2,1)S(1)} copy-done((bf16[1024,1024]{1,0:T(8,128)(2,1)S(1)}, bf16[1024,1024]{1,0:T(8,128)(2,1)}, u32[]{:S(2)}) %copy-start.3) | copy-done | bytes 2097176
  87.6 6.4 %shard_map.107 = bf16[1024,512]{1,0:T(8,128)(2,1)} custom-call(s32[1,15]{1,0:T(1,128)S(1)} %copy-done.6, s32[1,17]{1,0:T(1,128)S(1)} %copy-done.7, bf16[1024,512]{1,0:T(8,128)(2,1)S(1)} %copy-done.1, bf16[64,512]{1,0:T(8,128)(2,1)S(1)} %collective-permute-done.2.lo_ref, bf16[64,512]{1,0:T(8,128)(2,1)S(1)} %collective-permute-done.3.hi_ref, ...), custom_call_target="tpu_custom_call" | custom-call | flops 1069547520 | bytes 7340032 | tf_op jit(solution)/shard_map/pallas_call | solution.py:277
  (15 shorter events, 0.0 us)
Async XLA Ops:
  0.6 50.9 %copy-start.7 = (s32[1,17]{1,0:T(1,128)S(1)}, s32[1,17]{1,0:T(1,128)}, u32[]{:S(2)}) copy-start(s32[1,17]{1,0:T(1,128)} %ptr_ref.5) | copy-start | bytes 208
  0.6 50.9 %copy-start.6 = (s32[1,15]{1,0:T(1,128)S(1)}, s32[1,15]{1,0:T(1,128)}, u32[]{:S(2)}) copy-start(s32[1,15]{1,0:T(1,128)} %col_ref.5) | copy-start | bytes 184
  0.7 32.5 %copy-start.12 = (s32[16,2]{0,1:T(2,128)S(1)}, s32[16,2]{0,1:T(2,128)}, u32[]{:S(2)}) copy-start(s32[16,2]{0,1:T(2,128)} %param.17) | copy-start | bytes 388
  0.7 65.0 %copy-start.5 = (bf16[32,256]{1,0:T(8,128)(2,1)S(1)}, bf16[32,256]{1,0:T(8,128)(2,1)}, u32[]{:S(2)}) copy-start(bf16[32,256]{1,0:T(8,128)(2,1)} %sw_ref.1) | copy-start | bytes 49156
  4.1 12.6 %all-to-all-start = ((s32[16,1,1]{2,1,0:T(1,128)}), s32[16,1,1]{2,1,0:T(1,128)S(1)}, u32[]{:S(2)}, u32[]{:S(2)}) async-start(s32[16,1,1]{2,1,0:T(1,128)} %copy.36), calls=%async_computation | async-start | bytes 16384 | tf_op jit(solution)/shard_map/all_to_all | solution.py:331
  11.9 1.6 %copy-start.2 = (bf16[1024,1024]{1,0:T(8,128)(2,1)S(1)}, bf16[1024,1024]{1,0:T(8,128)(2,1)}, u32[]{:S(2)}) copy-start(bf16[1024,1024]{1,0:T(8,128)(2,1)} %x_ref.3) | copy-start | bytes 6291460
  13.5 0.7 copy-start.8
  14.2 19.0 %copy-start.10 = (bf16[64,960]{1,0:T(8,128)(2,1)S(1)}, bf16[64,960]{1,0:T(8,128)(2,1)}, u32[]{:S(2)}) copy-start(bf16[64,960]{1,0:T(8,128)(2,1)} %param.14) | copy-start | bytes 368644
  14.2 19.3 %copy-start.9 = (bf16[1024,192]{0,1:T(8,128)(2,1)S(1)}, bf16[1024,192]{0,1:T(8,128)(2,1)}, u32[]{:S(2)}) copy-start(bf16[1024,192]{0,1:T(8,128)(2,1)} %param.13) | copy-start | bytes 1179652
  19.9 31.6 %all-to-all-start.1 = ((bf16[16,64,512]{2,1,0:T(8,128)(2,1)}), bf16[16,64,512]{2,1,0:T(8,128)(2,1)S(1)}, u32[]{:S(2)}, u32[]{:S(2)}) async-start(bf16[16,64,512]{2,1,0:T(8,128)(2,1)} %gather_fusion), calls=%async_computation.1 | async-start | bytes 2097152 | tf_op jit(solution)/shard_map/all_to_all | solution.py:342
  26.6 44.4 %copy-start.11 = (bf16[96,32]{0,1:T(8,128)(2,1)S(1)}, bf16[96,32]{0,1:T(8,128)(2,1)}, u32[]{:S(2)}) copy-start(bf16[96,32]{0,1:T(8,128)(2,1)} %param.12) | copy-start | bytes 18436
  26.6 24.9 %collective-permute-start.1 = (bf16[64,512]{1,0:T(8,128)(2,1)}, bf16[64,512]{1,0:T(8,128)(2,1)S(1)}, u32[]{:S(2)}, u32[]{:S(2)}) collective-permute-start(bf16[64,512]{1,0:T(8,128)(2,1)} %get-tuple-element.6), channel_id=1, source_target_pairs={{1,0},{2,1},{3,2},{4,3},{5,4},{6,5},{7,6},{8,7},{9,8},{10,9},{11,1... | collective-permute-start | bytes 196616 | tf_op jit(solution)/shard_map/ppermute | solution.py:298
  29.0 22.5 %collective-permute-start = (bf16[64,512]{1,0:T(8,128)(2,1)S(1)}, bf16[64,512]{1,0:T(8,128)(2,1)S(1)}, u32[]{:S(2)}, u32[]{:S(2)}) collective-permute-start(bf16[64,512]{1,0:T(8,128)(2,1)S(1)} %get-tuple-element.7), channel_id=1, source_target_pairs={{0,1},{1,2},{2,3},{3,4},{4,5},{5,6},{6,7},{7,8},{8,9},{9,10},{10,1... | collective-permute-start | bytes 196616 | tf_op jit(solution)/shard_map/ppermute | solution.py:297
  53.7 1.0 %copy-start.4 = (bf16[16,64,512]{2,1,0:T(8,128)(2,1)}, bf16[16,64,512]{2,1,0:T(8,128)(2,1)S(1)}, u32[]{:S(2)}) copy-start(bf16[16,64,512]{2,1,0:T(8,128)(2,1)S(1)} %get-tuple-element.5) | copy-start | bytes 3145732
  54.6 30.1 %all-to-all-start.2 = ((bf16[16,64,512]{2,1,0:T(8,128)(2,1)}), bf16[16,64,512]{2,1,0:T(8,128)(2,1)}, u32[]{:S(2)}, u32[]{:S(2)}) async-start(bf16[16,64,512]{2,1,0:T(8,128)(2,1)} %copy-done.4), calls=%async_computation.2 | async-start | bytes 2097152 | tf_op jit(solution)/shard_map/all_to_all | solution.py:342
  59.2 25.5 %collective-permute-start.3 = (bf16[64,512]{1,0:T(8,128)(2,1)S(1)}, bf16[64,512]{1,0:T(8,128)(2,1)S(1)}, u32[]{:S(2)}, u32[]{:S(2)}) collective-permute-start(bf16[64,512]{1,0:T(8,128)(2,1)S(1)} %get-tuple-element.8), channel_id=1, source_target_pairs={{1,0},{2,1},{3,2},{4,3},{5,4},{6,5},{7,6},{8,7},{9,8},{10,9},{11,1... | collective-permute-start | bytes 196616 | tf_op jit(solution)/shard_map/ppermute | solution.py:298
  61.5 23.3 %collective-permute-start.2 = (bf16[64,512]{1,0:T(8,128)(2,1)S(1)}, bf16[64,512]{1,0:T(8,128)(2,1)S(1)}, u32[]{:S(2)}, u32[]{:S(2)}) collective-permute-start(bf16[64,512]{1,0:T(8,128)(2,1)S(1)} %get-tuple-element.9), channel_id=1, source_target_pairs={{0,1},{1,2},{2,3},{3,4},{4,5},{5,6},{6,7},{7,8},{8,9},{9,10},{10,1... | collective-permute-start | bytes 196616 | tf_op jit(solution)/shard_map/ppermute | solution.py:297
  74.7 1.0 %copy-start = (bf16[1024,512]{1,0:T(8,128)(2,1)}, bf16[1024,512]{1,0:T(8,128)(2,1)S(1)}, u32[]{:S(2)}) copy-start(bf16[1024,512]{1,0:T(8,128)(2,1)S(1)} %shard_map.105.field_ref) | copy-start | bytes 3145732
  84.7 1.2 %copy-start.1 = (bf16[1024,512]{1,0:T(8,128)(2,1)S(1)}, bf16[1024,512]{1,0:T(8,128)(2,1)}, u32[]{:S(2)}) copy-start(bf16[1024,512]{1,0:T(8,128)(2,1)} %copy-done) | copy-start | bytes 3145732
  86.0 1.6 %copy-start.3 = (bf16[1024,1024]{1,0:T(8,128)(2,1)S(1)}, bf16[1024,1024]{1,0:T(8,128)(2,1)}, u32[]{:S(2)}) copy-start(bf16[1024,1024]{1,0:T(8,128)(2,1)} %x_ref.3) | copy-start | bytes 6291460

commit v9 on v8

--- a/solution.py
+++ b/solution.py
@@ -200,20 +200,26 @@
 
 def hop2_kernel(
     col_ref, ptr_ref, field_ref, lo_ref, hi_ref, arr_ref, band_ref, farw_ref,
-    x_ref, h_ref, mix_ref, out_ref, acc, pad,
+    x_hbm, h_hbm, mix_ref, out_ref, acc, pad, xs, hs, sems,
 ):
+    nrows, width = field_ref.shape
+    half = x_hbm.shape[1] // 2
+    x_copy = pltpu.make_async_copy(x_hbm.at[:, pl.ds(half, width)], xs, sems.at[0])
+    h_copy = pltpu.make_async_copy(h_hbm, hs, sems.at[1])
+    x_copy.start()
+    h_copy.start()
     accumulate(col_ref, ptr_ref, field_ref, lo_ref, hi_ref, arr_ref, band_ref, farw_ref, acc, pad)
-    nrows, width = field_ref.shape
-    half = x_ref.shape[1] // 2
     cw = mix_ref.shape[1]
     per = CHUNK // cw
     mix = mix_ref[...]
     m = [bd_inkernel(mix[i * cw : (i + 1) * cw], per) for i in range(3)]
+    x_copy.wait()
+    h_copy.wait()
     for j in range(width // CHUNK):
         cols = slice(j * CHUNK, (j + 1) * CHUNK)
         two = acc[:nrows, cols].astype(bf16)
-        v = x_ref[:, half + j * CHUNK : half + (j + 1) * CHUNK].astype(f32)
-        v = v + jnp.dot(h_ref[:, cols], m[0], preferred_element_type=f32)
+        v = xs[:, cols].astype(f32)
+        v = v + jnp.dot(hs[:, cols], m[0], preferred_element_type=f32)
         v = v + jnp.dot(field_ref[:, cols], m[1], preferred_element_type=f32)
         v = v + jnp.dot(two, m[2], preferred_element_type=f32)
         out_ref[:, cols] = v.astype(bf16)
@@ -225,6 +231,10 @@
 
 def smem():
     return pl.BlockSpec(memory_space=pltpu.SMEM)
+
+
+def hbm():
+    return pl.BlockSpec(memory_space=pltpu.HBM)
 
 
 BIG_VMEM = pltpu.CompilerParams(vmem_limit_bytes=48 * 1024 * 1024)
@@ -276,11 +286,16 @@
     nrows, width = field.shape
     return pl.pallas_call(
         hop2_kernel,
-        in_specs=[smem(), smem()] + [vmem()] * 9,
+        in_specs=[smem(), smem()] + [vmem()] * 6 + [hbm(), hbm(), vmem()],
         out_specs=vmem(),
         out_shape=jax.ShapeDtypeStruct((nrows, width), bf16),
-        scratch_shapes=scratch(field),
-        compiler_params=BIG_VMEM,
+        scratch_shapes=scratch(field)
+        + [
+            pltpu.VMEM((nrows, width), bf16),
+            pltpu.VMEM((nrows, width), bf16),
+            pltpu.SemaphoreType.DMA((2,)),
+        ],
+        compiler_params=pltpu.CompilerParams(),
         cost_estimate=pl.CostEstimate(
             flops=2 * BLK * BLK * width * (3 * nrows // BLK + farw3.shape[0])
             + 2 * nrows * width * CHUNK * 3,

time: 94.7 us -> 93.2 us (0.984)
  local copies, waits for them, and re-layouts: 13.2 us -> 11.7 us
  Pallas kernels: 19.8 us -> 21.1 us
    unnamed x29 -> x35, local copies, waits for them, and re-layouts: 7.48 us -> 5.93 us
where the time goes in v9:
time: 93.2 us; the launch traced here: 92.4 us
  starting transfers between devices  29.8 us (32%)
  waiting for transfers between devices  25.9 us (28%)
  Pallas kernels  21.1 us (23%)
  local copies, waits for them, and re-layouts  11.7 us (13%)
  other arithmetic  3.1 us (3%)
    ppermute x2, waiting for transfers between devices, halo(): hi = lax.ppermute(first, 'node', backward)  25.8 us
    all_to_all x2, starting transfers between devices, exchange(): return lax.all_to_all(send, 'node', split_axis=0, concat_axis=0, tiled=True)  10.3 us
    ppermute x2, starting transfers between devices, halo(): lo = lax.ppermute(last, 'node', forward)  8.66 us
    pallas_call x1, Pallas kernels, hop2(): pl.pallas_call(hop2_kernel, in_specs=[smem(), smem()] + [vmem()] * 6 + [h...  7.18 us
    all_to_all x1, starting transfers between devices, local(): lax.all_to_all(wanted[:, None], 'node', split_axis=0, concat_axis=0, tile...  6.55 us
    unnamed x35, local copies, waits for them, and re-layouts  5.93 us
    pallas_call x1, Pallas kernels, front_skip(): pl.pallas_call(skip_kernel, grid=(rows // tile,), in_specs=[pl.BlockSpec(...  5.36 us
    ppermute x2, starting transfers between devices, halo(): hi = lax.ppermute(first, 'node', backward)  4.38 us
  transfers between devices with their start and end apart: 7, of which 2 were waited for; matrix products, arithmetic and copies ran while one was open for 3% of the time, Pallas kernels for 12%

profile of v9, /device:TPU:15, one launch (start us, length us, event | category | flops | bytes accessed | tf_op | source)
XLA Modules:
  0.0 92.4 jit_solution(2531141180927250346)
XLA Ops:
  0.6 0.0 copy-start.8
  0.6 0.0 copy-start.7
  0.7 0.0 copy-start.15
  0.7 0.0 copy-start.6
  0.7 1.3 %slice.18 = s32[1,1]{1,0:T(1,128)} slice(s32[1,17]{1,0:T(1,128)} %ptr_ref.5), slice={[0:1], [16:17]} | slice | bytes 8 | tf_op jit(solution)/shard_map/slice | solution.py:342
  1.9 0.6 iota_compare_fusion.1
  2.6 0.7 fusion.3
  3.3 0.1 select_reduce_fusion
  3.4 0.7 copy.36
  4.1 6.6 %all-to-all-start = ((s32[16,1,1]{2,1,0:T(1,128)}), s32[16,1,1]{2,1,0:T(1,128)S(1)}, u32[]{:S(2)}, u32[]{:S(2)}) async-start(s32[16,1,1]{2,1,0:T(1,128)} %copy.36), calls=%async_computation | async-start | bytes 16384 | tf_op jit(solution)/shard_map/all_to_all | solution.py:346
  10.6 0.7 constant_dynamic-slice_fusion
  11.4 0.5 fusion.5
  11.9 1.6 %copy-done.4 = bf16[1024,1024]{1,0:T(8,128)(2,1)S(1)} copy-done((bf16[1024,1024]{1,0:T(8,128)(2,1)S(1)}, bf16[1024,1024]{1,0:T(8,128)(2,1)}, u32[]{:S(2)}) %copy-start.4) | copy-done | bytes 2097176
  13.5 0.7 copy-done.9
  14.2 2.4 %shard_map.104.field_ref.h_hbm.h_ref = bf16[1024,512]{1,0:T(8,128)(2,1)S(1)} custom-call(bf16[1024,1024]{1,0:T(8,128)(2,1)S(1)} %copy-done.4, bf16[64,64]{1,0:T(8,128)(2,1)S(1)} %copy-done.9), custom_call_target="tpu_custom_call" | custom-call | flops 1073741824 | bytes 3145728 | tf_op jit(solution)/shard_map/pallas_call | solution.py:84
  16.6 0.0 copy-start
  16.6 0.0 all-to-all-done
  16.6 0.4 reduce.req_ref
  17.0 1.3 %fusion.2 = s32[16]{0:T(128)S(1)} fusion(s32[16]{0:T(128)S(1)} %reduce.req_ref, s32[]{:T(128)} %bitcast.6, s32[]{:T(128)} %bitcast.5), kind=kLoop, calls=%fused_computation.17 | loop fusion | flops 128 | bytes 136 | tf_op jit(solution)/shard_map/select_n | solution.py:359
  18.3 1.6 %gather_fusion = bf16[16,64,512]{2,1,0:T(8,128)(2,1)} fusion(bf16[16,64,512]{2,1,0:T(8,128)(2,1)S(1)} %bitcast.20, s32[1024]{0:T(1024)S(1)} %pad_clamp_fusion), kind=kCustom, calls=%fused_computation | custom fusion | bytes 2097216 | tf_op jit(solution)/shard_map/gather | solution.py:359
  19.9 6.0 %all-to-all-start.1 = ((bf16[16,64,512]{2,1,0:T(8,128)(2,1)}), bf16[16,64,512]{2,1,0:T(8,128)(2,1)S(1)}, u32[]{:S(2)}, u32[]{:S(2)}) async-start(bf16[16,64,512]{2,1,0:T(8,128)(2,1)} %gather_fusion), calls=%async_computation.1 | async-start | bytes 2097152 | tf_op jit(solution)/shard_map/all_to_all | solution.py:357
  25.9 0.6 fusion.4
  26.6 2.4 %collective-permute-start.1 = (bf16[64,512]{1,0:T(8,128)(2,1)}, bf16[64,512]{1,0:T(8,128)(2,1)S(1)}, u32[]{:S(2)}, u32[]{:S(2)}) collective-permute-start(bf16[64,512]{1,0:T(8,128)(2,1)} %get-tuple-element.6), channel_id=1, source_target_pairs={{1,0},{2,1},{3,2},{4,3},{5,4},{6,5},{7,6},{8,7},{9,8},{10,9},{11,1... | collective-permute-start | bytes 196616 | tf_op jit(solution)/shard_map/ppermute | solution.py:313
  29.0 4.2 %collective-permute-start = (bf16[64,512]{1,0:T(8,128)(2,1)S(1)}, bf16[64,512]{1,0:T(8,128)(2,1)S(1)}, u32[]{:S(2)}, u32[]{:S(2)}) collective-permute-start(bf16[64,512]{1,0:T(8,128)(2,1)S(1)} %get-tuple-element.7), channel_id=1, source_target_pairs={{0,1},{1,2},{2,3},{3,4},{4,5},{5,6},{6,7},{7,8},{8,9},{9,10},{10,1... | collective-permute-start | bytes 196616 | tf_op jit(solution)/shard_map/ppermute | solution.py:312
  33.2 0.1 copy.39.exp_ref
  33.3 0.2 reshape.61
  33.5 0.1 copy.44
  33.6 0.2 copy.38.band_ref
  33.8 0.0 copy-start.1
  33.8 17.7 %collective-permute-done.1.hi_ref = bf16[64,512]{1,0:T(8,128)(2,1)S(1)} collective-permute-done((bf16[64,512]{1,0:T(8,128)(2,1)}, bf16[64,512]{1,0:T(8,128)(2,1)S(1)}, u32[]{:S(2)}, u32[]{:S(2)}) %collective-permute-start.1) | collective-permute-done | bytes 65568 | tf_op jit(solution)/shard_map/ppermute | solution.py:313
  51.5 0.0 collective-permute-done.lo_ref
  51.5 0.0 all-to-all-done.1.arr_ref
  51.5 2.6 %shard_map.106 = (bf16[16,64,512]{2,1,0:T(8,128)(2,1)S(1)}, bf16[2,64,512]{2,1,0:T(8,128)(2,1)S(1)}) custom-call(s32[1,15]{1,0:T(1,128)S(1)} %copy-done.7, s32[1,17]{1,0:T(1,128)S(1)} %copy-done.8, s32[16]{0:T(128)S(1)} %reduce.req_ref, s32[16,2]{1,0:T(8,128)S(1)} %copy.39.exp_ref, bf16[1024,512]{1,0:T(8,128)(2,1)S(1)} %shard_map.104.field_ref.h_hbm.h_ref, ...), custom_call_target="tpu_custom_call" | custom-call | flops 113246208 | bytes 3145728 | tf_op jit(solution)/shard_map/pallas_call | solution.py:250
  54.1 0.0 copy-start.5
  54.1 1.0 %copy-done.5 = bf16[16,64,512]{2,1,0:T(8,128)(2,1)} copy-done((bf16[16,64,512]{2,1,0:T(8,128)(2,1)}, bf16[16,64,512]{2,1,0:T(8,128)(2,1)S(1)}, u32[]{:S(2)}) %copy-start.5) | copy-done | bytes 1048600
  55.1 4.2 %all-to-all-start.2 = ((bf16[16,64,512]{2,1,0:T(8,128)(2,1)}), bf16[16,64,512]{2,1,0:T(8,128)(2,1)}, u32[]{:S(2)}, u32[]{:S(2)}) async-start(bf16[16,64,512]{2,1,0:T(8,128)(2,1)} %copy-done.5), calls=%async_computation.2 | async-start | bytes 2097152 | tf_op jit(solution)/shard_map/all_to_all | solution.py:357
  59.3 2.0 %collective-permute-start.3 = (bf16[64,512]{1,0:T(8,128)(2,1)S(1)}, bf16[64,512]{1,0:T(8,128)(2,1)S(1)}, u32[]{:S(2)}, u32[]{:S(2)}) collective-permute-start(bf16[64,512]{1,0:T(8,128)(2,1)S(1)} %get-tuple-element.8), channel_id=1, source_target_pairs={{1,0},{2,1},{3,2},{4,3},{5,4},{6,5},{7,6},{8,7},{9,8},{10,9},{11,1... | collective-permute-start | bytes 196616 | tf_op jit(solution)/shard_map/ppermute | solution.py:313
  61.3 4.5 %collective-permute-start.2 = (bf16[64,512]{1,0:T(8,128)(2,1)S(1)}, bf16[64,512]{1,0:T(8,128)(2,1)S(1)}, u32[]{:S(2)}, u32[]{:S(2)}) collective-permute-start(bf16[64,512]{1,0:T(8,128)(2,1)S(1)} %get-tuple-element.9), channel_id=1, source_target_pairs={{0,1},{1,2},{2,3},{3,4},{4,5},{5,6},{6,7},{7,8},{8,9},{9,10},{10,1... | collective-permute-start | bytes 196616 | tf_op jit(solution)/shard_map/ppermute | solution.py:312
  65.8 5.4 %shard_map.108 = bf16[1024,4096]{1,0:T(8,128)(2,1)} custom-call(bf16[1024,512]{1,0:T(8,128)(2,1)S(1)} %shard_map.104.field_ref.h_hbm.h_ref, bf16[32,256]{1,0:T(8,128)(2,1)S(1)} %copy-done.6), custom_call_target="tpu_custom_call" | custom-call | flops 2147483648 | bytes 9437184 | tf_op jit(solution)/shard_map/pallas_call | solution.py:110
  71.2 0.7 copy.42.mix_ref
  71.9 3.6 %shard_map.105.field_ref = bf16[1024,512]{1,0:T(8,128)(2,1)S(1)} custom-call(s32[1,15]{1,0:T(1,128)S(1)} %copy-done.7, s32[1,17]{1,0:T(1,128)S(1)} %copy-done.8, bf16[1024,512]{1,0:T(8,128)(2,1)S(1)} %shard_map.104.field_ref.h_hbm.h_ref, bf16[64,512]{1,0:T(8,128)(2,1)S(1)} %collective-permute-done.lo_ref, bf16[64,512]{1,0:T(8,128)(2,1)S(1)} %collective-permute-done.1.hi_ref, ...), custom_call_target="tpu_custom_call" | custom-call | flops 264241152 | bytes 3145728 | tf_op jit(solution)/shard_map/pallas_call | solution.py:270
  75.5 1.0 %copy-done.2 = bf16[1024,512]{1,0:T(8,128)(2,1)} copy-done((bf16[1024,512]{1,0:T(8,128)(2,1)}, bf16[1024,512]{1,0:T(8,128)(2,1)S(1)}, u32[]{:S(2)}) %copy-start.2) | copy-done | bytes 1048600
  76.5 8.1 %collective-permute-done.3.hi_ref = bf16[64,512]{1,0:T(8,128)(2,1)S(1)} collective-permute-done((bf16[64,512]{1,0:T(8,128)(2,1)S(1)}, bf16[64,512]{1,0:T(8,128)(2,1)S(1)}, u32[]{:S(2)}, u32[]{:S(2)}) %collective-permute-start.3) | collective-permute-done | bytes 65568 | tf_op jit(solution)/shard_map/ppermute | solution.py:313
  84.6 0.0 collective-permute-done.2.lo_ref
  84.6 0.0 all-to-all-done.2.arr_ref
  84.6 0.6 copy-done.12
  85.2 0.0 copy-done.13
  85.3 7.2 %shard_map.107 = bf16[1024,512]{1,0:T(8,128)(2,1)} custom-call(s32[1,15]{1,0:T(1,128)} %col_ref.5, s32[1,17]{1,0:T(1,128)} %ptr_ref.5, bf16[1024,512]{1,0:T(8,128)(2,1)} %copy-done.2, bf16[64,512]{1,0:T(8,128)(2,1)} %copy-done.13, bf16[64,512]{1,0:T(8,128)(2,1)} %copy-done.12, bf16[16,64,512]{2,1,0:T(8,128)(2,1)} %all-to-all-done.2.arr_ref, ...), custom_call_target="tpu_custom_call" | custom-call | flops 1069547520 | bytes 7340032 | tf_op jit(solution)/shard_map/pallas_call | solution.py:287
  (21 shorter events, 0.1 us)
Async XLA Ops:
  0.6 50.9 %copy-start.8 = (s32[1,17]{1,0:T(1,128)S(1)}, s32[1,17]{1,0:T(1,128)}, u32[]{:S(2)}) copy-start(s32[1,17]{1,0:T(1,128)} %ptr_ref.5) | copy-start | bytes 208
  0.6 50.9 %copy-start.7 = (s32[1,15]{1,0:T(1,128)S(1)}, s32[1,15]{1,0:T(1,128)}, u32[]{:S(2)}) copy-start(s32[1,15]{1,0:T(1,128)} %col_ref.5) | copy-start | bytes 184
  0.7 32.5 %copy-start.15 = (s32[16,2]{0,1:T(2,128)S(1)}, s32[16,2]{0,1:T(2,128)}, u32[]{:S(2)}) copy-start(s32[16,2]{0,1:T(2,128)} %param.17) | copy-start | bytes 388
  0.7 65.1 %copy-start.6 = (bf16[32,256]{1,0:T(8,128)(2,1)S(1)}, bf16[32,256]{1,0:T(8,128)(2,1)}, u32[]{:S(2)}) copy-start(bf16[32,256]{1,0:T(8,128)(2,1)} %sw_ref.1) | copy-start | bytes 49156
  4.1 12.6 %all-to-all-start = ((s32[16,1,1]{2,1,0:T(1,128)}), s32[16,1,1]{2,1,0:T(1,128)S(1)}, u32[]{:S(2)}, u32[]{:S(2)}) async-start(s32[16,1,1]{2,1,0:T(1,128)} %copy.36), calls=%async_computation | async-start | bytes 16384 | tf_op jit(solution)/shard_map/all_to_all | solution.py:346
  11.9 1.6 %copy-start.4 = (bf16[1024,1024]{1,0:T(8,128)(2,1)S(1)}, bf16[1024,1024]{1,0:T(8,128)(2,1)}, u32[]{:S(2)}) copy-start(bf16[1024,1024]{1,0:T(8,128)(2,1)} %x_hbm.1) | copy-start | bytes 6291460
  13.5 0.7 copy-start.9
  14.2 19.0 %copy-start.11 = (bf16[64,960]{1,0:T(8,128)(2,1)S(1)}, bf16[64,960]{1,0:T(8,128)(2,1)}, u32[]{:S(2)}) copy-start(bf16[64,960]{1,0:T(8,128)(2,1)} %param.14) | copy-start | bytes 368644
  14.2 19.3 %copy-start.10 = (bf16[1024,192]{0,1:T(8,128)(2,1)S(1)}, bf16[1024,192]{0,1:T(8,128)(2,1)}, u32[]{:S(2)}) copy-start(bf16[1024,192]{0,1:T(8,128)(2,1)} %param.13) | copy-start | bytes 1179652
  16.6 55.3 %copy-start = (bf16[1024,512]{1,0:T(8,128)(2,1)}, bf16[1024,512]{1,0:T(8,128)(2,1)S(1)}, u32[]{:S(2)}) copy-start(bf16[1024,512]{1,0:T(8,128)(2,1)S(1)} %shard_map.104.field_ref.h_hbm.h_ref) | copy-start | bytes 3145732
  19.9 31.6 %all-to-all-start.1 = ((bf16[16,64,512]{2,1,0:T(8,128)(2,1)}), bf16[16,64,512]{2,1,0:T(8,128)(2,1)S(1)}, u32[]{:S(2)}, u32[]{:S(2)}) async-start(bf16[16,64,512]{2,1,0:T(8,128)(2,1)} %gather_fusion), calls=%async_computation.1 | async-start | bytes 2097152 | tf_op jit(solution)/shard_map/all_to_all | solution.py:357
  26.6 44.6 %copy-start.14 = (bf16[96,32]{0,1:T(8,128)(2,1)S(1)}, bf16[96,32]{0,1:T(8,128)(2,1)}, u32[]{:S(2)}) copy-start(bf16[96,32]{0,1:T(8,128)(2,1)} %param.12) | copy-start | bytes 18436
  26.6 24.9 %collective-permute-start.1 = (bf16[64,512]{1,0:T(8,128)(2,1)}, bf16[64,512]{1,0:T(8,128)(2,1)S(1)}, u32[]{:S(2)}, u32[]{:S(2)}) collective-permute-start(bf16[64,512]{1,0:T(8,128)(2,1)} %get-tuple-element.6), channel_id=1, source_target_pairs={{1,0},{2,1},{3,2},{4,3},{5,4},{6,5},{7,6},{8,7},{9,8},{10,9},{11,1... | collective-permute-start | bytes 196616 | tf_op jit(solution)/shard_map/ppermute | solution.py:313
  29.0 22.5 %collective-permute-start = (bf16[64,512]{1,0:T(8,128)(2,1)S(1)}, bf16[64,512]{1,0:T(8,128)(2,1)S(1)}, u32[]{:S(2)}, u32[]{:S(2)}) collective-permute-start(bf16[64,512]{1,0:T(8,128)(2,1)S(1)} %get-tuple-element.7), channel_id=1, source_target_pairs={{0,1},{1,2},{2,3},{3,4},{4,5},{5,6},{6,7},{7,8},{8,9},{9,10},{10,1... | collective-permute-start | bytes 196616 | tf_op jit(solution)/shard_map/ppermute | solution.py:312
  33.6 41.9 %copy-start.3 = (bf16[64,15,64]{2,0,1:T(8,128)(2,1)}, bf16[64,15,64]{2,0,1:T(8,128)(2,1)S(1)}, u32[]{:S(2)}) copy-start(bf16[64,15,64]{2,0,1:T(8,128)(2,1)S(1)} %copy.44) | copy-start | bytes 368644
  33.8 41.7 %copy-start.1 = (bf16[1024,192]{1,0:T(8,128)(2,1)}, bf16[1024,192]{1,0:T(8,128)(2,1)S(1)}, u32[]{:S(2)}) copy-start(bf16[1024,192]{1,0:T(8,128)(2,1)S(1)} %copy.38.band_ref) | copy-start | bytes 1179652
  54.1 1.0 %copy-start.5 = (bf16[16,64,512]{2,1,0:T(8,128)(2,1)}, bf16[16,64,512]{2,1,0:T(8,128)(2,1)S(1)}, u32[]{:S(2)}) copy-start(bf16[16,64,512]{2,1,0:T(8,128)(2,1)S(1)} %get-tuple-element.5) | copy-start | bytes 3145732
  55.1 29.5 %all-to-all-start.2 = ((bf16[16,64,512]{2,1,0:T(8,128)(2,1)}), bf16[16,64,512]{2,1,0:T(8,128)(2,1)}, u32[]{:S(2)}, u32[]{:S(2)}) async-start(bf16[16,64,512]{2,1,0:T(8,128)(2,1)} %copy-done.5), calls=%async_computation.2 | async-start | bytes 2097152 | tf_op jit(solution)/shard_map/all_to_all | solution.py:357
  59.3 25.3 %collective-permute-start.3 = (bf16[64,512]{1,0:T(8,128)(2,1)S(1)}, bf16[64,512]{1,0:T(8,128)(2,1)S(1)}, u32[]{:S(2)}, u32[]{:S(2)}) collective-permute-start(bf16[64,512]{1,0:T(8,128)(2,1)S(1)} %get-tuple-element.8), channel_id=1, source_target_pairs={{1,0},{2,1},{3,2},{4,3},{5,4},{6,5},{7,6},{8,7},{9,8},{10,9},{11,1... | collective-permute-start | bytes 196616 | tf_op jit(solution)/shard_map/ppermute | solution.py:313
  61.3 23.3 %collective-permute-start.2 = (bf16[64,512]{1,0:T(8,128)(2,1)S(1)}, bf16[64,512]{1,0:T(8,128)(2,1)S(1)}, u32[]{:S(2)}, u32[]{:S(2)}) collective-permute-start(bf16[64,512]{1,0:T(8,128)(2,1)S(1)} %get-tuple-element.9), channel_id=1, source_target_pairs={{0,1},{1,2},{2,3},{3,4},{4,5},{5,6},{6,7},{7,8},{8,9},{9,10},{10,1... | collective-permute-start | bytes 196616 | tf_op jit(solution)/shard_map/ppermute | solution.py:312
  75.5 1.0 %copy-start.2 = (bf16[1024,512]{1,0:T(8,128)(2,1)}, bf16[1024,512]{1,0:T(8,128)(2,1)S(1)}, u32[]{:S(2)}) copy-start(bf16[1024,512]{1,0:T(8,128)(2,1)S(1)} %shard_map.105.field_ref) | copy-start | bytes 3145732
  84.6 0.6 copy-start.12
  84.6 0.6 copy-start.13

commit v10 on v8

--- a/solution.py
+++ b/solution.py
@@ -191,31 +191,44 @@
 
 
 def hop1_kernel(
-    col_ref, ptr_ref, field_ref, lo_ref, hi_ref, arr_ref, band_ref, farw_ref, out_ref, acc, pad,
+    col_ref, ptr_ref, field_ref, lo_ref, hi_ref, arr_ref, band_ref, farw_ref, x_hbm, mix_ref,
+    out_ref, part_ref, acc, pad, xs, sems,
 ):
+    nrows, width = field_ref.shape
+    half = x_hbm.shape[1] // 2
+    x_copy = pltpu.make_async_copy(x_hbm.at[:, pl.ds(half, width)], xs, sems.at[0])
+    x_copy.start()
     accumulate(col_ref, ptr_ref, field_ref, lo_ref, hi_ref, arr_ref, band_ref, farw_ref, acc, pad)
-    nrows = field_ref.shape[0]
     out_ref[...] = acc[:nrows, :].astype(bf16)
-
-
-def hop2_kernel(
-    col_ref, ptr_ref, field_ref, lo_ref, hi_ref, arr_ref, band_ref, farw_ref,
-    x_ref, h_ref, mix_ref, out_ref, acc, pad,
-):
-    accumulate(col_ref, ptr_ref, field_ref, lo_ref, hi_ref, arr_ref, band_ref, farw_ref, acc, pad)
-    nrows, width = field_ref.shape
-    half = x_ref.shape[1] // 2
     cw = mix_ref.shape[1]
     per = CHUNK // cw
     mix = mix_ref[...]
-    m = [bd_inkernel(mix[i * cw : (i + 1) * cw], per) for i in range(3)]
+    m0 = bd_inkernel(mix[:cw], per)
+    m1 = bd_inkernel(mix[cw : 2 * cw], per)
+    x_copy.wait()
+    for j in range(width // CHUNK):
+        cols = slice(j * CHUNK, (j + 1) * CHUNK)
+        v = xs[:, cols].astype(f32)
+        v = v + jnp.dot(field_ref[:, cols], m0, preferred_element_type=f32)
+        v = v + jnp.dot(out_ref[:, cols], m1, preferred_element_type=f32)
+        part_ref[:, cols] = v
+
+
+def hop2_kernel(
+    col_ref, ptr_ref, field_ref, lo_ref, hi_ref, arr_ref, band_ref, farw_ref,
+    part_hbm, mix_ref, out_ref, acc, pad, ps, sems,
+):
+    nrows, width = field_ref.shape
+    p_copy = pltpu.make_async_copy(part_hbm, ps, sems.at[0])
+    p_copy.start()
+    accumulate(col_ref, ptr_ref, field_ref, lo_ref, hi_ref, arr_ref, band_ref, farw_ref, acc, pad)
+    cw = mix_ref.shape[1]
+    m2 = bd_inkernel(mix_ref[2 * cw :], CHUNK // cw)
+    p_copy.wait()
     for j in range(width // CHUNK):
         cols = slice(j * CHUNK, (j + 1) * CHUNK)
         two = acc[:nrows, cols].astype(bf16)
-        v = x_ref[:, half + j * CHUNK : half + (j + 1) * CHUNK].astype(f32)
-        v = v + jnp.dot(h_ref[:, cols], m[0], preferred_element_type=f32)
-        v = v + jnp.dot(field_ref[:, cols], m[1], preferred_element_type=f32)
-        v = v + jnp.dot(two, m[2], preferred_element_type=f32)
+        v = ps[:, cols] + jnp.dot(two, m2, preferred_element_type=f32)
         out_ref[:, cols] = v.astype(bf16)
 
 
@@ -225,6 +238,10 @@
 
 def smem():
     return pl.BlockSpec(memory_space=pltpu.SMEM)
+
+
+def hbm():
+    return pl.BlockSpec(memory_space=pltpu.HBM)
 
 
 BIG_VMEM = pltpu.CompilerParams(vmem_limit_bytes=48 * 1024 * 1024)
@@ -255,39 +272,45 @@
     )(far_col, far_ptr, requested, export_block, field, lo, hi, arrived, band, farw3)
 
 
-def hop1(far_col, far_ptr, field, lo, hi, arrived, band, farw3):
+def hop1(far_col, far_ptr, field, lo, hi, arrived, band, farw3, features, mix):
     nrows, width = field.shape
     return pl.pallas_call(
         hop1_kernel,
-        in_specs=[smem(), smem()] + [vmem()] * 6,
+        in_specs=[smem(), smem()] + [vmem()] * 6 + [hbm(), vmem()],
+        out_specs=[vmem(), vmem()],
+        out_shape=[
+            jax.ShapeDtypeStruct((nrows, width), bf16),
+            jax.ShapeDtypeStruct((nrows, width), f32),
+        ],
+        scratch_shapes=scratch(field)
+        + [pltpu.VMEM((nrows, width), bf16), pltpu.SemaphoreType.DMA((1,))],
+        compiler_params=pltpu.CompilerParams(),
+        cost_estimate=pl.CostEstimate(
+            flops=2 * BLK * BLK * width * (3 * nrows // BLK + farw3.shape[0])
+            + 2 * nrows * width * CHUNK * 2,
+            transcendentals=0,
+            bytes_accessed=2 * width * (nrows * 7 + arrived.shape[0] * BLK),
+        ),
+    )(far_col, far_ptr, field, lo, hi, arrived, band, farw3, features, mix)
+
+
+def hop2(far_col, far_ptr, field, lo, hi, arrived, band, farw3, part, mix):
+    nrows, width = field.shape
+    return pl.pallas_call(
+        hop2_kernel,
+        in_specs=[smem(), smem()] + [vmem()] * 6 + [hbm(), vmem()],
         out_specs=vmem(),
         out_shape=jax.ShapeDtypeStruct((nrows, width), bf16),
-        scratch_shapes=scratch(field),
-        compiler_params=BIG_VMEM,
-        cost_estimate=pl.CostEstimate(
-            flops=2 * BLK * BLK * width * (3 * nrows // BLK + farw3.shape[0]),
+        scratch_shapes=scratch(field)
+        + [pltpu.VMEM((nrows, width), f32), pltpu.SemaphoreType.DMA((1,))],
+        compiler_params=pltpu.CompilerParams(),
+        cost_estimate=pl.CostEstimate(
+            flops=2 * BLK * BLK * width * (3 * nrows // BLK + farw3.shape[0])
+            + 2 * nrows * width * CHUNK,
             transcendentals=0,
-            bytes_accessed=2 * width * (nrows * 2 + arrived.shape[0] * BLK),
-        ),
-    )(far_col, far_ptr, field, lo, hi, arrived, band, farw3)
-
-
-def hop2(far_col, far_ptr, field, lo, hi, arrived, band, farw3, features, hidden, mix):
-    nrows, width = field.shape
-    return pl.pallas_call(
-        hop2_kernel,
-        in_specs=[smem(), smem()] + [vmem()] * 9,
-        out_specs=vmem(),
-        out_shape=jax.ShapeDtypeStruct((nrows, width), bf16),
-        scratch_shapes=scratch(field),
-        compiler_params=BIG_VMEM,
-        cost_estimate=pl.CostEstimate(
-            flops=2 * BLK * BLK * width * (3 * nrows // BLK + farw3.shape[0])
-            + 2 * nrows * width * CHUNK * 3,
-            transcendentals=0,
-            bytes_accessed=2 * width * (nrows * 6 + arrived.shape[0] * BLK),
-        ),
-    )(far_col, far_ptr, field, lo, hi, arrived, band, farw3, features, hidden, mix)
+            bytes_accessed=2 * width * (nrows * 5 + arrived.shape[0] * BLK),
+        ),
+    )(far_col, far_ptr, field, lo, hi, arrived, band, farw3, part, mix)
 
 
 def halo(first, last):
@@ -316,23 +339,17 @@
 
     own_index = lax.axis_index("node")
     own_exports = lax.dynamic_slice_in_dim(export_block, own_index, 1, 0)[0].astype(jnp.int32)
-    columns = far_col[0].astype(jnp.int32)
-    sources = columns // EXPORT
-    pointers = far_ptr[0].astype(jnp.int32)
+    peer_count = far_cap + 1
+    info = jnp.concatenate([far_col[0], far_ptr[0, -1:]]).astype(jnp.int32)
+    info_all = lax.all_to_all(
+        jnp.broadcast_to(info[None, :], (peer_count, far_cap + 1)),
+        "node", split_axis=0, concat_axis=0, tiled=True,
+    )
     slot_ids = jnp.arange(far_cap, dtype=jnp.int32)
-    slot_rows = jnp.sum(
-        (pointers[1:, None] <= slot_ids[None, :]).astype(jnp.int32), axis=0
-    ).astype(jnp.int32)
-    slot_export = columns % EXPORT
-    in_use = slot_ids < pointers[-1]
-    peers = jnp.arange(far_col.shape[1] + 1, dtype=jnp.int32)
-    matches = (sources[None, :] == peers[:, None]) & in_use[None, :]
-    wanted = jnp.sum(jnp.where(matches, slot_export[None, :], 0), axis=1)
-    requested = lax.all_to_all(wanted[:, None], "node", split_axis=0, concat_axis=0, tiled=True)[
-        :, 0
-    ]
+    cols_all = info_all[:, :far_cap]
+    hits = (cols_all // EXPORT == own_index) & (slot_ids[None, :] < info_all[:, far_cap:])
+    requested = jnp.sum(jnp.where(hits, cols_all % EXPORT, 0), axis=1).astype(jnp.int32)
     send_rows = own_exports[requested].astype(jnp.int32)
-
     hidden = front_hidden(features, filter_gate_weight)
     blocks = node_rows // BLK
     width = hidden.shape[1]
@@ -349,10 +366,10 @@
     )
     arrived2 = exchange(send2)
     lo2, hi2 = halo(edge[0], edge[1])
-    hop_one = hop1(far_col, far_ptr, hidden, lo1, hi1, arrived1, band_weight, farw3)
-    residual = hop2(
-        far_col, far_ptr, hop_one, lo2, hi2, arrived2, band_weight, farw3, features, hidden, mix_weight
-    )
+    hop_one, part = hop1(
+        far_col, far_ptr, hidden, lo1, hi1, arrived1, band_weight, farw3, features, mix_weight
+    )
+    residual = hop2(far_col, far_ptr, hop_one, lo2, hi2, arrived2, band_weight, farw3, part, mix_weight)
     return residual, skip_out
 
 

time: 94.7 us -> 93 us (0.982)
  Pallas kernels: 19.8 us -> 23.6 us
  local copies, waits for them, and re-layouts: 13.2 us -> 10.2 us
  waiting for transfers between devices: 26.8 us -> 24.3 us
    pallas_call x2, Pallas kernels: 9.92 us -> 13.6 us  [the longest x1 7.13 us: hop1(): pl.pallas_call(hop1_kernel, in_specs=[smem(), smem()] + [vmem()] * 6 + [h...]
    unnamed x29 -> x39, local copies, waits for them, and re-layouts: 7.48 us -> 4.99 us
    ppermute x2, waiting for transfers between devices: 26.8 us -> 24.3 us  [halo(): hi = lax.ppermute(first, 'node', backward)]
    concatenate x0 -> x1, other arithmetic: none -> 1.37 us  [local(): info = jnp.concatenate([far_col[0], far_ptr[0, -1:]]).astype(jnp.int32)]
  transfers between devices with their start and end apart: 7 -> 7, of which waited for: 2 -> 2; matrix products, arithmetic and copies ran while one was open for 3% -> 3% of each run, Pallas kernels for 12% -> 16%
where the time goes in v10:
time: 93 us; the launch traced here: 92.2 us
  starting transfers between devices  30.2 us (32%)
  waiting for transfers between devices  24.3 us (26%)
  Pallas kernels  23.6 us (25%)
  local copies, waits for them, and re-layouts  10.2 us (11%)
  other arithmetic  2.93 us (3%)
    ppermute x2, waiting for transfers between devices, halo(): hi = lax.ppermute(first, 'node', backward)  24.3 us
    all_to_all x2, starting transfers between devices, exchange(): return lax.all_to_all(send, 'node', split_axis=0, concat_axis=0, tiled=True)  10.7 us
    ppermute x2, starting transfers between devices, halo(): lo = lax.ppermute(last, 'node', forward)  8.39 us
    pallas_call x1, Pallas kernels, hop1(): pl.pallas_call(hop1_kernel, in_specs=[smem(), smem()] + [vmem()] * 6 + [h...  7.13 us
    all_to_all x1, starting transfers between devices, local(): lax.all_to_all(jnp.broadcast_to(info[None, :], (peer_count, far_cap + 1))...  6.55 us
    pallas_call x1, Pallas kernels, hop2(): pl.pallas_call(hop2_kernel, in_specs=[smem(), smem()] + [vmem()] * 6 + [h...  6.46 us
    pallas_call x1, Pallas kernels, front_skip(): pl.pallas_call(skip_kernel, grid=(rows // tile,), in_specs=[pl.BlockSpec(...  5.33 us
    unnamed x39, local copies, waits for them, and re-layouts  4.99 us
  transfers between devices with their start and end apart: 7, of which 2 were waited for; matrix products, arithmetic and copies ran while one was open for 3% of the time, Pallas kernels for 16%

profile of v10, /device:TPU:15, one launch (start us, length us, event | category | flops | bytes accessed | tf_op | source)
XLA Modules:
  0.0 92.2 jit_solution(18095651092381140519)
XLA Ops:
  0.6 1.2 %slice.23 = s32[1,1]{1,0:T(1,128)} slice(s32[1,17]{1,0:T(1,128)} %ptr_ref.5), slice={[0:1], [16:17]} | slice | bytes 8 | tf_op jit(solution)/shard_map/slice | solution.py:343
  1.9 1.4 %pad_add_fusion = s32[16]{0:T(128)S(1)} fusion(s32[1]{0:T(128)} %bitcast.2, s32[15]{0:T(128)} %bitcast.21), kind=kLoop, calls=%fused_computation.22 | loop fusion | flops 16 | bytes 128 | tf_op jit(solution)/shard_map/concatenate | solution.py:343
  3.2 0.6 broadcast_in_dim.3
  3.8 6.6 %all-to-all-start = ((s32[16,1,16]{2,1,0:T(1,128)}), s32[16,1,16]{2,1,0:T(1,128)S(1)}, u32[]{:S(2)}, u32[]{:S(2)}) async-start(s32[16,1,16]{2,1,0:T(1,128)} %broadcast_in_dim.3), calls=%async_computation | async-start | bytes 16384 | tf_op jit(solution)/shard_map/all_to_all | solution.py:344
  10.4 0.7 constant_dynamic-slice_fusion
  11.2 0.6 fusion.7
  11.7 1.6 %copy-done.4 = bf16[1024,1024]{1,0:T(8,128)(2,1)S(1)} copy-done((bf16[1024,1024]{1,0:T(8,128)(2,1)S(1)}, bf16[1024,1024]{1,0:T(8,128)(2,1)}, u32[]{:S(2)}) %copy-start.4) | copy-done | bytes 2097176
  13.3 0.7 copy-done.11
  14.1 2.4 %shard_map.104.field_ref.h_ref = bf16[1024,512]{1,0:T(8,128)(2,1)S(1)} custom-call(bf16[1024,1024]{1,0:T(8,128)(2,1)S(1)} %copy-done.4, bf16[64,64]{1,0:T(8,128)(2,1)S(1)} %copy-done.11), custom_call_target="tpu_custom_call" | custom-call | flops 1073741824 | bytes 3145728 | tf_op jit(solution)/shard_map/pallas_call | solution.py:84
  16.5 0.0 copy-start
  16.5 0.0 all-to-all-done
  16.5 0.2 slice_reduce_fusion
  16.7 0.2 fusion.2.req_ref
  16.8 1.4 %fusion.5 = s32[16]{0:T(128)S(1)} fusion(s32[16]{0:T(128)S(1)} %fusion.2.req_ref, s32[]{:T(128)} %bitcast.6, s32[]{:T(128)} %bitcast.5), kind=kLoop, calls=%fused_computation.21 | loop fusion | flops 128 | bytes 136 | tf_op jit(solution)/shard_map/select_n | solution.py:361
  18.2 0.0 copy-start.17
  18.3 0.0 copy-start.13
  18.3 1.6 %gather_fusion = bf16[16,64,512]{2,1,0:T(8,128)(2,1)} fusion(bf16[16,64,512]{2,1,0:T(8,128)(2,1)S(1)} %bitcast.17, s32[1024]{0:T(1024)S(1)} %pad_clamp_fusion), kind=kCustom, calls=%fused_computation | custom fusion | bytes 2097216 | tf_op jit(solution)/shard_map/gather | solution.py:361
  19.9 6.1 %all-to-all-start.1 = ((bf16[16,64,512]{2,1,0:T(8,128)(2,1)}), bf16[16,64,512]{2,1,0:T(8,128)(2,1)S(1)}, u32[]{:S(2)}, u32[]{:S(2)}) async-start(bf16[16,64,512]{2,1,0:T(8,128)(2,1)} %gather_fusion), calls=%async_computation.1 | async-start | bytes 2097152 | tf_op jit(solution)/shard_map/all_to_all | solution.py:359
  26.0 2.3 %collective-permute-start.1 = (bf16[64,512]{1,0:T(8,128)(2,1)S(1)}, bf16[64,512]{1,0:T(8,128)(2,1)S(1)}, u32[]{:S(2)}, u32[]{:S(2)}) collective-permute-start(bf16[64,512]{1,0:T(8,128)(2,1)S(1)} %get-tuple-element.10), channel_id=1, source_target_pairs={{1,0},{2,1},{3,2},{4,3},{5,4},{6,5},{7,6},{8,7},{9,8},{10,9},{11,1... | collective-permute-start | bytes 196616 | tf_op jit(solution)/shard_map/ppermute | solution.py:321
  28.3 4.2 %collective-permute-start = (bf16[64,512]{1,0:T(8,128)(2,1)S(1)}, bf16[64,512]{1,0:T(8,128)(2,1)S(1)}, u32[]{:S(2)}, u32[]{:S(2)}) collective-permute-start(bf16[64,512]{1,0:T(8,128)(2,1)S(1)} %get-tuple-element.11), channel_id=1, source_target_pairs={{0,1},{1,2},{2,3},{3,4},{4,5},{5,6},{6,7},{7,8},{8,9},{9,10},{10,1... | collective-permute-start | bytes 196616 | tf_op jit(solution)/shard_map/ppermute | solution.py:320
  32.5 0.1 copy.34.exp_ref
  32.6 0.0 copy-done.13
  32.6 0.2 reshape.43
  32.8 0.1 copy.39
  32.9 0.2 copy.32.band_ref
  33.1 18.4 %collective-permute-done.1.hi_ref = bf16[64,512]{1,0:T(8,128)(2,1)S(1)} collective-permute-done((bf16[64,512]{1,0:T(8,128)(2,1)S(1)}, bf16[64,512]{1,0:T(8,128)(2,1)S(1)}, u32[]{:S(2)}, u32[]{:S(2)}) %collective-permute-start.1) | collective-permute-done | bytes 65568 | tf_op jit(solution)/shard_map/ppermute | solution.py:321
  51.6 0.0 collective-permute-done.lo_ref
  51.6 0.0 all-to-all-done.1.arr_ref
  51.6 0.0 copy-start.1
  51.6 0.0 copy-done.9
  51.6 0.0 copy-done.10
  51.6 0.0 copy-start.16
  51.6 0.0 copy-start.8
  51.6 2.3 %shard_map.106 = (bf16[16,64,512]{2,1,0:T(8,128)(2,1)S(1)}, bf16[2,64,512]{2,1,0:T(8,128)(2,1)S(1)}) custom-call(s32[1,15]{1,0:T(1,128)S(1)} %copy-done.9, s32[1,17]{1,0:T(1,128)S(1)} %copy-done.10, s32[16]{0:T(128)S(1)} %fusion.2.req_ref, s32[16,2]{1,0:T(8,128)S(1)} %copy.34.exp_ref, bf16[1024,512]{1,0:T(8,128)(2,1)S(1)} %shard_map.104.field_ref.h_ref, ...), custom_call_target="tpu_custom_call" | custom-call | flops 113246208 | bytes 3145728 | tf_op jit(solution)/shard_map/pallas_call | solution.py:257
  53.9 0.0 copy-start.5
  54.0 1.0 %copy-done.5 = bf16[16,64,512]{2,1,0:T(8,128)(2,1)} copy-done((bf16[16,64,512]{2,1,0:T(8,128)(2,1)}, bf16[16,64,512]{2,1,0:T(8,128)(2,1)S(1)}, u32[]{:S(2)}) %copy-start.5) | copy-done | bytes 1048600
  55.0 4.5 %all-to-all-start.2 = ((bf16[16,64,512]{2,1,0:T(8,128)(2,1)}), bf16[16,64,512]{2,1,0:T(8,128)(2,1)}, u32[]{:S(2)}, u32[]{:S(2)}) async-start(bf16[16,64,512]{2,1,0:T(8,128)(2,1)} %copy-done.5), calls=%async_computation.2 | async-start | bytes 2097152 | tf_op jit(solution)/shard_map/all_to_all | solution.py:359
  59.5 0.7 copy.33.mix_ref
  60.2 5.3 %shard_map.108 = bf16[1024,4096]{1,0:T(8,128)(2,1)} custom-call(bf16[1024,512]{1,0:T(8,128)(2,1)S(1)} %shard_map.104.field_ref.h_ref, bf16[32,256]{1,0:T(8,128)(2,1)S(1)} %copy-done.8), custom_call_target="tpu_custom_call" | custom-call | flops 2147483648 | bytes 9437184 | tf_op jit(solution)/shard_map/pallas_call | solution.py:110
  65.6 2.3 %collective-permute-start.3 = (bf16[64,512]{1,0:T(8,128)(2,1)S(1)}, bf16[64,512]{1,0:T(8,128)(2,1)S(1)}, u32[]{:S(2)}, u32[]{:S(2)}) collective-permute-start(bf16[64,512]{1,0:T(8,128)(2,1)S(1)} %get-tuple-element.12), channel_id=1, source_target_pairs={{1,0},{2,1},{3,2},{4,3},{5,4},{6,5},{7,6},{8,7},{9,8},{10,9},{11,1... | collective-permute-start | bytes 196616 | tf_op jit(solution)/shard_map/ppermute | solution.py:321
  67.8 4.2 %collective-permute-start.2 = (bf16[64,512]{1,0:T(8,128)(2,1)S(1)}, bf16[64,512]{1,0:T(8,128)(2,1)S(1)}, u32[]{:S(2)}, u32[]{:S(2)}) collective-permute-start(bf16[64,512]{1,0:T(8,128)(2,1)S(1)} %get-tuple-element.13), channel_id=1, source_target_pairs={{0,1},{1,2},{2,3},{3,4},{4,5},{5,6},{6,7},{7,8},{8,9},{9,10},{10,1... | collective-permute-start | bytes 196616 | tf_op jit(solution)/shard_map/ppermute | solution.py:320
  72.0 7.1 %shard_map.105 = (bf16[1024,512]{1,0:T(8,128)(2,1)}, f32[1024,512]{1,0:T(8,128)}) custom-call(s32[1,15]{1,0:T(1,128)} %col_ref.5, s32[1,17]{1,0:T(1,128)} %ptr_ref.5, bf16[1024,512]{1,0:T(8,128)(2,1)} %copy-done, bf16[64,512]{1,0:T(8,128)(2,1)} %copy-done.7, bf16[64,512]{1,0:T(8,128)(2,1)} %copy-done.6, bf16[16,64,512]{2,1,0:T(8,128)(2,1)} %copy-done.1, ...), custom_call_target="tpu_custom_call" | custom-call | flops 801112064 | bytes 8388608 | tf_op jit(solution)/shard_map/pallas_call | solution.py:277
  79.2 5.9 %collective-permute-done.3.hi_ref = bf16[64,512]{1,0:T(8,128)(2,1)S(1)} collective-permute-done((bf16[64,512]{1,0:T(8,128)(2,1)S(1)}, bf16[64,512]{1,0:T(8,128)(2,1)S(1)}, u32[]{:S(2)}, u32[]{:S(2)}) %collective-permute-start.3) | collective-permute-done | bytes 65568 | tf_op jit(solution)/shard_map/ppermute | solution.py:321
  85.1 0.0 collective-permute-done.2.lo_ref
  85.1 0.0 all-to-all-done.2.arr_ref
  85.1 0.6 copy-done.14
  85.7 0.0 copy-done.15
  85.7 6.5 %shard_map.107 = bf16[1024,512]{1,0:T(8,128)(2,1)} custom-call(s32[1,15]{1,0:T(1,128)} %col_ref.5, s32[1,17]{1,0:T(1,128)} %ptr_ref.5, bf16[1024,512]{1,0:T(8,128)(2,1)} %get-tuple-element.6.field_ref, bf16[64,512]{1,0:T(8,128)(2,1)} %copy-done.15, bf16[64,512]{1,0:T(8,128)(2,1)} %copy-done.14, bf16[16,64,512]{2,1,0:T(8,128)(2,1)} %all-to-all-done.2.arr_ref, ...), custom_call_target="tpu_custom_call" | custom-call | flops 532676608 | bytes 6291456 | tf_op jit(solution)/shard_map/pallas_call | solution.py:299
  (24 shorter events, 0.1 us)
Async XLA Ops:
  3.8 12.6 %all-to-all-start = ((s32[16,1,16]{2,1,0:T(1,128)}), s32[16,1,16]{2,1,0:T(1,128)S(1)}, u32[]{:S(2)}, u32[]{:S(2)}) async-start(s32[16,1,16]{2,1,0:T(1,128)} %broadcast_in_dim.3), calls=%async_computation | async-start | bytes 16384 | tf_op jit(solution)/shard_map/all_to_all | solution.py:344
  11.7 1.6 %copy-start.4 = (bf16[1024,1024]{1,0:T(8,128)(2,1)S(1)}, bf16[1024,1024]{1,0:T(8,128)(2,1)}, u32[]{:S(2)}) copy-start(bf16[1024,1024]{1,0:T(8,128)(2,1)} %x_hbm.1) | copy-start | bytes 6291460
  13.3 0.7 copy-start.11
  16.5 43.7 %copy-start = (bf16[1024,512]{1,0:T(8,128)(2,1)}, bf16[1024,512]{1,0:T(8,128)(2,1)S(1)}, u32[]{:S(2)}) copy-start(bf16[1024,512]{1,0:T(8,128)(2,1)S(1)} %shard_map.104.field_ref.h_ref) | copy-start | bytes 3145732
  18.2 14.3 %copy-start.17 = (s32[16,2]{0,1:T(2,128)S(1)}, s32[16,2]{0,1:T(2,128)}, u32[]{:S(2)}) copy-start(s32[16,2]{0,1:T(2,128)} %param.17) | copy-start | bytes 388
  18.3 14.3 %copy-start.13 = (bf16[64,960]{1,0:T(8,128)(2,1)S(1)}, bf16[64,960]{1,0:T(8,128)(2,1)}, u32[]{:S(2)}) copy-start(bf16[64,960]{1,0:T(8,128)(2,1)} %param.14) | copy-start | bytes 368644
  19.8 13.0 %copy-start.12 = (bf16[1024,192]{0,1:T(8,128)(2,1)S(1)}, bf16[1024,192]{0,1:T(8,128)(2,1)}, u32[]{:S(2)}) copy-start(bf16[1024,192]{0,1:T(8,128)(2,1)} %param.13) | copy-start | bytes 1179652
  19.8 31.7 %copy-start.9 = (s32[1,15]{1,0:T(1,128)S(1)}, s32[1,15]{1,0:T(1,128)}, u32[]{:S(2)}) copy-start(s32[1,15]{1,0:T(1,128)} %col_ref.5) | copy-start | bytes 184
  19.9 31.7 %copy-start.10 = (s32[1,17]{1,0:T(1,128)S(1)}, s32[1,17]{1,0:T(1,128)}, u32[]{:S(2)}) copy-start(s32[1,17]{1,0:T(1,128)} %ptr_ref.5) | copy-start | bytes 208
  19.9 31.7 %all-to-all-start.1 = ((bf16[16,64,512]{2,1,0:T(8,128)(2,1)}), bf16[16,64,512]{2,1,0:T(8,128)(2,1)S(1)}, u32[]{:S(2)}, u32[]{:S(2)}) async-start(bf16[16,64,512]{2,1,0:T(8,128)(2,1)} %gather_fusion), calls=%async_computation.1 | async-start | bytes 2097152 | tf_op jit(solution)/shard_map/all_to_all | solution.py:359
  26.0 25.5 %collective-permute-start.1 = (bf16[64,512]{1,0:T(8,128)(2,1)S(1)}, bf16[64,512]{1,0:T(8,128)(2,1)S(1)}, u32[]{:S(2)}, u32[]{:S(2)}) collective-permute-start(bf16[64,512]{1,0:T(8,128)(2,1)S(1)} %get-tuple-element.10), channel_id=1, source_target_pairs={{1,0},{2,1},{3,2},{4,3},{5,4},{6,5},{7,6},{8,7},{9,8},{10,9},{11,1... | collective-permute-start | bytes 196616 | tf_op jit(solution)/shard_map/ppermute | solution.py:321
  28.3 23.3 %collective-permute-start = (bf16[64,512]{1,0:T(8,128)(2,1)S(1)}, bf16[64,512]{1,0:T(8,128)(2,1)S(1)}, u32[]{:S(2)}, u32[]{:S(2)}) collective-permute-start(bf16[64,512]{1,0:T(8,128)(2,1)S(1)} %get-tuple-element.11), channel_id=1, source_target_pairs={{0,1},{1,2},{2,3},{3,4},{4,5},{5,6},{6,7},{7,8},{8,9},{9,10},{10,1... | collective-permute-start | bytes 196616 | tf_op jit(solution)/shard_map/ppermute | solution.py:320
  32.9 22.1 %copy-start.3 = (bf16[64,15,64]{2,0,1:T(8,128)(2,1)}, bf16[64,15,64]{2,0,1:T(8,128)(2,1)S(1)}, u32[]{:S(2)}) copy-start(bf16[64,15,64]{2,0,1:T(8,128)(2,1)S(1)} %copy.39) | copy-start | bytes 368644
  33.1 21.8 %copy-start.2 = (bf16[1024,192]{1,0:T(8,128)(2,1)}, bf16[1024,192]{1,0:T(8,128)(2,1)S(1)}, u32[]{:S(2)}) copy-start(bf16[1024,192]{1,0:T(8,128)(2,1)S(1)} %copy.32.band_ref) | copy-start | bytes 1179652
  51.6 3.4 %copy-start.6 = (bf16[64,512]{1,0:T(8,128)(2,1)}, bf16[64,512]{1,0:T(8,128)(2,1)S(1)}, u32[]{:S(2)}) copy-start(bf16[64,512]{1,0:T(8,128)(2,1)S(1)} %collective-permute-done.1.hi_ref) | copy-start | bytes 196612
  51.6 3.4 %copy-start.7 = (bf16[64,512]{1,0:T(8,128)(2,1)}, bf16[64,512]{1,0:T(8,128)(2,1)S(1)}, u32[]{:S(2)}) copy-start(bf16[64,512]{1,0:T(8,128)(2,1)S(1)} %collective-permute-done.lo_ref) | copy-start | bytes 196612
  51.6 3.4 %copy-start.1 = (bf16[16,64,512]{2,1,0:T(8,128)(2,1)}, bf16[16,64,512]{2,1,0:T(8,128)(2,1)S(1)}, u32[]{:S(2)}) copy-start(bf16[16,64,512]{2,1,0:T(8,128)(2,1)S(1)} %all-to-all-done.1.arr_ref) | copy-start | bytes 3145732
  51.6 7.9 %copy-start.16 = (bf16[96,32]{0,1:T(8,128)(2,1)S(1)}, bf16[96,32]{0,1:T(8,128)(2,1)}, u32[]{:S(2)}) copy-start(bf16[96,32]{0,1:T(8,128)(2,1)} %param.12) | copy-start | bytes 18436
  51.6 8.6 %copy-start.8 = (bf16[32,256]{1,0:T(8,128)(2,1)S(1)}, bf16[32,256]{1,0:T(8,128)(2,1)}, u32[]{:S(2)}) copy-start(bf16[32,256]{1,0:T(8,128)(2,1)} %sw_ref.1) | copy-start | bytes 49156
  53.9 1.0 %copy-start.5 = (bf16[16,64,512]{2,1,0:T(8,128)(2,1)}, bf16[16,64,512]{2,1,0:T(8,128)(2,1)S(1)}, u32[]{:S(2)}) copy-start(bf16[16,64,512]{2,1,0:T(8,128)(2,1)S(1)} %get-tuple-element.8) | copy-start | bytes 3145732
  55.0 30.1 %all-to-all-start.2 = ((bf16[16,64,512]{2,1,0:T(8,128)(2,1)}), bf16[16,64,512]{2,1,0:T(8,128)(2,1)}, u32[]{:S(2)}, u32[]{:S(2)}) async-start(bf16[16,64,512]{2,1,0:T(8,128)(2,1)} %copy-done.5), calls=%async_computation.2 | async-start | bytes 2097152 | tf_op jit(solution)/shard_map/all_to_all | solution.py:359
  65.6 19.5 %collective-permute-start.3 = (bf16[64,512]{1,0:T(8,128)(2,1)S(1)}, bf16[64,512]{1,0:T(8,128)(2,1)S(1)}, u32[]{:S(2)}, u32[]{:S(2)}) collective-permute-start(bf16[64,512]{1,0:T(8,128)(2,1)S(1)} %get-tuple-element.12), channel_id=1, source_target_pairs={{1,0},{2,1},{3,2},{4,3},{5,4},{6,5},{7,6},{8,7},{9,8},{10,9},{11,1... | collective-permute-start | bytes 196616 | tf_op jit(solution)/shard_map/ppermute | solution.py:321
  67.8 17.2 %collective-permute-start.2 = (bf16[64,512]{1,0:T(8,128)(2,1)S(1)}, bf16[64,512]{1,0:T(8,128)(2,1)S(1)}, u32[]{:S(2)}, u32[]{:S(2)}) collective-permute-start(bf16[64,512]{1,0:T(8,128)(2,1)S(1)} %get-tuple-element.13), channel_id=1, source_target_pairs={{0,1},{1,2},{2,3},{3,4},{4,5},{5,6},{6,7},{7,8},{8,9},{9,10},{10,1... | collective-permute-start | bytes 196616 | tf_op jit(solution)/shard_map/ppermute | solution.py:320
  85.1 0.6 copy-start.14
  85.1 0.6 copy-start.15

commit v11 on v10

--- a/solution.py
+++ b/solution.py
@@ -166,14 +166,24 @@
 
 def early_kernel(
     col_ref, ptr_ref, req_ref, exp_ref, field_ref, lo_ref, hi_ref, arr_ref, band_ref, farw_ref,
-    send_ref, edge_ref, pad, blk,
+    send_ref, edge_ref, blk,
 ):
     nblk = field_ref.shape[0] // BLK
     own = lax.axis_index("node")
-    fill_pad(field_ref, lo_ref, hi_ref, pad)
     targets = [exp_ref[own, 0], exp_ref[own, 1], 0, nblk - 1]
     for i, t in enumerate(targets):
-        v = band_block(band_ref, pad, t)
+        pieces = []
+        for s in range(3):
+            b = jnp.clip(t - 1 + s, 0, nblk - 1)
+            v = field_ref[pl.ds(pl.multiple_of(b * BLK, BLK), BLK), :]
+            if s == 0:
+                v = jnp.where(t == 0, lo_ref[...], v)
+            if s == 2:
+                v = jnp.where(t == nblk - 1, hi_ref[...], v)
+            pieces.append(v)
+        win = jnp.concatenate(pieces, axis=0)
+        start = pl.multiple_of(t * BLK, BLK)
+        v = jnp.dot(band_ref[pl.ds(start, BLK), :], win, preferred_element_type=f32)
 
         def slot(k, acc):
             return acc + slot_product(col_ref, farw_ref, arr_ref, k)
@@ -192,14 +202,19 @@
 
 def hop1_kernel(
     col_ref, ptr_ref, field_ref, lo_ref, hi_ref, arr_ref, band_ref, farw_ref, x_hbm, mix_ref,
-    out_ref, part_ref, acc, pad, xs, sems,
+    lo2_ref, hi2_ref, out_ref, part_ref, acc2_ref, acc, pad, xs, sems,
 ):
     nrows, width = field_ref.shape
+    nblk = nrows // BLK
     half = x_hbm.shape[1] // 2
     x_copy = pltpu.make_async_copy(x_hbm.at[:, pl.ds(half, width)], xs, sems.at[0])
     x_copy.start()
     accumulate(col_ref, ptr_ref, field_ref, lo_ref, hi_ref, arr_ref, band_ref, farw_ref, acc, pad)
     out_ref[...] = acc[:nrows, :].astype(bf16)
+    fill_pad(out_ref, lo2_ref, hi2_ref, pad)
+    for r in range(nblk):
+        acc2_ref[r * BLK : (r + 1) * BLK, :] = band_block(band_ref, pad, r)
+    acc2_ref[nblk * BLK :, :] = jnp.zeros((BLK, width), f32)
     cw = mix_ref.shape[1]
     per = CHUNK // cw
     mix = mix_ref[...]
@@ -214,20 +229,32 @@
         part_ref[:, cols] = v
 
 
-def hop2_kernel(
-    col_ref, ptr_ref, field_ref, lo_ref, hi_ref, arr_ref, band_ref, farw_ref,
-    part_hbm, mix_ref, out_ref, acc, pad, ps, sems,
-):
-    nrows, width = field_ref.shape
-    p_copy = pltpu.make_async_copy(part_hbm, ps, sems.at[0])
+def hop2_kernel(col_ref, ptr_ref, arr_ref, farw_ref, acc2_hbm, part_hbm, mix_ref, out_ref, far, a2, ps, sems):
+    nrows, width = out_ref.shape
+    a_copy = pltpu.make_async_copy(acc2_hbm, a2, sems.at[0])
+    p_copy = pltpu.make_async_copy(part_hbm, ps, sems.at[1])
+    a_copy.start()
     p_copy.start()
-    accumulate(col_ref, ptr_ref, field_ref, lo_ref, hi_ref, arr_ref, band_ref, farw_ref, acc, pad)
+    far[...] = jnp.zeros(far.shape, f32)
+    far_cap = farw_ref.shape[0]
+    nptr = ptr_ref.shape[1]
+
+    def slot(k, carry):
+        row = 0
+        for r in range(1, nptr):
+            row = row + jnp.where(ptr_ref[0, r] <= k, 1, 0)
+        start = pl.multiple_of(row * BLK, BLK)
+        far[pl.ds(start, BLK), :] += slot_product(col_ref, farw_ref, arr_ref, k)
+        return carry
+
+    lax.fori_loop(0, far_cap, slot, 0)
     cw = mix_ref.shape[1]
     m2 = bd_inkernel(mix_ref[2 * cw :], CHUNK // cw)
+    a_copy.wait()
     p_copy.wait()
     for j in range(width // CHUNK):
         cols = slice(j * CHUNK, (j + 1) * CHUNK)
-        two = acc[:nrows, cols].astype(bf16)
+        two = (a2[:nrows, cols] + far[:nrows, cols]).astype(bf16)
         v = ps[:, cols] + jnp.dot(two, m2, preferred_element_type=f32)
         out_ref[:, cols] = v.astype(bf16)
 
@@ -262,7 +289,7 @@
             jax.ShapeDtypeStruct(arrived.shape, bf16),
             jax.ShapeDtypeStruct((2, BLK, width), bf16),
         ],
-        scratch_shapes=[pltpu.VMEM((nrows + 2 * BLK, width), bf16), pltpu.VMEM((4, BLK, width), bf16)],
+        scratch_shapes=[pltpu.VMEM((4, BLK, width), bf16)],
         compiler_params=BIG_VMEM,
         cost_estimate=pl.CostEstimate(
             flops=2 * BLK * BLK * width * (12 + farw3.shape[0]),
@@ -272,45 +299,49 @@
     )(far_col, far_ptr, requested, export_block, field, lo, hi, arrived, band, farw3)
 
 
-def hop1(far_col, far_ptr, field, lo, hi, arrived, band, farw3, features, mix):
+def hop1(far_col, far_ptr, field, lo, hi, arrived, band, farw3, features, mix, lo2, hi2):
     nrows, width = field.shape
     return pl.pallas_call(
         hop1_kernel,
-        in_specs=[smem(), smem()] + [vmem()] * 6 + [hbm(), vmem()],
-        out_specs=[vmem(), vmem()],
+        in_specs=[smem(), smem()] + [vmem()] * 6 + [hbm(), vmem(), vmem(), vmem()],
+        out_specs=[vmem(), vmem(), vmem()],
         out_shape=[
             jax.ShapeDtypeStruct((nrows, width), bf16),
             jax.ShapeDtypeStruct((nrows, width), f32),
+            jax.ShapeDtypeStruct((nrows + BLK, width), f32),
         ],
         scratch_shapes=scratch(field)
         + [pltpu.VMEM((nrows, width), bf16), pltpu.SemaphoreType.DMA((1,))],
         compiler_params=pltpu.CompilerParams(),
         cost_estimate=pl.CostEstimate(
-            flops=2 * BLK * BLK * width * (3 * nrows // BLK + farw3.shape[0])
+            flops=2 * BLK * BLK * width * (6 * nrows // BLK + farw3.shape[0])
             + 2 * nrows * width * CHUNK * 2,
             transcendentals=0,
-            bytes_accessed=2 * width * (nrows * 7 + arrived.shape[0] * BLK),
+            bytes_accessed=2 * width * (nrows * 9 + arrived.shape[0] * BLK),
         ),
-    )(far_col, far_ptr, field, lo, hi, arrived, band, farw3, features, mix)
-
-
-def hop2(far_col, far_ptr, field, lo, hi, arrived, band, farw3, part, mix):
-    nrows, width = field.shape
+    )(far_col, far_ptr, field, lo, hi, arrived, band, farw3, features, mix, lo2, hi2)
+
+
+def hop2(far_col, far_ptr, arrived, farw3, acc2, part, mix):
+    nrows, width = part.shape
     return pl.pallas_call(
         hop2_kernel,
-        in_specs=[smem(), smem()] + [vmem()] * 6 + [hbm(), vmem()],
+        in_specs=[smem(), smem(), vmem(), vmem(), hbm(), hbm(), vmem()],
         out_specs=vmem(),
         out_shape=jax.ShapeDtypeStruct((nrows, width), bf16),
-        scratch_shapes=scratch(field)
-        + [pltpu.VMEM((nrows, width), f32), pltpu.SemaphoreType.DMA((1,))],
+        scratch_shapes=[
+            pltpu.VMEM((nrows + BLK, width), f32),
+            pltpu.VMEM((nrows + BLK, width), f32),
+            pltpu.VMEM((nrows, width), f32),
+            pltpu.SemaphoreType.DMA((2,)),
+        ],
         compiler_params=pltpu.CompilerParams(),
         cost_estimate=pl.CostEstimate(
-            flops=2 * BLK * BLK * width * (3 * nrows // BLK + farw3.shape[0])
-            + 2 * nrows * width * CHUNK,
+            flops=2 * BLK * BLK * width * farw3.shape[0] + 2 * nrows * width * CHUNK,
             transcendentals=0,
-            bytes_accessed=2 * width * (nrows * 5 + arrived.shape[0] * BLK),
+            bytes_accessed=4 * width * nrows * 3,
         ),
-    )(far_col, far_ptr, field, lo, hi, arrived, band, farw3, part, mix)
+    )(far_col, far_ptr, arrived, farw3, acc2, part, mix)
 
 
 def halo(first, last):
@@ -366,10 +397,11 @@
     )
     arrived2 = exchange(send2)
     lo2, hi2 = halo(edge[0], edge[1])
-    hop_one, part = hop1(
-        far_col, far_ptr, hidden, lo1, hi1, arrived1, band_weight, farw3, features, mix_weight
-    )
-    residual = hop2(far_col, far_ptr, hop_one, lo2, hi2, arrived2, band_weight, farw3, part, mix_weight)
+    hop_one, part, acc2 = hop1(
+        far_col, far_ptr, hidden, lo1, hi1, arrived1, band_weight, farw3, features, mix_weight,
+        lo2, hi2,
+    )
+    residual = hop2(far_col, far_ptr, arrived2, farw3, acc2, part, mix_weight)
     return residual, skip_out
 
 

time: 93 us -> 101 us (1.086)
  waiting for transfers between devices: 24.3 us -> 30.8 us
  local copies, waits for them, and re-layouts: 10.2 us -> 11.4 us
    ppermute x2, waiting for transfers between devices: 24.3 us -> 30.8 us  [halo(): hi = lax.ppermute(first, 'node', backward)]
    pallas_call x1, Pallas kernels: 7.13 us -> 8.4 us  [hop1(): pl.pallas_call(hop1_kernel, in_specs=[smem(), smem()] + [vmem()] * 6 + [h...]
where the time goes in v11:
time: 101 us; the launch traced here: 100 us
  waiting for transfers between devices  30.8 us (30%)
  starting transfers between devices  30 us (30%)
  Pallas kernels  23.9 us (24%)
  local copies, waits for them, and re-layouts  11.4 us (11%)
  other arithmetic  2.89 us (3%)
    ppermute x2, waiting for transfers between devices, halo(): hi = lax.ppermute(first, 'node', backward)  30.8 us
    all_to_all x2, starting transfers between devices, exchange(): return lax.all_to_all(send, 'node', split_axis=0, concat_axis=0, tiled=True)  10.6 us
    pallas_call x1, Pallas kernels, hop1(): pl.pallas_call(hop1_kernel, in_specs=[smem(), smem()] + [vmem()] * 6 + [h...  8.4 us
    ppermute x2, starting transfers between devices, halo(): lo = lax.ppermute(last, 'node', forward)  8.38 us
    all_to_all x1, starting transfers between devices, local(): lax.all_to_all(jnp.broadcast_to(info[None, :], (peer_count, far_cap + 1))...  6.55 us
    unnamed x39, local copies, waits for them, and re-layouts  5.57 us
    pallas_call x1, Pallas kernels, hop2(): pl.pallas_call(hop2_kernel, in_specs=[smem(), smem(), vmem(), vmem(), hbm...  5.49 us
    pallas_call x1, Pallas kernels, front_skip(): pl.pallas_call(skip_kernel, grid=(rows // tile,), in_specs=[pl.BlockSpec(...  5.37 us
  transfers between devices with their start and end apart: 7, of which 2 were waited for; matrix products, arithmetic and copies ran while one was open for 3% of the time, Pallas kernels for 16%

profile of v11, /device:TPU:15, one launch (start us, length us, event | category | flops | bytes accessed | tf_op | source)
XLA Modules:
  0.0 100.0 jit_solution(5349912261508464966)
XLA Ops:
  0.6 1.2 %slice.21 = s32[1,1]{1,0:T(1,128)} slice(s32[1,17]{1,0:T(1,128)} %ptr_ref.5), slice={[0:1], [16:17]} | slice | bytes 8 | tf_op jit(solution)/shard_map/slice | solution.py:374
  1.9 1.4 %pad_add_fusion = s32[16]{0:T(128)S(1)} fusion(s32[1]{0:T(128)} %bitcast.1, s32[15]{0:T(128)} %bitcast.21), kind=kLoop, calls=%fused_computation.22 | loop fusion | flops 16 | bytes 128 | tf_op jit(solution)/shard_map/concatenate | solution.py:374
  3.2 0.6 broadcast_in_dim.3
  3.8 6.6 %all-to-all-start = ((s32[16,1,16]{2,1,0:T(1,128)}), s32[16,1,16]{2,1,0:T(1,128)S(1)}, u32[]{:S(2)}, u32[]{:S(2)}) async-start(s32[16,1,16]{2,1,0:T(1,128)} %broadcast_in_dim.3), calls=%async_computation | async-start | bytes 16384 | tf_op jit(solution)/shard_map/all_to_all | solution.py:375
  10.4 0.7 constant_dynamic-slice_fusion
  11.2 0.6 fusion.7
  11.7 1.6 %copy-done.4 = bf16[1024,1024]{1,0:T(8,128)(2,1)S(1)} copy-done((bf16[1024,1024]{1,0:T(8,128)(2,1)S(1)}, bf16[1024,1024]{1,0:T(8,128)(2,1)}, u32[]{:S(2)}) %copy-start.4) | copy-done | bytes 2097176
  13.3 0.7 copy-done.11
  14.0 2.4 %shard_map.104.field_ref.h_ref = bf16[1024,512]{1,0:T(8,128)(2,1)S(1)} custom-call(bf16[1024,1024]{1,0:T(8,128)(2,1)S(1)} %copy-done.4, bf16[64,64]{1,0:T(8,128)(2,1)S(1)} %copy-done.11), custom_call_target="tpu_custom_call" | custom-call | flops 1073741824 | bytes 3145728 | tf_op jit(solution)/shard_map/pallas_call | solution.py:84
  16.5 0.0 all-to-all-done
  16.5 0.2 slice_reduce_fusion
  16.6 0.2 fusion.2.req_ref
  16.8 1.3 %fusion.5 = s32[16]{0:T(128)S(1)} fusion(s32[16]{0:T(128)S(1)} %fusion.2.req_ref, s32[]{:T(128)} %bitcast.6, s32[]{:T(128)} %bitcast.5), kind=kLoop, calls=%fused_computation.21 | loop fusion | flops 128 | bytes 136 | tf_op jit(solution)/shard_map/select_n | solution.py:392
  18.2 0.0 copy-start.17
  18.2 0.0 copy-start.13
  18.2 0.0 copy-start.12
  18.2 1.6 %gather_fusion = bf16[16,64,512]{2,1,0:T(8,128)(2,1)} fusion(bf16[16,64,512]{2,1,0:T(8,128)(2,1)S(1)} %bitcast.17, s32[1024]{0:T(1024)S(1)} %pad_clamp_fusion), kind=kCustom, calls=%fused_computation | custom fusion | bytes 2097216 | tf_op jit(solution)/shard_map/gather | solution.py:392
  19.8 6.1 %all-to-all-start.1 = ((bf16[16,64,512]{2,1,0:T(8,128)(2,1)}), bf16[16,64,512]{2,1,0:T(8,128)(2,1)S(1)}, u32[]{:S(2)}, u32[]{:S(2)}) async-start(bf16[16,64,512]{2,1,0:T(8,128)(2,1)} %gather_fusion), calls=%async_computation.1 | async-start | bytes 2097152 | tf_op jit(solution)/shard_map/all_to_all | solution.py:390
  26.0 0.6 fusion.6
  26.6 2.3 %collective-permute-start.1 = (bf16[64,512]{1,0:T(8,128)(2,1)}, bf16[64,512]{1,0:T(8,128)(2,1)S(1)}, u32[]{:S(2)}, u32[]{:S(2)}) collective-permute-start(bf16[64,512]{1,0:T(8,128)(2,1)} %get-tuple-element.10), channel_id=1, source_target_pairs={{1,0},{2,1},{3,2},{4,3},{5,4},{6,5},{7,6},{8,7},{9,8},{10,9},{11,1... | collective-permute-start | bytes 196616 | tf_op jit(solution)/shard_map/ppermute | solution.py:352
  28.9 4.2 %collective-permute-start = (bf16[64,512]{1,0:T(8,128)(2,1)S(1)}, bf16[64,512]{1,0:T(8,128)(2,1)S(1)}, u32[]{:S(2)}, u32[]{:S(2)}) collective-permute-start(bf16[64,512]{1,0:T(8,128)(2,1)S(1)} %get-tuple-element.11), channel_id=1, source_target_pairs={{0,1},{1,2},{2,3},{3,4},{4,5},{5,6},{6,7},{7,8},{8,9},{9,10},{10,1... | collective-permute-start | bytes 196616 | tf_op jit(solution)/shard_map/ppermute | solution.py:351
  33.1 0.0 copy-done.17
  33.1 0.1 copy.29.exp_ref
  33.2 0.2 reshape.43
  33.4 0.1 copy.35
  33.5 0.2 copy.30.band_ref
  33.7 17.8 %collective-permute-done.1.hi_ref = bf16[64,512]{1,0:T(8,128)(2,1)S(1)} collective-permute-done((bf16[64,512]{1,0:T(8,128)(2,1)}, bf16[64,512]{1,0:T(8,128)(2,1)S(1)}, u32[]{:S(2)}, u32[]{:S(2)}) %collective-permute-start.1) | collective-permute-done | bytes 65568 | tf_op jit(solution)/shard_map/ppermute | solution.py:352
  51.5 0.0 collective-permute-done.lo_ref
  51.5 0.0 all-to-all-done.1.arr_ref
  51.6 0.0 copy-start.8
  51.6 2.3 %shard_map.105 = (bf16[16,64,512]{2,1,0:T(8,128)(2,1)S(1)}, bf16[2,64,512]{2,1,0:T(8,128)(2,1)S(1)}) custom-call(s32[1,15]{1,0:T(1,128)S(1)} %copy-done.9, s32[1,17]{1,0:T(1,128)S(1)} %copy-done.10, s32[16]{0:T(128)S(1)} %fusion.2.req_ref, s32[16,2]{1,0:T(8,128)S(1)} %copy.29.exp_ref, bf16[1024,512]{1,0:T(8,128)(2,1)S(1)} %shard_map.104.field_ref.h_ref, ...), custom_call_target="tpu_custom_call" | custom-call | flops 113246208 | bytes 3145728 | tf_op jit(solution)/shard_map/pallas_call | solution.py:284
  53.8 0.0 copy-start.5
  53.9 1.0 copy-done.5
  54.8 0.0 copy-done.3
  54.8 0.0 copy-done.6
  54.8 4.4 %all-to-all-start.2 = ((bf16[16,64,512]{2,1,0:T(8,128)(2,1)}), bf16[16,64,512]{2,1,0:T(8,128)(2,1)}, u32[]{:S(2)}, u32[]{:S(2)}) async-start(bf16[16,64,512]{2,1,0:T(8,128)(2,1)} %copy-done.5), calls=%async_computation.2 | async-start | bytes 2097152 | tf_op jit(solution)/shard_map/all_to_all | solution.py:390
  59.3 2.3 %collective-permute-start.3 = (bf16[64,512]{1,0:T(8,128)(2,1)S(1)}, bf16[64,512]{1,0:T(8,128)(2,1)S(1)}, u32[]{:S(2)}, u32[]{:S(2)}) collective-permute-start(bf16[64,512]{1,0:T(8,128)(2,1)S(1)} %get-tuple-element.12), channel_id=1, source_target_pairs={{1,0},{2,1},{3,2},{4,3},{5,4},{6,5},{7,6},{8,7},{9,8},{10,9},{11,1... | collective-permute-start | bytes 196616 | tf_op jit(solution)/shard_map/ppermute | solution.py:352
  61.6 0.0 copy-start.16
  61.6 4.2 %collective-permute-start.2 = (bf16[64,512]{1,0:T(8,128)(2,1)S(1)}, bf16[64,512]{1,0:T(8,128)(2,1)S(1)}, u32[]{:S(2)}, u32[]{:S(2)}) collective-permute-start(bf16[64,512]{1,0:T(8,128)(2,1)S(1)} %get-tuple-element.13), channel_id=1, source_target_pairs={{0,1},{1,2},{2,3},{3,4},{4,5},{5,6},{6,7},{7,8},{8,9},{9,10},{10,1... | collective-permute-start | bytes 196616 | tf_op jit(solution)/shard_map/ppermute | solution.py:351
  65.8 5.4 %shard_map.108 = bf16[1024,4096]{1,0:T(8,128)(2,1)} custom-call(bf16[1024,512]{1,0:T(8,128)(2,1)S(1)} %shard_map.104.field_ref.h_ref, bf16[32,256]{1,0:T(8,128)(2,1)S(1)} %copy-done.8), custom_call_target="tpu_custom_call" | custom-call | flops 2147483648 | bytes 9437184 | tf_op jit(solution)/shard_map/pallas_call | solution.py:110
  71.2 0.7 copy.32.mix_ref
  71.9 13.0 %collective-permute-done.3.hi2_ref = bf16[64,512]{1,0:T(8,128)(2,1)S(1)} collective-permute-done((bf16[64,512]{1,0:T(8,128)(2,1)S(1)}, bf16[64,512]{1,0:T(8,128)(2,1)S(1)}, u32[]{:S(2)}, u32[]{:S(2)}) %collective-permute-start.3) | collective-permute-done | bytes 65568 | tf_op jit(solution)/shard_map/ppermute | solution.py:352
  84.8 0.0 collective-permute-done.2.lo2_ref
  84.8 0.6 copy-done.14
  85.5 0.6 copy-done.15
  86.1 8.4 %shard_map.106 = (bf16[1024,512]{1,0:T(8,128)(2,1)}, f32[1024,512]{1,0:T(8,128)}, f32[1088,512]{1,0:T(8,128)}) custom-call(s32[1,15]{1,0:T(1,128)} %col_ref.5, s32[1,17]{1,0:T(1,128)} %ptr_ref.5, bf16[1024,512]{1,0:T(8,128)(2,1)} %copy-done, bf16[64,512]{1,0:T(8,128)(2,1)} %copy-done.7, bf16[64,512]{1,0:T(8,128)(2,1)} %copy-done.6, ...), custom_call_target="tpu_custom_call" | custom-call | flops 1002438656 | bytes 10485760 | tf_op jit(solution)/shard_map/pallas_call | solution.py:304
  94.5 0.0 all-to-all-done.2.arr_ref
  94.5 5.5 %shard_map.107 = bf16[1024,512]{1,0:T(8,128)(2,1)} custom-call(s32[1,15]{1,0:T(1,128)} %col_ref.5, s32[1,17]{1,0:T(1,128)} %ptr_ref.5, bf16[16,64,512]{2,1,0:T(8,128)(2,1)} %all-to-all-done.2.arr_ref, bf16[15,64,64]{2,1,0:T(8,128)(2,1)} %bitcast.20, f32[1088,512]{1,0:T(8,128)} %get-tuple-element.8.acc2_hbm, f32[1024,512]{1,0:T(8,128)} %get-tuple-element.9.part_hbm, ...), custom_call_target="tpu_custom_call" | custom-call | flops 331350016 | bytes 6291456 | tf_op jit(solution)/shard_map/pallas_call | solution.py:327
  (24 shorter events, 0.1 us)
Async XLA Ops:
  3.8 12.6 %all-to-all-start = ((s32[16,1,16]{2,1,0:T(1,128)}), s32[16,1,16]{2,1,0:T(1,128)S(1)}, u32[]{:S(2)}, u32[]{:S(2)}) async-start(s32[16,1,16]{2,1,0:T(1,128)} %broadcast_in_dim.3), calls=%async_computation | async-start | bytes 16384 | tf_op jit(solution)/shard_map/all_to_all | solution.py:375
  11.7 1.6 %copy-start.4 = (bf16[1024,1024]{1,0:T(8,128)(2,1)S(1)}, bf16[1024,1024]{1,0:T(8,128)(2,1)}, u32[]{:S(2)}) copy-start(bf16[1024,1024]{1,0:T(8,128)(2,1)} %x_hbm.1) | copy-start | bytes 6291460
  13.3 0.7 copy-start.11
  16.4 49.3 %copy-start = (bf16[1024,512]{1,0:T(8,128)(2,1)}, bf16[1024,512]{1,0:T(8,128)(2,1)S(1)}, u32[]{:S(2)}) copy-start(bf16[1024,512]{1,0:T(8,128)(2,1)S(1)} %shard_map.104.field_ref.h_ref) | copy-start | bytes 3145732
  18.2 14.9 %copy-start.17 = (s32[16,2]{0,1:T(2,128)S(1)}, s32[16,2]{0,1:T(2,128)}, u32[]{:S(2)}) copy-start(s32[16,2]{0,1:T(2,128)} %param.17) | copy-start | bytes 388
  18.2 15.0 %copy-start.13 = (bf16[64,960]{1,0:T(8,128)(2,1)S(1)}, bf16[64,960]{1,0:T(8,128)(2,1)}, u32[]{:S(2)}) copy-start(bf16[64,960]{1,0:T(8,128)(2,1)} %param.14) | copy-start | bytes 368644
  18.2 15.2 %copy-start.12 = (bf16[1024,192]{0,1:T(8,128)(2,1)S(1)}, bf16[1024,192]{0,1:T(8,128)(2,1)}, u32[]{:S(2)}) copy-start(bf16[1024,192]{0,1:T(8,128)(2,1)} %param.13) | copy-start | bytes 1179652
  19.8 31.7 %copy-start.9 = (s32[1,15]{1,0:T(1,128)S(1)}, s32[1,15]{1,0:T(1,128)}, u32[]{:S(2)}) copy-start(s32[1,15]{1,0:T(1,128)} %col_ref.5) | copy-start | bytes 184
  19.8 31.7 %copy-start.10 = (s32[1,17]{1,0:T(1,128)S(1)}, s32[1,17]{1,0:T(1,128)}, u32[]{:S(2)}) copy-start(s32[1,17]{1,0:T(1,128)} %ptr_ref.5) | copy-start | bytes 208
  19.8 31.7 %all-to-all-start.1 = ((bf16[16,64,512]{2,1,0:T(8,128)(2,1)}), bf16[16,64,512]{2,1,0:T(8,128)(2,1)S(1)}, u32[]{:S(2)}, u32[]{:S(2)}) async-start(bf16[16,64,512]{2,1,0:T(8,128)(2,1)} %gather_fusion), calls=%async_computation.1 | async-start | bytes 2097152 | tf_op jit(solution)/shard_map/all_to_all | solution.py:390
  26.6 24.9 %collective-permute-start.1 = (bf16[64,512]{1,0:T(8,128)(2,1)}, bf16[64,512]{1,0:T(8,128)(2,1)S(1)}, u32[]{:S(2)}, u32[]{:S(2)}) collective-permute-start(bf16[64,512]{1,0:T(8,128)(2,1)} %get-tuple-element.10), channel_id=1, source_target_pairs={{1,0},{2,1},{3,2},{4,3},{5,4},{6,5},{7,6},{8,7},{9,8},{10,9},{11,1... | collective-permute-start | bytes 196616 | tf_op jit(solution)/shard_map/ppermute | solution.py:352
  28.9 22.7 %collective-permute-start = (bf16[64,512]{1,0:T(8,128)(2,1)S(1)}, bf16[64,512]{1,0:T(8,128)(2,1)S(1)}, u32[]{:S(2)}, u32[]{:S(2)}) collective-permute-start(bf16[64,512]{1,0:T(8,128)(2,1)S(1)} %get-tuple-element.11), channel_id=1, source_target_pairs={{0,1},{1,2},{2,3},{3,4},{4,5},{5,6},{6,7},{7,8},{8,9},{9,10},{10,1... | collective-permute-start | bytes 196616 | tf_op jit(solution)/shard_map/ppermute | solution.py:351
  33.5 21.4 %copy-start.3 = (bf16[64,15,64]{2,0,1:T(8,128)(2,1)}, bf16[64,15,64]{2,0,1:T(8,128)(2,1)S(1)}, u32[]{:S(2)}) copy-start(bf16[64,15,64]{2,0,1:T(8,128)(2,1)S(1)} %copy.35) | copy-start | bytes 368644
  33.7 21.2 %copy-start.2 = (bf16[1024,192]{1,0:T(8,128)(2,1)}, bf16[1024,192]{1,0:T(8,128)(2,1)S(1)}, u32[]{:S(2)}) copy-start(bf16[1024,192]{1,0:T(8,128)(2,1)S(1)} %copy.30.band_ref) | copy-start | bytes 1179652
  51.5 3.3 %copy-start.6 = (bf16[64,512]{1,0:T(8,128)(2,1)}, bf16[64,512]{1,0:T(8,128)(2,1)S(1)}, u32[]{:S(2)}) copy-start(bf16[64,512]{1,0:T(8,128)(2,1)S(1)} %collective-permute-done.1.hi_ref) | copy-start | bytes 196612
  51.5 3.3 %copy-start.7 = (bf16[64,512]{1,0:T(8,128)(2,1)}, bf16[64,512]{1,0:T(8,128)(2,1)S(1)}, u32[]{:S(2)}) copy-start(bf16[64,512]{1,0:T(8,128)(2,1)S(1)} %collective-permute-done.lo_ref) | copy-start | bytes 196612
  51.5 3.3 %copy-start.1 = (bf16[16,64,512]{2,1,0:T(8,128)(2,1)}, bf16[16,64,512]{2,1,0:T(8,128)(2,1)S(1)}, u32[]{:S(2)}) copy-start(bf16[16,64,512]{2,1,0:T(8,128)(2,1)S(1)} %all-to-all-done.1.arr_ref) | copy-start | bytes 3145732
  51.6 14.2 %copy-start.8 = (bf16[32,256]{1,0:T(8,128)(2,1)S(1)}, bf16[32,256]{1,0:T(8,128)(2,1)}, u32[]{:S(2)}) copy-start(bf16[32,256]{1,0:T(8,128)(2,1)} %sw_ref.1) | copy-start | bytes 49156
  53.8 1.0 copy-start.5
  54.8 39.7 %all-to-all-start.2 = ((bf16[16,64,512]{2,1,0:T(8,128)(2,1)}), bf16[16,64,512]{2,1,0:T(8,128)(2,1)}, u32[]{:S(2)}, u32[]{:S(2)}) async-start(bf16[16,64,512]{2,1,0:T(8,128)(2,1)} %copy-done.5), calls=%async_computation.2 | async-start | bytes 2097152 | tf_op jit(solution)/shard_map/all_to_all | solution.py:390
  59.3 25.5 %collective-permute-start.3 = (bf16[64,512]{1,0:T(8,128)(2,1)S(1)}, bf16[64,512]{1,0:T(8,128)(2,1)S(1)}, u32[]{:S(2)}, u32[]{:S(2)}) collective-permute-start(bf16[64,512]{1,0:T(8,128)(2,1)S(1)} %get-tuple-element.12), channel_id=1, source_target_pairs={{1,0},{2,1},{3,2},{4,3},{5,4},{6,5},{7,6},{8,7},{9,8},{10,9},{11,1... | collective-permute-start | bytes 196616 | tf_op jit(solution)/shard_map/ppermute | solution.py:352
  61.6 9.6 %copy-start.16 = (bf16[96,32]{0,1:T(8,128)(2,1)S(1)}, bf16[96,32]{0,1:T(8,128)(2,1)}, u32[]{:S(2)}) copy-start(bf16[96,32]{0,1:T(8,128)(2,1)} %param.12) | copy-start | bytes 18436
  61.6 23.3 %collective-permute-start.2 = (bf16[64,512]{1,0:T(8,128)(2,1)S(1)}, bf16[64,512]{1,0:T(8,128)(2,1)S(1)}, u32[]{:S(2)}, u32[]{:S(2)}) collective-permute-start(bf16[64,512]{1,0:T(8,128)(2,1)S(1)} %get-tuple-element.13), channel_id=1, source_target_pairs={{0,1},{1,2},{2,3},{3,4},{4,5},{5,6},{6,7},{7,8},{8,9},{9,10},{10,1... | collective-permute-start | bytes 196616 | tf_op jit(solution)/shard_map/ppermute | solution.py:351
  84.8 0.6 copy-start.14
  85.5 0.6 copy-start.15

commit v12 on v11

--- a/solution.py
+++ b/solution.py
@@ -166,24 +166,14 @@
 
 def early_kernel(
     col_ref, ptr_ref, req_ref, exp_ref, field_ref, lo_ref, hi_ref, arr_ref, band_ref, farw_ref,
-    send_ref, edge_ref, blk,
+    send_ref, edge_ref, pad, blk,
 ):
     nblk = field_ref.shape[0] // BLK
     own = lax.axis_index("node")
+    fill_pad(field_ref, lo_ref, hi_ref, pad)
     targets = [exp_ref[own, 0], exp_ref[own, 1], 0, nblk - 1]
     for i, t in enumerate(targets):
-        pieces = []
-        for s in range(3):
-            b = jnp.clip(t - 1 + s, 0, nblk - 1)
-            v = field_ref[pl.ds(pl.multiple_of(b * BLK, BLK), BLK), :]
-            if s == 0:
-                v = jnp.where(t == 0, lo_ref[...], v)
-            if s == 2:
-                v = jnp.where(t == nblk - 1, hi_ref[...], v)
-            pieces.append(v)
-        win = jnp.concatenate(pieces, axis=0)
-        start = pl.multiple_of(t * BLK, BLK)
-        v = jnp.dot(band_ref[pl.ds(start, BLK), :], win, preferred_element_type=f32)
+        v = band_block(band_ref, pad, t)
 
         def slot(k, acc):
             return acc + slot_product(col_ref, farw_ref, arr_ref, k)
@@ -202,7 +192,7 @@
 
 def hop1_kernel(
     col_ref, ptr_ref, field_ref, lo_ref, hi_ref, arr_ref, band_ref, farw_ref, x_hbm, mix_ref,
-    lo2_ref, hi2_ref, out_ref, part_ref, acc2_ref, acc, pad, xs, sems,
+    out_ref, part_ref, acc2_ref, acc, pad, xs, sems,
 ):
     nrows, width = field_ref.shape
     nblk = nrows // BLK
@@ -211,10 +201,10 @@
     x_copy.start()
     accumulate(col_ref, ptr_ref, field_ref, lo_ref, hi_ref, arr_ref, band_ref, farw_ref, acc, pad)
     out_ref[...] = acc[:nrows, :].astype(bf16)
-    fill_pad(out_ref, lo2_ref, hi2_ref, pad)
+    zero = jnp.zeros((BLK, width), bf16)
+    fill_pad(out_ref, zero, zero, pad)
     for r in range(nblk):
         acc2_ref[r * BLK : (r + 1) * BLK, :] = band_block(band_ref, pad, r)
-    acc2_ref[nblk * BLK :, :] = jnp.zeros((BLK, width), f32)
     cw = mix_ref.shape[1]
     per = CHUNK // cw
     mix = mix_ref[...]
@@ -229,13 +219,27 @@
         part_ref[:, cols] = v
 
 
-def hop2_kernel(col_ref, ptr_ref, arr_ref, farw_ref, acc2_hbm, part_hbm, mix_ref, out_ref, far, a2, ps, sems):
+def hop2_kernel(
+    col_ref, ptr_ref, lo_ref, hi_ref, arr_ref, band_ref, farw_ref, acc2_hbm, part_hbm, mix_ref,
+    out_ref, far, a2, ps, sems,
+):
     nrows, width = out_ref.shape
-    a_copy = pltpu.make_async_copy(acc2_hbm, a2, sems.at[0])
-    p_copy = pltpu.make_async_copy(part_hbm, ps, sems.at[1])
-    a_copy.start()
-    p_copy.start()
+    nblk = nrows // BLK
+    chunks = width // CHUNK
+    copies = []
+    for j in range(chunks):
+        cols = pl.ds(j * CHUNK, CHUNK)
+        ca = pltpu.make_async_copy(acc2_hbm.at[:, cols], a2.at[:, cols], sems.at[2 * j])
+        cp = pltpu.make_async_copy(part_hbm.at[:, cols], ps.at[:, cols], sems.at[2 * j + 1])
+        ca.start()
+        cp.start()
+        copies.append((ca, cp))
     far[...] = jnp.zeros(far.shape, f32)
+    far[:BLK, :] = jnp.dot(band_ref[:BLK, :BLK], lo_ref[...], preferred_element_type=f32)
+    last = (nblk - 1) * BLK
+    far[last : last + BLK, :] = jnp.dot(
+        band_ref[last : last + BLK, 2 * BLK :], hi_ref[...], preferred_element_type=f32
+    )
     far_cap = farw_ref.shape[0]
     nptr = ptr_ref.shape[1]
 
@@ -250,11 +254,12 @@
     lax.fori_loop(0, far_cap, slot, 0)
     cw = mix_ref.shape[1]
     m2 = bd_inkernel(mix_ref[2 * cw :], CHUNK // cw)
-    a_copy.wait()
-    p_copy.wait()
-    for j in range(width // CHUNK):
+    for j in range(chunks):
+        ca, cp = copies[j]
+        ca.wait()
+        cp.wait()
         cols = slice(j * CHUNK, (j + 1) * CHUNK)
-        two = (a2[:nrows, cols] + far[:nrows, cols]).astype(bf16)
+        two = (a2[:, cols] + far[:nrows, cols]).astype(bf16)
         v = ps[:, cols] + jnp.dot(two, m2, preferred_element_type=f32)
         out_ref[:, cols] = v.astype(bf16)
 
@@ -289,7 +294,7 @@
             jax.ShapeDtypeStruct(arrived.shape, bf16),
             jax.ShapeDtypeStruct((2, BLK, width), bf16),
         ],
-        scratch_shapes=[pltpu.VMEM((4, BLK, width), bf16)],
+        scratch_shapes=[pltpu.VMEM((nrows + 2 * BLK, width), bf16), pltpu.VMEM((4, BLK, width), bf16)],
         compiler_params=BIG_VMEM,
         cost_estimate=pl.CostEstimate(
             flops=2 * BLK * BLK * width * (12 + farw3.shape[0]),
@@ -299,16 +304,16 @@
     )(far_col, far_ptr, requested, export_block, field, lo, hi, arrived, band, farw3)
 
 
-def hop1(far_col, far_ptr, field, lo, hi, arrived, band, farw3, features, mix, lo2, hi2):
+def hop1(far_col, far_ptr, field, lo, hi, arrived, band, farw3, features, mix):
     nrows, width = field.shape
     return pl.pallas_call(
         hop1_kernel,
-        in_specs=[smem(), smem()] + [vmem()] * 6 + [hbm(), vmem(), vmem(), vmem()],
+        in_specs=[smem(), smem()] + [vmem()] * 6 + [hbm(), vmem()],
         out_specs=[vmem(), vmem(), vmem()],
         out_shape=[
             jax.ShapeDtypeStruct((nrows, width), bf16),
             jax.ShapeDtypeStruct((nrows, width), f32),
-            jax.ShapeDtypeStruct((nrows + BLK, width), f32),
+            jax.ShapeDtypeStruct((nrows, width), f32),
         ],
         scratch_shapes=scratch(field)
         + [pltpu.VMEM((nrows, width), bf16), pltpu.SemaphoreType.DMA((1,))],
@@ -319,29 +324,29 @@
             transcendentals=0,
             bytes_accessed=2 * width * (nrows * 9 + arrived.shape[0] * BLK),
         ),
-    )(far_col, far_ptr, field, lo, hi, arrived, band, farw3, features, mix, lo2, hi2)
-
-
-def hop2(far_col, far_ptr, arrived, farw3, acc2, part, mix):
+    )(far_col, far_ptr, field, lo, hi, arrived, band, farw3, features, mix)
+
+
+def hop2(far_col, far_ptr, lo, hi, arrived, band, farw3, acc2, part, mix):
     nrows, width = part.shape
     return pl.pallas_call(
         hop2_kernel,
-        in_specs=[smem(), smem(), vmem(), vmem(), hbm(), hbm(), vmem()],
+        in_specs=[smem(), smem()] + [vmem()] * 5 + [hbm(), hbm(), vmem()],
         out_specs=vmem(),
         out_shape=jax.ShapeDtypeStruct((nrows, width), bf16),
         scratch_shapes=[
             pltpu.VMEM((nrows + BLK, width), f32),
-            pltpu.VMEM((nrows + BLK, width), f32),
             pltpu.VMEM((nrows, width), f32),
-            pltpu.SemaphoreType.DMA((2,)),
+            pltpu.VMEM((nrows, width), f32),
+            pltpu.SemaphoreType.DMA((2 * (width // CHUNK),)),
         ],
         compiler_params=pltpu.CompilerParams(),
         cost_estimate=pl.CostEstimate(
-            flops=2 * BLK * BLK * width * farw3.shape[0] + 2 * nrows * width * CHUNK,
+            flops=2 * BLK * BLK * width * (farw3.shape[0] + 2) + 2 * nrows * width * CHUNK,
             transcendentals=0,
             bytes_accessed=4 * width * nrows * 3,
         ),
-    )(far_col, far_ptr, arrived, farw3, acc2, part, mix)
+    )(far_col, far_ptr, lo, hi, arrived, band, farw3, acc2, part, mix)
 
 
 def halo(first, last):
@@ -371,7 +376,7 @@
     own_index = lax.axis_index("node")
     own_exports = lax.dynamic_slice_in_dim(export_block, own_index, 1, 0)[0].astype(jnp.int32)
     peer_count = far_cap + 1
-    info = jnp.concatenate([far_col[0], far_ptr[0, -1:]]).astype(jnp.int32)
+    info = jnp.concatenate([far_col[0], jnp.max(far_ptr[0], keepdims=True)]).astype(jnp.int32)
     info_all = lax.all_to_all(
         jnp.broadcast_to(info[None, :], (peer_count, far_cap + 1)),
         "node", split_axis=0, concat_axis=0, tiled=True,
@@ -398,10 +403,11 @@
     arrived2 = exchange(send2)
     lo2, hi2 = halo(edge[0], edge[1])
     hop_one, part, acc2 = hop1(
-        far_col, far_ptr, hidden, lo1, hi1, arrived1, band_weight, farw3, features, mix_weight,
-        lo2, hi2,
-    )
-    residual = hop2(far_col, far_ptr, arrived2, farw3, acc2, part, mix_weight)
+        far_col, far_ptr, hidden, lo1, hi1, arrived1, band_weight, farw3, features, mix_weight
+    )
+    residual = hop2(
+        far_col, far_ptr, lo2, hi2, arrived2, band_weight, farw3, acc2, part, mix_weight
+    )
     return residual, skip_out
 
 

time: 101 us -> 91.9 us (0.910)
  waiting for transfers between devices: 30.8 us -> 23.2 us
  local copies, waits for them, and re-layouts: 11.4 us -> 8.9 us
  other arithmetic: 2.89 us -> 4.14 us
    ppermute x2, waiting for transfers between devices: 30.8 us -> 23.2 us  [halo(): hi = lax.ppermute(first, 'node', backward)]
    reduce_max x0 -> x1, other arithmetic: none -> 1.3 us  [local(): jnp.max(far_ptr[0], keepdims=True)]
    slice x1 -> x0, local copies, waits for them, and re-layouts: 1.24 us -> none  [local(): info = jnp.concatenate([far_col[0], far_ptr[0, -1:]]).astype(jnp.int32)]
  transfers between devices with their start and end apart: 7 -> 7, of which waited for: 2 -> 2; matrix products, arithmetic and copies ran while one was open for 3% -> 3% of each run, Pallas kernels for 16% -> 18%
where the time goes in v12:
time: 91.9 us; the launch traced here: 91.3 us
  starting transfers between devices  30.2 us (33%)
  Pallas kernels  24 us (26%)
  waiting for transfers between devices  23.2 us (25%)
  local copies, waits for them, and re-layouts  8.9 us (10%)
  other arithmetic  4.14 us (5%)
    ppermute x2, waiting for transfers between devices, halo(): hi = lax.ppermute(first, 'node', backward)  23.2 us
    all_to_all x2, starting transfers between devices, exchange(): return lax.all_to_all(send, 'node', split_axis=0, concat_axis=0, tiled=True)  10.7 us
    ppermute x2, starting transfers between devices, halo(): lo = lax.ppermute(last, 'node', forward)  8.37 us
    pallas_call x1, Pallas kernels, hop1(): pl.pallas_call(hop1_kernel, in_specs=[smem(), smem()] + [vmem()] * 6 + [h...  8.3 us
    all_to_all x1, starting transfers between devices, local(): lax.all_to_all(jnp.broadcast_to(info[None, :], (peer_count, far_cap + 1))...  6.55 us
    pallas_call x1, Pallas kernels, hop2(): pl.pallas_call(hop2_kernel, in_specs=[smem(), smem()] + [vmem()] * 5 + [h...  6 us
    pallas_call x1, Pallas kernels, front_skip(): pl.pallas_call(skip_kernel, grid=(rows // tile,), in_specs=[pl.BlockSpec(...  5.32 us
    unnamed x39, local copies, waits for them, and re-layouts  4.96 us
  transfers between devices with their start and end apart: 7, of which 2 were waited for; matrix products, arithmetic and copies ran while one was open for 3% of the time, Pallas kernels for 18%

profile of v12, /device:TPU:15, one launch (start us, length us, event | category | flops | bytes accessed | tf_op | source)
XLA Modules:
  0.0 91.3 jit_solution(1345488060075786507)
XLA Ops:
  0.6 1.3 %reduce_max.9 = s32[]{:T(128)} reduce(s32[1,17]{1,0:T(1,128)} %ptr_ref.5, s32[]{:T(128)} %constant.31.clone.1), dimensions={0,1}, to_apply=%region_0.0 | reduce | flops 16 | bytes 76 | tf_op jit(solution)/shard_map/reduce_max | solution.py:379
  1.9 1.4 %pad_add_fusion = s32[16]{0:T(128)S(1)} fusion(s32[1]{0:T(128)} %bitcast.1, s32[15]{0:T(128)} %bitcast.21), kind=kLoop, calls=%fused_computation.22 | loop fusion | flops 16 | bytes 128 | tf_op jit(solution)/shard_map/concatenate | solution.py:379
  3.3 0.6 broadcast_in_dim.6
  3.9 6.6 %all-to-all-start = ((s32[16,1,16]{2,1,0:T(1,128)}), s32[16,1,16]{2,1,0:T(1,128)S(1)}, u32[]{:S(2)}, u32[]{:S(2)}) async-start(s32[16,1,16]{2,1,0:T(1,128)} %broadcast_in_dim.6), calls=%async_computation | async-start | bytes 16384 | tf_op jit(solution)/shard_map/all_to_all | solution.py:380
  10.5 0.7 constant_dynamic-slice_fusion
  11.2 0.5 fusion.7
  11.7 1.6 %copy-done.4 = bf16[1024,1024]{1,0:T(8,128)(2,1)S(1)} copy-done((bf16[1024,1024]{1,0:T(8,128)(2,1)S(1)}, bf16[1024,1024]{1,0:T(8,128)(2,1)}, u32[]{:S(2)}) %copy-start.4) | copy-done | bytes 2097176
  13.3 0.7 copy-done.11
  14.0 2.4 %shard_map.104.field_ref.h_ref = bf16[1024,512]{1,0:T(8,128)(2,1)S(1)} custom-call(bf16[1024,1024]{1,0:T(8,128)(2,1)S(1)} %copy-done.4, bf16[64,64]{1,0:T(8,128)(2,1)S(1)} %copy-done.11), custom_call_target="tpu_custom_call" | custom-call | flops 1073741824 | bytes 3145728 | tf_op jit(solution)/shard_map/pallas_call | solution.py:84
  16.4 0.0 copy-start
  16.5 0.0 all-to-all-done
  16.5 0.2 slice_reduce_fusion
  16.6 0.2 fusion.2.req_ref
  16.8 1.3 %fusion.5 = s32[16]{0:T(128)S(1)} fusion(s32[16]{0:T(128)S(1)} %fusion.2.req_ref, s32[]{:T(128)} %bitcast.6, s32[]{:T(128)} %bitcast.5), kind=kLoop, calls=%fused_computation.21 | loop fusion | flops 128 | bytes 136 | tf_op jit(solution)/shard_map/select_n | solution.py:397
  18.1 0.0 copy-start.17
  18.1 0.0 copy-start.13
  18.2 1.6 %gather_fusion = bf16[16,64,512]{2,1,0:T(8,128)(2,1)} fusion(bf16[16,64,512]{2,1,0:T(8,128)(2,1)S(1)} %bitcast.17, s32[1024]{0:T(1024)S(1)} %pad_clamp_fusion), kind=kCustom, calls=%fused_computation | custom fusion | bytes 2097216 | tf_op jit(solution)/shard_map/gather | solution.py:397
  19.8 6.1 %all-to-all-start.1 = ((bf16[16,64,512]{2,1,0:T(8,128)(2,1)}), bf16[16,64,512]{2,1,0:T(8,128)(2,1)S(1)}, u32[]{:S(2)}, u32[]{:S(2)}) async-start(bf16[16,64,512]{2,1,0:T(8,128)(2,1)} %gather_fusion), calls=%async_computation.1 | async-start | bytes 2097152 | tf_op jit(solution)/shard_map/all_to_all | solution.py:395
  25.9 2.3 %collective-permute-start.1 = (bf16[64,512]{1,0:T(8,128)(2,1)S(1)}, bf16[64,512]{1,0:T(8,128)(2,1)S(1)}, u32[]{:S(2)}, u32[]{:S(2)}) collective-permute-start(bf16[64,512]{1,0:T(8,128)(2,1)S(1)} %get-tuple-element.10), channel_id=1, source_target_pairs={{1,0},{2,1},{3,2},{4,3},{5,4},{6,5},{7,6},{8,7},{9,8},{10,9},{11,1... | collective-permute-start | bytes 196616 | tf_op jit(solution)/shard_map/ppermute | solution.py:357
  28.2 4.2 %collective-permute-start = (bf16[64,512]{1,0:T(8,128)(2,1)S(1)}, bf16[64,512]{1,0:T(8,128)(2,1)S(1)}, u32[]{:S(2)}, u32[]{:S(2)}) collective-permute-start(bf16[64,512]{1,0:T(8,128)(2,1)S(1)} %get-tuple-element.11), channel_id=1, source_target_pairs={{0,1},{1,2},{2,3},{3,4},{4,5},{5,6},{6,7},{7,8},{8,9},{9,10},{10,1... | collective-permute-start | bytes 196616 | tf_op jit(solution)/shard_map/ppermute | solution.py:356
  32.4 0.0 copy-done.17
  32.4 0.1 copy.32.exp_ref
  32.5 0.0 copy-done.13
  32.5 0.2 reshape.43
  32.7 0.1 copy.39
  32.8 0.2 copy.33.band_ref
  33.0 18.4 %collective-permute-done.1.hi_ref = bf16[64,512]{1,0:T(8,128)(2,1)S(1)} collective-permute-done((bf16[64,512]{1,0:T(8,128)(2,1)S(1)}, bf16[64,512]{1,0:T(8,128)(2,1)S(1)}, u32[]{:S(2)}, u32[]{:S(2)}) %collective-permute-start.1) | collective-permute-done | bytes 65568 | tf_op jit(solution)/shard_map/ppermute | solution.py:357
  51.5 0.0 collective-permute-done.lo_ref
  51.5 0.0 all-to-all-done.1.arr_ref
  51.5 0.0 copy-start.16
  51.5 0.0 copy-start.8
  51.5 2.0 %shard_map.105 = (bf16[16,64,512]{2,1,0:T(8,128)(2,1)S(1)}, bf16[2,64,512]{2,1,0:T(8,128)(2,1)S(1)}) custom-call(s32[1,15]{1,0:T(1,128)S(1)} %copy-done.9, s32[1,17]{1,0:T(1,128)S(1)} %copy-done.10, s32[16]{0:T(128)S(1)} %fusion.2.req_ref, s32[16,2]{1,0:T(8,128)S(1)} %copy.32.exp_ref, bf16[1024,512]{1,0:T(8,128)(2,1)S(1)} %shard_map.104.field_ref.h_ref, ...), custom_call_target="tpu_custom_call" | custom-call | flops 113246208 | bytes 3145728 | tf_op jit(solution)/shard_map/pallas_call | solution.py:289
  53.5 0.0 copy-start.5
  53.5 1.0 %copy-done.5 = bf16[16,64,512]{2,1,0:T(8,128)(2,1)} copy-done((bf16[16,64,512]{2,1,0:T(8,128)(2,1)}, bf16[16,64,512]{2,1,0:T(8,128)(2,1)S(1)}, u32[]{:S(2)}) %copy-start.5) | copy-done | bytes 1048600
  54.5 0.0 copy-done.7
  54.5 0.0 copy-done.1
  54.5 4.5 %all-to-all-start.2 = ((bf16[16,64,512]{2,1,0:T(8,128)(2,1)}), bf16[16,64,512]{2,1,0:T(8,128)(2,1)}, u32[]{:S(2)}, u32[]{:S(2)}) async-start(bf16[16,64,512]{2,1,0:T(8,128)(2,1)} %copy-done.5), calls=%async_computation.2 | async-start | bytes 2097152 | tf_op jit(solution)/shard_map/all_to_all | solution.py:395
  59.1 0.7 copy.35.mix_ref
  59.8 5.3 %shard_map.108 = bf16[1024,4096]{1,0:T(8,128)(2,1)} custom-call(bf16[1024,512]{1,0:T(8,128)(2,1)S(1)} %shard_map.104.field_ref.h_ref, bf16[32,256]{1,0:T(8,128)(2,1)S(1)} %copy-done.8), custom_call_target="tpu_custom_call" | custom-call | flops 2147483648 | bytes 9437184 | tf_op jit(solution)/shard_map/pallas_call | solution.py:110
  65.1 2.3 %collective-permute-start.3 = (bf16[64,512]{1,0:T(8,128)(2,1)S(1)}, bf16[64,512]{1,0:T(8,128)(2,1)S(1)}, u32[]{:S(2)}, u32[]{:S(2)}) collective-permute-start(bf16[64,512]{1,0:T(8,128)(2,1)S(1)} %get-tuple-element.12), channel_id=1, source_target_pairs={{1,0},{2,1},{3,2},{4,3},{5,4},{6,5},{7,6},{8,7},{9,8},{10,9},{11,1... | collective-permute-start | bytes 196616 | tf_op jit(solution)/shard_map/ppermute | solution.py:357
  67.4 4.2 %collective-permute-start.2 = (bf16[64,512]{1,0:T(8,128)(2,1)S(1)}, bf16[64,512]{1,0:T(8,128)(2,1)S(1)}, u32[]{:S(2)}, u32[]{:S(2)}) collective-permute-start(bf16[64,512]{1,0:T(8,128)(2,1)S(1)} %get-tuple-element.13), channel_id=1, source_target_pairs={{0,1},{1,2},{2,3},{3,4},{4,5},{5,6},{6,7},{7,8},{8,9},{9,10},{10,1... | collective-permute-start | bytes 196616 | tf_op jit(solution)/shard_map/ppermute | solution.py:356
  71.6 8.3 %shard_map.106 = (bf16[1024,512]{1,0:T(8,128)(2,1)}, f32[1024,512]{1,0:T(8,128)}, f32[1024,512]{1,0:T(8,128)}) custom-call(s32[1,15]{1,0:T(1,128)} %col_ref.5, s32[1,17]{1,0:T(1,128)} %ptr_ref.5, bf16[1024,512]{1,0:T(8,128)(2,1)} %copy-done, bf16[64,512]{1,0:T(8,128)(2,1)} %copy-done.7, bf16[64,512]{1,0:T(8,128)(2,1)} %copy-done.6, ...), custom_call_target="tpu_custom_call" | custom-call | flops 1002438656 | bytes 10485760 | tf_op jit(solution)/shard_map/pallas_call | solution.py:309
  79.9 4.7 %collective-permute-done.3.hi_ref = bf16[64,512]{1,0:T(8,128)(2,1)S(1)} collective-permute-done((bf16[64,512]{1,0:T(8,128)(2,1)S(1)}, bf16[64,512]{1,0:T(8,128)(2,1)S(1)}, u32[]{:S(2)}, u32[]{:S(2)}) %collective-permute-start.3) | collective-permute-done | bytes 65568 | tf_op jit(solution)/shard_map/ppermute | solution.py:357
  84.6 0.0 collective-permute-done.2.lo_ref
  84.6 0.0 all-to-all-done.2.arr_ref
  84.6 0.6 copy-done.14
  85.2 0.0 copy-done.15
  85.3 6.0 %shard_map.107 = bf16[1024,512]{1,0:T(8,128)(2,1)} custom-call(s32[1,15]{1,0:T(1,128)} %col_ref.5, s32[1,17]{1,0:T(1,128)} %ptr_ref.5, bf16[64,512]{1,0:T(8,128)(2,1)} %copy-done.15, bf16[64,512]{1,0:T(8,128)(2,1)} %copy-done.14, bf16[16,64,512]{2,1,0:T(8,128)(2,1)} %all-to-all-done.2.arr_ref, bf16[1024,192]{1,0:T(8,128)(2,1)} %copy-done.2, ...), custom_call_target="tpu_custom_call" | custom-call | flops 339738624 | bytes 6291456 | tf_op jit(solution)/shard_map/pallas_call | solution.py:332
  (24 shorter events, 0.1 us)
Async XLA Ops:
  3.9 12.6 %all-to-all-start = ((s32[16,1,16]{2,1,0:T(1,128)}), s32[16,1,16]{2,1,0:T(1,128)S(1)}, u32[]{:S(2)}, u32[]{:S(2)}) async-start(s32[16,1,16]{2,1,0:T(1,128)} %broadcast_in_dim.6), calls=%async_computation | async-start | bytes 16384 | tf_op jit(solution)/shard_map/all_to_all | solution.py:380
  11.7 1.6 %copy-start.4 = (bf16[1024,1024]{1,0:T(8,128)(2,1)S(1)}, bf16[1024,1024]{1,0:T(8,128)(2,1)}, u32[]{:S(2)}) copy-start(bf16[1024,1024]{1,0:T(8,128)(2,1)} %x_hbm.1) | copy-start | bytes 6291460
  13.3 0.7 copy-start.11
  16.4 43.3 %copy-start = (bf16[1024,512]{1,0:T(8,128)(2,1)}, bf16[1024,512]{1,0:T(8,128)(2,1)S(1)}, u32[]{:S(2)}) copy-start(bf16[1024,512]{1,0:T(8,128)(2,1)S(1)} %shard_map.104.field_ref.h_ref) | copy-start | bytes 3145732
  18.1 14.3 %copy-start.17 = (s32[16,2]{0,1:T(2,128)S(1)}, s32[16,2]{0,1:T(2,128)}, u32[]{:S(2)}) copy-start(s32[16,2]{0,1:T(2,128)} %param.17) | copy-start | bytes 388
  18.1 14.3 %copy-start.13 = (bf16[64,960]{1,0:T(8,128)(2,1)S(1)}, bf16[64,960]{1,0:T(8,128)(2,1)}, u32[]{:S(2)}) copy-start(bf16[64,960]{1,0:T(8,128)(2,1)} %param.14) | copy-start | bytes 368644
  19.7 13.0 %copy-start.12 = (bf16[1024,192]{0,1:T(8,128)(2,1)S(1)}, bf16[1024,192]{0,1:T(8,128)(2,1)}, u32[]{:S(2)}) copy-start(bf16[1024,192]{0,1:T(8,128)(2,1)} %param.13) | copy-start | bytes 1179652
  19.7 31.7 %copy-start.9 = (s32[1,15]{1,0:T(1,128)S(1)}, s32[1,15]{1,0:T(1,128)}, u32[]{:S(2)}) copy-start(s32[1,15]{1,0:T(1,128)} %col_ref.5) | copy-start | bytes 184
  19.7 31.7 %copy-start.10 = (s32[1,17]{1,0:T(1,128)S(1)}, s32[1,17]{1,0:T(1,128)}, u32[]{:S(2)}) copy-start(s32[1,17]{1,0:T(1,128)} %ptr_ref.5) | copy-start | bytes 208
  19.8 31.7 %all-to-all-start.1 = ((bf16[16,64,512]{2,1,0:T(8,128)(2,1)}), bf16[16,64,512]{2,1,0:T(8,128)(2,1)S(1)}, u32[]{:S(2)}, u32[]{:S(2)}) async-start(bf16[16,64,512]{2,1,0:T(8,128)(2,1)} %gather_fusion), calls=%async_computation.1 | async-start | bytes 2097152 | tf_op jit(solution)/shard_map/all_to_all | solution.py:395
  25.9 25.5 %collective-permute-start.1 = (bf16[64,512]{1,0:T(8,128)(2,1)S(1)}, bf16[64,512]{1,0:T(8,128)(2,1)S(1)}, u32[]{:S(2)}, u32[]{:S(2)}) collective-permute-start(bf16[64,512]{1,0:T(8,128)(2,1)S(1)} %get-tuple-element.10), channel_id=1, source_target_pairs={{1,0},{2,1},{3,2},{4,3},{5,4},{6,5},{7,6},{8,7},{9,8},{10,9},{11,1... | collective-permute-start | bytes 196616 | tf_op jit(solution)/shard_map/ppermute | solution.py:357
  28.2 23.3 %collective-permute-start = (bf16[64,512]{1,0:T(8,128)(2,1)S(1)}, bf16[64,512]{1,0:T(8,128)(2,1)S(1)}, u32[]{:S(2)}, u32[]{:S(2)}) collective-permute-start(bf16[64,512]{1,0:T(8,128)(2,1)S(1)} %get-tuple-element.11), channel_id=1, source_target_pairs={{0,1},{1,2},{2,3},{3,4},{4,5},{5,6},{6,7},{7,8},{8,9},{9,10},{10,1... | collective-permute-start | bytes 196616 | tf_op jit(solution)/shard_map/ppermute | solution.py:356
  32.8 21.7 %copy-start.3 = (bf16[64,15,64]{2,0,1:T(8,128)(2,1)}, bf16[64,15,64]{2,0,1:T(8,128)(2,1)S(1)}, u32[]{:S(2)}) copy-start(bf16[64,15,64]{2,0,1:T(8,128)(2,1)S(1)} %copy.39) | copy-start | bytes 368644
  33.0 21.5 %copy-start.2 = (bf16[1024,192]{1,0:T(8,128)(2,1)}, bf16[1024,192]{1,0:T(8,128)(2,1)S(1)}, u32[]{:S(2)}) copy-start(bf16[1024,192]{1,0:T(8,128)(2,1)S(1)} %copy.33.band_ref) | copy-start | bytes 1179652
  51.5 3.1 %copy-start.6 = (bf16[64,512]{1,0:T(8,128)(2,1)}, bf16[64,512]{1,0:T(8,128)(2,1)S(1)}, u32[]{:S(2)}) copy-start(bf16[64,512]{1,0:T(8,128)(2,1)S(1)} %collective-permute-done.1.hi_ref) | copy-start | bytes 196612
  51.5 3.1 %copy-start.7 = (bf16[64,512]{1,0:T(8,128)(2,1)}, bf16[64,512]{1,0:T(8,128)(2,1)S(1)}, u32[]{:S(2)}) copy-start(bf16[64,512]{1,0:T(8,128)(2,1)S(1)} %collective-permute-done.lo_ref) | copy-start | bytes 196612
  51.5 3.1 %copy-start.1 = (bf16[16,64,512]{2,1,0:T(8,128)(2,1)}, bf16[16,64,512]{2,1,0:T(8,128)(2,1)S(1)}, u32[]{:S(2)}) copy-start(bf16[16,64,512]{2,1,0:T(8,128)(2,1)S(1)} %all-to-all-done.1.arr_ref) | copy-start | bytes 3145732
  51.5 7.6 %copy-start.16 = (bf16[96,32]{0,1:T(8,128)(2,1)S(1)}, bf16[96,32]{0,1:T(8,128)(2,1)}, u32[]{:S(2)}) copy-start(bf16[96,32]{0,1:T(8,128)(2,1)} %param.12) | copy-start | bytes 18436
  51.5 8.3 %copy-start.8 = (bf16[32,256]{1,0:T(8,128)(2,1)S(1)}, bf16[32,256]{1,0:T(8,128)(2,1)}, u32[]{:S(2)}) copy-start(bf16[32,256]{1,0:T(8,128)(2,1)} %sw_ref.1) | copy-start | bytes 49156
  53.5 1.0 %copy-start.5 = (bf16[16,64,512]{2,1,0:T(8,128)(2,1)}, bf16[16,64,512]{2,1,0:T(8,128)(2,1)S(1)}, u32[]{:S(2)}) copy-start(bf16[16,64,512]{2,1,0:T(8,128)(2,1)S(1)} %get-tuple-element.7) | copy-start | bytes 3145732
  54.5 30.1 %all-to-all-start.2 = ((bf16[16,64,512]{2,1,0:T(8,128)(2,1)}), bf16[16,64,512]{2,1,0:T(8,128)(2,1)}, u32[]{:S(2)}, u32[]{:S(2)}) async-start(bf16[16,64,512]{2,1,0:T(8,128)(2,1)} %copy-done.5), calls=%async_computation.2 | async-start | bytes 2097152 | tf_op jit(solution)/shard_map/all_to_all | solution.py:395
  65.1 19.5 %collective-permute-start.3 = (bf16[64,512]{1,0:T(8,128)(2,1)S(1)}, bf16[64,512]{1,0:T(8,128)(2,1)S(1)}, u32[]{:S(2)}, u32[]{:S(2)}) collective-permute-start(bf16[64,512]{1,0:T(8,128)(2,1)S(1)} %get-tuple-element.12), channel_id=1, source_target_pairs={{1,0},{2,1},{3,2},{4,3},{5,4},{6,5},{7,6},{8,7},{9,8},{10,9},{11,1... | collective-permute-start | bytes 196616 | tf_op jit(solution)/shard_map/ppermute | solution.py:357
  67.4 17.2 %collective-permute-start.2 = (bf16[64,512]{1,0:T(8,128)(2,1)S(1)}, bf16[64,512]{1,0:T(8,128)(2,1)S(1)}, u32[]{:S(2)}, u32[]{:S(2)}) collective-permute-start(bf16[64,512]{1,0:T(8,128)(2,1)S(1)} %get-tuple-element.13), channel_id=1, source_target_pairs={{0,1},{1,2},{2,3},{3,4},{4,5},{5,6},{6,7},{7,8},{8,9},{9,10},{10,1... | collective-permute-start | bytes 196616 | tf_op jit(solution)/shard_map/ppermute | solution.py:356
  84.6 0.6 copy-start.14
  84.6 0.6 copy-start.15

commit v13 on v12

--- a/solution.py
+++ b/solution.py
@@ -63,6 +63,69 @@
         ).astype(bf16)
 
 
+def prep_kernel(col_ref, ptr_ref, out_ref):
+    far_cap = col_ref.shape[1]
+    peers = out_ref.shape[0]
+    used = jnp.max(ptr_ref[...], axis=1, keepdims=True)
+    out_ref[:, :far_cap] = jnp.broadcast_to(col_ref[...], (peers, far_cap))
+    out_ref[:, far_cap:] = jnp.broadcast_to(used, (peers, 1))
+
+
+def prep(far_col, far_ptr):
+    far_cap = far_col.shape[1]
+    return pl.pallas_call(
+        prep_kernel,
+        in_specs=[vmem(), vmem()],
+        out_specs=vmem(),
+        out_shape=jax.ShapeDtypeStruct((far_cap + 1, far_cap + 1), jnp.int32),
+    )(far_col, far_ptr)
+
+
+def pack_kernel(info_ref, exp_ref, h_hbm, send_hbm, req_ref, sems):
+    peers = send_hbm.shape[0]
+    far_cap = info_ref.shape[1] - 1
+    own = lax.axis_index("node")
+
+    def peer(p, carry):
+        used = info_ref[p, far_cap]
+
+        def scan(k, acc):
+            col = info_ref[p, k]
+            hit = jnp.logical_and(col // EXPORT == own, k < used)
+            return acc + jnp.where(hit, col % EXPORT, 0)
+
+        req = lax.fori_loop(0, far_cap, scan, 0)
+        req_ref[p] = req
+        row = exp_ref[own, req]
+        start = pl.multiple_of(row * BLK, BLK)
+        pltpu.make_async_copy(h_hbm.at[pl.ds(start, BLK)], send_hbm.at[p], sems.at[p]).start()
+        return carry
+
+    lax.fori_loop(0, peers, peer, 0)
+
+    def finish(p, carry):
+        start = pl.multiple_of(exp_ref[own, req_ref[p]] * BLK, BLK)
+        pltpu.make_async_copy(h_hbm.at[pl.ds(start, BLK)], send_hbm.at[p], sems.at[p]).wait()
+        return carry
+
+    lax.fori_loop(0, peers, finish, 0)
+
+
+def pack(info_all, export_block, hidden):
+    nrows, width = hidden.shape
+    peers = info_all.shape[0]
+    return pl.pallas_call(
+        pack_kernel,
+        in_specs=[smem(), smem(), hbm()],
+        out_specs=[hbm(), smem()],
+        out_shape=[
+            jax.ShapeDtypeStruct((peers, BLK, width), bf16),
+            jax.ShapeDtypeStruct((peers,), jnp.int32),
+        ],
+        scratch_shapes=[pltpu.SemaphoreType.DMA((peers,))],
+    )(info_all, export_block, hidden)
+
+
 def skip_kernel(h_ref, sw_ref, s_ref, ws):
     cw = sw_ref.shape[0]
 
@@ -79,7 +142,7 @@
 
 def front_hidden(features, fgw):
     rows, cols = features.shape
-    chunks = cols // 2 // CHUNK
+    half = cols // 2
     tile = min(ROW_TILE, rows)
     return pl.pallas_call(
         hidden_kernel,
@@ -88,14 +151,13 @@
             pl.BlockSpec((tile, cols), lambda i: (i, 0)),
             pl.BlockSpec(fgw.shape, lambda i: (0, 0)),
         ],
-        out_specs=pl.BlockSpec((tile, chunks * CHUNK), lambda i: (i, 0)),
-        out_shape=jax.ShapeDtypeStruct((rows, chunks * CHUNK), bf16),
+        out_specs=pl.BlockSpec((tile, half), lambda i: (i, 0)),
+        out_shape=jax.ShapeDtypeStruct((rows, half), bf16),
         scratch_shapes=[pltpu.VMEM((CHUNK, 2 * CHUNK), bf16), pltpu.VMEM((CHUNK, 2 * CHUNK), bf16)],
-        compiler_params=pltpu.CompilerParams(vmem_limit_bytes=48 * 1024 * 1024),
         cost_estimate=pl.CostEstimate(
-            flops=2 * rows * CHUNK * 4 * CHUNK * chunks,
-            transcendentals=rows * CHUNK * chunks * 2,
-            bytes_accessed=2 * rows * (cols + CHUNK * chunks),
+            flops=2 * rows * CHUNK * 4 * CHUNK * (half // CHUNK),
+            transcendentals=rows * half * 2,
+            bytes_accessed=2 * rows * (cols + half),
         ),
     )(features, fgw)
 
@@ -373,20 +435,9 @@
     blocks = node_rows // BLK
     far_cap = far_col.shape[1]
 
-    own_index = lax.axis_index("node")
-    own_exports = lax.dynamic_slice_in_dim(export_block, own_index, 1, 0)[0].astype(jnp.int32)
-    peer_count = far_cap + 1
-    info = jnp.concatenate([far_col[0], jnp.max(far_ptr[0], keepdims=True)]).astype(jnp.int32)
-    info_all = lax.all_to_all(
-        jnp.broadcast_to(info[None, :], (peer_count, far_cap + 1)),
-        "node", split_axis=0, concat_axis=0, tiled=True,
-    )
-    slot_ids = jnp.arange(far_cap, dtype=jnp.int32)
-    cols_all = info_all[:, :far_cap]
-    hits = (cols_all // EXPORT == own_index) & (slot_ids[None, :] < info_all[:, far_cap:])
-    requested = jnp.sum(jnp.where(hits, cols_all % EXPORT, 0), axis=1).astype(jnp.int32)
-    send_rows = own_exports[requested].astype(jnp.int32)
+    info_all = lax.all_to_all(prep(far_col, far_ptr), "node", split_axis=0, concat_axis=0, tiled=True)
     hidden = front_hidden(features, filter_gate_weight)
+    send1, requested = pack(info_all, export_block, hidden)
     blocks = node_rows // BLK
     width = hidden.shape[1]
     farw3 = far_weight.reshape(BLK, far_cap, BLK).transpose(1, 0, 2)
@@ -394,7 +445,7 @@
     def exchange(send):
         return lax.all_to_all(send, "node", split_axis=0, concat_axis=0, tiled=True)
 
-    arrived1 = exchange(hidden.reshape(blocks, BLK, width)[send_rows])
+    arrived1 = exchange(send1)
     lo1, hi1 = halo(hidden[:BLK], hidden[node_rows - BLK :])
     skip_out = front_skip(hidden, skip_weight)
     send2, edge = early(

time: 91.9 us -> 122 us (1.33)
  Pallas kernels: 24 us -> 63.4 us
  local copies, waits for them, and re-layouts: 8.9 us -> 4.18 us
  other arithmetic: 4.14 us -> 0 us
    pallas_call x0 -> x2, Pallas kernels: none -> 36.3 us  [the longest x1 34.8 us: pack(): pl.pallas_call(pack_kernel, in_specs=[smem(), smem(), hbm()], out_specs=[...]
    pallas_call x1, Pallas kernels: 2.39 us -> 5 us  [front_hidden(): pl.pallas_call(hidden_kernel, grid=(rows // tile,), in_specs=[pl.BlockSpe...]
    gather x2 -> x0, local copies, waits for them, and re-layouts: 2.11 us -> none  [the longest x1 1.58 us: local(): arrived1 = exchange(hidden.reshape(blocks, BLK, width)[send_rows])]
    concatenate x1 -> x0, other arithmetic: 1.37 us -> none  [local(): jnp.concatenate([far_col[0], jnp.max(far_ptr[0], keepdims=True)])]
    reduce_max x1 -> x0, other arithmetic: 1.3 us -> none  [local(): jnp.max(far_ptr[0], keepdims=True)]
    select_n x1 -> x0, other arithmetic: 1.28 us -> none  [local(): arrived1 = exchange(hidden.reshape(blocks, BLK, width)[send_rows])]
    unnamed x39 -> x41, local copies, waits for them, and re-layouts: 4.96 us -> 3.88 us
  transfers between devices with their start and end apart: 7 -> 7, of which waited for: 2 -> 2; matrix products, arithmetic and copies ran while one was open for 3% -> 2% of each run, Pallas kernels for 18% -> 15%
where the time goes in v13:
time: 122 us
  Pallas kernels  63.4 us (52%)
  starting transfers between devices  29.9 us (25%)
  waiting for transfers between devices  23.2 us (19%)
  local copies, waits for them, and re-layouts  4.18 us (3%)
    pallas_call x1, Pallas kernels, pack(): pl.pallas_call(pack_kernel, in_specs=[smem(), smem(), hbm()], out_specs=[...  34.8 us
    ppermute x2, waiting for transfers between devices, halo(): hi = lax.ppermute(first, 'node', backward)  23.2 us
    all_to_all x2, starting transfers between devices, exchange(): return lax.all_to_all(send, 'node', split_axis=0, concat_axis=0, tiled=True)  10.4 us
    ppermute x2, starting transfers between devices, halo(): lo = lax.ppermute(last, 'node', forward)  8.38 us
    pallas_call x1, Pallas kernels, hop1(): pl.pallas_call(hop1_kernel, in_specs=[smem(), smem()] + [vmem()] * 6 + [h...  8.31 us
    all_to_all x1, starting transfers between devices, local(): lax.all_to_all(prep(far_col, far_ptr), 'node', split_axis=0, concat_axis=...  6.55 us
    pallas_call x1, Pallas kernels, hop2(): pl.pallas_call(hop2_kernel, in_specs=[smem(), smem()] + [vmem()] * 5 + [h...  6.05 us
    pallas_call x1, Pallas kernels, front_skip(): pl.pallas_call(skip_kernel, grid=(rows // tile,), in_specs=[pl.BlockSpec(...  5.34 us
  transfers between devices with their start and end apart: 7, of which 2 were waited for; matrix products, arithmetic and copies ran while one was open for 2% of the time, Pallas kernels for 15%

profile of v13, /device:TPU:15, one launch (start us, length us, event | category | flops | bytes accessed | tf_op | source)
XLA Modules:
  0.0 121.6 jit_solution(9961161018225802011)
XLA Ops:
  0.6 0.0 copy-start.18
  0.6 1.4 %shard_map.104 = s32[16,16]{1,0:T(8,128)} custom-call(s32[1,15]{1,0:T(1,128)} %col_ref.7, s32[1,17]{1,0:T(1,128)} %ptr_ref.7), custom_call_target="tpu_custom_call" | custom-call | tf_op jit(solution)/shard_map/pallas_call | solution.py:76
  2.1 6.6 %all-to-all-start = ((s32[16,1,16]{2,1,0:T(1,128)}), s32[16,1,16]{2,1,0:T(1,128)S(1)}, u32[]{:S(2)}, u32[]{:S(2)}) async-start(s32[16,1,16]{2,1,0:T(1,128)} %bitcast.15), calls=%async_computation | async-start | bytes 16384 | tf_op jit(solution)/shard_map/all_to_all | solution.py:438
  8.6 5.0 %shard_map.105.h_hbm.field_ref.h_ref = bf16[1024,512]{1,0:T(8,128)(2,1)} custom-call(bf16[1024,1024]{1,0:T(8,128)(2,1)} %x_hbm.1, bf16[64,64]{1,0:T(8,128)(2,1)} %fgw_ref.1), custom_call_target="tpu_custom_call" | custom-call | flops 1073741824 | bytes 3145728 | tf_op jit(solution)/shard_map/pallas_call | solution.py:147
  13.6 0.0 copy-done.18
  13.6 0.7 copy.27.exp_ref
  14.3 0.0 all-to-all-done
  14.3 0.6 copy-done.16
  14.9 34.8 %shard_map.106 = (bf16[16,64,512]{2,1,0:T(8,128)(2,1)}, s32[16]{0:T(128)}) custom-call(s32[16,16]{1,0:T(8,128)} %bitcast.14, s32[16,2]{1,0:T(8,128)} %copy.27.exp_ref, bf16[1024,512]{1,0:T(8,128)(2,1)} %shard_map.105.h_hbm.field_ref.h_ref), custom_call_target="tpu_custom_call" | custom-call | tf_op jit(solution)/shard_map/pallas_call | solution.py:117
  49.7 0.0 copy-start.7
  49.7 0.0 copy-start.9
  49.8 0.0 copy-start.10
  49.8 0.0 copy-start.11
  49.8 6.0 %all-to-all-start.1 = ((bf16[16,64,512]{2,1,0:T(8,128)(2,1)}), bf16[16,64,512]{2,1,0:T(8,128)(2,1)S(1)}, u32[]{:S(2)}, u32[]{:S(2)}) async-start(bf16[16,64,512]{2,1,0:T(8,128)(2,1)} %get-tuple-element.9), calls=%async_computation.1 | async-start | bytes 2097152 | tf_op jit(solution)/shard_map/all_to_all | solution.py:446
  55.8 0.0 copy-done
  55.8 2.3 %collective-permute-start.1 = (bf16[64,512]{1,0:T(8,128)(2,1)S(1)}, bf16[64,512]{1,0:T(8,128)(2,1)S(1)}, u32[]{:S(2)}, u32[]{:S(2)}) collective-permute-start(bf16[64,512]{1,0:T(8,128)(2,1)S(1)} %get-tuple-element.14), channel_id=1, source_target_pairs={{1,0},{2,1},{3,2},{4,3},{5,4},{6,5},{7,6},{8,7},{9,8},{10,9},{11,1... | collective-permute-start | bytes 196616 | tf_op jit(solution)/shard_map/ppermute | solution.py:419
  58.1 4.2 %collective-permute-start = (bf16[64,512]{1,0:T(8,128)(2,1)S(1)}, bf16[64,512]{1,0:T(8,128)(2,1)S(1)}, u32[]{:S(2)}, u32[]{:S(2)}) collective-permute-start(bf16[64,512]{1,0:T(8,128)(2,1)S(1)} %get-tuple-element.15), channel_id=1, source_target_pairs={{0,1},{1,2},{2,3},{3,4},{4,5},{5,6},{6,7},{7,8},{8,9},{9,10},{10,1... | collective-permute-start | bytes 196616 | tf_op jit(solution)/shard_map/ppermute | solution.py:418
  62.3 0.2 reshape.9
  62.5 0.1 copy.36
  62.6 0.0 copy-done.12
  62.6 0.0 copy-start.3
  62.6 0.2 copy.30.band_ref
  62.9 18.5 %collective-permute-done.1.hi_ref = bf16[64,512]{1,0:T(8,128)(2,1)S(1)} collective-permute-done((bf16[64,512]{1,0:T(8,128)(2,1)S(1)}, bf16[64,512]{1,0:T(8,128)(2,1)S(1)}, u32[]{:S(2)}, u32[]{:S(2)}) %collective-permute-start.1) | collective-permute-done | bytes 65568 | tf_op jit(solution)/shard_map/ppermute | solution.py:419
  81.4 0.0 collective-permute-done.lo_ref
  81.4 0.0 all-to-all-done.1.arr_ref
  81.4 0.0 copy-start.1
  81.4 0.0 copy-done.7
  81.4 0.0 copy-done.9
  81.4 0.0 copy-done.10
  81.4 0.0 copy-done.11
  81.4 0.0 copy-start.17
  81.4 0.0 copy-start.8
  81.5 2.4 %shard_map.107 = (bf16[16,64,512]{2,1,0:T(8,128)(2,1)S(1)}, bf16[2,64,512]{2,1,0:T(8,128)(2,1)S(1)}) custom-call(s32[1,15]{1,0:T(1,128)S(1)} %copy-done.9, s32[1,17]{1,0:T(1,128)S(1)} %copy-done.10, s32[16]{0:T(128)S(1)} %copy-done.11, s32[16,2]{1,0:T(8,128)S(1)} %copy-done.7, bf16[1024,512]{1,0:T(8,128)(2,1)S(1)} %copy-done, ...), custom_call_target="tpu_custom_call" | custom-call | flops 113246208 | bytes 3145728 | tf_op jit(solution)/shard_map/pallas_call | solution.py:351
  83.9 0.0 copy-start.4
  83.9 1.0 copy-done.4
  84.9 4.4 %all-to-all-start.2 = ((bf16[16,64,512]{2,1,0:T(8,128)(2,1)}), bf16[16,64,512]{2,1,0:T(8,128)(2,1)}, u32[]{:S(2)}, u32[]{:S(2)}) async-start(bf16[16,64,512]{2,1,0:T(8,128)(2,1)} %copy-done.4), calls=%async_computation.2 | async-start | bytes 2097152 | tf_op jit(solution)/shard_map/all_to_all | solution.py:446
  89.3 0.0 copy-done.17
  89.3 0.7 copy.32.mix_ref
  90.0 5.3 %shard_map.110 = bf16[1024,4096]{1,0:T(8,128)(2,1)} custom-call(bf16[1024,512]{1,0:T(8,128)(2,1)S(1)} %copy-done, bf16[32,256]{1,0:T(8,128)(2,1)S(1)} %copy-done.8), custom_call_target="tpu_custom_call" | custom-call | flops 2147483648 | bytes 9437184 | tf_op jit(solution)/shard_map/pallas_call | solution.py:172
  95.4 2.3 %collective-permute-start.3 = (bf16[64,512]{1,0:T(8,128)(2,1)S(1)}, bf16[64,512]{1,0:T(8,128)(2,1)S(1)}, u32[]{:S(2)}, u32[]{:S(2)}) collective-permute-start(bf16[64,512]{1,0:T(8,128)(2,1)S(1)} %get-tuple-element.16), channel_id=1, source_target_pairs={{1,0},{2,1},{3,2},{4,3},{5,4},{6,5},{7,6},{8,7},{9,8},{10,9},{11,1... | collective-permute-start | bytes 196616 | tf_op jit(solution)/shard_map/ppermute | solution.py:419
  97.7 4.2 %collective-permute-start.2 = (bf16[64,512]{1,0:T(8,128)(2,1)S(1)}, bf16[64,512]{1,0:T(8,128)(2,1)S(1)}, u32[]{:S(2)}, u32[]{:S(2)}) collective-permute-start(bf16[64,512]{1,0:T(8,128)(2,1)S(1)} %get-tuple-element.17), channel_id=1, source_target_pairs={{0,1},{1,2},{2,3},{3,4},{4,5},{5,6},{6,7},{7,8},{8,9},{9,10},{10,1... | collective-permute-start | bytes 196616 | tf_op jit(solution)/shard_map/ppermute | solution.py:418
  101.9 8.3 %shard_map.108 = (bf16[1024,512]{1,0:T(8,128)(2,1)}, f32[1024,512]{1,0:T(8,128)}, f32[1024,512]{1,0:T(8,128)}) custom-call(s32[1,15]{1,0:T(1,128)} %col_ref.7, s32[1,17]{1,0:T(1,128)} %ptr_ref.7, bf16[1024,512]{1,0:T(8,128)(2,1)} %shard_map.105.h_hbm.field_ref.h_ref, bf16[64,512]{1,0:T(8,128)(2,1)} %copy-done.6, bf16[64,512]{1,0:T(8,128)(2,1)} %copy-done.5, ...), custom_call_target="tpu_custom_call" | custom-call | flops 1002438656 | bytes 10485760 | tf_op jit(solution)/shard_map/pallas_call | solution.py:371
  110.2 4.7 %collective-permute-done.3.hi_ref = bf16[64,512]{1,0:T(8,128)(2,1)S(1)} collective-permute-done((bf16[64,512]{1,0:T(8,128)(2,1)S(1)}, bf16[64,512]{1,0:T(8,128)(2,1)S(1)}, u32[]{:S(2)}, u32[]{:S(2)}) %collective-permute-start.3) | collective-permute-done | bytes 65568 | tf_op jit(solution)/shard_map/ppermute | solution.py:419
  114.9 0.0 collective-permute-done.2.lo_ref
  114.9 0.0 all-to-all-done.2.arr_ref
  114.9 0.6 copy-done.14
  115.5 0.0 copy-done.15
  115.5 6.0 %shard_map.109 = bf16[1024,512]{1,0:T(8,128)(2,1)} custom-call(s32[1,15]{1,0:T(1,128)} %col_ref.7, s32[1,17]{1,0:T(1,128)} %ptr_ref.7, bf16[64,512]{1,0:T(8,128)(2,1)} %copy-done.15, bf16[64,512]{1,0:T(8,128)(2,1)} %copy-done.14, bf16[16,64,512]{2,1,0:T(8,128)(2,1)} %all-to-all-done.2.arr_ref, bf16[1024,192]{1,0:T(8,128)(2,1)} %copy-done.2, ...), custom_call_target="tpu_custom_call" | custom-call | flops 339738624 | bytes 6291456 | tf_op jit(solution)/shard_map/pallas_call | solution.py:394
  (18 shorter events, 0.0 us)
Async XLA Ops:
  0.6 13.0 %copy-start.18 = (s32[16,2]{0,1:T(2,128)S(1)}, s32[16,2]{0,1:T(2,128)}, u32[]{:S(2)}) copy-start(s32[16,2]{0,1:T(2,128)} %param.17) | copy-start | bytes 388
  2.1 12.2 %all-to-all-start = ((s32[16,1,16]{2,1,0:T(1,128)}), s32[16,1,16]{2,1,0:T(1,128)S(1)}, u32[]{:S(2)}, u32[]{:S(2)}) async-start(s32[16,1,16]{2,1,0:T(1,128)} %bitcast.15), calls=%async_computation | async-start | bytes 16384 | tf_op jit(solution)/shard_map/all_to_all | solution.py:438
  13.6 42.2 %copy-start = (bf16[1024,512]{1,0:T(8,128)(2,1)S(1)}, bf16[1024,512]{1,0:T(8,128)(2,1)}, u32[]{:S(2)}) copy-start(bf16[1024,512]{1,0:T(8,128)(2,1)} %shard_map.105.h_hbm.field_ref.h_ref) | copy-start | bytes 3145732
  13.6 48.7 %copy-start.13 = (bf16[64,960]{1,0:T(8,128)(2,1)S(1)}, bf16[64,960]{1,0:T(8,128)(2,1)}, u32[]{:S(2)}) copy-start(bf16[64,960]{1,0:T(8,128)(2,1)} %param.14) | copy-start | bytes 368644
  14.3 0.6 copy-start.16
  14.9 47.7 %copy-start.12 = (bf16[1024,192]{0,1:T(8,128)(2,1)S(1)}, bf16[1024,192]{0,1:T(8,128)(2,1)}, u32[]{:S(2)}) copy-start(bf16[1024,192]{0,1:T(8,128)(2,1)} %param.13) | copy-start | bytes 1179652
  49.7 31.7 %copy-start.7 = (s32[16,2]{1,0:T(8,128)S(1)}, s32[16,2]{1,0:T(8,128)}, u32[]{:S(2)}) copy-start(s32[16,2]{1,0:T(8,128)} %copy.27.exp_ref) | copy-start | bytes 388
  49.7 31.7 %copy-start.9 = (s32[1,15]{1,0:T(1,128)S(1)}, s32[1,15]{1,0:T(1,128)}, u32[]{:S(2)}) copy-start(s32[1,15]{1,0:T(1,128)} %col_ref.7) | copy-start | bytes 184
  49.8 31.7 %copy-start.10 = (s32[1,17]{1,0:T(1,128)S(1)}, s32[1,17]{1,0:T(1,128)}, u32[]{:S(2)}) copy-start(s32[1,17]{1,0:T(1,128)} %ptr_ref.7) | copy-start | bytes 208
  49.8 31.7 %copy-start.11 = (s32[16]{0:T(128)S(1)}, s32[16]{0:T(128)}, u32[]{:S(2)}) copy-start(s32[16]{0:T(128)} %get-tuple-element.8.req_ref) | copy-start | bytes 196
  49.8 31.6 %all-to-all-start.1 = ((bf16[16,64,512]{2,1,0:T(8,128)(2,1)}), bf16[16,64,512]{2,1,0:T(8,128)(2,1)S(1)}, u32[]{:S(2)}, u32[]{:S(2)}) async-start(bf16[16,64,512]{2,1,0:T(8,128)(2,1)} %get-tuple-element.9), calls=%async_computation.1 | async-start | bytes 2097152 | tf_op jit(solution)/shard_map/all_to_all | solution.py:446
  55.8 25.5 %collective-permute-start.1 = (bf16[64,512]{1,0:T(8,128)(2,1)S(1)}, bf16[64,512]{1,0:T(8,128)(2,1)S(1)}, u32[]{:S(2)}, u32[]{:S(2)}) collective-permute-start(bf16[64,512]{1,0:T(8,128)(2,1)S(1)} %get-tuple-element.14), channel_id=1, source_target_pairs={{1,0},{2,1},{3,2},{4,3},{5,4},{6,5},{7,6},{8,7},{9,8},{10,9},{11,1... | collective-permute-start | bytes 196616 | tf_op jit(solution)/shard_map/ppermute | solution.py:419
  58.1 23.3 %collective-permute-start = (bf16[64,512]{1,0:T(8,128)(2,1)S(1)}, bf16[64,512]{1,0:T(8,128)(2,1)S(1)}, u32[]{:S(2)}, u32[]{:S(2)}) collective-permute-start(bf16[64,512]{1,0:T(8,128)(2,1)S(1)} %get-tuple-element.15), channel_id=1, source_target_pairs={{0,1},{1,2},{2,3},{3,4},{4,5},{5,6},{6,7},{7,8},{8,9},{9,10},{10,1... | collective-permute-start | bytes 196616 | tf_op jit(solution)/shard_map/ppermute | solution.py:418
  62.6 22.3 %copy-start.3 = (bf16[64,15,64]{2,0,1:T(8,128)(2,1)}, bf16[64,15,64]{2,0,1:T(8,128)(2,1)S(1)}, u32[]{:S(2)}) copy-start(bf16[64,15,64]{2,0,1:T(8,128)(2,1)S(1)} %copy.36) | copy-start | bytes 368644
  62.8 22.1 %copy-start.2 = (bf16[1024,192]{1,0:T(8,128)(2,1)}, bf16[1024,192]{1,0:T(8,128)(2,1)S(1)}, u32[]{:S(2)}) copy-start(bf16[1024,192]{1,0:T(8,128)(2,1)S(1)} %copy.30.band_ref) | copy-start | bytes 1179652
  81.4 3.6 %copy-start.5 = (bf16[64,512]{1,0:T(8,128)(2,1)}, bf16[64,512]{1,0:T(8,128)(2,1)S(1)}, u32[]{:S(2)}) copy-start(bf16[64,512]{1,0:T(8,128)(2,1)S(1)} %collective-permute-done.1.hi_ref) | copy-start | bytes 196612
  81.4 3.5 %copy-start.6 = (bf16[64,512]{1,0:T(8,128)(2,1)}, bf16[64,512]{1,0:T(8,128)(2,1)S(1)}, u32[]{:S(2)}) copy-start(bf16[64,512]{1,0:T(8,128)(2,1)S(1)} %collective-permute-done.lo_ref) | copy-start | bytes 196612
  81.4 3.5 %copy-start.1 = (bf16[16,64,512]{2,1,0:T(8,128)(2,1)}, bf16[16,64,512]{2,1,0:T(8,128)(2,1)S(1)}, u32[]{:S(2)}) copy-start(bf16[16,64,512]{2,1,0:T(8,128)(2,1)S(1)} %all-to-all-done.1.arr_ref) | copy-start | bytes 3145732
  81.4 7.9 %copy-start.17 = (bf16[96,32]{0,1:T(8,128)(2,1)S(1)}, bf16[96,32]{0,1:T(8,128)(2,1)}, u32[]{:S(2)}) copy-start(bf16[96,32]{0,1:T(8,128)(2,1)} %param.12) | copy-start | bytes 18436
  81.4 8.6 %copy-start.8 = (bf16[32,256]{1,0:T(8,128)(2,1)S(1)}, bf16[32,256]{1,0:T(8,128)(2,1)}, u32[]{:S(2)}) copy-start(bf16[32,256]{1,0:T(8,128)(2,1)} %sw_ref.1) | copy-start | bytes 49156
  83.9 1.0 copy-start.4
  84.9 30.0 %all-to-all-start.2 = ((bf16[16,64,512]{2,1,0:T(8,128)(2,1)}), bf16[16,64,512]{2,1,0:T(8,128)(2,1)}, u32[]{:S(2)}, u32[]{:S(2)}) async-start(bf16[16,64,512]{2,1,0:T(8,128)(2,1)} %copy-done.4), calls=%async_computation.2 | async-start | bytes 2097152 | tf_op jit(solution)/shard_map/all_to_all | solution.py:446
  95.4 19.5 %collective-permute-start.3 = (bf16[64,512]{1,0:T(8,128)(2,1)S(1)}, bf16[64,512]{1,0:T(8,128)(2,1)S(1)}, u32[]{:S(2)}, u32[]{:S(2)}) collective-permute-start(bf16[64,512]{1,0:T(8,128)(2,1)S(1)} %get-tuple-element.16), channel_id=1, source_target_pairs={{1,0},{2,1},{3,2},{4,3},{5,4},{6,5},{7,6},{8,7},{9,8},{10,9},{11,1... | collective-permute-start | bytes 196616 | tf_op jit(solution)/shard_map/ppermute | solution.py:419
  97.7 17.2 %collective-permute-start.2 = (bf16[64,512]{1,0:T(8,128)(2,1)S(1)}, bf16[64,512]{1,0:T(8,128)(2,1)S(1)}, u32[]{:S(2)}, u32[]{:S(2)}) collective-permute-start(bf16[64,512]{1,0:T(8,128)(2,1)S(1)} %get-tuple-element.17), channel_id=1, source_target_pairs={{0,1},{1,2},{2,3},{3,4},{4,5},{5,6},{6,7},{7,8},{8,9},{9,10},{10,1... | collective-permute-start | bytes 196616 | tf_op jit(solution)/shard_map/ppermute | solution.py:418
  114.9 0.6 copy-start.14
  114.9 0.6 copy-start.15

commit v14 on v12

--- a/solution.py
+++ b/solution.py
@@ -61,6 +61,24 @@
         h_ref[:, j * CHUNK : (j + 1) * CHUNK] = (
             jnp.tanh(pre[:, :CHUNK]) * jax.nn.sigmoid(pre[:, CHUNK:])
         ).astype(bf16)
+
+
+def prep_kernel(col_ref, ptr_ref, out_ref):
+    far_cap = col_ref.shape[1]
+    peers = out_ref.shape[0]
+    used = jnp.max(ptr_ref[...], axis=1, keepdims=True)
+    out_ref[:, :far_cap] = jnp.broadcast_to(col_ref[...], (peers, far_cap))
+    out_ref[:, far_cap:] = jnp.broadcast_to(used, (peers, 1))
+
+
+def prep(far_col, far_ptr):
+    far_cap = far_col.shape[1]
+    return pl.pallas_call(
+        prep_kernel,
+        in_specs=[vmem(), vmem()],
+        out_specs=vmem(),
+        out_shape=jax.ShapeDtypeStruct((far_cap + 1, far_cap + 1), jnp.int32),
+    )(far_col, far_ptr)
 
 
 def skip_kernel(h_ref, sw_ref, s_ref, ws):
@@ -376,11 +394,7 @@
     own_index = lax.axis_index("node")
     own_exports = lax.dynamic_slice_in_dim(export_block, own_index, 1, 0)[0].astype(jnp.int32)
     peer_count = far_cap + 1
-    info = jnp.concatenate([far_col[0], jnp.max(far_ptr[0], keepdims=True)]).astype(jnp.int32)
-    info_all = lax.all_to_all(
-        jnp.broadcast_to(info[None, :], (peer_count, far_cap + 1)),
-        "node", split_axis=0, concat_axis=0, tiled=True,
-    )
+    info_all = lax.all_to_all(prep(far_col, far_ptr), "node", split_axis=0, concat_axis=0, tiled=True)
     slot_ids = jnp.arange(far_cap, dtype=jnp.int32)
     cols_all = info_all[:, :far_cap]
     hits = (cols_all // EXPORT == own_index) & (slot_ids[None, :] < info_all[:, far_cap:])

time: 91.9 us -> 90.4 us (0.984)
  other arithmetic: 4.14 us -> 1.52 us
  Pallas kernels: 24 us -> 25.7 us
    pallas_call x0 -> x1, Pallas kernels: none -> 1.43 us  [prep(): pl.pallas_call(prep_kernel, in_specs=[vmem(), vmem()], out_specs=vmem(),...]
    concatenate x1 -> x0, other arithmetic: 1.37 us -> none  [local(): jnp.concatenate([far_col[0], jnp.max(far_ptr[0], keepdims=True)])]
    reduce_max x1 -> x0, other arithmetic: 1.3 us -> none  [local(): jnp.max(far_ptr[0], keepdims=True)]
where the time goes in v14:
time: 90.4 us; the launch traced here: 89.6 us
  starting transfers between devices  30 us (33%)
  Pallas kernels  25.7 us (28%)
  waiting for transfers between devices  23.1 us (26%)
  local copies, waits for them, and re-layouts  8.36 us (9%)
  other arithmetic  1.52 us (2%)
    ppermute x2, waiting for transfers between devices, halo(): hi = lax.ppermute(first, 'node', backward)  23.1 us
    all_to_all x2, starting transfers between devices, exchange(): return lax.all_to_all(send, 'node', split_axis=0, concat_axis=0, tiled=True)  10.5 us
    ppermute x2, starting transfers between devices, halo(): lo = lax.ppermute(last, 'node', forward)  8.39 us
    pallas_call x1, Pallas kernels, hop1(): pl.pallas_call(hop1_kernel, in_specs=[smem(), smem()] + [vmem()] * 6 + [h...  8.3 us
    all_to_all x1, starting transfers between devices, local(): lax.all_to_all(prep(far_col, far_ptr), 'node', split_axis=0, concat_axis=...  6.55 us
    pallas_call x1, Pallas kernels, hop2(): pl.pallas_call(hop2_kernel, in_specs=[smem(), smem()] + [vmem()] * 5 + [h...  6.06 us
    pallas_call x1, Pallas kernels, front_skip(): pl.pallas_call(skip_kernel, grid=(rows // tile,), in_specs=[pl.BlockSpec(...  5.34 us
    unnamed x39, local copies, waits for them, and re-layouts  4.98 us
  transfers between devices with their start and end apart: 7, of which 2 were waited for; matrix products, arithmetic and copies ran while one was open for 3% of the time, Pallas kernels for 18%

profile of v14, /device:TPU:15, one launch (start us, length us, event | category | flops | bytes accessed | tf_op | source)
XLA Modules:
  0.0 89.6 jit_solution(5431340347561341196)
XLA Ops:
  0.6 1.4 %shard_map.104 = s32[16,16]{1,0:T(8,128)} custom-call(s32[1,15]{1,0:T(1,128)} %col_ref.7, s32[1,17]{1,0:T(1,128)} %ptr_ref.7), custom_call_target="tpu_custom_call" | custom-call | tf_op jit(solution)/shard_map/pallas_call | solution.py:76
  2.1 6.6 %all-to-all-start = ((s32[16,1,16]{2,1,0:T(1,128)}), s32[16,1,16]{2,1,0:T(1,128)S(1)}, u32[]{:S(2)}, u32[]{:S(2)}) async-start(s32[16,1,16]{2,1,0:T(1,128)} %bitcast.24), calls=%async_computation | async-start | bytes 16384 | tf_op jit(solution)/shard_map/all_to_all | solution.py:397
  8.6 0.7 constant_dynamic-slice_fusion
  9.4 0.6 fusion.7
  9.9 1.6 %copy-done.4 = bf16[1024,1024]{1,0:T(8,128)(2,1)S(1)} copy-done((bf16[1024,1024]{1,0:T(8,128)(2,1)S(1)}, bf16[1024,1024]{1,0:T(8,128)(2,1)}, u32[]{:S(2)}) %copy-start.4) | copy-done | bytes 2097176
  11.5 0.7 copy-done.11
  12.3 2.4 %shard_map.105.field_ref.h_ref = bf16[1024,512]{1,0:T(8,128)(2,1)S(1)} custom-call(bf16[1024,1024]{1,0:T(8,128)(2,1)S(1)} %copy-done.4, bf16[64,64]{1,0:T(8,128)(2,1)S(1)} %copy-done.11), custom_call_target="tpu_custom_call" | custom-call | flops 1073741824 | bytes 3145728 | tf_op jit(solution)/shard_map/pallas_call | solution.py:102
  14.7 0.0 all-to-all-done
  14.7 0.2 slice_reduce_fusion
  14.9 0.2 fusion.2.req_ref
  15.0 1.3 %fusion.5 = s32[16]{0:T(128)S(1)} fusion(s32[16]{0:T(128)S(1)} %fusion.2.req_ref, s32[]{:T(128)} %bitcast.6, s32[]{:T(128)} %bitcast.5), kind=kLoop, calls=%fused_computation.21 | loop fusion | flops 128 | bytes 136 | tf_op jit(solution)/shard_map/select_n | solution.py:411
  16.4 0.0 copy-start.17
  16.4 0.0 copy-start.13
  16.4 1.6 %gather_fusion = bf16[16,64,512]{2,1,0:T(8,128)(2,1)} fusion(bf16[16,64,512]{2,1,0:T(8,128)(2,1)S(1)} %bitcast.18, s32[1024]{0:T(1024)S(1)} %pad_clamp_fusion), kind=kCustom, calls=%fused_computation | custom fusion | bytes 2097216 | tf_op jit(solution)/shard_map/gather | solution.py:411
  18.0 6.1 %all-to-all-start.1 = ((bf16[16,64,512]{2,1,0:T(8,128)(2,1)}), bf16[16,64,512]{2,1,0:T(8,128)(2,1)S(1)}, u32[]{:S(2)}, u32[]{:S(2)}) async-start(bf16[16,64,512]{2,1,0:T(8,128)(2,1)} %gather_fusion), calls=%async_computation.1 | async-start | bytes 2097152 | tf_op jit(solution)/shard_map/all_to_all | solution.py:409
  24.2 2.3 %collective-permute-start.1 = (bf16[64,512]{1,0:T(8,128)(2,1)S(1)}, bf16[64,512]{1,0:T(8,128)(2,1)S(1)}, u32[]{:S(2)}, u32[]{:S(2)}) collective-permute-start(bf16[64,512]{1,0:T(8,128)(2,1)S(1)} %get-tuple-element.10), channel_id=1, source_target_pairs={{1,0},{2,1},{3,2},{4,3},{5,4},{6,5},{7,6},{8,7},{9,8},{10,9},{11,1... | collective-permute-start | bytes 196616 | tf_op jit(solution)/shard_map/ppermute | solution.py:375
  26.4 4.2 %collective-permute-start = (bf16[64,512]{1,0:T(8,128)(2,1)S(1)}, bf16[64,512]{1,0:T(8,128)(2,1)S(1)}, u32[]{:S(2)}, u32[]{:S(2)}) collective-permute-start(bf16[64,512]{1,0:T(8,128)(2,1)S(1)} %get-tuple-element.11), channel_id=1, source_target_pairs={{0,1},{1,2},{2,3},{3,4},{4,5},{5,6},{6,7},{7,8},{8,9},{9,10},{10,1... | collective-permute-start | bytes 196616 | tf_op jit(solution)/shard_map/ppermute | solution.py:374
  30.7 0.1 copy.26.exp_ref
  30.7 0.2 reshape.39
  31.0 0.1 copy.33
  31.1 0.2 copy.27.band_ref
  31.3 0.0 copy-start.2
  31.3 18.4 %collective-permute-done.1.hi_ref = bf16[64,512]{1,0:T(8,128)(2,1)S(1)} collective-permute-done((bf16[64,512]{1,0:T(8,128)(2,1)S(1)}, bf16[64,512]{1,0:T(8,128)(2,1)S(1)}, u32[]{:S(2)}, u32[]{:S(2)}) %collective-permute-start.1) | collective-permute-done | bytes 65568 | tf_op jit(solution)/shard_map/ppermute | solution.py:375
  49.7 0.0 collective-permute-done.lo_ref
  49.7 0.0 all-to-all-done.1.arr_ref
  49.7 0.0 copy-start.1
  49.7 0.0 copy-done.9
  49.7 0.0 copy-done.10
  49.8 0.0 copy-start.16
  49.8 0.0 copy-start.8
  49.8 2.2 %shard_map.106 = (bf16[16,64,512]{2,1,0:T(8,128)(2,1)S(1)}, bf16[2,64,512]{2,1,0:T(8,128)(2,1)S(1)}) custom-call(s32[1,15]{1,0:T(1,128)S(1)} %copy-done.9, s32[1,17]{1,0:T(1,128)S(1)} %copy-done.10, s32[16]{0:T(128)S(1)} %fusion.2.req_ref, s32[16,2]{1,0:T(8,128)S(1)} %copy.26.exp_ref, bf16[1024,512]{1,0:T(8,128)(2,1)S(1)} %shard_map.105.field_ref.h_ref, ...), custom_call_target="tpu_custom_call" | custom-call | flops 113246208 | bytes 3145728 | tf_op jit(solution)/shard_map/pallas_call | solution.py:307
  51.9 0.0 copy-start.5
  52.0 1.0 %copy-done.5 = bf16[16,64,512]{2,1,0:T(8,128)(2,1)} copy-done((bf16[16,64,512]{2,1,0:T(8,128)(2,1)}, bf16[16,64,512]{2,1,0:T(8,128)(2,1)S(1)}, u32[]{:S(2)}) %copy-start.5) | copy-done | bytes 1048600
  52.9 0.0 copy-done.7
  52.9 0.0 copy-done.1
  52.9 4.4 %all-to-all-start.2 = ((bf16[16,64,512]{2,1,0:T(8,128)(2,1)}), bf16[16,64,512]{2,1,0:T(8,128)(2,1)}, u32[]{:S(2)}, u32[]{:S(2)}) async-start(bf16[16,64,512]{2,1,0:T(8,128)(2,1)} %copy-done.5), calls=%async_computation.2 | async-start | bytes 2097152 | tf_op jit(solution)/shard_map/all_to_all | solution.py:409
  57.3 0.0 copy-done.16
  57.3 0.7 copy.29.mix_ref
  58.0 5.3 %shard_map.109 = bf16[1024,4096]{1,0:T(8,128)(2,1)} custom-call(bf16[1024,512]{1,0:T(8,128)(2,1)S(1)} %shard_map.105.field_ref.h_ref, bf16[32,256]{1,0:T(8,128)(2,1)S(1)} %copy-done.8), custom_call_target="tpu_custom_call" | custom-call | flops 2147483648 | bytes 9437184 | tf_op jit(solution)/shard_map/pallas_call | solution.py:128
  63.4 2.3 %collective-permute-start.3 = (bf16[64,512]{1,0:T(8,128)(2,1)S(1)}, bf16[64,512]{1,0:T(8,128)(2,1)S(1)}, u32[]{:S(2)}, u32[]{:S(2)}) collective-permute-start(bf16[64,512]{1,0:T(8,128)(2,1)S(1)} %get-tuple-element.12), channel_id=1, source_target_pairs={{1,0},{2,1},{3,2},{4,3},{5,4},{6,5},{7,6},{8,7},{9,8},{10,9},{11,1... | collective-permute-start | bytes 196616 | tf_op jit(solution)/shard_map/ppermute | solution.py:375
  65.7 4.2 %collective-permute-start.2 = (bf16[64,512]{1,0:T(8,128)(2,1)S(1)}, bf16[64,512]{1,0:T(8,128)(2,1)S(1)}, u32[]{:S(2)}, u32[]{:S(2)}) collective-permute-start(bf16[64,512]{1,0:T(8,128)(2,1)S(1)} %get-tuple-element.13), channel_id=1, source_target_pairs={{0,1},{1,2},{2,3},{3,4},{4,5},{5,6},{6,7},{7,8},{8,9},{9,10},{10,1... | collective-permute-start | bytes 196616 | tf_op jit(solution)/shard_map/ppermute | solution.py:374
  69.9 8.3 %shard_map.107 = (bf16[1024,512]{1,0:T(8,128)(2,1)}, f32[1024,512]{1,0:T(8,128)}, f32[1024,512]{1,0:T(8,128)}) custom-call(s32[1,15]{1,0:T(1,128)} %col_ref.7, s32[1,17]{1,0:T(1,128)} %ptr_ref.7, bf16[1024,512]{1,0:T(8,128)(2,1)} %copy-done, bf16[64,512]{1,0:T(8,128)(2,1)} %copy-done.7, bf16[64,512]{1,0:T(8,128)(2,1)} %copy-done.6, ...), custom_call_target="tpu_custom_call" | custom-call | flops 1002438656 | bytes 10485760 | tf_op jit(solution)/shard_map/pallas_call | solution.py:327
  78.2 4.7 %collective-permute-done.3.hi_ref = bf16[64,512]{1,0:T(8,128)(2,1)S(1)} collective-permute-done((bf16[64,512]{1,0:T(8,128)(2,1)S(1)}, bf16[64,512]{1,0:T(8,128)(2,1)S(1)}, u32[]{:S(2)}, u32[]{:S(2)}) %collective-permute-start.3) | collective-permute-done | bytes 65568 | tf_op jit(solution)/shard_map/ppermute | solution.py:375
  82.9 0.0 collective-permute-done.2.lo_ref
  82.9 0.0 all-to-all-done.2.arr_ref
  82.9 0.6 copy-done.14
  83.5 0.0 copy-done.15
  83.5 6.1 %shard_map.108 = bf16[1024,512]{1,0:T(8,128)(2,1)} custom-call(s32[1,15]{1,0:T(1,128)} %col_ref.7, s32[1,17]{1,0:T(1,128)} %ptr_ref.7, bf16[64,512]{1,0:T(8,128)(2,1)} %copy-done.15, bf16[64,512]{1,0:T(8,128)(2,1)} %copy-done.14, bf16[16,64,512]{2,1,0:T(8,128)(2,1)} %all-to-all-done.2.arr_ref, bf16[1024,192]{1,0:T(8,128)(2,1)} %copy-done.2, ...), custom_call_target="tpu_custom_call" | custom-call | flops 339738624 | bytes 6291456 | tf_op jit(solution)/shard_map/pallas_call | solution.py:350
  (22 shorter events, 0.1 us)
Async XLA Ops:
  2.1 12.6 %all-to-all-start = ((s32[16,1,16]{2,1,0:T(1,128)}), s32[16,1,16]{2,1,0:T(1,128)S(1)}, u32[]{:S(2)}, u32[]{:S(2)}) async-start(s32[16,1,16]{2,1,0:T(1,128)} %bitcast.24), calls=%async_computation | async-start | bytes 16384 | tf_op jit(solution)/shard_map/all_to_all | solution.py:397
  9.9 1.6 %copy-start.4 = (bf16[1024,1024]{1,0:T(8,128)(2,1)S(1)}, bf16[1024,1024]{1,0:T(8,128)(2,1)}, u32[]{:S(2)}) copy-start(bf16[1024,1024]{1,0:T(8,128)(2,1)} %x_hbm.1) | copy-start | bytes 6291460
  11.5 0.7 copy-start.11
  14.7 43.4 %copy-start = (bf16[1024,512]{1,0:T(8,128)(2,1)}, bf16[1024,512]{1,0:T(8,128)(2,1)S(1)}, u32[]{:S(2)}) copy-start(bf16[1024,512]{1,0:T(8,128)(2,1)S(1)} %shard_map.105.field_ref.h_ref) | copy-start | bytes 3145732
  16.4 14.3 %copy-start.17 = (s32[16,2]{0,1:T(2,128)S(1)}, s32[16,2]{0,1:T(2,128)}, u32[]{:S(2)}) copy-start(s32[16,2]{0,1:T(2,128)} %param.17) | copy-start | bytes 388
  16.4 14.3 %copy-start.13 = (bf16[64,960]{1,0:T(8,128)(2,1)S(1)}, bf16[64,960]{1,0:T(8,128)(2,1)}, u32[]{:S(2)}) copy-start(bf16[64,960]{1,0:T(8,128)(2,1)} %param.14) | copy-start | bytes 368644
  18.0 13.0 %copy-start.12 = (bf16[1024,192]{0,1:T(8,128)(2,1)S(1)}, bf16[1024,192]{0,1:T(8,128)(2,1)}, u32[]{:S(2)}) copy-start(bf16[1024,192]{0,1:T(8,128)(2,1)} %param.13) | copy-start | bytes 1179652
  18.0 31.7 %copy-start.9 = (s32[1,15]{1,0:T(1,128)S(1)}, s32[1,15]{1,0:T(1,128)}, u32[]{:S(2)}) copy-start(s32[1,15]{1,0:T(1,128)} %col_ref.7) | copy-start | bytes 184
  18.0 31.7 %copy-start.10 = (s32[1,17]{1,0:T(1,128)S(1)}, s32[1,17]{1,0:T(1,128)}, u32[]{:S(2)}) copy-start(s32[1,17]{1,0:T(1,128)} %ptr_ref.7) | copy-start | bytes 208
  18.0 31.7 %all-to-all-start.1 = ((bf16[16,64,512]{2,1,0:T(8,128)(2,1)}), bf16[16,64,512]{2,1,0:T(8,128)(2,1)S(1)}, u32[]{:S(2)}, u32[]{:S(2)}) async-start(bf16[16,64,512]{2,1,0:T(8,128)(2,1)} %gather_fusion), calls=%async_computation.1 | async-start | bytes 2097152 | tf_op jit(solution)/shard_map/all_to_all | solution.py:409
  24.2 25.5 %collective-permute-start.1 = (bf16[64,512]{1,0:T(8,128)(2,1)S(1)}, bf16[64,512]{1,0:T(8,128)(2,1)S(1)}, u32[]{:S(2)}, u32[]{:S(2)}) collective-permute-start(bf16[64,512]{1,0:T(8,128)(2,1)S(1)} %get-tuple-element.10), channel_id=1, source_target_pairs={{1,0},{2,1},{3,2},{4,3},{5,4},{6,5},{7,6},{8,7},{9,8},{10,9},{11,1... | collective-permute-start | bytes 196616 | tf_op jit(solution)/shard_map/ppermute | solution.py:375
  26.4 23.3 %collective-permute-start = (bf16[64,512]{1,0:T(8,128)(2,1)S(1)}, bf16[64,512]{1,0:T(8,128)(2,1)S(1)}, u32[]{:S(2)}, u32[]{:S(2)}) collective-permute-start(bf16[64,512]{1,0:T(8,128)(2,1)S(1)} %get-tuple-element.11), channel_id=1, source_target_pairs={{0,1},{1,2},{2,3},{3,4},{4,5},{5,6},{6,7},{7,8},{8,9},{9,10},{10,1... | collective-permute-start | bytes 196616 | tf_op jit(solution)/shard_map/ppermute | solution.py:374
  31.0 21.9 %copy-start.3 = (bf16[64,15,64]{2,0,1:T(8,128)(2,1)}, bf16[64,15,64]{2,0,1:T(8,128)(2,1)S(1)}, u32[]{:S(2)}) copy-start(bf16[64,15,64]{2,0,1:T(8,128)(2,1)S(1)} %copy.33) | copy-start | bytes 368644
  31.3 21.7 %copy-start.2 = (bf16[1024,192]{1,0:T(8,128)(2,1)}, bf16[1024,192]{1,0:T(8,128)(2,1)S(1)}, u32[]{:S(2)}) copy-start(bf16[1024,192]{1,0:T(8,128)(2,1)S(1)} %copy.27.band_ref) | copy-start | bytes 1179652
  49.7 3.2 %copy-start.6 = (bf16[64,512]{1,0:T(8,128)(2,1)}, bf16[64,512]{1,0:T(8,128)(2,1)S(1)}, u32[]{:S(2)}) copy-start(bf16[64,512]{1,0:T(8,128)(2,1)S(1)} %collective-permute-done.1.hi_ref) | copy-start | bytes 196612
  49.7 3.2 %copy-start.7 = (bf16[64,512]{1,0:T(8,128)(2,1)}, bf16[64,512]{1,0:T(8,128)(2,1)S(1)}, u32[]{:S(2)}) copy-start(bf16[64,512]{1,0:T(8,128)(2,1)S(1)} %collective-permute-done.lo_ref) | copy-start | bytes 196612
  49.7 3.2 %copy-start.1 = (bf16[16,64,512]{2,1,0:T(8,128)(2,1)}, bf16[16,64,512]{2,1,0:T(8,128)(2,1)S(1)}, u32[]{:S(2)}) copy-start(bf16[16,64,512]{2,1,0:T(8,128)(2,1)S(1)} %all-to-all-done.1.arr_ref) | copy-start | bytes 3145732
  49.8 7.6 %copy-start.16 = (bf16[96,32]{0,1:T(8,128)(2,1)S(1)}, bf16[96,32]{0,1:T(8,128)(2,1)}, u32[]{:S(2)}) copy-start(bf16[96,32]{0,1:T(8,128)(2,1)} %param.12) | copy-start | bytes 18436
  49.8 8.3 %copy-start.8 = (bf16[32,256]{1,0:T(8,128)(2,1)S(1)}, bf16[32,256]{1,0:T(8,128)(2,1)}, u32[]{:S(2)}) copy-start(bf16[32,256]{1,0:T(8,128)(2,1)} %sw_ref.1) | copy-start | bytes 49156
  51.9 1.0 %copy-start.5 = (bf16[16,64,512]{2,1,0:T(8,128)(2,1)}, bf16[16,64,512]{2,1,0:T(8,128)(2,1)S(1)}, u32[]{:S(2)}) copy-start(bf16[16,64,512]{2,1,0:T(8,128)(2,1)S(1)} %get-tuple-element.7) | copy-start | bytes 3145732
  52.9 30.0 %all-to-all-start.2 = ((bf16[16,64,512]{2,1,0:T(8,128)(2,1)}), bf16[16,64,512]{2,1,0:T(8,128)(2,1)}, u32[]{:S(2)}, u32[]{:S(2)}) async-start(bf16[16,64,512]{2,1,0:T(8,128)(2,1)} %copy-done.5), calls=%async_computation.2 | async-start | bytes 2097152 | tf_op jit(solution)/shard_map/all_to_all | solution.py:409
  63.4 19.5 %collective-permute-start.3 = (bf16[64,512]{1,0:T(8,128)(2,1)S(1)}, bf16[64,512]{1,0:T(8,128)(2,1)S(1)}, u32[]{:S(2)}, u32[]{:S(2)}) collective-permute-start(bf16[64,512]{1,0:T(8,128)(2,1)S(1)} %get-tuple-element.12), channel_id=1, source_target_pairs={{1,0},{2,1},{3,2},{4,3},{5,4},{6,5},{7,6},{8,7},{9,8},{10,9},{11,1... | collective-permute-start | bytes 196616 | tf_op jit(solution)/shard_map/ppermute | solution.py:375
  65.7 17.2 %collective-permute-start.2 = (bf16[64,512]{1,0:T(8,128)(2,1)S(1)}, bf16[64,512]{1,0:T(8,128)(2,1)S(1)}, u32[]{:S(2)}, u32[]{:S(2)}) collective-permute-start(bf16[64,512]{1,0:T(8,128)(2,1)S(1)} %get-tuple-element.13), channel_id=1, source_target_pairs={{0,1},{1,2},{2,3},{3,4},{4,5},{5,6},{6,7},{7,8},{8,9},{9,10},{10,1... | collective-permute-start | bytes 196616 | tf_op jit(solution)/shard_map/ppermute | solution.py:374
  82.9 0.6 copy-start.14
  82.9 0.6 copy-start.15

commit v15 on v14

--- a/solution.py
+++ b/solution.py
@@ -40,27 +40,28 @@
     return jnp.where(mask, tiled, 0.0).astype(bf16)
 
 
-def hidden_kernel(x_ref, fgw_ref, h_ref, wlo, whi):
-    half = x_ref.shape[1] // 2
+def hidden_kernel(exp_ref, x_ref, fgw_ref, h_ref, ex_ref):
+    rows, cols = x_ref.shape
+    half = cols // 2
     cw = fgw_ref.shape[0] // 2
     per = CHUNK // cw
-
-    @pl.when(pl.program_id(0) == 0)
-    def _():
-        w = fgw_ref[...]
-        wlo[:, :CHUNK] = bd_inkernel(w[:cw, :cw], per)
-        wlo[:, CHUNK:] = bd_inkernel(w[:cw, cw:], per)
-        whi[:, :CHUNK] = bd_inkernel(w[cw:, :cw], per)
-        whi[:, CHUNK:] = bd_inkernel(w[cw:, cw:], per)
-
-    for j in range(half // CHUNK):
-        x0 = x_ref[:, j * CHUNK : (j + 1) * CHUNK]
-        x1 = x_ref[:, half + j * CHUNK : half + (j + 1) * CHUNK]
-        pre = jnp.dot(x0, wlo[...], preferred_element_type=f32)
-        pre = pre + jnp.dot(x1, whi[...], preferred_element_type=f32)
-        h_ref[:, j * CHUNK : (j + 1) * CHUNK] = (
-            jnp.tanh(pre[:, :CHUNK]) * jax.nn.sigmoid(pre[:, CHUNK:])
-        ).astype(bf16)
+    w = fgw_ref[...]
+    wlo = jnp.concatenate([bd_inkernel(w[:cw, :cw], per), bd_inkernel(w[:cw, cw:], per)], axis=1)
+    whi = jnp.concatenate([bd_inkernel(w[cw:, :cw], per), bd_inkernel(w[cw:, cw:], per)], axis=1)
+    tile = min(ROW_TILE, rows)
+    for t in range(rows // tile):
+        rs = slice(t * tile, (t + 1) * tile)
+        for j in range(half // CHUNK):
+            x0 = x_ref[rs, j * CHUNK : (j + 1) * CHUNK]
+            x1 = x_ref[rs, half + j * CHUNK : half + (j + 1) * CHUNK]
+            pre = jnp.dot(x0, wlo, preferred_element_type=f32)
+            pre = pre + jnp.dot(x1, whi, preferred_element_type=f32)
+            h_ref[rs, j * CHUNK : (j + 1) * CHUNK] = (
+                jnp.tanh(pre[:, :CHUNK]) * jax.nn.sigmoid(pre[:, CHUNK:])
+            ).astype(bf16)
+    own = lax.axis_index("node")
+    for e in range(ex_ref.shape[0]):
+        ex_ref[e] = h_ref[pl.ds(pl.multiple_of(exp_ref[own, e] * BLK, BLK), BLK), :]
 
 
 def prep_kernel(col_ref, ptr_ref, out_ref):
@@ -95,27 +96,24 @@
         ).astype(bf16)
 
 
-def front_hidden(features, fgw):
+def front_hidden(export_block, features, fgw):
     rows, cols = features.shape
-    chunks = cols // 2 // CHUNK
-    tile = min(ROW_TILE, rows)
+    half = cols // 2
     return pl.pallas_call(
         hidden_kernel,
-        grid=(rows // tile,),
-        in_specs=[
-            pl.BlockSpec((tile, cols), lambda i: (i, 0)),
-            pl.BlockSpec(fgw.shape, lambda i: (0, 0)),
+        in_specs=[smem(), vmem(), vmem()],
+        out_specs=[vmem(), vmem()],
+        out_shape=[
+            jax.ShapeDtypeStruct((rows, half), bf16),
+            jax.ShapeDtypeStruct((export_block.shape[1], BLK, half), bf16),
         ],
-        out_specs=pl.BlockSpec((tile, chunks * CHUNK), lambda i: (i, 0)),
-        out_shape=jax.ShapeDtypeStruct((rows, chunks * CHUNK), bf16),
-        scratch_shapes=[pltpu.VMEM((CHUNK, 2 * CHUNK), bf16), pltpu.VMEM((CHUNK, 2 * CHUNK), bf16)],
         compiler_params=pltpu.CompilerParams(vmem_limit_bytes=48 * 1024 * 1024),
         cost_estimate=pl.CostEstimate(
-            flops=2 * rows * CHUNK * 4 * CHUNK * chunks,
-            transcendentals=rows * CHUNK * chunks * 2,
-            bytes_accessed=2 * rows * (cols + CHUNK * chunks),
+            flops=2 * rows * CHUNK * 4 * CHUNK * (half // CHUNK),
+            transcendentals=rows * half * 2,
+            bytes_accessed=2 * rows * (cols + half),
         ),
-    )(features, fgw)
+    )(export_block, features, fgw)
 
 
 def front_skip(hidden, skip_weight):
@@ -399,8 +397,7 @@
     cols_all = info_all[:, :far_cap]
     hits = (cols_all // EXPORT == own_index) & (slot_ids[None, :] < info_all[:, far_cap:])
     requested = jnp.sum(jnp.where(hits, cols_all % EXPORT, 0), axis=1).astype(jnp.int32)
-    send_rows = own_exports[requested].astype(jnp.int32)
-    hidden = front_hidden(features, filter_gate_weight)
+    hidden, ex2 = front_hidden(export_block, features, filter_gate_weight)
     blocks = node_rows // BLK
     width = hidden.shape[1]
     farw3 = far_weight.reshape(BLK, far_cap, BLK).transpose(1, 0, 2)
@@ -408,7 +405,7 @@
     def exchange(send):
         return lax.all_to_all(send, "node", split_axis=0, concat_axis=0, tiled=True)
 
-    arrived1 = exchange(hidden.reshape(blocks, BLK, width)[send_rows])
+    arrived1 = exchange(jnp.where((requested == 0)[:, None, None], ex2[0][None], ex2[1][None]))
     lo1, hi1 = halo(hidden[:BLK], hidden[node_rows - BLK :])
     skip_out = front_skip(hidden, skip_weight)
     send2, edge = early(

time: 90.4 us -> 88.3 us (0.977)
  local copies, waits for them, and re-layouts: 8.36 us -> 6.13 us
    gather x2 -> x0, local copies, waits for them, and re-layouts: 2.16 us -> none  [the longest x1 1.58 us: local(): arrived1 = exchange(hidden.reshape(blocks, BLK, width)[send_rows])]
    unnamed x39 -> x37, local copies, waits for them, and re-layouts: 4.98 us -> 5.64 us
  transfers between devices with their start and end apart: 7 -> 7, of which waited for: 2 -> 2; matrix products, arithmetic and copies ran while one was open for 3% -> 2% of each run, Pallas kernels for 18% -> 18%
where the time goes in v15:
time: 88.3 us; the launch traced here: 87.3 us
  starting transfers between devices  30.3 us (34%)
  Pallas kernels  25.4 us (29%)
  waiting for transfers between devices  23.2 us (26%)
  local copies, waits for them, and re-layouts  6.13 us (7%)
  other arithmetic  1.3 us (1%)
    ppermute x2, waiting for transfers between devices, halo(): hi = lax.ppermute(first, 'node', backward)  23.2 us
    all_to_all x2, starting transfers between devices, exchange(): return lax.all_to_all(send, 'node', split_axis=0, concat_axis=0, tiled=True)  10.8 us
    ppermute x2, starting transfers between devices, halo(): lo = lax.ppermute(last, 'node', forward)  8.39 us
    pallas_call x1, Pallas kernels, hop1(): pl.pallas_call(hop1_kernel, in_specs=[smem(), smem()] + [vmem()] * 6 + [h...  8.3 us
    all_to_all x1, starting transfers between devices, local(): lax.all_to_all(prep(far_col, far_ptr), 'node', split_axis=0, concat_axis=...  6.55 us
    pallas_call x1, Pallas kernels, hop2(): pl.pallas_call(hop2_kernel, in_specs=[smem(), smem()] + [vmem()] * 5 + [h...  6.07 us
    unnamed x37, local copies, waits for them, and re-layouts  5.64 us
    pallas_call x1, Pallas kernels, front_skip(): pl.pallas_call(skip_kernel, grid=(rows // tile,), in_specs=[pl.BlockSpec(...  5.34 us
  transfers between devices with their start and end apart: 7, of which 2 were waited for; matrix products, arithmetic and copies ran while one was open for 2% of the time, Pallas kernels for 18%

profile of v15, /device:TPU:15, one launch (start us, length us, event | category | flops | bytes accessed | tf_op | source)
XLA Modules:
  0.0 87.3 jit_solution(7025218688666269232)
XLA Ops:
  0.6 1.4 %shard_map.104 = s32[16,16]{1,0:T(8,128)} custom-call(s32[1,15]{1,0:T(1,128)} %col_ref.7, s32[1,17]{1,0:T(1,128)} %ptr_ref.7), custom_call_target="tpu_custom_call" | custom-call | tf_op jit(solution)/shard_map/pallas_call | solution.py:77
  2.1 6.6 %all-to-all-start = ((s32[16,1,16]{2,1,0:T(1,128)}), s32[16,1,16]{2,1,0:T(1,128)S(1)}, u32[]{:S(2)}, u32[]{:S(2)}) async-start(s32[16,1,16]{2,1,0:T(1,128)} %bitcast.20), calls=%async_computation | async-start | bytes 16384 | tf_op jit(solution)/shard_map/all_to_all | solution.py:395
  8.6 0.8 copy.29.exp_ref
  9.4 1.6 %copy-done.4 = bf16[1024,1024]{1,0:T(8,128)(2,1)S(1)} copy-done((bf16[1024,1024]{1,0:T(8,128)(2,1)S(1)}, bf16[1024,1024]{1,0:T(8,128)(2,1)}, u32[]{:S(2)}) %copy-start.4) | copy-done | bytes 2097176
  11.0 0.7 copy-done.11
  11.7 2.5 %shard_map.105 = (bf16[1024,512]{1,0:T(8,128)(2,1)S(1)}, bf16[2,64,512]{2,1,0:T(8,128)(2,1)S(1)}) custom-call(s32[16,2]{1,0:T(8,128)S(1)} %copy.29.exp_ref, bf16[1024,1024]{1,0:T(8,128)(2,1)S(1)} %copy-done.4, bf16[64,64]{1,0:T(8,128)(2,1)S(1)} %copy-done.11), custom_call_target="tpu_custom_call" | custom-call | flops 1073741824 | bytes 3145728 | tf_op jit(solution)/shard_map/pallas_call | solution.py:102
  14.1 0.0 copy-start
  14.1 0.0 copy-start.13
  14.2 0.0 all-to-all-done
  14.2 0.2 slice_reduce_fusion
  14.4 0.2 fusion.2.req_ref
  14.6 0.0 copy-start.12
  14.6 1.1 %broadcast_select_fusion = bf16[16,64,512]{2,1,0:T(8,128)(2,1)} fusion(pred[16]{0:T(512)(128)(4,1)S(1)} %broadcast_compare_fusion, bf16[64,512]{1,0:T(8,128)(2,1)S(1)} %get-tuple-element.19, bf16[64,512]{1,0:T(8,128)(2,1)S(1)} %get-tuple-element.18), kind=kLoop, calls=%fused_computation | loop fusion | flops 524288 | bytes 1179664 | tf_op jit(solution)/shard_map/jit(_where)/select_n | solution.py:408
  15.7 6.2 %all-to-all-start.1 = ((bf16[16,64,512]{2,1,0:T(8,128)(2,1)}), bf16[16,64,512]{2,1,0:T(8,128)(2,1)S(1)}, u32[]{:S(2)}, u32[]{:S(2)}) async-start(bf16[16,64,512]{2,1,0:T(8,128)(2,1)} %broadcast_select_fusion), calls=%async_computation.1 | async-start | bytes 2097152 | tf_op jit(solution)/shard_map/all_to_all | solution.py:406
  21.9 2.3 %collective-permute-start.1 = (bf16[64,512]{1,0:T(8,128)(2,1)S(1)}, bf16[64,512]{1,0:T(8,128)(2,1)S(1)}, u32[]{:S(2)}, u32[]{:S(2)}) collective-permute-start(bf16[64,512]{1,0:T(8,128)(2,1)S(1)} %get-tuple-element.14), channel_id=1, source_target_pairs={{1,0},{2,1},{3,2},{4,3},{5,4},{6,5},{7,6},{8,7},{9,8},{10,9},{11,1... | collective-permute-start | bytes 196616 | tf_op jit(solution)/shard_map/ppermute | solution.py:373
  24.1 4.2 %collective-permute-start = (bf16[64,512]{1,0:T(8,128)(2,1)S(1)}, bf16[64,512]{1,0:T(8,128)(2,1)S(1)}, u32[]{:S(2)}, u32[]{:S(2)}) collective-permute-start(bf16[64,512]{1,0:T(8,128)(2,1)S(1)} %get-tuple-element.15), channel_id=1, source_target_pairs={{0,1},{1,2},{2,3},{3,4},{4,5},{5,6},{6,7},{7,8},{8,9},{9,10},{10,1... | collective-permute-start | bytes 196616 | tf_op jit(solution)/shard_map/ppermute | solution.py:372
  28.3 0.0 copy-done.13
  28.3 0.2 reshape.12
  28.6 0.1 copy.36
  28.6 0.0 copy-done.12
  28.7 0.0 copy-start.3
  28.7 0.2 copy.30.band_ref
  28.9 0.0 copy-start.2
  28.9 18.5 %collective-permute-done.1.hi_ref = bf16[64,512]{1,0:T(8,128)(2,1)S(1)} collective-permute-done((bf16[64,512]{1,0:T(8,128)(2,1)S(1)}, bf16[64,512]{1,0:T(8,128)(2,1)S(1)}, u32[]{:S(2)}, u32[]{:S(2)}) %collective-permute-start.1) | collective-permute-done | bytes 65568 | tf_op jit(solution)/shard_map/ppermute | solution.py:373
  47.4 0.0 collective-permute-done.lo_ref
  47.4 0.0 all-to-all-done.1.arr_ref
  47.4 0.0 copy-start.1
  47.4 0.0 copy-start.16
  47.5 0.0 copy-start.8
  47.5 1.9 %shard_map.106 = (bf16[16,64,512]{2,1,0:T(8,128)(2,1)S(1)}, bf16[2,64,512]{2,1,0:T(8,128)(2,1)S(1)}) custom-call(s32[1,15]{1,0:T(1,128)S(1)} %copy-done.9, s32[1,17]{1,0:T(1,128)S(1)} %copy-done.10, s32[16]{0:T(128)S(1)} %fusion.2.req_ref, s32[16,2]{1,0:T(8,128)S(1)} %copy.29.exp_ref, bf16[1024,512]{1,0:T(8,128)(2,1)S(1)} %get-tuple-element.8.field_ref.h_ref, ...), custom_call_target="tpu_custom_call" | custom-call | flops 113246208 | bytes 3145728 | tf_op jit(solution)/shard_map/pallas_call | solution.py:305
  49.3 0.0 copy-start.5
  49.3 1.0 %copy-done.5 = bf16[16,64,512]{2,1,0:T(8,128)(2,1)} copy-done((bf16[16,64,512]{2,1,0:T(8,128)(2,1)}, bf16[16,64,512]{2,1,0:T(8,128)(2,1)S(1)}, u32[]{:S(2)}) %copy-start.5) | copy-done | bytes 1048600
  50.3 0.0 copy-done.3
  50.3 0.0 copy-done.6
  50.3 4.7 %all-to-all-start.2 = ((bf16[16,64,512]{2,1,0:T(8,128)(2,1)}), bf16[16,64,512]{2,1,0:T(8,128)(2,1)}, u32[]{:S(2)}, u32[]{:S(2)}) async-start(bf16[16,64,512]{2,1,0:T(8,128)(2,1)} %copy-done.5), calls=%async_computation.2 | async-start | bytes 2097152 | tf_op jit(solution)/shard_map/all_to_all | solution.py:406
  55.0 0.0 copy-done.16
  55.0 0.7 copy.32.mix_ref
  55.7 0.0 copy-done.8
  55.7 5.3 %shard_map.109 = bf16[1024,4096]{1,0:T(8,128)(2,1)} custom-call(bf16[1024,512]{1,0:T(8,128)(2,1)S(1)} %get-tuple-element.8.field_ref.h_ref, bf16[32,256]{1,0:T(8,128)(2,1)S(1)} %copy-done.8), custom_call_target="tpu_custom_call" | custom-call | flops 2147483648 | bytes 9437184 | tf_op jit(solution)/shard_map/pallas_call | solution.py:126
  61.1 2.3 %collective-permute-start.3 = (bf16[64,512]{1,0:T(8,128)(2,1)S(1)}, bf16[64,512]{1,0:T(8,128)(2,1)S(1)}, u32[]{:S(2)}, u32[]{:S(2)}) collective-permute-start(bf16[64,512]{1,0:T(8,128)(2,1)S(1)} %get-tuple-element.16), channel_id=1, source_target_pairs={{1,0},{2,1},{3,2},{4,3},{5,4},{6,5},{7,6},{8,7},{9,8},{10,9},{11,1... | collective-permute-start | bytes 196616 | tf_op jit(solution)/shard_map/ppermute | solution.py:373
  63.4 4.2 %collective-permute-start.2 = (bf16[64,512]{1,0:T(8,128)(2,1)S(1)}, bf16[64,512]{1,0:T(8,128)(2,1)S(1)}, u32[]{:S(2)}, u32[]{:S(2)}) collective-permute-start(bf16[64,512]{1,0:T(8,128)(2,1)S(1)} %get-tuple-element.17), channel_id=1, source_target_pairs={{0,1},{1,2},{2,3},{3,4},{4,5},{5,6},{6,7},{7,8},{8,9},{9,10},{10,1... | collective-permute-start | bytes 196616 | tf_op jit(solution)/shard_map/ppermute | solution.py:372
  67.6 8.3 %shard_map.107 = (bf16[1024,512]{1,0:T(8,128)(2,1)}, f32[1024,512]{1,0:T(8,128)}, f32[1024,512]{1,0:T(8,128)}) custom-call(s32[1,15]{1,0:T(1,128)} %col_ref.7, s32[1,17]{1,0:T(1,128)} %ptr_ref.7, bf16[1024,512]{1,0:T(8,128)(2,1)} %copy-done, bf16[64,512]{1,0:T(8,128)(2,1)} %copy-done.7, bf16[64,512]{1,0:T(8,128)(2,1)} %copy-done.6, ...), custom_call_target="tpu_custom_call" | custom-call | flops 1002438656 | bytes 10485760 | tf_op jit(solution)/shard_map/pallas_call | solution.py:325
  75.9 4.7 %collective-permute-done.3.hi_ref = bf16[64,512]{1,0:T(8,128)(2,1)S(1)} collective-permute-done((bf16[64,512]{1,0:T(8,128)(2,1)S(1)}, bf16[64,512]{1,0:T(8,128)(2,1)S(1)}, u32[]{:S(2)}, u32[]{:S(2)}) %collective-permute-start.3) | collective-permute-done | bytes 65568 | tf_op jit(solution)/shard_map/ppermute | solution.py:373
  80.6 0.0 collective-permute-done.2.lo_ref
  80.6 0.0 all-to-all-done.2.arr_ref
  80.6 0.6 copy-done.14
  81.2 0.0 copy-done.15
  81.2 6.1 %shard_map.108 = bf16[1024,512]{1,0:T(8,128)(2,1)} custom-call(s32[1,15]{1,0:T(1,128)} %col_ref.7, s32[1,17]{1,0:T(1,128)} %ptr_ref.7, bf16[64,512]{1,0:T(8,128)(2,1)} %copy-done.15, bf16[64,512]{1,0:T(8,128)(2,1)} %copy-done.14, bf16[16,64,512]{2,1,0:T(8,128)(2,1)} %all-to-all-done.2.arr_ref, bf16[1024,192]{1,0:T(8,128)(2,1)} %copy-done.2, ...), custom_call_target="tpu_custom_call" | custom-call | flops 339738624 | bytes 6291456 | tf_op jit(solution)/shard_map/pallas_call | solution.py:348
  (18 shorter events, 0.1 us)
Async XLA Ops:
  2.1 12.1 %all-to-all-start = ((s32[16,1,16]{2,1,0:T(1,128)}), s32[16,1,16]{2,1,0:T(1,128)S(1)}, u32[]{:S(2)}, u32[]{:S(2)}) async-start(s32[16,1,16]{2,1,0:T(1,128)} %bitcast.20), calls=%async_computation | async-start | bytes 16384 | tf_op jit(solution)/shard_map/all_to_all | solution.py:395
  9.4 1.6 %copy-start.4 = (bf16[1024,1024]{1,0:T(8,128)(2,1)S(1)}, bf16[1024,1024]{1,0:T(8,128)(2,1)}, u32[]{:S(2)}) copy-start(bf16[1024,1024]{1,0:T(8,128)(2,1)} %x_hbm.1) | copy-start | bytes 6291460
  11.0 0.7 copy-start.11
  14.1 41.6 %copy-start = (bf16[1024,512]{1,0:T(8,128)(2,1)}, bf16[1024,512]{1,0:T(8,128)(2,1)S(1)}, u32[]{:S(2)}) copy-start(bf16[1024,512]{1,0:T(8,128)(2,1)S(1)} %get-tuple-element.8.field_ref.h_ref) | copy-start | bytes 3145732
  14.1 14.2 %copy-start.13 = (bf16[64,960]{1,0:T(8,128)(2,1)S(1)}, bf16[64,960]{1,0:T(8,128)(2,1)}, u32[]{:S(2)}) copy-start(bf16[64,960]{1,0:T(8,128)(2,1)} %param.14) | copy-start | bytes 368644
  14.6 14.1 %copy-start.12 = (bf16[1024,192]{0,1:T(8,128)(2,1)S(1)}, bf16[1024,192]{0,1:T(8,128)(2,1)}, u32[]{:S(2)}) copy-start(bf16[1024,192]{0,1:T(8,128)(2,1)} %param.13) | copy-start | bytes 1179652
  15.7 31.7 %copy-start.9 = (s32[1,15]{1,0:T(1,128)S(1)}, s32[1,15]{1,0:T(1,128)}, u32[]{:S(2)}) copy-start(s32[1,15]{1,0:T(1,128)} %col_ref.7) | copy-start | bytes 184
  15.7 31.7 %copy-start.10 = (s32[1,17]{1,0:T(1,128)S(1)}, s32[1,17]{1,0:T(1,128)}, u32[]{:S(2)}) copy-start(s32[1,17]{1,0:T(1,128)} %ptr_ref.7) | copy-start | bytes 208
  15.7 31.7 %all-to-all-start.1 = ((bf16[16,64,512]{2,1,0:T(8,128)(2,1)}), bf16[16,64,512]{2,1,0:T(8,128)(2,1)S(1)}, u32[]{:S(2)}, u32[]{:S(2)}) async-start(bf16[16,64,512]{2,1,0:T(8,128)(2,1)} %broadcast_select_fusion), calls=%async_computation.1 | async-start | bytes 2097152 | tf_op jit(solution)/shard_map/all_to_all | solution.py:406
  21.9 25.5 %collective-permute-start.1 = (bf16[64,512]{1,0:T(8,128)(2,1)S(1)}, bf16[64,512]{1,0:T(8,128)(2,1)S(1)}, u32[]{:S(2)}, u32[]{:S(2)}) collective-permute-start(bf16[64,512]{1,0:T(8,128)(2,1)S(1)} %get-tuple-element.14), channel_id=1, source_target_pairs={{1,0},{2,1},{3,2},{4,3},{5,4},{6,5},{7,6},{8,7},{9,8},{10,9},{11,1... | collective-permute-start | bytes 196616 | tf_op jit(solution)/shard_map/ppermute | solution.py:373
  24.1 23.3 %collective-permute-start = (bf16[64,512]{1,0:T(8,128)(2,1)S(1)}, bf16[64,512]{1,0:T(8,128)(2,1)S(1)}, u32[]{:S(2)}, u32[]{:S(2)}) collective-permute-start(bf16[64,512]{1,0:T(8,128)(2,1)S(1)} %get-tuple-element.15), channel_id=1, source_target_pairs={{0,1},{1,2},{2,3},{3,4},{4,5},{5,6},{6,7},{7,8},{8,9},{9,10},{10,1... | collective-permute-start | bytes 196616 | tf_op jit(solution)/shard_map/ppermute | solution.py:372
  28.7 21.7 %copy-start.3 = (bf16[64,15,64]{2,0,1:T(8,128)(2,1)}, bf16[64,15,64]{2,0,1:T(8,128)(2,1)S(1)}, u32[]{:S(2)}) copy-start(bf16[64,15,64]{2,0,1:T(8,128)(2,1)S(1)} %copy.36) | copy-start | bytes 368644
  28.9 21.4 %copy-start.2 = (bf16[1024,192]{1,0:T(8,128)(2,1)}, bf16[1024,192]{1,0:T(8,128)(2,1)S(1)}, u32[]{:S(2)}) copy-start(bf16[1024,192]{1,0:T(8,128)(2,1)S(1)} %copy.30.band_ref) | copy-start | bytes 1179652
  47.4 2.9 %copy-start.6 = (bf16[64,512]{1,0:T(8,128)(2,1)}, bf16[64,512]{1,0:T(8,128)(2,1)S(1)}, u32[]{:S(2)}) copy-start(bf16[64,512]{1,0:T(8,128)(2,1)S(1)} %collective-permute-done.1.hi_ref) | copy-start | bytes 196612
  47.4 2.9 %copy-start.7 = (bf16[64,512]{1,0:T(8,128)(2,1)}, bf16[64,512]{1,0:T(8,128)(2,1)S(1)}, u32[]{:S(2)}) copy-start(bf16[64,512]{1,0:T(8,128)(2,1)S(1)} %collective-permute-done.lo_ref) | copy-start | bytes 196612
  47.4 2.9 %copy-start.1 = (bf16[16,64,512]{2,1,0:T(8,128)(2,1)}, bf16[16,64,512]{2,1,0:T(8,128)(2,1)S(1)}, u32[]{:S(2)}) copy-start(bf16[16,64,512]{2,1,0:T(8,128)(2,1)S(1)} %all-to-all-done.1.arr_ref) | copy-start | bytes 3145732
  47.4 7.6 %copy-start.16 = (bf16[96,32]{0,1:T(8,128)(2,1)S(1)}, bf16[96,32]{0,1:T(8,128)(2,1)}, u32[]{:S(2)}) copy-start(bf16[96,32]{0,1:T(8,128)(2,1)} %param.12) | copy-start | bytes 18436
  47.5 8.3 %copy-start.8 = (bf16[32,256]{1,0:T(8,128)(2,1)S(1)}, bf16[32,256]{1,0:T(8,128)(2,1)}, u32[]{:S(2)}) copy-start(bf16[32,256]{1,0:T(8,128)(2,1)} %sw_ref.1) | copy-start | bytes 49156
  49.3 1.0 %copy-start.5 = (bf16[16,64,512]{2,1,0:T(8,128)(2,1)}, bf16[16,64,512]{2,1,0:T(8,128)(2,1)S(1)}, u32[]{:S(2)}) copy-start(bf16[16,64,512]{2,1,0:T(8,128)(2,1)S(1)} %get-tuple-element.11) | copy-start | bytes 3145732
  50.3 30.3 %all-to-all-start.2 = ((bf16[16,64,512]{2,1,0:T(8,128)(2,1)}), bf16[16,64,512]{2,1,0:T(8,128)(2,1)}, u32[]{:S(2)}, u32[]{:S(2)}) async-start(bf16[16,64,512]{2,1,0:T(8,128)(2,1)} %copy-done.5), calls=%async_computation.2 | async-start | bytes 2097152 | tf_op jit(solution)/shard_map/all_to_all | solution.py:406
  61.1 19.5 %collective-permute-start.3 = (bf16[64,512]{1,0:T(8,128)(2,1)S(1)}, bf16[64,512]{1,0:T(8,128)(2,1)S(1)}, u32[]{:S(2)}, u32[]{:S(2)}) collective-permute-start(bf16[64,512]{1,0:T(8,128)(2,1)S(1)} %get-tuple-element.16), channel_id=1, source_target_pairs={{1,0},{2,1},{3,2},{4,3},{5,4},{6,5},{7,6},{8,7},{9,8},{10,9},{11,1... | collective-permute-start | bytes 196616 | tf_op jit(solution)/shard_map/ppermute | solution.py:373
  63.4 17.2 %collective-permute-start.2 = (bf16[64,512]{1,0:T(8,128)(2,1)S(1)}, bf16[64,512]{1,0:T(8,128)(2,1)S(1)}, u32[]{:S(2)}, u32[]{:S(2)}) collective-permute-start(bf16[64,512]{1,0:T(8,128)(2,1)S(1)} %get-tuple-element.17), channel_id=1, source_target_pairs={{0,1},{1,2},{2,3},{3,4},{4,5},{5,6},{6,7},{7,8},{8,9},{9,10},{10,1... | collective-permute-start | bytes 196616 | tf_op jit(solution)/shard_map/ppermute | solution.py:372
  80.6 0.6 copy-start.14
  80.6 0.6 copy-start.15

commit v16 on v15

--- a/solution.py
+++ b/solution.py
@@ -182,7 +182,7 @@
 
 def early_kernel(
     col_ref, ptr_ref, req_ref, exp_ref, field_ref, lo_ref, hi_ref, arr_ref, band_ref, farw_ref,
-    send_ref, edge_ref, pad, blk,
+    send_ref, edge_ref, pad, blk, sems,
 ):
     nblk = field_ref.shape[0] // BLK
     own = lax.axis_index("node")
@@ -198,12 +198,18 @@
         blk[i] = v.astype(bf16)
 
     def body(p, carry):
-        send_ref[p] = blk[req_ref[p]]
+        pltpu.make_async_copy(blk.at[req_ref[p]], send_ref.at[p], sems.at[p]).start()
         return carry
 
     lax.fori_loop(0, send_ref.shape[0], body, 0)
     edge_ref[0] = blk[2]
     edge_ref[1] = blk[3]
+
+    def finish(p, carry):
+        pltpu.make_async_copy(blk.at[req_ref[p]], send_ref.at[p], sems.at[p]).wait()
+        return carry
+
+    lax.fori_loop(0, send_ref.shape[0], finish, 0)
 
 
 def hop1_kernel(
@@ -305,13 +311,17 @@
     return pl.pallas_call(
         early_kernel,
         in_specs=[smem()] * 4 + [vmem()] * 6,
-        out_specs=[vmem(), vmem()],
+        out_specs=[hbm(), vmem()],
         out_shape=[
             jax.ShapeDtypeStruct(arrived.shape, bf16),
             jax.ShapeDtypeStruct((2, BLK, width), bf16),
         ],
-        scratch_shapes=[pltpu.VMEM((nrows + 2 * BLK, width), bf16), pltpu.VMEM((4, BLK, width), bf16)],
-        compiler_params=BIG_VMEM,
+        scratch_shapes=[
+            pltpu.VMEM((nrows + 2 * BLK, width), bf16),
+            pltpu.VMEM((4, BLK, width), bf16),
+            pltpu.SemaphoreType.DMA((arrived.shape[0],)),
+        ],
+        compiler_params=pltpu.CompilerParams(),
         cost_estimate=pl.CostEstimate(
             flops=2 * BLK * BLK * width * (12 + farw3.shape[0]),
             transcendentals=0,

time: 88.3 us -> 91 us (1.031)
  Pallas kernels: 25.4 us -> 28.6 us
  local copies, waits for them, and re-layouts: 6.13 us -> 8.1 us
  waiting for transfers between devices: 23.2 us -> 21.7 us
    pallas_call x1, Pallas kernels: 1.85 us -> 5 us  [early(): pl.pallas_call(early_kernel, in_specs=[smem()] * 4 + [vmem()] * 6, out_sp...]
    ppermute x2, waiting for transfers between devices: 23.2 us -> 21.7 us  [halo(): hi = lax.ppermute(first, 'node', backward)]
    unnamed x37, local copies, waits for them, and re-layouts: 5.64 us -> 6.87 us
  transfers between devices with their start and end apart: 7 -> 7, of which waited for: 2 -> 2; matrix products, arithmetic and copies ran while one was open for 2% -> 4% of each run, Pallas kernels for 18% -> 18%
where the time goes in v16:
time: 91 us; the launch traced here: 90.7 us
  starting transfers between devices  30.2 us (33%)
  Pallas kernels  28.6 us (31%)
  waiting for transfers between devices  21.7 us (24%)
  local copies, waits for them, and re-layouts  8.1 us (9%)
  other arithmetic  1.3 us (1%)
    ppermute x2, waiting for transfers between devices, halo(): hi = lax.ppermute(first, 'node', backward)  21.7 us
    all_to_all x2, starting transfers between devices, exchange(): return lax.all_to_all(send, 'node', split_axis=0, concat_axis=0, tiled=True)  10.7 us
    ppermute x2, starting transfers between devices, halo(): lo = lax.ppermute(last, 'node', forward)  8.38 us
    pallas_call x1, Pallas kernels, hop1(): pl.pallas_call(hop1_kernel, in_specs=[smem(), smem()] + [vmem()] * 6 + [h...  8.3 us
    unnamed x37, local copies, waits for them, and re-layouts  6.87 us
    all_to_all x1, starting transfers between devices, local(): lax.all_to_all(prep(far_col, far_ptr), 'node', split_axis=0, concat_axis=...  6.55 us
    pallas_call x1, Pallas kernels, hop2(): pl.pallas_call(hop2_kernel, in_specs=[smem(), smem()] + [vmem()] * 5 + [h...  6.02 us
    pallas_call x1, Pallas kernels, front_skip(): pl.pallas_call(skip_kernel, grid=(rows // tile,), in_specs=[pl.BlockSpec(...  5.36 us
  transfers between devices with their start and end apart: 7, of which 2 were waited for; matrix products, arithmetic and copies ran while one was open for 4% of the time, Pallas kernels for 18%

profile of v16, /device:TPU:15, one launch (start us, length us, event | category | flops | bytes accessed | tf_op | source)
XLA Modules:
  0.0 90.7 jit_solution(11260997183479621468)
XLA Ops:
  0.6 1.4 %shard_map.104 = s32[16,16]{1,0:T(8,128)} custom-call(s32[1,15]{1,0:T(1,128)} %col_ref.7, s32[1,17]{1,0:T(1,128)} %ptr_ref.7), custom_call_target="tpu_custom_call" | custom-call | tf_op jit(solution)/shard_map/pallas_call | solution.py:77
  2.1 6.6 %all-to-all-start = ((s32[16,1,16]{2,1,0:T(1,128)}), s32[16,1,16]{2,1,0:T(1,128)S(1)}, u32[]{:S(2)}, u32[]{:S(2)}) async-start(s32[16,1,16]{2,1,0:T(1,128)} %bitcast.20), calls=%async_computation | async-start | bytes 16384 | tf_op jit(solution)/shard_map/all_to_all | solution.py:405
  8.6 0.8 copy.29.exp_ref
  9.4 1.6 %copy-done.2 = bf16[1024,1024]{1,0:T(8,128)(2,1)S(1)} copy-done((bf16[1024,1024]{1,0:T(8,128)(2,1)S(1)}, bf16[1024,1024]{1,0:T(8,128)(2,1)}, u32[]{:S(2)}) %copy-start.2) | copy-done | bytes 2097176
  11.0 0.7 copy-done.5
  11.7 2.5 %shard_map.105 = (bf16[1024,512]{1,0:T(8,128)(2,1)S(1)}, bf16[2,64,512]{2,1,0:T(8,128)(2,1)S(1)}) custom-call(s32[16,2]{1,0:T(8,128)S(1)} %copy.29.exp_ref, bf16[1024,1024]{1,0:T(8,128)(2,1)S(1)} %copy-done.2, bf16[64,64]{1,0:T(8,128)(2,1)S(1)} %copy-done.5), custom_call_target="tpu_custom_call" | custom-call | flops 1073741824 | bytes 3145728 | tf_op jit(solution)/shard_map/pallas_call | solution.py:102
  14.1 0.0 copy-start
  14.2 0.0 copy-start.11
  14.2 0.0 copy-done.3
  14.2 0.0 all-to-all-done
  14.2 0.2 slice_reduce_fusion
  14.4 0.2 fusion.2.req_ref
  14.6 0.0 copy-start.8
  14.6 1.1 %broadcast_select_fusion = bf16[16,64,512]{2,1,0:T(8,128)(2,1)} fusion(pred[16]{0:T(512)(128)(4,1)S(1)} %broadcast_compare_fusion, bf16[64,512]{1,0:T(8,128)(2,1)S(1)} %get-tuple-element.19, bf16[64,512]{1,0:T(8,128)(2,1)S(1)} %get-tuple-element.18), kind=kLoop, calls=%fused_computation | loop fusion | flops 524288 | bytes 1179664 | tf_op jit(solution)/shard_map/jit(_where)/select_n | solution.py:418
  15.7 6.0 %all-to-all-start.1 = ((bf16[16,64,512]{2,1,0:T(8,128)(2,1)}), bf16[16,64,512]{2,1,0:T(8,128)(2,1)S(1)}, u32[]{:S(2)}, u32[]{:S(2)}) async-start(bf16[16,64,512]{2,1,0:T(8,128)(2,1)} %broadcast_select_fusion), calls=%async_computation.1 | async-start | bytes 2097152 | tf_op jit(solution)/shard_map/all_to_all | solution.py:416
  21.8 2.3 %collective-permute-start.1 = (bf16[64,512]{1,0:T(8,128)(2,1)S(1)}, bf16[64,512]{1,0:T(8,128)(2,1)S(1)}, u32[]{:S(2)}, u32[]{:S(2)}) collective-permute-start(bf16[64,512]{1,0:T(8,128)(2,1)S(1)} %get-tuple-element.14), channel_id=1, source_target_pairs={{1,0},{2,1},{3,2},{4,3},{5,4},{6,5},{7,6},{8,7},{9,8},{10,9},{11,1... | collective-permute-start | bytes 196616 | tf_op jit(solution)/shard_map/ppermute | solution.py:383
  24.0 4.2 %collective-permute-start = (bf16[64,512]{1,0:T(8,128)(2,1)S(1)}, bf16[64,512]{1,0:T(8,128)(2,1)S(1)}, u32[]{:S(2)}, u32[]{:S(2)}) collective-permute-start(bf16[64,512]{1,0:T(8,128)(2,1)S(1)} %get-tuple-element.15), channel_id=1, source_target_pairs={{0,1},{1,2},{2,3},{3,4},{4,5},{5,6},{6,7},{7,8},{8,9},{9,10},{10,1... | collective-permute-start | bytes 196616 | tf_op jit(solution)/shard_map/ppermute | solution.py:382
  28.2 0.0 copy-done.11
  28.2 0.2 reshape.12
  28.5 0.0 copy-done
  28.5 0.8 copy.36
  29.3 0.0 copy-done.16
  29.3 0.0 copy-done.8
  29.3 1.0 %copy.30.band_ref = bf16[1024,192]{1,0:T(8,128)(2,1)} copy(bf16[1024,192]{0,1:T(8,128)(2,1)S(1)} %copy-done.8) | data formatting | bytes 786432 | tf_op args[4]
  30.3 17.0 %collective-permute-done.1.hi_ref = bf16[64,512]{1,0:T(8,128)(2,1)S(1)} collective-permute-done((bf16[64,512]{1,0:T(8,128)(2,1)S(1)}, bf16[64,512]{1,0:T(8,128)(2,1)S(1)}, u32[]{:S(2)}, u32[]{:S(2)}) %collective-permute-start.1) | collective-permute-done | bytes 65568 | tf_op jit(solution)/shard_map/ppermute | solution.py:383
  47.3 0.0 collective-permute-done.lo_ref
  47.3 0.0 all-to-all-done.1.arr_ref
  47.3 0.0 copy-start.6
  47.3 0.6 copy-done.9
  47.9 0.0 copy-done.10
  48.0 0.4 copy-done.6
  48.3 5.0 %shard_map.106 = (bf16[16,64,512]{2,1,0:T(8,128)(2,1)}, bf16[2,64,512]{2,1,0:T(8,128)(2,1)}) custom-call(s32[1,15]{1,0:T(1,128)} %col_ref.7, s32[1,17]{1,0:T(1,128)} %ptr_ref.7, s32[16]{0:T(128)} %copy-done.16, s32[16,2]{1,0:T(8,128)} %copy-done.3, bf16[1024,512]{1,0:T(8,128)(2,1)} %copy-done, bf16[64,512]{1,0:T(8,128)(2,1)} %copy-done.10, ...), custom_call_target="tpu_custom_call" | custom-call | flops 113246208 | bytes 3145728 | tf_op jit(solution)/shard_map/pallas_call | solution.py:311
  53.3 4.7 %all-to-all-start.2 = ((bf16[16,64,512]{2,1,0:T(8,128)(2,1)}), bf16[16,64,512]{2,1,0:T(8,128)(2,1)S(1)}, u32[]{:S(2)}, u32[]{:S(2)}) async-start(bf16[16,64,512]{2,1,0:T(8,128)(2,1)} %get-tuple-element.11), calls=%async_computation.2 | async-start | bytes 2097152 | tf_op jit(solution)/shard_map/all_to_all | solution.py:416
  58.0 0.0 copy-done.15
  58.0 0.7 copy.32.mix_ref
  58.7 0.0 copy-done.1
  58.7 5.4 %shard_map.109 = bf16[1024,4096]{1,0:T(8,128)(2,1)} custom-call(bf16[1024,512]{1,0:T(8,128)(2,1)S(1)} %copy-done.1, bf16[32,256]{1,0:T(8,128)(2,1)S(1)} %copy-done.4), custom_call_target="tpu_custom_call" | custom-call | flops 2147483648 | bytes 9437184 | tf_op jit(solution)/shard_map/pallas_call | solution.py:126
  64.1 0.0 copy-done.12
  64.1 2.3 %collective-permute-start.3 = (bf16[64,512]{1,0:T(8,128)(2,1)S(1)}, bf16[64,512]{1,0:T(8,128)(2,1)S(1)}, u32[]{:S(2)}, u32[]{:S(2)}) collective-permute-start(bf16[64,512]{1,0:T(8,128)(2,1)S(1)} %get-tuple-element.16), channel_id=1, source_target_pairs={{1,0},{2,1},{3,2},{4,3},{5,4},{6,5},{7,6},{8,7},{9,8},{10,9},{11,1... | collective-permute-start | bytes 196616 | tf_op jit(solution)/shard_map/ppermute | solution.py:383
  66.4 4.2 %collective-permute-start.2 = (bf16[64,512]{1,0:T(8,128)(2,1)S(1)}, bf16[64,512]{1,0:T(8,128)(2,1)S(1)}, u32[]{:S(2)}, u32[]{:S(2)}) collective-permute-start(bf16[64,512]{1,0:T(8,128)(2,1)S(1)} %get-tuple-element.17), channel_id=1, source_target_pairs={{0,1},{1,2},{2,3},{3,4},{4,5},{5,6},{6,7},{7,8},{8,9},{9,10},{10,1... | collective-permute-start | bytes 196616 | tf_op jit(solution)/shard_map/ppermute | solution.py:382
  70.6 8.3 %shard_map.107 = (bf16[1024,512]{1,0:T(8,128)(2,1)}, f32[1024,512]{1,0:T(8,128)}, f32[1024,512]{1,0:T(8,128)}) custom-call(s32[1,15]{1,0:T(1,128)} %col_ref.7, s32[1,17]{1,0:T(1,128)} %ptr_ref.7, bf16[1024,512]{1,0:T(8,128)(2,1)} %copy-done, bf16[64,512]{1,0:T(8,128)(2,1)} %copy-done.10, bf16[64,512]{1,0:T(8,128)(2,1)} %copy-done.9, ...), custom_call_target="tpu_custom_call" | custom-call | flops 1002438656 | bytes 10485760 | tf_op jit(solution)/shard_map/pallas_call | solution.py:335
  78.9 4.7 %collective-permute-done.3.hi_ref = bf16[64,512]{1,0:T(8,128)(2,1)S(1)} collective-permute-done((bf16[64,512]{1,0:T(8,128)(2,1)S(1)}, bf16[64,512]{1,0:T(8,128)(2,1)S(1)}, u32[]{:S(2)}, u32[]{:S(2)}) %collective-permute-start.3) | collective-permute-done | bytes 65568 | tf_op jit(solution)/shard_map/ppermute | solution.py:383
  83.6 0.0 collective-permute-done.2.lo_ref
  83.6 0.0 all-to-all-done.2.arr_ref
  83.6 0.6 copy-done.13
  84.2 0.0 copy-done.14
  84.2 0.4 copy-done.7
  84.6 6.0 %shard_map.108 = bf16[1024,512]{1,0:T(8,128)(2,1)} custom-call(s32[1,15]{1,0:T(1,128)} %col_ref.7, s32[1,17]{1,0:T(1,128)} %ptr_ref.7, bf16[64,512]{1,0:T(8,128)(2,1)} %copy-done.14, bf16[64,512]{1,0:T(8,128)(2,1)} %copy-done.13, bf16[16,64,512]{2,1,0:T(8,128)(2,1)} %copy-done.7, bf16[1024,192]{1,0:T(8,128)(2,1)} %copy.30.band_ref, ...), custom_call_target="tpu_custom_call" | custom-call | flops 339738624 | bytes 6291456 | tf_op jit(solution)/shard_map/pallas_call | solution.py:358
  (18 shorter events, 0.1 us)
Async XLA Ops:
  2.1 12.1 %all-to-all-start = ((s32[16,1,16]{2,1,0:T(1,128)}), s32[16,1,16]{2,1,0:T(1,128)S(1)}, u32[]{:S(2)}, u32[]{:S(2)}) async-start(s32[16,1,16]{2,1,0:T(1,128)} %bitcast.20), calls=%async_computation | async-start | bytes 16384 | tf_op jit(solution)/shard_map/all_to_all | solution.py:405
  9.4 1.6 %copy-start.2 = (bf16[1024,1024]{1,0:T(8,128)(2,1)S(1)}, bf16[1024,1024]{1,0:T(8,128)(2,1)}, u32[]{:S(2)}) copy-start(bf16[1024,1024]{1,0:T(8,128)(2,1)} %x_hbm.1) | copy-start | bytes 6291460
  11.0 0.7 copy-start.5
  11.7 2.5 %copy-start.3 = (s32[16,2]{1,0:T(8,128)}, s32[16,2]{1,0:T(8,128)S(1)}, u32[]{:S(2)}) copy-start(s32[16,2]{1,0:T(8,128)S(1)} %copy.29.exp_ref) | copy-start | bytes 388
  14.1 14.3 %copy-start = (bf16[1024,512]{1,0:T(8,128)(2,1)}, bf16[1024,512]{1,0:T(8,128)(2,1)S(1)}, u32[]{:S(2)}) copy-start(bf16[1024,512]{1,0:T(8,128)(2,1)S(1)} %get-tuple-element.8.field_ref.h_ref) | copy-start | bytes 3145732
  14.2 14.1 %copy-start.11 = (bf16[64,960]{1,0:T(8,128)(2,1)S(1)}, bf16[64,960]{1,0:T(8,128)(2,1)}, u32[]{:S(2)}) copy-start(bf16[64,960]{1,0:T(8,128)(2,1)} %param.14) | copy-start | bytes 368644
  14.6 14.7 %copy-start.16 = (s32[16]{0:T(128)}, s32[16]{0:T(128)S(1)}, u32[]{:S(2)}) copy-start(s32[16]{0:T(128)S(1)} %fusion.2.req_ref) | copy-start | bytes 196
  14.6 14.7 %copy-start.8 = (bf16[1024,192]{0,1:T(8,128)(2,1)S(1)}, bf16[1024,192]{0,1:T(8,128)(2,1)}, u32[]{:S(2)}) copy-start(bf16[1024,192]{0,1:T(8,128)(2,1)} %param.13) | copy-start | bytes 1179652
  15.7 31.6 %all-to-all-start.1 = ((bf16[16,64,512]{2,1,0:T(8,128)(2,1)}), bf16[16,64,512]{2,1,0:T(8,128)(2,1)S(1)}, u32[]{:S(2)}, u32[]{:S(2)}) async-start(bf16[16,64,512]{2,1,0:T(8,128)(2,1)} %broadcast_select_fusion), calls=%async_computation.1 | async-start | bytes 2097152 | tf_op jit(solution)/shard_map/all_to_all | solution.py:416
  21.8 25.5 %collective-permute-start.1 = (bf16[64,512]{1,0:T(8,128)(2,1)S(1)}, bf16[64,512]{1,0:T(8,128)(2,1)S(1)}, u32[]{:S(2)}, u32[]{:S(2)}) collective-permute-start(bf16[64,512]{1,0:T(8,128)(2,1)S(1)} %get-tuple-element.14), channel_id=1, source_target_pairs={{1,0},{2,1},{3,2},{4,3},{5,4},{6,5},{7,6},{8,7},{9,8},{10,9},{11,1... | collective-permute-start | bytes 196616 | tf_op jit(solution)/shard_map/ppermute | solution.py:383
  24.0 23.3 %collective-permute-start = (bf16[64,512]{1,0:T(8,128)(2,1)S(1)}, bf16[64,512]{1,0:T(8,128)(2,1)S(1)}, u32[]{:S(2)}, u32[]{:S(2)}) collective-permute-start(bf16[64,512]{1,0:T(8,128)(2,1)S(1)} %get-tuple-element.15), channel_id=1, source_target_pairs={{0,1},{1,2},{2,3},{3,4},{4,5},{5,6},{6,7},{7,8},{8,9},{9,10},{10,1... | collective-permute-start | bytes 196616 | tf_op jit(solution)/shard_map/ppermute | solution.py:382
  47.3 0.6 copy-start.9
  47.3 0.7 copy-start.10
  47.3 1.0 %copy-start.6 = (bf16[16,64,512]{2,1,0:T(8,128)(2,1)}, bf16[16,64,512]{2,1,0:T(8,128)(2,1)S(1)}, u32[]{:S(2)}) copy-start(bf16[16,64,512]{2,1,0:T(8,128)(2,1)S(1)} %all-to-all-done.1.arr_ref) | copy-start | bytes 3145732
  48.3 9.7 %copy-start.15 = (bf16[96,32]{0,1:T(8,128)(2,1)S(1)}, bf16[96,32]{0,1:T(8,128)(2,1)}, u32[]{:S(2)}) copy-start(bf16[96,32]{0,1:T(8,128)(2,1)} %param.12) | copy-start | bytes 18436
  48.3 10.4 %copy-start.1 = (bf16[1024,512]{1,0:T(8,128)(2,1)S(1)}, bf16[1024,512]{1,0:T(8,128)(2,1)}, u32[]{:S(2)}) copy-start(bf16[1024,512]{1,0:T(8,128)(2,1)} %copy-done) | copy-start | bytes 3145732
  48.3 10.4 %copy-start.4 = (bf16[32,256]{1,0:T(8,128)(2,1)S(1)}, bf16[32,256]{1,0:T(8,128)(2,1)}, u32[]{:S(2)}) copy-start(bf16[32,256]{1,0:T(8,128)(2,1)} %sw_ref.1) | copy-start | bytes 49156
  53.3 30.2 %all-to-all-start.2 = ((bf16[16,64,512]{2,1,0:T(8,128)(2,1)}), bf16[16,64,512]{2,1,0:T(8,128)(2,1)S(1)}, u32[]{:S(2)}, u32[]{:S(2)}) async-start(bf16[16,64,512]{2,1,0:T(8,128)(2,1)} %get-tuple-element.11), calls=%async_computation.2 | async-start | bytes 2097152 | tf_op jit(solution)/shard_map/all_to_all | solution.py:416
  58.7 5.4 %copy-start.12 = (bf16[2,64,512]{2,1,0:T(8,128)(2,1)S(1)}, bf16[2,64,512]{2,1,0:T(8,128)(2,1)}, u32[]{:S(2)}) copy-start(bf16[2,64,512]{2,1,0:T(8,128)(2,1)} %get-tuple-element.10) | copy-start | bytes 393220
  64.1 19.5 %collective-permute-start.3 = (bf16[64,512]{1,0:T(8,128)(2,1)S(1)}, bf16[64,512]{1,0:T(8,128)(2,1)S(1)}, u32[]{:S(2)}, u32[]{:S(2)}) collective-permute-start(bf16[64,512]{1,0:T(8,128)(2,1)S(1)} %get-tuple-element.16), channel_id=1, source_target_pairs={{1,0},{2,1},{3,2},{4,3},{5,4},{6,5},{7,6},{8,7},{9,8},{10,9},{11,1... | collective-permute-start | bytes 196616 | tf_op jit(solution)/shard_map/ppermute | solution.py:383
  66.4 17.2 %collective-permute-start.2 = (bf16[64,512]{1,0:T(8,128)(2,1)S(1)}, bf16[64,512]{1,0:T(8,128)(2,1)S(1)}, u32[]{:S(2)}, u32[]{:S(2)}) collective-permute-start(bf16[64,512]{1,0:T(8,128)(2,1)S(1)} %get-tuple-element.17), channel_id=1, source_target_pairs={{0,1},{1,2},{2,3},{3,4},{4,5},{5,6},{6,7},{7,8},{8,9},{9,10},{10,1... | collective-permute-start | bytes 196616 | tf_op jit(solution)/shard_map/ppermute | solution.py:382
  83.6 0.6 copy-start.13
  83.6 0.6 copy-start.14
  83.6 1.1 %copy-start.7 = (bf16[16,64,512]{2,1,0:T(8,128)(2,1)}, bf16[16,64,512]{2,1,0:T(8,128)(2,1)S(1)}, u32[]{:S(2)}) copy-start(bf16[16,64,512]{2,1,0:T(8,128)(2,1)S(1)} %all-to-all-done.2.arr_ref) | copy-start | bytes 3145732

commit v17 on v15

--- a/solution.py
+++ b/solution.py
@@ -40,20 +40,32 @@
     return jnp.where(mask, tiled, 0.0).astype(bf16)
 
 
-def hidden_kernel(exp_ref, x_ref, fgw_ref, h_ref, ex_ref):
-    rows, cols = x_ref.shape
+def hidden_kernel(exp_ref, x_hbm, fgw_ref, h_ref, ex_ref, xbuf, sems):
+    rows, cols = x_hbm.shape
     half = cols // 2
     cw = fgw_ref.shape[0] // 2
     per = CHUNK // cw
+    tile = min(ROW_TILE, rows)
+    tiles = rows // tile
+
+    def load(t):
+        return pltpu.make_async_copy(
+            x_hbm.at[pl.ds(t * tile, tile)], xbuf.at[t % 2], sems.at[t % 2]
+        )
+
+    load(0).start()
     w = fgw_ref[...]
     wlo = jnp.concatenate([bd_inkernel(w[:cw, :cw], per), bd_inkernel(w[:cw, cw:], per)], axis=1)
     whi = jnp.concatenate([bd_inkernel(w[cw:, :cw], per), bd_inkernel(w[cw:, cw:], per)], axis=1)
-    tile = min(ROW_TILE, rows)
-    for t in range(rows // tile):
+    for t in range(tiles):
+        if t + 1 < tiles:
+            load(t + 1).start()
+        load(t).wait()
+        x_ref = xbuf.at[t % 2]
         rs = slice(t * tile, (t + 1) * tile)
         for j in range(half // CHUNK):
-            x0 = x_ref[rs, j * CHUNK : (j + 1) * CHUNK]
-            x1 = x_ref[rs, half + j * CHUNK : half + (j + 1) * CHUNK]
+            x0 = x_ref[:, j * CHUNK : (j + 1) * CHUNK]
+            x1 = x_ref[:, half + j * CHUNK : half + (j + 1) * CHUNK]
             pre = jnp.dot(x0, wlo, preferred_element_type=f32)
             pre = pre + jnp.dot(x1, whi, preferred_element_type=f32)
             h_ref[rs, j * CHUNK : (j + 1) * CHUNK] = (
@@ -101,13 +113,17 @@
     half = cols // 2
     return pl.pallas_call(
         hidden_kernel,
-        in_specs=[smem(), vmem(), vmem()],
+        in_specs=[smem(), hbm(), vmem()],
         out_specs=[vmem(), vmem()],
         out_shape=[
             jax.ShapeDtypeStruct((rows, half), bf16),
             jax.ShapeDtypeStruct((export_block.shape[1], BLK, half), bf16),
         ],
-        compiler_params=pltpu.CompilerParams(vmem_limit_bytes=48 * 1024 * 1024),
+        scratch_shapes=[
+            pltpu.VMEM((2, min(ROW_TILE, rows), cols), bf16),
+            pltpu.SemaphoreType.DMA((2,)),
+        ],
+        compiler_params=pltpu.CompilerParams(),
         cost_estimate=pl.CostEstimate(
             flops=2 * rows * CHUNK * 4 * CHUNK * (half // CHUNK),
             transcendentals=rows * half * 2,

time: 88.3 us -> 89.9 us (1.018)
  Pallas kernels: 25.4 us -> 27.9 us
    pallas_call x1, Pallas kernels: 2.45 us -> 5.13 us  [front_hidden(): pl.pallas_call(hidden_kernel, in_specs=[smem(), hbm(), vmem()], out_specs...]
    unnamed x37 -> x35, local copies, waits for them, and re-layouts: 5.64 us -> 3.96 us
    broadcast_in_dim x1, local copies, waits for them, and re-layouts: 0.01 us -> 0.98 us  [local(): jnp.where((requested == 0)[:, None, None], ex2[0][None], ex2[1][None])]
  transfers between devices with their start and end apart: 7 -> 7, of which waited for: 2 -> 2; matrix products, arithmetic and copies ran while one was open for 2% -> 4% of each run, Pallas kernels for 18% -> 21%
where the time goes in v17:
time: 89.9 us; the launch traced here: 89.5 us
  starting transfers between devices  30.8 us (34%)
  Pallas kernels  27.9 us (31%)
  waiting for transfers between devices  23.2 us (26%)
  local copies, waits for them, and re-layouts  5.41 us (6%)
  other arithmetic  1.3 us (1%)
    ppermute x2, waiting for transfers between devices, halo(): hi = lax.ppermute(first, 'node', backward)  23.2 us
    all_to_all x2, starting transfers between devices, exchange(): return lax.all_to_all(send, 'node', split_axis=0, concat_axis=0, tiled=True)  11.3 us
    ppermute x2, starting transfers between devices, halo(): lo = lax.ppermute(last, 'node', forward)  8.38 us
    pallas_call x1, Pallas kernels, hop1(): pl.pallas_call(hop1_kernel, in_specs=[smem(), smem()] + [vmem()] * 6 + [h...  8.29 us
    all_to_all x1, starting transfers between devices, local(): lax.all_to_all(prep(far_col, far_ptr), 'node', split_axis=0, concat_axis=...  6.55 us
    pallas_call x1, Pallas kernels, hop2(): pl.pallas_call(hop2_kernel, in_specs=[smem(), smem()] + [vmem()] * 5 + [h...  6.01 us
    pallas_call x1, Pallas kernels, front_skip(): pl.pallas_call(skip_kernel, grid=(rows // tile,), in_specs=[pl.BlockSpec(...  5.34 us
    pallas_call x1, Pallas kernels, front_hidden(): pl.pallas_call(hidden_kernel, in_specs=[smem(), hbm(), vmem()], out_specs...  5.13 us
  transfers between devices with their start and end apart: 7, of which 2 were waited for; matrix products, arithmetic and copies ran while one was open for 4% of the time, Pallas kernels for 21%

profile of v17, /device:TPU:15, one launch (start us, length us, event | category | flops | bytes accessed | tf_op | source)
XLA Modules:
  0.0 89.5 jit_solution(7842290026593873818)
XLA Ops:
  0.6 1.4 %shard_map.104 = s32[16,16]{1,0:T(8,128)} custom-call(s32[1,15]{1,0:T(1,128)} %col_ref.7, s32[1,17]{1,0:T(1,128)} %ptr_ref.7), custom_call_target="tpu_custom_call" | custom-call | tf_op jit(solution)/shard_map/pallas_call | solution.py:89
  2.1 6.6 %all-to-all-start = ((s32[16,1,16]{2,1,0:T(1,128)}), s32[16,1,16]{2,1,0:T(1,128)S(1)}, u32[]{:S(2)}, u32[]{:S(2)}) async-start(s32[16,1,16]{2,1,0:T(1,128)} %bitcast.20), calls=%async_computation | async-start | bytes 16384 | tf_op jit(solution)/shard_map/all_to_all | solution.py:411
  8.6 1.4 %copy.29.exp_ref = s32[16,2]{1,0:T(8,128)} copy(s32[16,2]{0,1:T(2,128)} %param.17) | data formatting | bytes 256 | tf_op args[8]
  10.0 5.1 %shard_map.105 = (bf16[1024,512]{1,0:T(8,128)(2,1)}, bf16[2,64,512]{2,1,0:T(8,128)(2,1)}) custom-call(s32[16,2]{1,0:T(8,128)} %copy.29.exp_ref, bf16[1024,1024]{1,0:T(8,128)(2,1)} %x_hbm.3, bf16[64,64]{1,0:T(8,128)(2,1)} %fgw_ref.1), custom_call_target="tpu_custom_call" | custom-call | flops 1073741824 | bytes 3145728 | tf_op jit(solution)/shard_map/pallas_call | solution.py:114
  15.1 0.0 copy-start
  15.1 0.0 copy-start.12
  15.1 1.0 %slice_bitcast_fusion.3 = (bf16[64,512]{1,0:T(8,128)(2,1)S(1)}, bf16[64,512]{1,0:T(8,128)(2,1)S(1)}) fusion(bf16[2,64,512]{2,1,0:T(8,128)(2,1)} %get-tuple-element.9), kind=kLoop, calls=%fused_computation.5 | loop fusion | bytes 262144 | tf_op jit(solution)/shard_map/jit(_where)/broadcast_in_dim | solution.py:424
  16.1 0.0 all-to-all-done
  16.1 0.2 slice_reduce_fusion
  16.3 0.2 fusion.2.req_ref
  16.5 0.0 copy-start.11
  16.5 1.1 %broadcast_select_fusion = bf16[16,64,512]{2,1,0:T(8,128)(2,1)} fusion(pred[16]{0:T(512)(128)(4,1)S(1)} %broadcast_compare_fusion, bf16[64,512]{1,0:T(8,128)(2,1)S(1)} %get-tuple-element.19, bf16[64,512]{1,0:T(8,128)(2,1)S(1)} %get-tuple-element.18), kind=kLoop, calls=%fused_computation | loop fusion | flops 524288 | bytes 1179664 | tf_op jit(solution)/shard_map/jit(_where)/select_n | solution.py:424
  17.6 6.1 %all-to-all-start.1 = ((bf16[16,64,512]{2,1,0:T(8,128)(2,1)}), bf16[16,64,512]{2,1,0:T(8,128)(2,1)S(1)}, u32[]{:S(2)}, u32[]{:S(2)}) async-start(bf16[16,64,512]{2,1,0:T(8,128)(2,1)} %broadcast_select_fusion), calls=%async_computation.1 | async-start | bytes 2097152 | tf_op jit(solution)/shard_map/all_to_all | solution.py:422
  23.8 0.0 copy-done
  23.8 2.3 %collective-permute-start.1 = (bf16[64,512]{1,0:T(8,128)(2,1)S(1)}, bf16[64,512]{1,0:T(8,128)(2,1)S(1)}, u32[]{:S(2)}, u32[]{:S(2)}) collective-permute-start(bf16[64,512]{1,0:T(8,128)(2,1)S(1)} %get-tuple-element.14), channel_id=1, source_target_pairs={{1,0},{2,1},{3,2},{4,3},{5,4},{6,5},{7,6},{8,7},{9,8},{10,9},{11,1... | collective-permute-start | bytes 196616 | tf_op jit(solution)/shard_map/ppermute | solution.py:389
  26.1 4.2 %collective-permute-start = (bf16[64,512]{1,0:T(8,128)(2,1)S(1)}, bf16[64,512]{1,0:T(8,128)(2,1)S(1)}, u32[]{:S(2)}, u32[]{:S(2)}) collective-permute-start(bf16[64,512]{1,0:T(8,128)(2,1)S(1)} %get-tuple-element.15), channel_id=1, source_target_pairs={{0,1},{1,2},{2,3},{3,4},{4,5},{5,6},{6,7},{7,8},{8,9},{9,10},{10,1... | collective-permute-start | bytes 196616 | tf_op jit(solution)/shard_map/ppermute | solution.py:388
  30.3 0.0 copy-done.12
  30.3 0.2 reshape.12
  30.5 0.1 copy.36
  30.6 0.0 copy-done.11
  30.6 0.0 copy-start.3
  30.6 0.2 copy.30.band_ref
  30.8 0.0 copy-start.2
  30.8 18.5 %collective-permute-done.1.hi_ref = bf16[64,512]{1,0:T(8,128)(2,1)S(1)} collective-permute-done((bf16[64,512]{1,0:T(8,128)(2,1)S(1)}, bf16[64,512]{1,0:T(8,128)(2,1)S(1)}, u32[]{:S(2)}, u32[]{:S(2)}) %collective-permute-start.1) | collective-permute-done | bytes 65568 | tf_op jit(solution)/shard_map/ppermute | solution.py:389
  49.3 0.0 collective-permute-done.lo_ref
  49.3 0.0 all-to-all-done.1.arr_ref
  49.3 0.0 copy-start.1
  49.4 0.0 copy-done.7
  49.4 0.0 copy-done.9
  49.4 0.0 copy-done.10
  49.4 0.0 copy-start.15
  49.4 0.0 copy-start.8
  49.4 1.7 %shard_map.106 = (bf16[16,64,512]{2,1,0:T(8,128)(2,1)S(1)}, bf16[2,64,512]{2,1,0:T(8,128)(2,1)S(1)}) custom-call(s32[1,15]{1,0:T(1,128)S(1)} %copy-done.9, s32[1,17]{1,0:T(1,128)S(1)} %copy-done.10, s32[16]{0:T(128)S(1)} %fusion.2.req_ref, s32[16,2]{1,0:T(8,128)S(1)} %copy-done.7, bf16[1024,512]{1,0:T(8,128)(2,1)S(1)} %copy-done, ...), custom_call_target="tpu_custom_call" | custom-call | flops 113246208 | bytes 3145728 | tf_op jit(solution)/shard_map/pallas_call | solution.py:321
  51.1 1.0 %copy-done.4 = bf16[16,64,512]{2,1,0:T(8,128)(2,1)} copy-done((bf16[16,64,512]{2,1,0:T(8,128)(2,1)}, bf16[16,64,512]{2,1,0:T(8,128)(2,1)S(1)}, u32[]{:S(2)}) %copy-start.4) | copy-done | bytes 1048600
  52.1 0.0 copy-done.3
  52.1 0.0 copy-done.1
  52.1 5.1 %all-to-all-start.2 = ((bf16[16,64,512]{2,1,0:T(8,128)(2,1)}), bf16[16,64,512]{2,1,0:T(8,128)(2,1)}, u32[]{:S(2)}, u32[]{:S(2)}) async-start(bf16[16,64,512]{2,1,0:T(8,128)(2,1)} %copy-done.4), calls=%async_computation.2 | async-start | bytes 2097152 | tf_op jit(solution)/shard_map/all_to_all | solution.py:422
  57.3 0.7 copy.32.mix_ref
  58.0 5.3 %shard_map.109 = bf16[1024,4096]{1,0:T(8,128)(2,1)} custom-call(bf16[1024,512]{1,0:T(8,128)(2,1)S(1)} %copy-done, bf16[32,256]{1,0:T(8,128)(2,1)S(1)} %copy-done.8), custom_call_target="tpu_custom_call" | custom-call | flops 2147483648 | bytes 9437184 | tf_op jit(solution)/shard_map/pallas_call | solution.py:142
  63.3 2.3 %collective-permute-start.3 = (bf16[64,512]{1,0:T(8,128)(2,1)S(1)}, bf16[64,512]{1,0:T(8,128)(2,1)S(1)}, u32[]{:S(2)}, u32[]{:S(2)}) collective-permute-start(bf16[64,512]{1,0:T(8,128)(2,1)S(1)} %get-tuple-element.16), channel_id=1, source_target_pairs={{1,0},{2,1},{3,2},{4,3},{5,4},{6,5},{7,6},{8,7},{9,8},{10,9},{11,1... | collective-permute-start | bytes 196616 | tf_op jit(solution)/shard_map/ppermute | solution.py:389
  65.6 4.2 %collective-permute-start.2 = (bf16[64,512]{1,0:T(8,128)(2,1)S(1)}, bf16[64,512]{1,0:T(8,128)(2,1)S(1)}, u32[]{:S(2)}, u32[]{:S(2)}) collective-permute-start(bf16[64,512]{1,0:T(8,128)(2,1)S(1)} %get-tuple-element.17), channel_id=1, source_target_pairs={{0,1},{1,2},{2,3},{3,4},{4,5},{5,6},{6,7},{7,8},{8,9},{9,10},{10,1... | collective-permute-start | bytes 196616 | tf_op jit(solution)/shard_map/ppermute | solution.py:388
  69.8 8.3 %shard_map.107 = (bf16[1024,512]{1,0:T(8,128)(2,1)}, f32[1024,512]{1,0:T(8,128)}, f32[1024,512]{1,0:T(8,128)}) custom-call(s32[1,15]{1,0:T(1,128)} %col_ref.7, s32[1,17]{1,0:T(1,128)} %ptr_ref.7, bf16[1024,512]{1,0:T(8,128)(2,1)} %get-tuple-element.8.field_ref.h_ref, bf16[64,512]{1,0:T(8,128)(2,1)} %copy-done.6, bf16[64,512]{1,0:T(8,128)(2,1)} %copy-done.5, ...), custom_call_target="tpu_custom_call" | custom-call | flops 1002438656 | bytes 10485760 | tf_op jit(solution)/shard_map/pallas_call | solution.py:341
  78.1 4.7 %collective-permute-done.3.hi_ref = bf16[64,512]{1,0:T(8,128)(2,1)S(1)} collective-permute-done((bf16[64,512]{1,0:T(8,128)(2,1)S(1)}, bf16[64,512]{1,0:T(8,128)(2,1)S(1)}, u32[]{:S(2)}, u32[]{:S(2)}) %collective-permute-start.3) | collective-permute-done | bytes 65568 | tf_op jit(solution)/shard_map/ppermute | solution.py:389
  82.8 0.0 collective-permute-done.2.lo_ref
  82.8 0.0 all-to-all-done.2.arr_ref
  82.8 0.6 copy-done.13
  83.4 0.0 copy-done.14
  83.5 6.0 %shard_map.108 = bf16[1024,512]{1,0:T(8,128)(2,1)} custom-call(s32[1,15]{1,0:T(1,128)} %col_ref.7, s32[1,17]{1,0:T(1,128)} %ptr_ref.7, bf16[64,512]{1,0:T(8,128)(2,1)} %copy-done.14, bf16[64,512]{1,0:T(8,128)(2,1)} %copy-done.13, bf16[16,64,512]{2,1,0:T(8,128)(2,1)} %all-to-all-done.2.arr_ref, bf16[1024,192]{1,0:T(8,128)(2,1)} %copy-done.2, ...), custom_call_target="tpu_custom_call" | custom-call | flops 339738624 | bytes 6291456 | tf_op jit(solution)/shard_map/pallas_call | solution.py:364
  (16 shorter events, 0.1 us)
Async XLA Ops:
  2.1 14.1 %all-to-all-start = ((s32[16,1,16]{2,1,0:T(1,128)}), s32[16,1,16]{2,1,0:T(1,128)S(1)}, u32[]{:S(2)}, u32[]{:S(2)}) async-start(s32[16,1,16]{2,1,0:T(1,128)} %bitcast.20), calls=%async_computation | async-start | bytes 16384 | tf_op jit(solution)/shard_map/all_to_all | solution.py:411
  15.1 8.7 %copy-start = (bf16[1024,512]{1,0:T(8,128)(2,1)S(1)}, bf16[1024,512]{1,0:T(8,128)(2,1)}, u32[]{:S(2)}) copy-start(bf16[1024,512]{1,0:T(8,128)(2,1)} %get-tuple-element.8.field_ref.h_ref) | copy-start | bytes 3145732
  15.1 15.2 %copy-start.12 = (bf16[64,960]{1,0:T(8,128)(2,1)S(1)}, bf16[64,960]{1,0:T(8,128)(2,1)}, u32[]{:S(2)}) copy-start(bf16[64,960]{1,0:T(8,128)(2,1)} %param.14) | copy-start | bytes 368644
  16.5 14.1 %copy-start.11 = (bf16[1024,192]{0,1:T(8,128)(2,1)S(1)}, bf16[1024,192]{0,1:T(8,128)(2,1)}, u32[]{:S(2)}) copy-start(bf16[1024,192]{0,1:T(8,128)(2,1)} %param.13) | copy-start | bytes 1179652
  17.6 31.7 %copy-start.7 = (s32[16,2]{1,0:T(8,128)S(1)}, s32[16,2]{1,0:T(8,128)}, u32[]{:S(2)}) copy-start(s32[16,2]{1,0:T(8,128)} %copy.29.exp_ref) | copy-start | bytes 388
  17.6 31.7 %copy-start.9 = (s32[1,15]{1,0:T(1,128)S(1)}, s32[1,15]{1,0:T(1,128)}, u32[]{:S(2)}) copy-start(s32[1,15]{1,0:T(1,128)} %col_ref.7) | copy-start | bytes 184
  17.6 31.8 %copy-start.10 = (s32[1,17]{1,0:T(1,128)S(1)}, s32[1,17]{1,0:T(1,128)}, u32[]{:S(2)}) copy-start(s32[1,17]{1,0:T(1,128)} %ptr_ref.7) | copy-start | bytes 208
  17.6 31.7 %all-to-all-start.1 = ((bf16[16,64,512]{2,1,0:T(8,128)(2,1)}), bf16[16,64,512]{2,1,0:T(8,128)(2,1)S(1)}, u32[]{:S(2)}, u32[]{:S(2)}) async-start(bf16[16,64,512]{2,1,0:T(8,128)(2,1)} %broadcast_select_fusion), calls=%async_computation.1 | async-start | bytes 2097152 | tf_op jit(solution)/shard_map/all_to_all | solution.py:422
  23.8 25.5 %collective-permute-start.1 = (bf16[64,512]{1,0:T(8,128)(2,1)S(1)}, bf16[64,512]{1,0:T(8,128)(2,1)S(1)}, u32[]{:S(2)}, u32[]{:S(2)}) collective-permute-start(bf16[64,512]{1,0:T(8,128)(2,1)S(1)} %get-tuple-element.14), channel_id=1, source_target_pairs={{1,0},{2,1},{3,2},{4,3},{5,4},{6,5},{7,6},{8,7},{9,8},{10,9},{11,1... | collective-permute-start | bytes 196616 | tf_op jit(solution)/shard_map/ppermute | solution.py:389
  26.1 23.3 %collective-permute-start = (bf16[64,512]{1,0:T(8,128)(2,1)S(1)}, bf16[64,512]{1,0:T(8,128)(2,1)S(1)}, u32[]{:S(2)}, u32[]{:S(2)}) collective-permute-start(bf16[64,512]{1,0:T(8,128)(2,1)S(1)} %get-tuple-element.15), channel_id=1, source_target_pairs={{0,1},{1,2},{2,3},{3,4},{4,5},{5,6},{6,7},{7,8},{8,9},{9,10},{10,1... | collective-permute-start | bytes 196616 | tf_op jit(solution)/shard_map/ppermute | solution.py:388
  30.6 21.5 %copy-start.3 = (bf16[64,15,64]{2,0,1:T(8,128)(2,1)}, bf16[64,15,64]{2,0,1:T(8,128)(2,1)S(1)}, u32[]{:S(2)}) copy-start(bf16[64,15,64]{2,0,1:T(8,128)(2,1)S(1)} %copy.36) | copy-start | bytes 368644
  30.8 21.3 %copy-start.2 = (bf16[1024,192]{1,0:T(8,128)(2,1)}, bf16[1024,192]{1,0:T(8,128)(2,1)S(1)}, u32[]{:S(2)}) copy-start(bf16[1024,192]{1,0:T(8,128)(2,1)S(1)} %copy.30.band_ref) | copy-start | bytes 1179652
  49.3 2.8 %copy-start.5 = (bf16[64,512]{1,0:T(8,128)(2,1)}, bf16[64,512]{1,0:T(8,128)(2,1)S(1)}, u32[]{:S(2)}) copy-start(bf16[64,512]{1,0:T(8,128)(2,1)S(1)} %collective-permute-done.1.hi_ref) | copy-start | bytes 196612
  49.3 2.8 %copy-start.6 = (bf16[64,512]{1,0:T(8,128)(2,1)}, bf16[64,512]{1,0:T(8,128)(2,1)S(1)}, u32[]{:S(2)}) copy-start(bf16[64,512]{1,0:T(8,128)(2,1)S(1)} %collective-permute-done.lo_ref) | copy-start | bytes 196612
  49.3 2.8 %copy-start.1 = (bf16[16,64,512]{2,1,0:T(8,128)(2,1)}, bf16[16,64,512]{2,1,0:T(8,128)(2,1)S(1)}, u32[]{:S(2)}) copy-start(bf16[16,64,512]{2,1,0:T(8,128)(2,1)S(1)} %all-to-all-done.1.arr_ref) | copy-start | bytes 3145732
  49.4 7.9 %copy-start.15 = (bf16[96,32]{0,1:T(8,128)(2,1)S(1)}, bf16[96,32]{0,1:T(8,128)(2,1)}, u32[]{:S(2)}) copy-start(bf16[96,32]{0,1:T(8,128)(2,1)} %param.12) | copy-start | bytes 18436
  49.4 8.6 %copy-start.8 = (bf16[32,256]{1,0:T(8,128)(2,1)S(1)}, bf16[32,256]{1,0:T(8,128)(2,1)}, u32[]{:S(2)}) copy-start(bf16[32,256]{1,0:T(8,128)(2,1)} %sw_ref.1) | copy-start | bytes 49156
  51.1 1.0 %copy-start.4 = (bf16[16,64,512]{2,1,0:T(8,128)(2,1)}, bf16[16,64,512]{2,1,0:T(8,128)(2,1)S(1)}, u32[]{:S(2)}) copy-start(bf16[16,64,512]{2,1,0:T(8,128)(2,1)S(1)} %get-tuple-element.11) | copy-start | bytes 3145732
  52.1 30.7 %all-to-all-start.2 = ((bf16[16,64,512]{2,1,0:T(8,128)(2,1)}), bf16[16,64,512]{2,1,0:T(8,128)(2,1)}, u32[]{:S(2)}, u32[]{:S(2)}) async-start(bf16[16,64,512]{2,1,0:T(8,128)(2,1)} %copy-done.4), calls=%async_computation.2 | async-start | bytes 2097152 | tf_op jit(solution)/shard_map/all_to_all | solution.py:422
  63.3 19.5 %collective-permute-start.3 = (bf16[64,512]{1,0:T(8,128)(2,1)S(1)}, bf16[64,512]{1,0:T(8,128)(2,1)S(1)}, u32[]{:S(2)}, u32[]{:S(2)}) collective-permute-start(bf16[64,512]{1,0:T(8,128)(2,1)S(1)} %get-tuple-element.16), channel_id=1, source_target_pairs={{1,0},{2,1},{3,2},{4,3},{5,4},{6,5},{7,6},{8,7},{9,8},{10,9},{11,1... | collective-permute-start | bytes 196616 | tf_op jit(solution)/shard_map/ppermute | solution.py:389
  65.6 17.2 %collective-permute-start.2 = (bf16[64,512]{1,0:T(8,128)(2,1)S(1)}, bf16[64,512]{1,0:T(8,128)(2,1)S(1)}, u32[]{:S(2)}, u32[]{:S(2)}) collective-permute-start(bf16[64,512]{1,0:T(8,128)(2,1)S(1)} %get-tuple-element.17), channel_id=1, source_target_pairs={{0,1},{1,2},{2,3},{3,4},{4,5},{5,6},{6,7},{7,8},{8,9},{9,10},{10,1... | collective-permute-start | bytes 196616 | tf_op jit(solution)/shard_map/ppermute | solution.py:388
  82.8 0.6 copy-start.13
  82.8 0.7 copy-start.14

commit v18 on v15

--- a/solution.py
+++ b/solution.py
@@ -182,14 +182,24 @@
 
 def early_kernel(
     col_ref, ptr_ref, req_ref, exp_ref, field_ref, lo_ref, hi_ref, arr_ref, band_ref, farw_ref,
-    send_ref, edge_ref, pad, blk,
+    send_ref, edge_ref, blk,
 ):
     nblk = field_ref.shape[0] // BLK
     own = lax.axis_index("node")
-    fill_pad(field_ref, lo_ref, hi_ref, pad)
     targets = [exp_ref[own, 0], exp_ref[own, 1], 0, nblk - 1]
     for i, t in enumerate(targets):
-        v = band_block(band_ref, pad, t)
+        pieces = []
+        for s in range(3):
+            b = jnp.clip(t - 1 + s, 0, nblk - 1)
+            v = field_ref[pl.ds(pl.multiple_of(b * BLK, BLK), BLK), :]
+            if s == 0:
+                v = jnp.where(t == 0, lo_ref[...], v)
+            if s == 2:
+                v = jnp.where(t == nblk - 1, hi_ref[...], v)
+            pieces.append(v)
+        win = jnp.concatenate(pieces, axis=0)
+        start = pl.multiple_of(t * BLK, BLK)
+        v = jnp.dot(band_ref[pl.ds(start, BLK), :], win, preferred_element_type=f32)
 
         def slot(k, acc):
             return acc + slot_product(col_ref, farw_ref, arr_ref, k)
@@ -310,7 +320,7 @@
             jax.ShapeDtypeStruct(arrived.shape, bf16),
             jax.ShapeDtypeStruct((2, BLK, width), bf16),
         ],
-        scratch_shapes=[pltpu.VMEM((nrows + 2 * BLK, width), bf16), pltpu.VMEM((4, BLK, width), bf16)],
+        scratch_shapes=[pltpu.VMEM((4, BLK, width), bf16)],
         compiler_params=BIG_VMEM,
         cost_estimate=pl.CostEstimate(
             flops=2 * BLK * BLK * width * (12 + farw3.shape[0]),

time: 88.3 us -> 87.8 us (level)
  no operation moved by 1% of the time
where the time goes in v18:
time: 87.8 us; the launch traced here: 87.4 us
  starting transfers between devices  30.2 us (34%)
  Pallas kernels  25.7 us (29%)
  waiting for transfers between devices  23.2 us (26%)
  local copies, waits for them, and re-layouts  6.13 us (7%)
  other arithmetic  1.3 us (1%)
    ppermute x2, waiting for transfers between devices, halo(): hi = lax.ppermute(first, 'node', backward)  23.2 us
    all_to_all x2, starting transfers between devices, exchange(): return lax.all_to_all(send, 'node', split_axis=0, concat_axis=0, tiled=True)  10.7 us
    ppermute x2, starting transfers between devices, halo(): lo = lax.ppermute(last, 'node', forward)  8.39 us
    pallas_call x1, Pallas kernels, hop1(): pl.pallas_call(hop1_kernel, in_specs=[smem(), smem()] + [vmem()] * 6 + [h...  8.3 us
    all_to_all x1, starting transfers between devices, local(): lax.all_to_all(prep(far_col, far_ptr), 'node', split_axis=0, concat_axis=...  6.55 us
    pallas_call x1, Pallas kernels, hop2(): pl.pallas_call(hop2_kernel, in_specs=[smem(), smem()] + [vmem()] * 5 + [h...  6.06 us
    unnamed x37, local copies, waits for them, and re-layouts  5.64 us
    pallas_call x1, Pallas kernels, front_skip(): pl.pallas_call(skip_kernel, grid=(rows // tile,), in_specs=[pl.BlockSpec(...  5.34 us
  transfers between devices with their start and end apart: 7, of which 2 were waited for; matrix products, arithmetic and copies ran while one was open for 2% of the time, Pallas kernels for 18%

profile of v18, /device:TPU:15, one launch (start us, length us, event | category | flops | bytes accessed | tf_op | source)
XLA Modules:
  0.0 87.4 jit_solution(3058220096856989200)
XLA Ops:
  0.6 1.4 %shard_map.104 = s32[16,16]{1,0:T(8,128)} custom-call(s32[1,15]{1,0:T(1,128)} %col_ref.7, s32[1,17]{1,0:T(1,128)} %ptr_ref.7), custom_call_target="tpu_custom_call" | custom-call | tf_op jit(solution)/shard_map/pallas_call | solution.py:77
  2.1 6.6 %all-to-all-start = ((s32[16,1,16]{2,1,0:T(1,128)}), s32[16,1,16]{2,1,0:T(1,128)S(1)}, u32[]{:S(2)}, u32[]{:S(2)}) async-start(s32[16,1,16]{2,1,0:T(1,128)} %bitcast.20), calls=%async_computation | async-start | bytes 16384 | tf_op jit(solution)/shard_map/all_to_all | solution.py:405
  8.6 0.8 copy.29.exp_ref
  9.4 1.6 %copy-done.4 = bf16[1024,1024]{1,0:T(8,128)(2,1)S(1)} copy-done((bf16[1024,1024]{1,0:T(8,128)(2,1)S(1)}, bf16[1024,1024]{1,0:T(8,128)(2,1)}, u32[]{:S(2)}) %copy-start.4) | copy-done | bytes 2097176
  11.0 0.7 copy-done.11
  11.7 2.5 %shard_map.105 = (bf16[1024,512]{1,0:T(8,128)(2,1)S(1)}, bf16[2,64,512]{2,1,0:T(8,128)(2,1)S(1)}) custom-call(s32[16,2]{1,0:T(8,128)S(1)} %copy.29.exp_ref, bf16[1024,1024]{1,0:T(8,128)(2,1)S(1)} %copy-done.4, bf16[64,64]{1,0:T(8,128)(2,1)S(1)} %copy-done.11), custom_call_target="tpu_custom_call" | custom-call | flops 1073741824 | bytes 3145728 | tf_op jit(solution)/shard_map/pallas_call | solution.py:102
  14.1 0.0 copy-start
  14.1 0.0 copy-start.13
  14.2 0.0 all-to-all-done
  14.2 0.2 slice_reduce_fusion
  14.4 0.2 fusion.2.req_ref
  14.6 0.0 copy-start.12
  14.6 1.1 %broadcast_select_fusion = bf16[16,64,512]{2,1,0:T(8,128)(2,1)} fusion(pred[16]{0:T(512)(128)(4,1)S(1)} %broadcast_compare_fusion, bf16[64,512]{1,0:T(8,128)(2,1)S(1)} %get-tuple-element.19, bf16[64,512]{1,0:T(8,128)(2,1)S(1)} %get-tuple-element.18), kind=kLoop, calls=%fused_computation | loop fusion | flops 524288 | bytes 1179664 | tf_op jit(solution)/shard_map/jit(_where)/select_n | solution.py:418
  15.7 6.2 %all-to-all-start.1 = ((bf16[16,64,512]{2,1,0:T(8,128)(2,1)}), bf16[16,64,512]{2,1,0:T(8,128)(2,1)S(1)}, u32[]{:S(2)}, u32[]{:S(2)}) async-start(bf16[16,64,512]{2,1,0:T(8,128)(2,1)} %broadcast_select_fusion), calls=%async_computation.1 | async-start | bytes 2097152 | tf_op jit(solution)/shard_map/all_to_all | solution.py:416
  21.9 2.3 %collective-permute-start.1 = (bf16[64,512]{1,0:T(8,128)(2,1)S(1)}, bf16[64,512]{1,0:T(8,128)(2,1)S(1)}, u32[]{:S(2)}, u32[]{:S(2)}) collective-permute-start(bf16[64,512]{1,0:T(8,128)(2,1)S(1)} %get-tuple-element.14), channel_id=1, source_target_pairs={{1,0},{2,1},{3,2},{4,3},{5,4},{6,5},{7,6},{8,7},{9,8},{10,9},{11,1... | collective-permute-start | bytes 196616 | tf_op jit(solution)/shard_map/ppermute | solution.py:383
  24.1 4.2 %collective-permute-start = (bf16[64,512]{1,0:T(8,128)(2,1)S(1)}, bf16[64,512]{1,0:T(8,128)(2,1)S(1)}, u32[]{:S(2)}, u32[]{:S(2)}) collective-permute-start(bf16[64,512]{1,0:T(8,128)(2,1)S(1)} %get-tuple-element.15), channel_id=1, source_target_pairs={{0,1},{1,2},{2,3},{3,4},{4,5},{5,6},{6,7},{7,8},{8,9},{9,10},{10,1... | collective-permute-start | bytes 196616 | tf_op jit(solution)/shard_map/ppermute | solution.py:382
  28.3 0.0 copy-done.13
  28.3 0.2 reshape.12
  28.6 0.1 copy.36
  28.6 0.0 copy-done.12
  28.7 0.0 copy-start.3
  28.7 0.2 copy.30.band_ref
  28.9 0.0 copy-start.2
  28.9 18.5 %collective-permute-done.1.hi_ref = bf16[64,512]{1,0:T(8,128)(2,1)S(1)} collective-permute-done((bf16[64,512]{1,0:T(8,128)(2,1)S(1)}, bf16[64,512]{1,0:T(8,128)(2,1)S(1)}, u32[]{:S(2)}, u32[]{:S(2)}) %collective-permute-start.1) | collective-permute-done | bytes 65568 | tf_op jit(solution)/shard_map/ppermute | solution.py:383
  47.4 0.0 collective-permute-done.lo_ref
  47.4 0.0 all-to-all-done.1.arr_ref
  47.4 0.0 copy-start.1
  47.4 0.0 copy-done.9
  47.4 0.0 copy-done.10
  47.4 0.0 copy-start.16
  47.5 0.0 copy-start.8
  47.5 2.1 %shard_map.106 = (bf16[16,64,512]{2,1,0:T(8,128)(2,1)S(1)}, bf16[2,64,512]{2,1,0:T(8,128)(2,1)S(1)}) custom-call(s32[1,15]{1,0:T(1,128)S(1)} %copy-done.9, s32[1,17]{1,0:T(1,128)S(1)} %copy-done.10, s32[16]{0:T(128)S(1)} %fusion.2.req_ref, s32[16,2]{1,0:T(8,128)S(1)} %copy.29.exp_ref, bf16[1024,512]{1,0:T(8,128)(2,1)S(1)} %get-tuple-element.8.field_ref.h_ref, ...), custom_call_target="tpu_custom_call" | custom-call | flops 113246208 | bytes 3145728 | tf_op jit(solution)/shard_map/pallas_call | solution.py:315
  49.6 0.0 copy-start.5
  49.6 1.0 %copy-done.5 = bf16[16,64,512]{2,1,0:T(8,128)(2,1)} copy-done((bf16[16,64,512]{2,1,0:T(8,128)(2,1)}, bf16[16,64,512]{2,1,0:T(8,128)(2,1)S(1)}, u32[]{:S(2)}) %copy-start.5) | copy-done | bytes 1048600
  50.6 0.0 copy-done.3
  50.6 0.0 copy-done.2
  50.6 4.5 %all-to-all-start.2 = ((bf16[16,64,512]{2,1,0:T(8,128)(2,1)}), bf16[16,64,512]{2,1,0:T(8,128)(2,1)}, u32[]{:S(2)}, u32[]{:S(2)}) async-start(bf16[16,64,512]{2,1,0:T(8,128)(2,1)} %copy-done.5), calls=%async_computation.2 | async-start | bytes 2097152 | tf_op jit(solution)/shard_map/all_to_all | solution.py:416
  55.1 0.7 copy.32.mix_ref
  55.9 5.3 %shard_map.109 = bf16[1024,4096]{1,0:T(8,128)(2,1)} custom-call(bf16[1024,512]{1,0:T(8,128)(2,1)S(1)} %get-tuple-element.8.field_ref.h_ref, bf16[32,256]{1,0:T(8,128)(2,1)S(1)} %copy-done.8), custom_call_target="tpu_custom_call" | custom-call | flops 2147483648 | bytes 9437184 | tf_op jit(solution)/shard_map/pallas_call | solution.py:126
  61.2 2.3 %collective-permute-start.3 = (bf16[64,512]{1,0:T(8,128)(2,1)S(1)}, bf16[64,512]{1,0:T(8,128)(2,1)S(1)}, u32[]{:S(2)}, u32[]{:S(2)}) collective-permute-start(bf16[64,512]{1,0:T(8,128)(2,1)S(1)} %get-tuple-element.16), channel_id=1, source_target_pairs={{1,0},{2,1},{3,2},{4,3},{5,4},{6,5},{7,6},{8,7},{9,8},{10,9},{11,1... | collective-permute-start | bytes 196616 | tf_op jit(solution)/shard_map/ppermute | solution.py:383
  63.5 4.2 %collective-permute-start.2 = (bf16[64,512]{1,0:T(8,128)(2,1)S(1)}, bf16[64,512]{1,0:T(8,128)(2,1)S(1)}, u32[]{:S(2)}, u32[]{:S(2)}) collective-permute-start(bf16[64,512]{1,0:T(8,128)(2,1)S(1)} %get-tuple-element.17), channel_id=1, source_target_pairs={{0,1},{1,2},{2,3},{3,4},{4,5},{5,6},{6,7},{7,8},{8,9},{9,10},{10,1... | collective-permute-start | bytes 196616 | tf_op jit(solution)/shard_map/ppermute | solution.py:382
  67.7 8.3 %shard_map.107 = (bf16[1024,512]{1,0:T(8,128)(2,1)}, f32[1024,512]{1,0:T(8,128)}, f32[1024,512]{1,0:T(8,128)}) custom-call(s32[1,15]{1,0:T(1,128)} %col_ref.7, s32[1,17]{1,0:T(1,128)} %ptr_ref.7, bf16[1024,512]{1,0:T(8,128)(2,1)} %copy-done, bf16[64,512]{1,0:T(8,128)(2,1)} %copy-done.7, bf16[64,512]{1,0:T(8,128)(2,1)} %copy-done.6, ...), custom_call_target="tpu_custom_call" | custom-call | flops 1002438656 | bytes 10485760 | tf_op jit(solution)/shard_map/pallas_call | solution.py:335
  76.0 4.7 %collective-permute-done.3.hi_ref = bf16[64,512]{1,0:T(8,128)(2,1)S(1)} collective-permute-done((bf16[64,512]{1,0:T(8,128)(2,1)S(1)}, bf16[64,512]{1,0:T(8,128)(2,1)S(1)}, u32[]{:S(2)}, u32[]{:S(2)}) %collective-permute-start.3) | collective-permute-done | bytes 65568 | tf_op jit(solution)/shard_map/ppermute | solution.py:383
  80.7 0.0 collective-permute-done.2.lo_ref
  80.7 0.0 all-to-all-done.2.arr_ref
  80.7 0.6 copy-done.14
  81.3 0.0 copy-done.15
  81.3 6.1 %shard_map.108 = bf16[1024,512]{1,0:T(8,128)(2,1)} custom-call(s32[1,15]{1,0:T(1,128)} %col_ref.7, s32[1,17]{1,0:T(1,128)} %ptr_ref.7, bf16[64,512]{1,0:T(8,128)(2,1)} %copy-done.15, bf16[64,512]{1,0:T(8,128)(2,1)} %copy-done.14, bf16[16,64,512]{2,1,0:T(8,128)(2,1)} %all-to-all-done.2.arr_ref, bf16[1024,192]{1,0:T(8,128)(2,1)} %copy-done.2, ...), custom_call_target="tpu_custom_call" | custom-call | flops 339738624 | bytes 6291456 | tf_op jit(solution)/shard_map/pallas_call | solution.py:358
  (18 shorter events, 0.1 us)
Async XLA Ops:
  2.1 12.1 %all-to-all-start = ((s32[16,1,16]{2,1,0:T(1,128)}), s32[16,1,16]{2,1,0:T(1,128)S(1)}, u32[]{:S(2)}, u32[]{:S(2)}) async-start(s32[16,1,16]{2,1,0:T(1,128)} %bitcast.20), calls=%async_computation | async-start | bytes 16384 | tf_op jit(solution)/shard_map/all_to_all | solution.py:405
  9.4 1.6 %copy-start.4 = (bf16[1024,1024]{1,0:T(8,128)(2,1)S(1)}, bf16[1024,1024]{1,0:T(8,128)(2,1)}, u32[]{:S(2)}) copy-start(bf16[1024,1024]{1,0:T(8,128)(2,1)} %x_hbm.1) | copy-start | bytes 6291460
  11.0 0.7 copy-start.11
  14.1 41.7 %copy-start = (bf16[1024,512]{1,0:T(8,128)(2,1)}, bf16[1024,512]{1,0:T(8,128)(2,1)S(1)}, u32[]{:S(2)}) copy-start(bf16[1024,512]{1,0:T(8,128)(2,1)S(1)} %get-tuple-element.8.field_ref.h_ref) | copy-start | bytes 3145732
  14.1 14.2 %copy-start.13 = (bf16[64,960]{1,0:T(8,128)(2,1)S(1)}, bf16[64,960]{1,0:T(8,128)(2,1)}, u32[]{:S(2)}) copy-start(bf16[64,960]{1,0:T(8,128)(2,1)} %param.14) | copy-start | bytes 368644
  14.6 14.1 %copy-start.12 = (bf16[1024,192]{0,1:T(8,128)(2,1)S(1)}, bf16[1024,192]{0,1:T(8,128)(2,1)}, u32[]{:S(2)}) copy-start(bf16[1024,192]{0,1:T(8,128)(2,1)} %param.13) | copy-start | bytes 1179652
  15.7 31.7 %copy-start.9 = (s32[1,15]{1,0:T(1,128)S(1)}, s32[1,15]{1,0:T(1,128)}, u32[]{:S(2)}) copy-start(s32[1,15]{1,0:T(1,128)} %col_ref.7) | copy-start | bytes 184
  15.7 31.7 %copy-start.10 = (s32[1,17]{1,0:T(1,128)S(1)}, s32[1,17]{1,0:T(1,128)}, u32[]{:S(2)}) copy-start(s32[1,17]{1,0:T(1,128)} %ptr_ref.7) | copy-start | bytes 208
  15.7 31.7 %all-to-all-start.1 = ((bf16[16,64,512]{2,1,0:T(8,128)(2,1)}), bf16[16,64,512]{2,1,0:T(8,128)(2,1)S(1)}, u32[]{:S(2)}, u32[]{:S(2)}) async-start(bf16[16,64,512]{2,1,0:T(8,128)(2,1)} %broadcast_select_fusion), calls=%async_computation.1 | async-start | bytes 2097152 | tf_op jit(solution)/shard_map/all_to_all | solution.py:416
  21.9 25.5 %collective-permute-start.1 = (bf16[64,512]{1,0:T(8,128)(2,1)S(1)}, bf16[64,512]{1,0:T(8,128)(2,1)S(1)}, u32[]{:S(2)}, u32[]{:S(2)}) collective-permute-start(bf16[64,512]{1,0:T(8,128)(2,1)S(1)} %get-tuple-element.14), channel_id=1, source_target_pairs={{1,0},{2,1},{3,2},{4,3},{5,4},{6,5},{7,6},{8,7},{9,8},{10,9},{11,1... | collective-permute-start | bytes 196616 | tf_op jit(solution)/shard_map/ppermute | solution.py:383
  24.1 23.3 %collective-permute-start = (bf16[64,512]{1,0:T(8,128)(2,1)S(1)}, bf16[64,512]{1,0:T(8,128)(2,1)S(1)}, u32[]{:S(2)}, u32[]{:S(2)}) collective-permute-start(bf16[64,512]{1,0:T(8,128)(2,1)S(1)} %get-tuple-element.15), channel_id=1, source_target_pairs={{0,1},{1,2},{2,3},{3,4},{4,5},{5,6},{6,7},{7,8},{8,9},{9,10},{10,1... | collective-permute-start | bytes 196616 | tf_op jit(solution)/shard_map/ppermute | solution.py:382
  28.7 21.9 %copy-start.3 = (bf16[64,15,64]{2,0,1:T(8,128)(2,1)}, bf16[64,15,64]{2,0,1:T(8,128)(2,1)S(1)}, u32[]{:S(2)}) copy-start(bf16[64,15,64]{2,0,1:T(8,128)(2,1)S(1)} %copy.36) | copy-start | bytes 368644
  28.9 21.7 %copy-start.2 = (bf16[1024,192]{1,0:T(8,128)(2,1)}, bf16[1024,192]{1,0:T(8,128)(2,1)S(1)}, u32[]{:S(2)}) copy-start(bf16[1024,192]{1,0:T(8,128)(2,1)S(1)} %copy.30.band_ref) | copy-start | bytes 1179652
  47.4 3.2 %copy-start.6 = (bf16[64,512]{1,0:T(8,128)(2,1)}, bf16[64,512]{1,0:T(8,128)(2,1)S(1)}, u32[]{:S(2)}) copy-start(bf16[64,512]{1,0:T(8,128)(2,1)S(1)} %collective-permute-done.1.hi_ref) | copy-start | bytes 196612
  47.4 3.2 %copy-start.7 = (bf16[64,512]{1,0:T(8,128)(2,1)}, bf16[64,512]{1,0:T(8,128)(2,1)S(1)}, u32[]{:S(2)}) copy-start(bf16[64,512]{1,0:T(8,128)(2,1)S(1)} %collective-permute-done.lo_ref) | copy-start | bytes 196612
  47.4 3.2 %copy-start.1 = (bf16[16,64,512]{2,1,0:T(8,128)(2,1)}, bf16[16,64,512]{2,1,0:T(8,128)(2,1)S(1)}, u32[]{:S(2)}) copy-start(bf16[16,64,512]{2,1,0:T(8,128)(2,1)S(1)} %all-to-all-done.1.arr_ref) | copy-start | bytes 3145732
  47.4 7.7 %copy-start.16 = (bf16[96,32]{0,1:T(8,128)(2,1)S(1)}, bf16[96,32]{0,1:T(8,128)(2,1)}, u32[]{:S(2)}) copy-start(bf16[96,32]{0,1:T(8,128)(2,1)} %param.12) | copy-start | bytes 18436
  47.5 8.4 %copy-start.8 = (bf16[32,256]{1,0:T(8,128)(2,1)S(1)}, bf16[32,256]{1,0:T(8,128)(2,1)}, u32[]{:S(2)}) copy-start(bf16[32,256]{1,0:T(8,128)(2,1)} %sw_ref.1) | copy-start | bytes 49156
  49.6 1.0 %copy-start.5 = (bf16[16,64,512]{2,1,0:T(8,128)(2,1)}, bf16[16,64,512]{2,1,0:T(8,128)(2,1)S(1)}, u32[]{:S(2)}) copy-start(bf16[16,64,512]{2,1,0:T(8,128)(2,1)S(1)} %get-tuple-element.11) | copy-start | bytes 3145732
  50.6 30.1 %all-to-all-start.2 = ((bf16[16,64,512]{2,1,0:T(8,128)(2,1)}), bf16[16,64,512]{2,1,0:T(8,128)(2,1)}, u32[]{:S(2)}, u32[]{:S(2)}) async-start(bf16[16,64,512]{2,1,0:T(8,128)(2,1)} %copy-done.5), calls=%async_computation.2 | async-start | bytes 2097152 | tf_op jit(solution)/shard_map/all_to_all | solution.py:416
  61.2 19.5 %collective-permute-start.3 = (bf16[64,512]{1,0:T(8,128)(2,1)S(1)}, bf16[64,512]{1,0:T(8,128)(2,1)S(1)}, u32[]{:S(2)}, u32[]{:S(2)}) collective-permute-start(bf16[64,512]{1,0:T(8,128)(2,1)S(1)} %get-tuple-element.16), channel_id=1, source_target_pairs={{1,0},{2,1},{3,2},{4,3},{5,4},{6,5},{7,6},{8,7},{9,8},{10,9},{11,1... | collective-permute-start | bytes 196616 | tf_op jit(solution)/shard_map/ppermute | solution.py:383
  63.5 17.2 %collective-permute-start.2 = (bf16[64,512]{1,0:T(8,128)(2,1)S(1)}, bf16[64,512]{1,0:T(8,128)(2,1)S(1)}, u32[]{:S(2)}, u32[]{:S(2)}) collective-permute-start(bf16[64,512]{1,0:T(8,128)(2,1)S(1)} %get-tuple-element.17), channel_id=1, source_target_pairs={{0,1},{1,2},{2,3},{3,4},{4,5},{5,6},{6,7},{7,8},{8,9},{9,10},{10,1... | collective-permute-start | bytes 196616 | tf_op jit(solution)/shard_map/ppermute | solution.py:382
  80.7 0.6 copy-start.14
  80.7 0.6 copy-start.15

commit v19 on v15

--- a/solution.py
+++ b/solution.py
@@ -208,7 +208,7 @@
 
 def hop1_kernel(
     col_ref, ptr_ref, field_ref, lo_ref, hi_ref, arr_ref, band_ref, farw_ref, x_hbm, mix_ref,
-    out_ref, part_ref, acc2_ref, acc, pad, xs, sems,
+    out_ref, part_ref, acc2_ref, m2_ref, acc, pad, xs, sems,
 ):
     nrows, width = field_ref.shape
     nblk = nrows // BLK
@@ -226,6 +226,7 @@
     mix = mix_ref[...]
     m0 = bd_inkernel(mix[:cw], per)
     m1 = bd_inkernel(mix[cw : 2 * cw], per)
+    m2_ref[...] = bd_inkernel(mix[2 * cw :], per)
     x_copy.wait()
     for j in range(width // CHUNK):
         cols = slice(j * CHUNK, (j + 1) * CHUNK)
@@ -236,7 +237,7 @@
 
 
 def hop2_kernel(
-    col_ref, ptr_ref, lo_ref, hi_ref, arr_ref, band_ref, farw_ref, acc2_hbm, part_hbm, mix_ref,
+    col_ref, ptr_ref, lo_ref, hi_ref, arr_ref, band_ref, farw_ref, acc2_hbm, part_hbm, m2_ref,
     out_ref, far, a2, ps, sems,
 ):
     nrows, width = out_ref.shape
@@ -268,8 +269,7 @@
         return carry
 
     lax.fori_loop(0, far_cap, slot, 0)
-    cw = mix_ref.shape[1]
-    m2 = bd_inkernel(mix_ref[2 * cw :], CHUNK // cw)
+    m2 = m2_ref[...]
     for j in range(chunks):
         ca, cp = copies[j]
         ca.wait()
@@ -325,11 +325,12 @@
     return pl.pallas_call(
         hop1_kernel,
         in_specs=[smem(), smem()] + [vmem()] * 6 + [hbm(), vmem()],
-        out_specs=[vmem(), vmem(), vmem()],
+        out_specs=[vmem(), vmem(), vmem(), vmem()],
         out_shape=[
             jax.ShapeDtypeStruct((nrows, width), bf16),
             jax.ShapeDtypeStruct((nrows, width), f32),
             jax.ShapeDtypeStruct((nrows, width), f32),
+            jax.ShapeDtypeStruct((CHUNK, CHUNK), bf16),
         ],
         scratch_shapes=scratch(field)
         + [pltpu.VMEM((nrows, width), bf16), pltpu.SemaphoreType.DMA((1,))],
@@ -343,7 +344,7 @@
     )(far_col, far_ptr, field, lo, hi, arrived, band, farw3, features, mix)
 
 
-def hop2(far_col, far_ptr, lo, hi, arrived, band, farw3, acc2, part, mix):
+def hop2(far_col, far_ptr, lo, hi, arrived, band, farw3, acc2, part, m2):
     nrows, width = part.shape
     return pl.pallas_call(
         hop2_kernel,
@@ -362,7 +363,7 @@
             transcendentals=0,
             bytes_accessed=4 * width * nrows * 3,
         ),
-    )(far_col, far_ptr, lo, hi, arrived, band, farw3, acc2, part, mix)
+    )(far_col, far_ptr, lo, hi, arrived, band, farw3, acc2, part, m2)
 
 
 def halo(first, last):
@@ -413,11 +414,11 @@
     )
     arrived2 = exchange(send2)
     lo2, hi2 = halo(edge[0], edge[1])
-    hop_one, part, acc2 = hop1(
+    hop_one, part, acc2, m2 = hop1(
         far_col, far_ptr, hidden, lo1, hi1, arrived1, band_weight, farw3, features, mix_weight
     )
     residual = hop2(
-        far_col, far_ptr, lo2, hi2, arrived2, band_weight, farw3, acc2, part, mix_weight
+        far_col, far_ptr, lo2, hi2, arrived2, band_weight, farw3, acc2, part, m2
     )
     return residual, skip_out
 

time: 88.3 us -> 88 us (level)
  no operation moved by 1% of the time
where the time goes in v19:
time: 88 us; the launch traced here: 87.6 us
  starting transfers between devices  30.8 us (35%)
  Pallas kernels  25.4 us (29%)
  waiting for transfers between devices  23.2 us (26%)
  local copies, waits for them, and re-layouts  6.14 us (7%)
  other arithmetic  1.3 us (1%)
    ppermute x2, waiting for transfers between devices, halo(): hi = lax.ppermute(first, 'node', backward)  23.1 us
    all_to_all x2, starting transfers between devices, exchange(): return lax.all_to_all(send, 'node', split_axis=0, concat_axis=0, tiled=True)  11.3 us
    pallas_call x1, Pallas kernels, hop1(): pl.pallas_call(hop1_kernel, in_specs=[smem(), smem()] + [vmem()] * 6 + [h...  8.39 us
    ppermute x2, starting transfers between devices, halo(): lo = lax.ppermute(last, 'node', forward)  8.37 us
    all_to_all x1, starting transfers between devices, local(): lax.all_to_all(prep(far_col, far_ptr), 'node', split_axis=0, concat_axis=...  6.55 us
    pallas_call x1, Pallas kernels, hop2(): pl.pallas_call(hop2_kernel, in_specs=[smem(), smem()] + [vmem()] * 5 + [h...  5.77 us
    unnamed x37, local copies, waits for them, and re-layouts  5.65 us
    pallas_call x1, Pallas kernels, front_skip(): pl.pallas_call(skip_kernel, grid=(rows // tile,), in_specs=[pl.BlockSpec(...  5.32 us
  transfers between devices with their start and end apart: 7, of which 2 were waited for; matrix products, arithmetic and copies ran while one was open for 2% of the time, Pallas kernels for 18%

profile of v19, /device:TPU:15, one launch (start us, length us, event | category | flops | bytes accessed | tf_op | source)
XLA Modules:
  0.0 87.6 jit_solution(12953561449074486397)
XLA Ops:
  0.6 1.4 %shard_map.104 = s32[16,16]{1,0:T(8,128)} custom-call(s32[1,15]{1,0:T(1,128)} %col_ref.7, s32[1,17]{1,0:T(1,128)} %ptr_ref.7), custom_call_target="tpu_custom_call" | custom-call | tf_op jit(solution)/shard_map/pallas_call | solution.py:77
  2.1 6.6 %all-to-all-start = ((s32[16,1,16]{2,1,0:T(1,128)}), s32[16,1,16]{2,1,0:T(1,128)S(1)}, u32[]{:S(2)}, u32[]{:S(2)}) async-start(s32[16,1,16]{2,1,0:T(1,128)} %bitcast.20), calls=%async_computation | async-start | bytes 16384 | tf_op jit(solution)/shard_map/all_to_all | solution.py:396
  8.6 0.8 copy.27.exp_ref
  9.4 1.6 %copy-done.4 = bf16[1024,1024]{1,0:T(8,128)(2,1)S(1)} copy-done((bf16[1024,1024]{1,0:T(8,128)(2,1)S(1)}, bf16[1024,1024]{1,0:T(8,128)(2,1)}, u32[]{:S(2)}) %copy-start.4) | copy-done | bytes 2097176
  11.0 0.7 copy-done.11
  11.7 2.5 %shard_map.105 = (bf16[1024,512]{1,0:T(8,128)(2,1)S(1)}, bf16[2,64,512]{2,1,0:T(8,128)(2,1)S(1)}) custom-call(s32[16,2]{1,0:T(8,128)S(1)} %copy.27.exp_ref, bf16[1024,1024]{1,0:T(8,128)(2,1)S(1)} %copy-done.4, bf16[64,64]{1,0:T(8,128)(2,1)S(1)} %copy-done.11), custom_call_target="tpu_custom_call" | custom-call | flops 1073741824 | bytes 3145728 | tf_op jit(solution)/shard_map/pallas_call | solution.py:102
  14.1 0.0 copy-start
  14.1 0.0 copy-start.13
  14.2 0.0 all-to-all-done
  14.2 0.2 slice_reduce_fusion
  14.4 0.2 fusion.2.req_ref
  14.6 0.0 copy-start.12
  14.6 1.1 %broadcast_select_fusion = bf16[16,64,512]{2,1,0:T(8,128)(2,1)} fusion(pred[16]{0:T(512)(128)(4,1)S(1)} %broadcast_compare_fusion, bf16[64,512]{1,0:T(8,128)(2,1)S(1)} %get-tuple-element.21, bf16[64,512]{1,0:T(8,128)(2,1)S(1)} %get-tuple-element.20), kind=kLoop, calls=%fused_computation | loop fusion | flops 524288 | bytes 1179664 | tf_op jit(solution)/shard_map/jit(_where)/select_n | solution.py:409
  15.7 6.2 %all-to-all-start.1 = ((bf16[16,64,512]{2,1,0:T(8,128)(2,1)}), bf16[16,64,512]{2,1,0:T(8,128)(2,1)S(1)}, u32[]{:S(2)}, u32[]{:S(2)}) async-start(bf16[16,64,512]{2,1,0:T(8,128)(2,1)} %broadcast_select_fusion), calls=%async_computation.1 | async-start | bytes 2097152 | tf_op jit(solution)/shard_map/all_to_all | solution.py:407
  21.9 2.3 %collective-permute-start.1 = (bf16[64,512]{1,0:T(8,128)(2,1)S(1)}, bf16[64,512]{1,0:T(8,128)(2,1)S(1)}, u32[]{:S(2)}, u32[]{:S(2)}) collective-permute-start(bf16[64,512]{1,0:T(8,128)(2,1)S(1)} %get-tuple-element.16), channel_id=1, source_target_pairs={{1,0},{2,1},{3,2},{4,3},{5,4},{6,5},{7,6},{8,7},{9,8},{10,9},{11,1... | collective-permute-start | bytes 196616 | tf_op jit(solution)/shard_map/ppermute | solution.py:374
  24.1 4.2 %collective-permute-start = (bf16[64,512]{1,0:T(8,128)(2,1)S(1)}, bf16[64,512]{1,0:T(8,128)(2,1)S(1)}, u32[]{:S(2)}, u32[]{:S(2)}) collective-permute-start(bf16[64,512]{1,0:T(8,128)(2,1)S(1)} %get-tuple-element.17), channel_id=1, source_target_pairs={{0,1},{1,2},{2,3},{3,4},{4,5},{5,6},{6,7},{7,8},{8,9},{9,10},{10,1... | collective-permute-start | bytes 196616 | tf_op jit(solution)/shard_map/ppermute | solution.py:373
  28.3 0.0 copy-done.13
  28.3 0.2 reshape.12
  28.6 0.1 copy.33
  28.6 0.0 copy-done.12
  28.7 0.0 copy-start.3
  28.7 0.2 copy.28.band_ref
  28.9 0.0 copy-start.2
  28.9 18.5 %collective-permute-done.1.hi_ref = bf16[64,512]{1,0:T(8,128)(2,1)S(1)} collective-permute-done((bf16[64,512]{1,0:T(8,128)(2,1)S(1)}, bf16[64,512]{1,0:T(8,128)(2,1)S(1)}, u32[]{:S(2)}, u32[]{:S(2)}) %collective-permute-start.1) | collective-permute-done | bytes 65568 | tf_op jit(solution)/shard_map/ppermute | solution.py:374
  47.4 0.0 collective-permute-done.lo_ref
  47.4 0.0 all-to-all-done.1.arr_ref
  47.4 0.0 copy-start.1
  47.4 0.0 copy-done.9
  47.4 0.0 copy-done.10
  47.4 0.0 copy-start.16
  47.5 0.0 copy-start.8
  47.5 2.0 %shard_map.106 = (bf16[16,64,512]{2,1,0:T(8,128)(2,1)S(1)}, bf16[2,64,512]{2,1,0:T(8,128)(2,1)S(1)}) custom-call(s32[1,15]{1,0:T(1,128)S(1)} %copy-done.9, s32[1,17]{1,0:T(1,128)S(1)} %copy-done.10, s32[16]{0:T(128)S(1)} %fusion.2.req_ref, s32[16,2]{1,0:T(8,128)S(1)} %copy.27.exp_ref, bf16[1024,512]{1,0:T(8,128)(2,1)S(1)} %get-tuple-element.9.field_ref.h_ref, ...), custom_call_target="tpu_custom_call" | custom-call | flops 113246208 | bytes 3145728 | tf_op jit(solution)/shard_map/pallas_call | solution.py:305
  49.5 0.0 copy-start.5
  49.5 1.0 %copy-done.5 = bf16[16,64,512]{2,1,0:T(8,128)(2,1)} copy-done((bf16[16,64,512]{2,1,0:T(8,128)(2,1)}, bf16[16,64,512]{2,1,0:T(8,128)(2,1)S(1)}, u32[]{:S(2)}) %copy-start.5) | copy-done | bytes 1048600
  50.5 0.0 copy-done.6
  50.5 5.1 %all-to-all-start.2 = ((bf16[16,64,512]{2,1,0:T(8,128)(2,1)}), bf16[16,64,512]{2,1,0:T(8,128)(2,1)}, u32[]{:S(2)}, u32[]{:S(2)}) async-start(bf16[16,64,512]{2,1,0:T(8,128)(2,1)} %copy-done.5), calls=%async_computation.2 | async-start | bytes 2097152 | tf_op jit(solution)/shard_map/all_to_all | solution.py:407
  55.6 0.7 copy.30.mix_ref
  56.3 0.0 copy-done
  56.4 5.3 %shard_map.109 = bf16[1024,4096]{1,0:T(8,128)(2,1)} custom-call(bf16[1024,512]{1,0:T(8,128)(2,1)S(1)} %get-tuple-element.9.field_ref.h_ref, bf16[32,256]{1,0:T(8,128)(2,1)S(1)} %copy-done.8), custom_call_target="tpu_custom_call" | custom-call | flops 2147483648 | bytes 9437184 | tf_op jit(solution)/shard_map/pallas_call | solution.py:126
  61.7 2.3 %collective-permute-start.3 = (bf16[64,512]{1,0:T(8,128)(2,1)S(1)}, bf16[64,512]{1,0:T(8,128)(2,1)S(1)}, u32[]{:S(2)}, u32[]{:S(2)}) collective-permute-start(bf16[64,512]{1,0:T(8,128)(2,1)S(1)} %get-tuple-element.18), channel_id=1, source_target_pairs={{1,0},{2,1},{3,2},{4,3},{5,4},{6,5},{7,6},{8,7},{9,8},{10,9},{11,1... | collective-permute-start | bytes 196616 | tf_op jit(solution)/shard_map/ppermute | solution.py:374
  64.0 4.2 %collective-permute-start.2 = (bf16[64,512]{1,0:T(8,128)(2,1)S(1)}, bf16[64,512]{1,0:T(8,128)(2,1)S(1)}, u32[]{:S(2)}, u32[]{:S(2)}) collective-permute-start(bf16[64,512]{1,0:T(8,128)(2,1)S(1)} %get-tuple-element.19), channel_id=1, source_target_pairs={{0,1},{1,2},{2,3},{3,4},{4,5},{5,6},{6,7},{7,8},{8,9},{9,10},{10,1... | collective-permute-start | bytes 196616 | tf_op jit(solution)/shard_map/ppermute | solution.py:373
  68.2 8.4 %shard_map.107 = (bf16[1024,512]{1,0:T(8,128)(2,1)}, f32[1024,512]{1,0:T(8,128)}, f32[1024,512]{1,0:T(8,128)}, bf16[256,256]{1,0:T(8,128)(2,1)}) custom-call(s32[1,15]{1,0:T(1,128)} %col_ref.7, s32[1,17]{1,0:T(1,128)} %ptr_ref.7, bf16[1024,512]{1,0:T(8,128)(2,1)} %copy-done, bf16[64,512]{1,0:T(8,128)(2,1)} %copy-done.7, bf16[64,512]{1,0:T(8,128)(2,1)} %copy-done.6, ...), custom_call_target="tpu_custom_call" | custom-call | flops 1002438656 | bytes 10485760 | tf_op jit(solution)/shard_map/pallas_call | solution.py:325
  76.6 4.6 %collective-permute-done.3.hi_ref = bf16[64,512]{1,0:T(8,128)(2,1)S(1)} collective-permute-done((bf16[64,512]{1,0:T(8,128)(2,1)S(1)}, bf16[64,512]{1,0:T(8,128)(2,1)S(1)}, u32[]{:S(2)}, u32[]{:S(2)}) %collective-permute-start.3) | collective-permute-done | bytes 65568 | tf_op jit(solution)/shard_map/ppermute | solution.py:374
  81.2 0.0 collective-permute-done.2.lo_ref
  81.2 0.0 all-to-all-done.2.arr_ref
  81.2 0.6 copy-done.14
  81.8 0.0 copy-done.15
  81.8 5.8 %shard_map.108 = bf16[1024,512]{1,0:T(8,128)(2,1)} custom-call(s32[1,15]{1,0:T(1,128)} %col_ref.7, s32[1,17]{1,0:T(1,128)} %ptr_ref.7, bf16[64,512]{1,0:T(8,128)(2,1)} %copy-done.15, bf16[64,512]{1,0:T(8,128)(2,1)} %copy-done.14, bf16[16,64,512]{2,1,0:T(8,128)(2,1)} %all-to-all-done.2.arr_ref, bf16[1024,192]{1,0:T(8,128)(2,1)} %copy-done.2, ...), custom_call_target="tpu_custom_call" | custom-call | flops 339738624 | bytes 6291456 | tf_op jit(solution)/shard_map/pallas_call | solution.py:349
  (18 shorter events, 0.1 us)
Async XLA Ops:
  2.1 12.1 %all-to-all-start = ((s32[16,1,16]{2,1,0:T(1,128)}), s32[16,1,16]{2,1,0:T(1,128)S(1)}, u32[]{:S(2)}, u32[]{:S(2)}) async-start(s32[16,1,16]{2,1,0:T(1,128)} %bitcast.20), calls=%async_computation | async-start | bytes 16384 | tf_op jit(solution)/shard_map/all_to_all | solution.py:396
  9.4 1.6 %copy-start.4 = (bf16[1024,1024]{1,0:T(8,128)(2,1)S(1)}, bf16[1024,1024]{1,0:T(8,128)(2,1)}, u32[]{:S(2)}) copy-start(bf16[1024,1024]{1,0:T(8,128)(2,1)} %x_hbm.1) | copy-start | bytes 6291460
  11.0 0.7 copy-start.11
  14.1 42.2 %copy-start = (bf16[1024,512]{1,0:T(8,128)(2,1)}, bf16[1024,512]{1,0:T(8,128)(2,1)S(1)}, u32[]{:S(2)}) copy-start(bf16[1024,512]{1,0:T(8,128)(2,1)S(1)} %get-tuple-element.9.field_ref.h_ref) | copy-start | bytes 3145732
  14.1 14.2 %copy-start.13 = (bf16[64,960]{1,0:T(8,128)(2,1)S(1)}, bf16[64,960]{1,0:T(8,128)(2,1)}, u32[]{:S(2)}) copy-start(bf16[64,960]{1,0:T(8,128)(2,1)} %param.14) | copy-start | bytes 368644
  14.6 14.1 %copy-start.12 = (bf16[1024,192]{0,1:T(8,128)(2,1)S(1)}, bf16[1024,192]{0,1:T(8,128)(2,1)}, u32[]{:S(2)}) copy-start(bf16[1024,192]{0,1:T(8,128)(2,1)} %param.13) | copy-start | bytes 1179652
  15.7 31.7 %copy-start.9 = (s32[1,15]{1,0:T(1,128)S(1)}, s32[1,15]{1,0:T(1,128)}, u32[]{:S(2)}) copy-start(s32[1,15]{1,0:T(1,128)} %col_ref.7) | copy-start | bytes 184
  15.7 31.7 %copy-start.10 = (s32[1,17]{1,0:T(1,128)S(1)}, s32[1,17]{1,0:T(1,128)}, u32[]{:S(2)}) copy-start(s32[1,17]{1,0:T(1,128)} %ptr_ref.7) | copy-start | bytes 208
  15.7 31.7 %all-to-all-start.1 = ((bf16[16,64,512]{2,1,0:T(8,128)(2,1)}), bf16[16,64,512]{2,1,0:T(8,128)(2,1)S(1)}, u32[]{:S(2)}, u32[]{:S(2)}) async-start(bf16[16,64,512]{2,1,0:T(8,128)(2,1)} %broadcast_select_fusion), calls=%async_computation.1 | async-start | bytes 2097152 | tf_op jit(solution)/shard_map/all_to_all | solution.py:407
  21.9 25.5 %collective-permute-start.1 = (bf16[64,512]{1,0:T(8,128)(2,1)S(1)}, bf16[64,512]{1,0:T(8,128)(2,1)S(1)}, u32[]{:S(2)}, u32[]{:S(2)}) collective-permute-start(bf16[64,512]{1,0:T(8,128)(2,1)S(1)} %get-tuple-element.16), channel_id=1, source_target_pairs={{1,0},{2,1},{3,2},{4,3},{5,4},{6,5},{7,6},{8,7},{9,8},{10,9},{11,1... | collective-permute-start | bytes 196616 | tf_op jit(solution)/shard_map/ppermute | solution.py:374
  24.1 23.3 %collective-permute-start = (bf16[64,512]{1,0:T(8,128)(2,1)S(1)}, bf16[64,512]{1,0:T(8,128)(2,1)S(1)}, u32[]{:S(2)}, u32[]{:S(2)}) collective-permute-start(bf16[64,512]{1,0:T(8,128)(2,1)S(1)} %get-tuple-element.17), channel_id=1, source_target_pairs={{0,1},{1,2},{2,3},{3,4},{4,5},{5,6},{6,7},{7,8},{8,9},{9,10},{10,1... | collective-permute-start | bytes 196616 | tf_op jit(solution)/shard_map/ppermute | solution.py:373
  28.7 21.8 %copy-start.3 = (bf16[64,15,64]{2,0,1:T(8,128)(2,1)}, bf16[64,15,64]{2,0,1:T(8,128)(2,1)S(1)}, u32[]{:S(2)}) copy-start(bf16[64,15,64]{2,0,1:T(8,128)(2,1)S(1)} %copy.33) | copy-start | bytes 368644
  28.9 21.6 %copy-start.2 = (bf16[1024,192]{1,0:T(8,128)(2,1)}, bf16[1024,192]{1,0:T(8,128)(2,1)S(1)}, u32[]{:S(2)}) copy-start(bf16[1024,192]{1,0:T(8,128)(2,1)S(1)} %copy.28.band_ref) | copy-start | bytes 1179652
  47.4 3.1 %copy-start.6 = (bf16[64,512]{1,0:T(8,128)(2,1)}, bf16[64,512]{1,0:T(8,128)(2,1)S(1)}, u32[]{:S(2)}) copy-start(bf16[64,512]{1,0:T(8,128)(2,1)S(1)} %collective-permute-done.1.hi_ref) | copy-start | bytes 196612
  47.4 3.1 %copy-start.7 = (bf16[64,512]{1,0:T(8,128)(2,1)}, bf16[64,512]{1,0:T(8,128)(2,1)S(1)}, u32[]{:S(2)}) copy-start(bf16[64,512]{1,0:T(8,128)(2,1)S(1)} %collective-permute-done.lo_ref) | copy-start | bytes 196612
  47.4 3.1 %copy-start.1 = (bf16[16,64,512]{2,1,0:T(8,128)(2,1)}, bf16[16,64,512]{2,1,0:T(8,128)(2,1)S(1)}, u32[]{:S(2)}) copy-start(bf16[16,64,512]{2,1,0:T(8,128)(2,1)S(1)} %all-to-all-done.1.arr_ref) | copy-start | bytes 3145732
  47.4 8.2 %copy-start.16 = (bf16[96,32]{0,1:T(8,128)(2,1)S(1)}, bf16[96,32]{0,1:T(8,128)(2,1)}, u32[]{:S(2)}) copy-start(bf16[96,32]{0,1:T(8,128)(2,1)} %param.12) | copy-start | bytes 18436
  47.5 8.9 %copy-start.8 = (bf16[32,256]{1,0:T(8,128)(2,1)S(1)}, bf16[32,256]{1,0:T(8,128)(2,1)}, u32[]{:S(2)}) copy-start(bf16[32,256]{1,0:T(8,128)(2,1)} %sw_ref.1) | copy-start | bytes 49156
  49.5 1.0 %copy-start.5 = (bf16[16,64,512]{2,1,0:T(8,128)(2,1)}, bf16[16,64,512]{2,1,0:T(8,128)(2,1)S(1)}, u32[]{:S(2)}) copy-start(bf16[16,64,512]{2,1,0:T(8,128)(2,1)S(1)} %get-tuple-element.12) | copy-start | bytes 3145732
  50.5 30.7 %all-to-all-start.2 = ((bf16[16,64,512]{2,1,0:T(8,128)(2,1)}), bf16[16,64,512]{2,1,0:T(8,128)(2,1)}, u32[]{:S(2)}, u32[]{:S(2)}) async-start(bf16[16,64,512]{2,1,0:T(8,128)(2,1)} %copy-done.5), calls=%async_computation.2 | async-start | bytes 2097152 | tf_op jit(solution)/shard_map/all_to_all | solution.py:407
  61.7 19.5 %collective-permute-start.3 = (bf16[64,512]{1,0:T(8,128)(2,1)S(1)}, bf16[64,512]{1,0:T(8,128)(2,1)S(1)}, u32[]{:S(2)}, u32[]{:S(2)}) collective-permute-start(bf16[64,512]{1,0:T(8,128)(2,1)S(1)} %get-tuple-element.18), channel_id=1, source_target_pairs={{1,0},{2,1},{3,2},{4,3},{5,4},{6,5},{7,6},{8,7},{9,8},{10,9},{11,1... | collective-permute-start | bytes 196616 | tf_op jit(solution)/shard_map/ppermute | solution.py:374
  64.0 17.2 %collective-permute-start.2 = (bf16[64,512]{1,0:T(8,128)(2,1)S(1)}, bf16[64,512]{1,0:T(8,128)(2,1)S(1)}, u32[]{:S(2)}, u32[]{:S(2)}) collective-permute-start(bf16[64,512]{1,0:T(8,128)(2,1)S(1)} %get-tuple-element.19), channel_id=1, source_target_pairs={{0,1},{1,2},{2,3},{3,4},{4,5},{5,6},{6,7},{7,8},{8,9},{9,10},{10,1... | collective-permute-start | bytes 196616 | tf_op jit(solution)/shard_map/ppermute | solution.py:373
  81.2 0.6 copy-start.14
  81.2 0.6 copy-start.15

commit v20 on v19

--- a/solution.py
+++ b/solution.py
@@ -182,14 +182,24 @@
 
 def early_kernel(
     col_ref, ptr_ref, req_ref, exp_ref, field_ref, lo_ref, hi_ref, arr_ref, band_ref, farw_ref,
-    send_ref, edge_ref, pad, blk,
+    send_ref, edge_ref, blk,
 ):
     nblk = field_ref.shape[0] // BLK
     own = lax.axis_index("node")
-    fill_pad(field_ref, lo_ref, hi_ref, pad)
     targets = [exp_ref[own, 0], exp_ref[own, 1], 0, nblk - 1]
     for i, t in enumerate(targets):
-        v = band_block(band_ref, pad, t)
+        pieces = []
+        for s in range(3):
+            b = jnp.clip(t - 1 + s, 0, nblk - 1)
+            v = field_ref[pl.ds(pl.multiple_of(b * BLK, BLK), BLK), :]
+            if s == 0:
+                v = jnp.where(t == 0, lo_ref[...], v)
+            if s == 2:
+                v = jnp.where(t == nblk - 1, hi_ref[...], v)
+            pieces.append(v)
+        win = jnp.concatenate(pieces, axis=0)
+        start = pl.multiple_of(t * BLK, BLK)
+        v = jnp.dot(band_ref[pl.ds(start, BLK), :], win, preferred_element_type=f32)
 
         def slot(k, acc):
             return acc + slot_product(col_ref, farw_ref, arr_ref, k)
@@ -310,7 +320,7 @@
             jax.ShapeDtypeStruct(arrived.shape, bf16),
             jax.ShapeDtypeStruct((2, BLK, width), bf16),
         ],
-        scratch_shapes=[pltpu.VMEM((nrows + 2 * BLK, width), bf16), pltpu.VMEM((4, BLK, width), bf16)],
+        scratch_shapes=[pltpu.VMEM((4, BLK, width), bf16)],
         compiler_params=BIG_VMEM,
         cost_estimate=pl.CostEstimate(
             flops=2 * BLK * BLK * width * (12 + farw3.shape[0]),

time: 88 us -> 88.3 us (level)
  no operation moved by 1% of the time
where the time goes in v20:
time: 88.3 us; the launch traced here: 87.6 us
  starting transfers between devices  30.5 us (35%)
  Pallas kernels  25.7 us (29%)
  waiting for transfers between devices  23.1 us (26%)
  local copies, waits for them, and re-layouts  6.14 us (7%)
  other arithmetic  1.3 us (1%)
    ppermute x2, waiting for transfers between devices, halo(): hi = lax.ppermute(first, 'node', backward)  23.1 us
    all_to_all x2, starting transfers between devices, exchange(): return lax.all_to_all(send, 'node', split_axis=0, concat_axis=0, tiled=True)  11 us
    ppermute x2, starting transfers between devices, halo(): lo = lax.ppermute(last, 'node', forward)  8.4 us
    pallas_call x1, Pallas kernels, hop1(): pl.pallas_call(hop1_kernel, in_specs=[smem(), smem()] + [vmem()] * 6 + [h...  8.38 us
    all_to_all x1, starting transfers between devices, local(): lax.all_to_all(prep(far_col, far_ptr), 'node', split_axis=0, concat_axis=...  6.55 us
    pallas_call x1, Pallas kernels, hop2(): pl.pallas_call(hop2_kernel, in_specs=[smem(), smem()] + [vmem()] * 5 + [h...  5.76 us
    unnamed x37, local copies, waits for them, and re-layouts  5.65 us
    pallas_call x1, Pallas kernels, front_skip(): pl.pallas_call(skip_kernel, grid=(rows // tile,), in_specs=[pl.BlockSpec(...  5.34 us
  transfers between devices with their start and end apart: 7, of which 2 were waited for; matrix products, arithmetic and copies ran while one was open for 2% of the time, Pallas kernels for 18%

profile of v20, /device:TPU:15, one launch (start us, length us, event | category | flops | bytes accessed | tf_op | source)
XLA Modules:
  0.0 87.6 jit_solution(9074708983438692295)
XLA Ops:
  0.6 1.4 %shard_map.104 = s32[16,16]{1,0:T(8,128)} custom-call(s32[1,15]{1,0:T(1,128)} %col_ref.7, s32[1,17]{1,0:T(1,128)} %ptr_ref.7), custom_call_target="tpu_custom_call" | custom-call | tf_op jit(solution)/shard_map/pallas_call | solution.py:77
  2.1 6.6 %all-to-all-start = ((s32[16,1,16]{2,1,0:T(1,128)}), s32[16,1,16]{2,1,0:T(1,128)S(1)}, u32[]{:S(2)}, u32[]{:S(2)}) async-start(s32[16,1,16]{2,1,0:T(1,128)} %bitcast.20), calls=%async_computation | async-start | bytes 16384 | tf_op jit(solution)/shard_map/all_to_all | solution.py:406
  8.6 0.8 copy.27.exp_ref
  9.4 1.6 %copy-done.4 = bf16[1024,1024]{1,0:T(8,128)(2,1)S(1)} copy-done((bf16[1024,1024]{1,0:T(8,128)(2,1)S(1)}, bf16[1024,1024]{1,0:T(8,128)(2,1)}, u32[]{:S(2)}) %copy-start.4) | copy-done | bytes 2097176
  11.0 0.7 copy-done.11
  11.7 2.5 %shard_map.105 = (bf16[1024,512]{1,0:T(8,128)(2,1)S(1)}, bf16[2,64,512]{2,1,0:T(8,128)(2,1)S(1)}) custom-call(s32[16,2]{1,0:T(8,128)S(1)} %copy.27.exp_ref, bf16[1024,1024]{1,0:T(8,128)(2,1)S(1)} %copy-done.4, bf16[64,64]{1,0:T(8,128)(2,1)S(1)} %copy-done.11), custom_call_target="tpu_custom_call" | custom-call | flops 1073741824 | bytes 3145728 | tf_op jit(solution)/shard_map/pallas_call | solution.py:102
  14.1 0.0 copy-start
  14.1 0.0 copy-start.13
  14.2 0.0 all-to-all-done
  14.2 0.2 slice_reduce_fusion
  14.4 0.2 fusion.2.req_ref
  14.6 0.0 copy-start.12
  14.6 1.1 %broadcast_select_fusion = bf16[16,64,512]{2,1,0:T(8,128)(2,1)} fusion(pred[16]{0:T(512)(128)(4,1)S(1)} %broadcast_compare_fusion, bf16[64,512]{1,0:T(8,128)(2,1)S(1)} %get-tuple-element.21, bf16[64,512]{1,0:T(8,128)(2,1)S(1)} %get-tuple-element.20), kind=kLoop, calls=%fused_computation | loop fusion | flops 524288 | bytes 1179664 | tf_op jit(solution)/shard_map/jit(_where)/select_n | solution.py:419
  15.7 6.2 %all-to-all-start.1 = ((bf16[16,64,512]{2,1,0:T(8,128)(2,1)}), bf16[16,64,512]{2,1,0:T(8,128)(2,1)S(1)}, u32[]{:S(2)}, u32[]{:S(2)}) async-start(bf16[16,64,512]{2,1,0:T(8,128)(2,1)} %broadcast_select_fusion), calls=%async_computation.1 | async-start | bytes 2097152 | tf_op jit(solution)/shard_map/all_to_all | solution.py:417
  21.9 2.3 %collective-permute-start.1 = (bf16[64,512]{1,0:T(8,128)(2,1)S(1)}, bf16[64,512]{1,0:T(8,128)(2,1)S(1)}, u32[]{:S(2)}, u32[]{:S(2)}) collective-permute-start(bf16[64,512]{1,0:T(8,128)(2,1)S(1)} %get-tuple-element.16), channel_id=1, source_target_pairs={{1,0},{2,1},{3,2},{4,3},{5,4},{6,5},{7,6},{8,7},{9,8},{10,9},{11,1... | collective-permute-start | bytes 196616 | tf_op jit(solution)/shard_map/ppermute | solution.py:384
  24.1 4.2 %collective-permute-start = (bf16[64,512]{1,0:T(8,128)(2,1)S(1)}, bf16[64,512]{1,0:T(8,128)(2,1)S(1)}, u32[]{:S(2)}, u32[]{:S(2)}) collective-permute-start(bf16[64,512]{1,0:T(8,128)(2,1)S(1)} %get-tuple-element.17), channel_id=1, source_target_pairs={{0,1},{1,2},{2,3},{3,4},{4,5},{5,6},{6,7},{7,8},{8,9},{9,10},{10,1... | collective-permute-start | bytes 196616 | tf_op jit(solution)/shard_map/ppermute | solution.py:383
  28.3 0.0 copy-done.13
  28.3 0.2 reshape.12
  28.6 0.1 copy.33
  28.6 0.0 copy-done.12
  28.7 0.0 copy-start.3
  28.7 0.2 copy.28.band_ref
  28.9 0.0 copy-start.2
  28.9 18.5 %collective-permute-done.1.hi_ref = bf16[64,512]{1,0:T(8,128)(2,1)S(1)} collective-permute-done((bf16[64,512]{1,0:T(8,128)(2,1)S(1)}, bf16[64,512]{1,0:T(8,128)(2,1)S(1)}, u32[]{:S(2)}, u32[]{:S(2)}) %collective-permute-start.1) | collective-permute-done | bytes 65568 | tf_op jit(solution)/shard_map/ppermute | solution.py:384
  47.4 0.0 collective-permute-done.lo_ref
  47.4 0.0 all-to-all-done.1.arr_ref
  47.4 0.0 copy-start.1
  47.4 0.0 copy-start.16
  47.5 0.0 copy-start.8
  47.5 2.3 %shard_map.106 = (bf16[16,64,512]{2,1,0:T(8,128)(2,1)S(1)}, bf16[2,64,512]{2,1,0:T(8,128)(2,1)S(1)}) custom-call(s32[1,15]{1,0:T(1,128)S(1)} %copy-done.9, s32[1,17]{1,0:T(1,128)S(1)} %copy-done.10, s32[16]{0:T(128)S(1)} %fusion.2.req_ref, s32[16,2]{1,0:T(8,128)S(1)} %copy.27.exp_ref, bf16[1024,512]{1,0:T(8,128)(2,1)S(1)} %get-tuple-element.9.field_ref.h_ref, ...), custom_call_target="tpu_custom_call" | custom-call | flops 113246208 | bytes 3145728 | tf_op jit(solution)/shard_map/pallas_call | solution.py:315
  49.8 0.0 copy-start.5
  49.8 1.0 %copy-done.5 = bf16[16,64,512]{2,1,0:T(8,128)(2,1)} copy-done((bf16[16,64,512]{2,1,0:T(8,128)(2,1)}, bf16[16,64,512]{2,1,0:T(8,128)(2,1)S(1)}, u32[]{:S(2)}) %copy-start.5) | copy-done | bytes 1048600
  50.7 0.0 copy-done.3
  50.7 0.0 copy-done.1
  50.8 4.8 %all-to-all-start.2 = ((bf16[16,64,512]{2,1,0:T(8,128)(2,1)}), bf16[16,64,512]{2,1,0:T(8,128)(2,1)}, u32[]{:S(2)}, u32[]{:S(2)}) async-start(bf16[16,64,512]{2,1,0:T(8,128)(2,1)} %copy-done.5), calls=%async_computation.2 | async-start | bytes 2097152 | tf_op jit(solution)/shard_map/all_to_all | solution.py:417
  55.6 0.0 copy-done.16
  55.6 0.7 copy.30.mix_ref
  56.3 0.0 copy-done.8
  56.3 5.3 %shard_map.109 = bf16[1024,4096]{1,0:T(8,128)(2,1)} custom-call(bf16[1024,512]{1,0:T(8,128)(2,1)S(1)} %get-tuple-element.9.field_ref.h_ref, bf16[32,256]{1,0:T(8,128)(2,1)S(1)} %copy-done.8), custom_call_target="tpu_custom_call" | custom-call | flops 2147483648 | bytes 9437184 | tf_op jit(solution)/shard_map/pallas_call | solution.py:126
  61.7 2.3 %collective-permute-start.3 = (bf16[64,512]{1,0:T(8,128)(2,1)S(1)}, bf16[64,512]{1,0:T(8,128)(2,1)S(1)}, u32[]{:S(2)}, u32[]{:S(2)}) collective-permute-start(bf16[64,512]{1,0:T(8,128)(2,1)S(1)} %get-tuple-element.18), channel_id=1, source_target_pairs={{1,0},{2,1},{3,2},{4,3},{5,4},{6,5},{7,6},{8,7},{9,8},{10,9},{11,1... | collective-permute-start | bytes 196616 | tf_op jit(solution)/shard_map/ppermute | solution.py:384
  63.9 4.2 %collective-permute-start.2 = (bf16[64,512]{1,0:T(8,128)(2,1)S(1)}, bf16[64,512]{1,0:T(8,128)(2,1)S(1)}, u32[]{:S(2)}, u32[]{:S(2)}) collective-permute-start(bf16[64,512]{1,0:T(8,128)(2,1)S(1)} %get-tuple-element.19), channel_id=1, source_target_pairs={{0,1},{1,2},{2,3},{3,4},{4,5},{5,6},{6,7},{7,8},{8,9},{9,10},{10,1... | collective-permute-start | bytes 196616 | tf_op jit(solution)/shard_map/ppermute | solution.py:383
  68.1 8.4 %shard_map.107 = (bf16[1024,512]{1,0:T(8,128)(2,1)}, f32[1024,512]{1,0:T(8,128)}, f32[1024,512]{1,0:T(8,128)}, bf16[256,256]{1,0:T(8,128)(2,1)}) custom-call(s32[1,15]{1,0:T(1,128)} %col_ref.7, s32[1,17]{1,0:T(1,128)} %ptr_ref.7, bf16[1024,512]{1,0:T(8,128)(2,1)} %copy-done, bf16[64,512]{1,0:T(8,128)(2,1)} %copy-done.7, bf16[64,512]{1,0:T(8,128)(2,1)} %copy-done.6, ...), custom_call_target="tpu_custom_call" | custom-call | flops 1002438656 | bytes 10485760 | tf_op jit(solution)/shard_map/pallas_call | solution.py:335
  76.5 4.6 %collective-permute-done.3.hi_ref = bf16[64,512]{1,0:T(8,128)(2,1)S(1)} collective-permute-done((bf16[64,512]{1,0:T(8,128)(2,1)S(1)}, bf16[64,512]{1,0:T(8,128)(2,1)S(1)}, u32[]{:S(2)}, u32[]{:S(2)}) %collective-permute-start.3) | collective-permute-done | bytes 65568 | tf_op jit(solution)/shard_map/ppermute | solution.py:384
  81.1 0.0 collective-permute-done.2.lo_ref
  81.2 0.0 all-to-all-done.2.arr_ref
  81.2 0.6 copy-done.14
  81.8 0.0 copy-done.15
  81.8 5.8 %shard_map.108 = bf16[1024,512]{1,0:T(8,128)(2,1)} custom-call(s32[1,15]{1,0:T(1,128)} %col_ref.7, s32[1,17]{1,0:T(1,128)} %ptr_ref.7, bf16[64,512]{1,0:T(8,128)(2,1)} %copy-done.15, bf16[64,512]{1,0:T(8,128)(2,1)} %copy-done.14, bf16[16,64,512]{2,1,0:T(8,128)(2,1)} %all-to-all-done.2.arr_ref, bf16[1024,192]{1,0:T(8,128)(2,1)} %copy-done.2, ...), custom_call_target="tpu_custom_call" | custom-call | flops 339738624 | bytes 6291456 | tf_op jit(solution)/shard_map/pallas_call | solution.py:359
  (18 shorter events, 0.1 us)
Async XLA Ops:
  2.1 12.1 %all-to-all-start = ((s32[16,1,16]{2,1,0:T(1,128)}), s32[16,1,16]{2,1,0:T(1,128)S(1)}, u32[]{:S(2)}, u32[]{:S(2)}) async-start(s32[16,1,16]{2,1,0:T(1,128)} %bitcast.20), calls=%async_computation | async-start | bytes 16384 | tf_op jit(solution)/shard_map/all_to_all | solution.py:406
  9.4 1.6 %copy-start.4 = (bf16[1024,1024]{1,0:T(8,128)(2,1)S(1)}, bf16[1024,1024]{1,0:T(8,128)(2,1)}, u32[]{:S(2)}) copy-start(bf16[1024,1024]{1,0:T(8,128)(2,1)} %x_hbm.1) | copy-start | bytes 6291460
  11.0 0.7 copy-start.11
  14.1 42.2 %copy-start = (bf16[1024,512]{1,0:T(8,128)(2,1)}, bf16[1024,512]{1,0:T(8,128)(2,1)S(1)}, u32[]{:S(2)}) copy-start(bf16[1024,512]{1,0:T(8,128)(2,1)S(1)} %get-tuple-element.9.field_ref.h_ref) | copy-start | bytes 3145732
  14.1 14.2 %copy-start.13 = (bf16[64,960]{1,0:T(8,128)(2,1)S(1)}, bf16[64,960]{1,0:T(8,128)(2,1)}, u32[]{:S(2)}) copy-start(bf16[64,960]{1,0:T(8,128)(2,1)} %param.14) | copy-start | bytes 368644
  14.6 14.1 %copy-start.12 = (bf16[1024,192]{0,1:T(8,128)(2,1)S(1)}, bf16[1024,192]{0,1:T(8,128)(2,1)}, u32[]{:S(2)}) copy-start(bf16[1024,192]{0,1:T(8,128)(2,1)} %param.13) | copy-start | bytes 1179652
  15.7 31.7 %copy-start.9 = (s32[1,15]{1,0:T(1,128)S(1)}, s32[1,15]{1,0:T(1,128)}, u32[]{:S(2)}) copy-start(s32[1,15]{1,0:T(1,128)} %col_ref.7) | copy-start | bytes 184
  15.7 31.7 %copy-start.10 = (s32[1,17]{1,0:T(1,128)S(1)}, s32[1,17]{1,0:T(1,128)}, u32[]{:S(2)}) copy-start(s32[1,17]{1,0:T(1,128)} %ptr_ref.7) | copy-start | bytes 208
  15.7 31.7 %all-to-all-start.1 = ((bf16[16,64,512]{2,1,0:T(8,128)(2,1)}), bf16[16,64,512]{2,1,0:T(8,128)(2,1)S(1)}, u32[]{:S(2)}, u32[]{:S(2)}) async-start(bf16[16,64,512]{2,1,0:T(8,128)(2,1)} %broadcast_select_fusion), calls=%async_computation.1 | async-start | bytes 2097152 | tf_op jit(solution)/shard_map/all_to_all | solution.py:417
  21.9 25.5 %collective-permute-start.1 = (bf16[64,512]{1,0:T(8,128)(2,1)S(1)}, bf16[64,512]{1,0:T(8,128)(2,1)S(1)}, u32[]{:S(2)}, u32[]{:S(2)}) collective-permute-start(bf16[64,512]{1,0:T(8,128)(2,1)S(1)} %get-tuple-element.16), channel_id=1, source_target_pairs={{1,0},{2,1},{3,2},{4,3},{5,4},{6,5},{7,6},{8,7},{9,8},{10,9},{11,1... | collective-permute-start | bytes 196616 | tf_op jit(solution)/shard_map/ppermute | solution.py:384
  24.1 23.3 %collective-permute-start = (bf16[64,512]{1,0:T(8,128)(2,1)S(1)}, bf16[64,512]{1,0:T(8,128)(2,1)S(1)}, u32[]{:S(2)}, u32[]{:S(2)}) collective-permute-start(bf16[64,512]{1,0:T(8,128)(2,1)S(1)} %get-tuple-element.17), channel_id=1, source_target_pairs={{0,1},{1,2},{2,3},{3,4},{4,5},{5,6},{6,7},{7,8},{8,9},{9,10},{10,1... | collective-permute-start | bytes 196616 | tf_op jit(solution)/shard_map/ppermute | solution.py:383
  28.7 22.1 %copy-start.3 = (bf16[64,15,64]{2,0,1:T(8,128)(2,1)}, bf16[64,15,64]{2,0,1:T(8,128)(2,1)S(1)}, u32[]{:S(2)}) copy-start(bf16[64,15,64]{2,0,1:T(8,128)(2,1)S(1)} %copy.33) | copy-start | bytes 368644
  28.9 21.9 %copy-start.2 = (bf16[1024,192]{1,0:T(8,128)(2,1)}, bf16[1024,192]{1,0:T(8,128)(2,1)S(1)}, u32[]{:S(2)}) copy-start(bf16[1024,192]{1,0:T(8,128)(2,1)S(1)} %copy.28.band_ref) | copy-start | bytes 1179652
  47.4 3.3 %copy-start.6 = (bf16[64,512]{1,0:T(8,128)(2,1)}, bf16[64,512]{1,0:T(8,128)(2,1)S(1)}, u32[]{:S(2)}) copy-start(bf16[64,512]{1,0:T(8,128)(2,1)S(1)} %collective-permute-done.1.hi_ref) | copy-start | bytes 196612
  47.4 3.3 %copy-start.7 = (bf16[64,512]{1,0:T(8,128)(2,1)}, bf16[64,512]{1,0:T(8,128)(2,1)S(1)}, u32[]{:S(2)}) copy-start(bf16[64,512]{1,0:T(8,128)(2,1)S(1)} %collective-permute-done.lo_ref) | copy-start | bytes 196612
  47.4 3.3 %copy-start.1 = (bf16[16,64,512]{2,1,0:T(8,128)(2,1)}, bf16[16,64,512]{2,1,0:T(8,128)(2,1)S(1)}, u32[]{:S(2)}) copy-start(bf16[16,64,512]{2,1,0:T(8,128)(2,1)S(1)} %all-to-all-done.1.arr_ref) | copy-start | bytes 3145732
  47.4 8.1 %copy-start.16 = (bf16[96,32]{0,1:T(8,128)(2,1)S(1)}, bf16[96,32]{0,1:T(8,128)(2,1)}, u32[]{:S(2)}) copy-start(bf16[96,32]{0,1:T(8,128)(2,1)} %param.12) | copy-start | bytes 18436
  47.5 8.9 %copy-start.8 = (bf16[32,256]{1,0:T(8,128)(2,1)S(1)}, bf16[32,256]{1,0:T(8,128)(2,1)}, u32[]{:S(2)}) copy-start(bf16[32,256]{1,0:T(8,128)(2,1)} %sw_ref.1) | copy-start | bytes 49156
  49.8 1.0 %copy-start.5 = (bf16[16,64,512]{2,1,0:T(8,128)(2,1)}, bf16[16,64,512]{2,1,0:T(8,128)(2,1)S(1)}, u32[]{:S(2)}) copy-start(bf16[16,64,512]{2,1,0:T(8,128)(2,1)S(1)} %get-tuple-element.12) | copy-start | bytes 3145732
  50.8 30.4 %all-to-all-start.2 = ((bf16[16,64,512]{2,1,0:T(8,128)(2,1)}), bf16[16,64,512]{2,1,0:T(8,128)(2,1)}, u32[]{:S(2)}, u32[]{:S(2)}) async-start(bf16[16,64,512]{2,1,0:T(8,128)(2,1)} %copy-done.5), calls=%async_computation.2 | async-start | bytes 2097152 | tf_op jit(solution)/shard_map/all_to_all | solution.py:417
  61.7 19.5 %collective-permute-start.3 = (bf16[64,512]{1,0:T(8,128)(2,1)S(1)}, bf16[64,512]{1,0:T(8,128)(2,1)S(1)}, u32[]{:S(2)}, u32[]{:S(2)}) collective-permute-start(bf16[64,512]{1,0:T(8,128)(2,1)S(1)} %get-tuple-element.18), channel_id=1, source_target_pairs={{1,0},{2,1},{3,2},{4,3},{5,4},{6,5},{7,6},{8,7},{9,8},{10,9},{11,1... | collective-permute-start | bytes 196616 | tf_op jit(solution)/shard_map/ppermute | solution.py:384
  63.9 17.2 %collective-permute-start.2 = (bf16[64,512]{1,0:T(8,128)(2,1)S(1)}, bf16[64,512]{1,0:T(8,128)(2,1)S(1)}, u32[]{:S(2)}, u32[]{:S(2)}) collective-permute-start(bf16[64,512]{1,0:T(8,128)(2,1)S(1)} %get-tuple-element.19), channel_id=1, source_target_pairs={{0,1},{1,2},{2,3},{3,4},{4,5},{5,6},{6,7},{7,8},{8,9},{9,10},{10,1... | collective-permute-start | bytes 196616 | tf_op jit(solution)/shard_map/ppermute | solution.py:383
  81.1 0.6 copy-start.14
  81.2 0.6 copy-start.15

commit v21 on v19

--- a/solution.py
+++ b/solution.py
@@ -61,7 +61,7 @@
             ).astype(bf16)
     own = lax.axis_index("node")
     for e in range(ex_ref.shape[0]):
-        ex_ref[e] = h_ref[pl.ds(pl.multiple_of(exp_ref[own, e] * BLK, BLK), BLK), :]
+        ex_ref[e] = h_ref[pl.ds(pl.multiple_of(exp_ref[e, own] * BLK, BLK), BLK), :]
 
 
 def prep_kernel(col_ref, ptr_ref, out_ref):
@@ -105,7 +105,7 @@
         out_specs=[vmem(), vmem()],
         out_shape=[
             jax.ShapeDtypeStruct((rows, half), bf16),
-            jax.ShapeDtypeStruct((export_block.shape[1], BLK, half), bf16),
+            jax.ShapeDtypeStruct((export_block.shape[0], BLK, half), bf16),
         ],
         compiler_params=pltpu.CompilerParams(vmem_limit_bytes=48 * 1024 * 1024),
         cost_estimate=pl.CostEstimate(
@@ -398,7 +398,7 @@
     cols_all = info_all[:, :far_cap]
     hits = (cols_all // EXPORT == own_index) & (slot_ids[None, :] < info_all[:, far_cap:])
     requested = jnp.sum(jnp.where(hits, cols_all % EXPORT, 0), axis=1).astype(jnp.int32)
-    hidden, ex2 = front_hidden(export_block, features, filter_gate_weight)
+    hidden, ex2 = front_hidden(export_block.T, features, filter_gate_weight)
     blocks = node_rows // BLK
     width = hidden.shape[1]
     farw3 = far_weight.reshape(BLK, far_cap, BLK).transpose(1, 0, 2)

time: 88 us -> 87.3 us (level)
  starting transfers between devices: 30.8 us -> 29.9 us
    all_to_all x2, starting transfers between devices: 11.3 us -> 10.4 us  [exchange(): return lax.all_to_all(send, 'node', split_axis=0, concat_axis=0, tiled=True)]
    unnamed x37 -> x41, local copies, waits for them, and re-layouts: 5.65 us -> 5.63 us
  transfers between devices with their start and end apart: 7 -> 7, of which waited for: 2 -> 2; matrix products, arithmetic and copies ran while one was open for 2% -> 2% of each run, Pallas kernels for 18% -> 19%
where the time goes in v21:
time: 87.3 us; the launch traced here: 86.7 us
  starting transfers between devices  29.9 us (34%)
  Pallas kernels  25.7 us (29%)
  waiting for transfers between devices  22.8 us (26%)
  local copies, waits for them, and re-layouts  6.12 us (7%)
  other arithmetic  1.3 us (1%)
  between operations  0.9 us (1%)
    ppermute x2, waiting for transfers between devices, halo(): hi = lax.ppermute(first, 'node', backward)  22.8 us
    all_to_all x2, starting transfers between devices, exchange(): return lax.all_to_all(send, 'node', split_axis=0, concat_axis=0, tiled=True)  10.4 us
    ppermute x2, starting transfers between devices, halo(): lo = lax.ppermute(last, 'node', forward)  8.66 us
    pallas_call x1, Pallas kernels, hop1(): pl.pallas_call(hop1_kernel, in_specs=[smem(), smem()] + [vmem()] * 6 + [h...  8.39 us
    all_to_all x1, starting transfers between devices, local(): lax.all_to_all(prep(far_col, far_ptr), 'node', split_axis=0, concat_axis=...  6.55 us
    pallas_call x1, Pallas kernels, hop2(): pl.pallas_call(hop2_kernel, in_specs=[smem(), smem()] + [vmem()] * 5 + [h...  5.77 us
    unnamed x41, local copies, waits for them, and re-layouts  5.63 us
    pallas_call x1, Pallas kernels, front_skip(): pl.pallas_call(skip_kernel, grid=(rows // tile,), in_specs=[pl.BlockSpec(...  5.34 us
  transfers between devices with their start and end apart: 7, of which 2 were waited for; matrix products, arithmetic and copies ran while one was open for 2% of the time, Pallas kernels for 19%

profile of v21, /device:TPU:15, one launch (start us, length us, event | category | flops | bytes accessed | tf_op | source)
XLA Modules:
  0.0 86.7 jit_solution(10592663068538795446)
XLA Ops:
  0.6 1.4 %shard_map.104 = s32[16,16]{1,0:T(8,128)} custom-call(s32[1,15]{1,0:T(1,128)} %col_ref.7, s32[1,17]{1,0:T(1,128)} %ptr_ref.7), custom_call_target="tpu_custom_call" | custom-call | tf_op jit(solution)/shard_map/pallas_call | solution.py:77
  2.1 6.6 %all-to-all-start = ((s32[16,1,16]{2,1,0:T(1,128)}), s32[16,1,16]{2,1,0:T(1,128)S(1)}, u32[]{:S(2)}, u32[]{:S(2)}) async-start(s32[16,1,16]{2,1,0:T(1,128)} %bitcast.22), calls=%async_computation | async-start | bytes 16384 | tf_op jit(solution)/shard_map/all_to_all | solution.py:396
  8.6 1.6 %copy-done.4 = bf16[1024,1024]{1,0:T(8,128)(2,1)S(1)} copy-done((bf16[1024,1024]{1,0:T(8,128)(2,1)S(1)}, bf16[1024,1024]{1,0:T(8,128)(2,1)}, u32[]{:S(2)}) %copy-start.4) | copy-done | bytes 2097176
  10.2 0.7 copy-done.11
  10.9 0.7 copy-done.13
  11.6 2.3 %shard_map.105 = (bf16[1024,512]{1,0:T(8,128)(2,1)S(1)}, bf16[2,64,512]{2,1,0:T(8,128)(2,1)S(1)}) custom-call(s32[2,16]{1,0:T(2,128)S(1)} %bitcast.19, bf16[1024,1024]{1,0:T(8,128)(2,1)S(1)} %copy-done.4, bf16[64,64]{1,0:T(8,128)(2,1)S(1)} %copy-done.13), custom_call_target="tpu_custom_call" | custom-call | flops 1073741824 | bytes 3145728 | tf_op jit(solution)/shard_map/pallas_call | solution.py:102
  13.9 0.0 copy-start
  14.0 0.0 copy-start.12
  14.0 0.0 copy-start.15
  14.0 0.0 all-to-all-done
  14.0 0.2 slice_reduce_fusion
  14.2 0.2 fusion.2.req_ref
  14.4 0.0 copy-start.14
  14.4 1.1 %broadcast_select_fusion = bf16[16,64,512]{2,1,0:T(8,128)(2,1)} fusion(pred[16]{0:T(512)(128)(4,1)S(1)} %broadcast_compare_fusion, bf16[64,512]{1,0:T(8,128)(2,1)S(1)} %get-tuple-element.21, bf16[64,512]{1,0:T(8,128)(2,1)S(1)} %get-tuple-element.20), kind=kLoop, calls=%fused_computation | loop fusion | flops 524288 | bytes 1179664 | tf_op jit(solution)/shard_map/jit(_where)/select_n | solution.py:409
  15.5 6.2 %all-to-all-start.1 = ((bf16[16,64,512]{2,1,0:T(8,128)(2,1)}), bf16[16,64,512]{2,1,0:T(8,128)(2,1)S(1)}, u32[]{:S(2)}, u32[]{:S(2)}) async-start(bf16[16,64,512]{2,1,0:T(8,128)(2,1)} %broadcast_select_fusion), calls=%async_computation.1 | async-start | bytes 2097152 | tf_op jit(solution)/shard_map/all_to_all | solution.py:407
  21.7 2.3 %collective-permute-start.1 = (bf16[64,512]{1,0:T(8,128)(2,1)S(1)}, bf16[64,512]{1,0:T(8,128)(2,1)S(1)}, u32[]{:S(2)}, u32[]{:S(2)}) collective-permute-start(bf16[64,512]{1,0:T(8,128)(2,1)S(1)} %get-tuple-element.16), channel_id=1, source_target_pairs={{1,0},{2,1},{3,2},{4,3},{5,4},{6,5},{7,6},{8,7},{9,8},{10,9},{11,1... | collective-permute-start | bytes 196616 | tf_op jit(solution)/shard_map/ppermute | solution.py:374
  24.0 4.2 %collective-permute-start = (bf16[64,512]{1,0:T(8,128)(2,1)S(1)}, bf16[64,512]{1,0:T(8,128)(2,1)S(1)}, u32[]{:S(2)}, u32[]{:S(2)}) collective-permute-start(bf16[64,512]{1,0:T(8,128)(2,1)S(1)} %get-tuple-element.17), channel_id=1, source_target_pairs={{0,1},{1,2},{2,3},{3,4},{4,5},{5,6},{6,7},{7,8},{8,9},{9,10},{10,1... | collective-permute-start | bytes 196616 | tf_op jit(solution)/shard_map/ppermute | solution.py:373
  28.2 0.0 copy-done.12
  28.2 0.1 copy.24.exp_ref
  28.3 0.0 copy-done.15
  28.3 0.2 reshape.12
  28.5 0.1 copy.30
  28.5 0.0 copy-done.14
  28.6 0.0 copy-start.3
  28.6 0.2 copy.25.band_ref
  28.8 0.0 copy-start.2
  28.8 18.4 %collective-permute-done.1.hi_ref = bf16[64,512]{1,0:T(8,128)(2,1)S(1)} collective-permute-done((bf16[64,512]{1,0:T(8,128)(2,1)S(1)}, bf16[64,512]{1,0:T(8,128)(2,1)S(1)}, u32[]{:S(2)}, u32[]{:S(2)}) %collective-permute-start.1) | collective-permute-done | bytes 65568 | tf_op jit(solution)/shard_map/ppermute | solution.py:374
  47.2 0.0 collective-permute-done.lo_ref
  47.2 0.0 all-to-all-done.1.arr_ref
  47.3 0.0 copy-start.18
  47.3 0.0 copy-start.8
  47.3 2.5 %shard_map.106 = (bf16[16,64,512]{2,1,0:T(8,128)(2,1)S(1)}, bf16[2,64,512]{2,1,0:T(8,128)(2,1)S(1)}) custom-call(s32[1,15]{1,0:T(1,128)S(1)} %copy-done.9, s32[1,17]{1,0:T(1,128)S(1)} %copy-done.10, s32[16]{0:T(128)S(1)} %fusion.2.req_ref, s32[16,2]{1,0:T(8,128)S(1)} %copy.24.exp_ref, bf16[1024,512]{1,0:T(8,128)(2,1)S(1)} %get-tuple-element.9.field_ref.h_ref, ...), custom_call_target="tpu_custom_call" | custom-call | flops 113246208 | bytes 3145728 | tf_op jit(solution)/shard_map/pallas_call | solution.py:305
  49.8 0.0 copy-start.5
  49.8 1.0 %copy-done.5 = bf16[16,64,512]{2,1,0:T(8,128)(2,1)} copy-done((bf16[16,64,512]{2,1,0:T(8,128)(2,1)}, bf16[16,64,512]{2,1,0:T(8,128)(2,1)S(1)}, u32[]{:S(2)}) %copy-start.5) | copy-done | bytes 1048600
  50.7 0.0 copy-done.6
  50.7 4.2 %all-to-all-start.2 = ((bf16[16,64,512]{2,1,0:T(8,128)(2,1)}), bf16[16,64,512]{2,1,0:T(8,128)(2,1)}, u32[]{:S(2)}, u32[]{:S(2)}) async-start(bf16[16,64,512]{2,1,0:T(8,128)(2,1)} %copy-done.5), calls=%async_computation.2 | async-start | bytes 2097152 | tf_op jit(solution)/shard_map/all_to_all | solution.py:407
  55.0 0.0 copy-done.18
  55.0 0.7 copy.27.mix_ref
  55.7 5.3 %shard_map.109 = bf16[1024,4096]{1,0:T(8,128)(2,1)} custom-call(bf16[1024,512]{1,0:T(8,128)(2,1)S(1)} %get-tuple-element.9.field_ref.h_ref, bf16[32,256]{1,0:T(8,128)(2,1)S(1)} %copy-done.8), custom_call_target="tpu_custom_call" | custom-call | flops 2147483648 | bytes 9437184 | tf_op jit(solution)/shard_map/pallas_call | solution.py:126
  61.1 2.0 %collective-permute-start.3 = (bf16[64,512]{1,0:T(8,128)(2,1)S(1)}, bf16[64,512]{1,0:T(8,128)(2,1)S(1)}, u32[]{:S(2)}, u32[]{:S(2)}) collective-permute-start(bf16[64,512]{1,0:T(8,128)(2,1)S(1)} %get-tuple-element.18), channel_id=1, source_target_pairs={{1,0},{2,1},{3,2},{4,3},{5,4},{6,5},{7,6},{8,7},{9,8},{10,9},{11,1... | collective-permute-start | bytes 196616 | tf_op jit(solution)/shard_map/ppermute | solution.py:374
  63.1 4.5 %collective-permute-start.2 = (bf16[64,512]{1,0:T(8,128)(2,1)S(1)}, bf16[64,512]{1,0:T(8,128)(2,1)S(1)}, u32[]{:S(2)}, u32[]{:S(2)}) collective-permute-start(bf16[64,512]{1,0:T(8,128)(2,1)S(1)} %get-tuple-element.19), channel_id=1, source_target_pairs={{0,1},{1,2},{2,3},{3,4},{4,5},{5,6},{6,7},{7,8},{8,9},{9,10},{10,1... | collective-permute-start | bytes 196616 | tf_op jit(solution)/shard_map/ppermute | solution.py:373
  67.6 8.4 %shard_map.107 = (bf16[1024,512]{1,0:T(8,128)(2,1)}, f32[1024,512]{1,0:T(8,128)}, f32[1024,512]{1,0:T(8,128)}, bf16[256,256]{1,0:T(8,128)(2,1)}) custom-call(s32[1,15]{1,0:T(1,128)} %col_ref.7, s32[1,17]{1,0:T(1,128)} %ptr_ref.7, bf16[1024,512]{1,0:T(8,128)(2,1)} %copy-done, bf16[64,512]{1,0:T(8,128)(2,1)} %copy-done.7, bf16[64,512]{1,0:T(8,128)(2,1)} %copy-done.6, ...), custom_call_target="tpu_custom_call" | custom-call | flops 1002438656 | bytes 10485760 | tf_op jit(solution)/shard_map/pallas_call | solution.py:325
  76.0 4.3 %collective-permute-done.3.hi_ref = bf16[64,512]{1,0:T(8,128)(2,1)S(1)} collective-permute-done((bf16[64,512]{1,0:T(8,128)(2,1)S(1)}, bf16[64,512]{1,0:T(8,128)(2,1)S(1)}, u32[]{:S(2)}, u32[]{:S(2)}) %collective-permute-start.3) | collective-permute-done | bytes 65568 | tf_op jit(solution)/shard_map/ppermute | solution.py:374
  80.3 0.0 collective-permute-done.2.lo_ref
  80.3 0.0 all-to-all-done.2.arr_ref
  80.3 0.6 copy-done.16
  80.9 0.0 copy-done.17
  80.9 5.8 %shard_map.108 = bf16[1024,512]{1,0:T(8,128)(2,1)} custom-call(s32[1,15]{1,0:T(1,128)} %col_ref.7, s32[1,17]{1,0:T(1,128)} %ptr_ref.7, bf16[64,512]{1,0:T(8,128)(2,1)} %copy-done.17, bf16[64,512]{1,0:T(8,128)(2,1)} %copy-done.16, bf16[16,64,512]{2,1,0:T(8,128)(2,1)} %all-to-all-done.2.arr_ref, bf16[1024,192]{1,0:T(8,128)(2,1)} %copy-done.2, ...), custom_call_target="tpu_custom_call" | custom-call | flops 339738624 | bytes 6291456 | tf_op jit(solution)/shard_map/pallas_call | solution.py:349
  (22 shorter events, 0.1 us)
Async XLA Ops:
  2.1 11.9 %all-to-all-start = ((s32[16,1,16]{2,1,0:T(1,128)}), s32[16,1,16]{2,1,0:T(1,128)S(1)}, u32[]{:S(2)}, u32[]{:S(2)}) async-start(s32[16,1,16]{2,1,0:T(1,128)} %bitcast.22), calls=%async_computation | async-start | bytes 16384 | tf_op jit(solution)/shard_map/all_to_all | solution.py:396
  8.6 1.6 %copy-start.4 = (bf16[1024,1024]{1,0:T(8,128)(2,1)S(1)}, bf16[1024,1024]{1,0:T(8,128)(2,1)}, u32[]{:S(2)}) copy-start(bf16[1024,1024]{1,0:T(8,128)(2,1)} %x_hbm.1) | copy-start | bytes 6291460
  10.2 0.7 copy-start.11
  10.9 0.7 copy-start.13
  13.9 41.8 %copy-start = (bf16[1024,512]{1,0:T(8,128)(2,1)}, bf16[1024,512]{1,0:T(8,128)(2,1)S(1)}, u32[]{:S(2)}) copy-start(bf16[1024,512]{1,0:T(8,128)(2,1)S(1)} %get-tuple-element.9.field_ref.h_ref) | copy-start | bytes 3145732
  14.0 14.2 %copy-start.12 = (s32[16,2]{0,1:T(2,128)S(1)}, s32[16,2]{0,1:T(2,128)}, u32[]{:S(2)}) copy-start(s32[16,2]{0,1:T(2,128)} %param.17) | copy-start | bytes 388
  14.0 14.3 %copy-start.15 = (bf16[64,960]{1,0:T(8,128)(2,1)S(1)}, bf16[64,960]{1,0:T(8,128)(2,1)}, u32[]{:S(2)}) copy-start(bf16[64,960]{1,0:T(8,128)(2,1)} %param.14) | copy-start | bytes 368644
  14.4 14.2 %copy-start.14 = (bf16[1024,192]{0,1:T(8,128)(2,1)S(1)}, bf16[1024,192]{0,1:T(8,128)(2,1)}, u32[]{:S(2)}) copy-start(bf16[1024,192]{0,1:T(8,128)(2,1)} %param.13) | copy-start | bytes 1179652
  15.5 31.7 %copy-start.9 = (s32[1,15]{1,0:T(1,128)S(1)}, s32[1,15]{1,0:T(1,128)}, u32[]{:S(2)}) copy-start(s32[1,15]{1,0:T(1,128)} %col_ref.7) | copy-start | bytes 184
  15.5 31.7 %copy-start.10 = (s32[1,17]{1,0:T(1,128)S(1)}, s32[1,17]{1,0:T(1,128)}, u32[]{:S(2)}) copy-start(s32[1,17]{1,0:T(1,128)} %ptr_ref.7) | copy-start | bytes 208
  15.5 31.7 %all-to-all-start.1 = ((bf16[16,64,512]{2,1,0:T(8,128)(2,1)}), bf16[16,64,512]{2,1,0:T(8,128)(2,1)S(1)}, u32[]{:S(2)}, u32[]{:S(2)}) async-start(bf16[16,64,512]{2,1,0:T(8,128)(2,1)} %broadcast_select_fusion), calls=%async_computation.1 | async-start | bytes 2097152 | tf_op jit(solution)/shard_map/all_to_all | solution.py:407
  21.7 25.5 %collective-permute-start.1 = (bf16[64,512]{1,0:T(8,128)(2,1)S(1)}, bf16[64,512]{1,0:T(8,128)(2,1)S(1)}, u32[]{:S(2)}, u32[]{:S(2)}) collective-permute-start(bf16[64,512]{1,0:T(8,128)(2,1)S(1)} %get-tuple-element.16), channel_id=1, source_target_pairs={{1,0},{2,1},{3,2},{4,3},{5,4},{6,5},{7,6},{8,7},{9,8},{10,9},{11,1... | collective-permute-start | bytes 196616 | tf_op jit(solution)/shard_map/ppermute | solution.py:374
  24.0 23.3 %collective-permute-start = (bf16[64,512]{1,0:T(8,128)(2,1)S(1)}, bf16[64,512]{1,0:T(8,128)(2,1)S(1)}, u32[]{:S(2)}, u32[]{:S(2)}) collective-permute-start(bf16[64,512]{1,0:T(8,128)(2,1)S(1)} %get-tuple-element.17), channel_id=1, source_target_pairs={{0,1},{1,2},{2,3},{3,4},{4,5},{5,6},{6,7},{7,8},{8,9},{9,10},{10,1... | collective-permute-start | bytes 196616 | tf_op jit(solution)/shard_map/ppermute | solution.py:373
  28.6 22.2 %copy-start.3 = (bf16[64,15,64]{2,0,1:T(8,128)(2,1)}, bf16[64,15,64]{2,0,1:T(8,128)(2,1)S(1)}, u32[]{:S(2)}) copy-start(bf16[64,15,64]{2,0,1:T(8,128)(2,1)S(1)} %copy.30) | copy-start | bytes 368644
  28.8 22.0 %copy-start.2 = (bf16[1024,192]{1,0:T(8,128)(2,1)}, bf16[1024,192]{1,0:T(8,128)(2,1)S(1)}, u32[]{:S(2)}) copy-start(bf16[1024,192]{1,0:T(8,128)(2,1)S(1)} %copy.25.band_ref) | copy-start | bytes 1179652
  47.2 3.5 %copy-start.6 = (bf16[64,512]{1,0:T(8,128)(2,1)}, bf16[64,512]{1,0:T(8,128)(2,1)S(1)}, u32[]{:S(2)}) copy-start(bf16[64,512]{1,0:T(8,128)(2,1)S(1)} %collective-permute-done.1.hi_ref) | copy-start | bytes 196612
  47.2 3.5 %copy-start.7 = (bf16[64,512]{1,0:T(8,128)(2,1)}, bf16[64,512]{1,0:T(8,128)(2,1)S(1)}, u32[]{:S(2)}) copy-start(bf16[64,512]{1,0:T(8,128)(2,1)S(1)} %collective-permute-done.lo_ref) | copy-start | bytes 196612
  47.2 3.5 %copy-start.1 = (bf16[16,64,512]{2,1,0:T(8,128)(2,1)}, bf16[16,64,512]{2,1,0:T(8,128)(2,1)S(1)}, u32[]{:S(2)}) copy-start(bf16[16,64,512]{2,1,0:T(8,128)(2,1)S(1)} %all-to-all-done.1.arr_ref) | copy-start | bytes 3145732
  47.3 7.7 %copy-start.18 = (bf16[96,32]{0,1:T(8,128)(2,1)S(1)}, bf16[96,32]{0,1:T(8,128)(2,1)}, u32[]{:S(2)}) copy-start(bf16[96,32]{0,1:T(8,128)(2,1)} %param.12) | copy-start | bytes 18436
  47.3 8.4 %copy-start.8 = (bf16[32,256]{1,0:T(8,128)(2,1)S(1)}, bf16[32,256]{1,0:T(8,128)(2,1)}, u32[]{:S(2)}) copy-start(bf16[32,256]{1,0:T(8,128)(2,1)} %sw_ref.1) | copy-start | bytes 49156
  49.8 1.0 %copy-start.5 = (bf16[16,64,512]{2,1,0:T(8,128)(2,1)}, bf16[16,64,512]{2,1,0:T(8,128)(2,1)S(1)}, u32[]{:S(2)}) copy-start(bf16[16,64,512]{2,1,0:T(8,128)(2,1)S(1)} %get-tuple-element.12) | copy-start | bytes 3145732
  50.7 29.5 %all-to-all-start.2 = ((bf16[16,64,512]{2,1,0:T(8,128)(2,1)}), bf16[16,64,512]{2,1,0:T(8,128)(2,1)}, u32[]{:S(2)}, u32[]{:S(2)}) async-start(bf16[16,64,512]{2,1,0:T(8,128)(2,1)} %copy-done.5), calls=%async_computation.2 | async-start | bytes 2097152 | tf_op jit(solution)/shard_map/all_to_all | solution.py:407
  61.1 19.2 %collective-permute-start.3 = (bf16[64,512]{1,0:T(8,128)(2,1)S(1)}, bf16[64,512]{1,0:T(8,128)(2,1)S(1)}, u32[]{:S(2)}, u32[]{:S(2)}) collective-permute-start(bf16[64,512]{1,0:T(8,128)(2,1)S(1)} %get-tuple-element.18), channel_id=1, source_target_pairs={{1,0},{2,1},{3,2},{4,3},{5,4},{6,5},{7,6},{8,7},{9,8},{10,9},{11,1... | collective-permute-start | bytes 196616 | tf_op jit(solution)/shard_map/ppermute | solution.py:374
  63.1 17.2 %collective-permute-start.2 = (bf16[64,512]{1,0:T(8,128)(2,1)S(1)}, bf16[64,512]{1,0:T(8,128)(2,1)S(1)}, u32[]{:S(2)}, u32[]{:S(2)}) collective-permute-start(bf16[64,512]{1,0:T(8,128)(2,1)S(1)} %get-tuple-element.19), channel_id=1, source_target_pairs={{0,1},{1,2},{2,3},{3,4},{4,5},{5,6},{6,7},{7,8},{8,9},{9,10},{10,1... | collective-permute-start | bytes 196616 | tf_op jit(solution)/shard_map/ppermute | solution.py:373
  80.3 0.6 copy-start.16
  80.3 0.6 copy-start.17

commit v22 on v20

--- a/solution.py
+++ b/solution.py
@@ -61,7 +61,7 @@
             ).astype(bf16)
     own = lax.axis_index("node")
     for e in range(ex_ref.shape[0]):
-        ex_ref[e] = h_ref[pl.ds(pl.multiple_of(exp_ref[own, e] * BLK, BLK), BLK), :]
+        ex_ref[e] = h_ref[pl.ds(pl.multiple_of(exp_ref[e, own] * BLK, BLK), BLK), :]
 
 
 def prep_kernel(col_ref, ptr_ref, out_ref):
@@ -105,7 +105,7 @@
         out_specs=[vmem(), vmem()],
         out_shape=[
             jax.ShapeDtypeStruct((rows, half), bf16),
-            jax.ShapeDtypeStruct((export_block.shape[1], BLK, half), bf16),
+            jax.ShapeDtypeStruct((export_block.shape[0], BLK, half), bf16),
         ],
         compiler_params=pltpu.CompilerParams(vmem_limit_bytes=48 * 1024 * 1024),
         cost_estimate=pl.CostEstimate(
@@ -408,7 +408,7 @@
     cols_all = info_all[:, :far_cap]
     hits = (cols_all // EXPORT == own_index) & (slot_ids[None, :] < info_all[:, far_cap:])
     requested = jnp.sum(jnp.where(hits, cols_all % EXPORT, 0), axis=1).astype(jnp.int32)
-    hidden, ex2 = front_hidden(export_block, features, filter_gate_weight)
+    hidden, ex2 = front_hidden(export_block.T, features, filter_gate_weight)
     blocks = node_rows // BLK
     width = hidden.shape[1]
     farw3 = far_weight.reshape(BLK, far_cap, BLK).transpose(1, 0, 2)

time: 88.3 us -> 87.7 us (level)
    unnamed x37 -> x41, local copies, waits for them, and re-layouts: 5.65 us -> 5.63 us
  transfers between devices with their start and end apart: 7 -> 7, of which waited for: 2 -> 2; matrix products, arithmetic and copies ran while one was open for 2% -> 1% of each run, Pallas kernels for 18% -> 19%
where the time goes in v22:
time: 87.7 us; the launch traced here: 86.8 us
  starting transfers between devices  30.5 us (35%)
  Pallas kernels  24.9 us (28%)
  waiting for transfers between devices  23.1 us (26%)
  local copies, waits for them, and re-layouts  6.12 us (7%)
  other arithmetic  1.3 us (1%)
  between operations  0.89 us (1%)
    ppermute x2, waiting for transfers between devices, halo(): hi = lax.ppermute(first, 'node', backward)  23.1 us
    all_to_all x2, starting transfers between devices, exchange(): return lax.all_to_all(send, 'node', split_axis=0, concat_axis=0, tiled=True)  11 us
    pallas_call x1, Pallas kernels, hop1(): pl.pallas_call(hop1_kernel, in_specs=[smem(), smem()] + [vmem()] * 6 + [h...  8.39 us
    ppermute x2, starting transfers between devices, halo(): lo = lax.ppermute(last, 'node', forward)  8.38 us
    all_to_all x1, starting transfers between devices, local(): lax.all_to_all(prep(far_col, far_ptr), 'node', split_axis=0, concat_axis=...  6.55 us
    pallas_call x1, Pallas kernels, hop2(): pl.pallas_call(hop2_kernel, in_specs=[smem(), smem()] + [vmem()] * 5 + [h...  5.76 us
    unnamed x41, local copies, waits for them, and re-layouts  5.63 us
    pallas_call x1, Pallas kernels, front_skip(): pl.pallas_call(skip_kernel, grid=(rows // tile,), in_specs=[pl.BlockSpec(...  5.34 us
  transfers between devices with their start and end apart: 7, of which 2 were waited for; matrix products, arithmetic and copies ran while one was open for 1% of the time, Pallas kernels for 19%

profile of v22, /device:TPU:15, one launch (start us, length us, event | category | flops | bytes accessed | tf_op | source)
XLA Modules:
  0.0 86.8 jit_solution(6659965442763950629)
XLA Ops:
  0.6 1.4 %shard_map.104 = s32[16,16]{1,0:T(8,128)} custom-call(s32[1,15]{1,0:T(1,128)} %col_ref.7, s32[1,17]{1,0:T(1,128)} %ptr_ref.7), custom_call_target="tpu_custom_call" | custom-call | tf_op jit(solution)/shard_map/pallas_call | solution.py:77
  2.1 6.6 %all-to-all-start = ((s32[16,1,16]{2,1,0:T(1,128)}), s32[16,1,16]{2,1,0:T(1,128)S(1)}, u32[]{:S(2)}, u32[]{:S(2)}) async-start(s32[16,1,16]{2,1,0:T(1,128)} %bitcast.22), calls=%async_computation | async-start | bytes 16384 | tf_op jit(solution)/shard_map/all_to_all | solution.py:406
  8.6 1.6 %copy-done.4 = bf16[1024,1024]{1,0:T(8,128)(2,1)S(1)} copy-done((bf16[1024,1024]{1,0:T(8,128)(2,1)S(1)}, bf16[1024,1024]{1,0:T(8,128)(2,1)}, u32[]{:S(2)}) %copy-start.4) | copy-done | bytes 2097176
  10.2 0.7 copy-done.11
  10.9 0.7 copy-done.13
  11.6 2.3 %shard_map.105 = (bf16[1024,512]{1,0:T(8,128)(2,1)S(1)}, bf16[2,64,512]{2,1,0:T(8,128)(2,1)S(1)}) custom-call(s32[2,16]{1,0:T(2,128)S(1)} %bitcast.19, bf16[1024,1024]{1,0:T(8,128)(2,1)S(1)} %copy-done.4, bf16[64,64]{1,0:T(8,128)(2,1)S(1)} %copy-done.13), custom_call_target="tpu_custom_call" | custom-call | flops 1073741824 | bytes 3145728 | tf_op jit(solution)/shard_map/pallas_call | solution.py:102
  13.9 0.0 copy-start
  14.0 0.0 copy-start.12
  14.0 0.0 copy-start.15
  14.0 0.0 all-to-all-done
  14.0 0.2 slice_reduce_fusion
  14.2 0.2 fusion.2.req_ref
  14.4 0.0 copy-start.14
  14.4 1.1 %broadcast_select_fusion = bf16[16,64,512]{2,1,0:T(8,128)(2,1)} fusion(pred[16]{0:T(512)(128)(4,1)S(1)} %broadcast_compare_fusion, bf16[64,512]{1,0:T(8,128)(2,1)S(1)} %get-tuple-element.21, bf16[64,512]{1,0:T(8,128)(2,1)S(1)} %get-tuple-element.20), kind=kLoop, calls=%fused_computation | loop fusion | flops 524288 | bytes 1179664 | tf_op jit(solution)/shard_map/jit(_where)/select_n | solution.py:419
  15.5 6.2 %all-to-all-start.1 = ((bf16[16,64,512]{2,1,0:T(8,128)(2,1)}), bf16[16,64,512]{2,1,0:T(8,128)(2,1)S(1)}, u32[]{:S(2)}, u32[]{:S(2)}) async-start(bf16[16,64,512]{2,1,0:T(8,128)(2,1)} %broadcast_select_fusion), calls=%async_computation.1 | async-start | bytes 2097152 | tf_op jit(solution)/shard_map/all_to_all | solution.py:417
  21.7 2.3 %collective-permute-start.1 = (bf16[64,512]{1,0:T(8,128)(2,1)S(1)}, bf16[64,512]{1,0:T(8,128)(2,1)S(1)}, u32[]{:S(2)}, u32[]{:S(2)}) collective-permute-start(bf16[64,512]{1,0:T(8,128)(2,1)S(1)} %get-tuple-element.16), channel_id=1, source_target_pairs={{1,0},{2,1},{3,2},{4,3},{5,4},{6,5},{7,6},{8,7},{9,8},{10,9},{11,1... | collective-permute-start | bytes 196616 | tf_op jit(solution)/shard_map/ppermute | solution.py:384
  24.0 4.2 %collective-permute-start = (bf16[64,512]{1,0:T(8,128)(2,1)S(1)}, bf16[64,512]{1,0:T(8,128)(2,1)S(1)}, u32[]{:S(2)}, u32[]{:S(2)}) collective-permute-start(bf16[64,512]{1,0:T(8,128)(2,1)S(1)} %get-tuple-element.17), channel_id=1, source_target_pairs={{0,1},{1,2},{2,3},{3,4},{4,5},{5,6},{6,7},{7,8},{8,9},{9,10},{10,1... | collective-permute-start | bytes 196616 | tf_op jit(solution)/shard_map/ppermute | solution.py:383
  28.2 0.0 copy-done.12
  28.2 0.1 copy.24.exp_ref
  28.3 0.0 copy-done.15
  28.3 0.2 reshape.12
  28.5 0.1 copy.30
  28.5 0.0 copy-done.14
  28.6 0.2 copy.25.band_ref
  28.8 0.0 copy-start.2
  28.8 18.4 %collective-permute-done.1.hi_ref = bf16[64,512]{1,0:T(8,128)(2,1)S(1)} collective-permute-done((bf16[64,512]{1,0:T(8,128)(2,1)S(1)}, bf16[64,512]{1,0:T(8,128)(2,1)S(1)}, u32[]{:S(2)}, u32[]{:S(2)}) %collective-permute-start.1) | collective-permute-done | bytes 65568 | tf_op jit(solution)/shard_map/ppermute | solution.py:384
  47.2 0.0 collective-permute-done.lo_ref
  47.2 0.0 all-to-all-done.1.arr_ref
  47.3 0.0 copy-start.18
  47.3 0.0 copy-start.8
  47.3 1.7 %shard_map.106 = (bf16[16,64,512]{2,1,0:T(8,128)(2,1)S(1)}, bf16[2,64,512]{2,1,0:T(8,128)(2,1)S(1)}) custom-call(s32[1,15]{1,0:T(1,128)S(1)} %copy-done.9, s32[1,17]{1,0:T(1,128)S(1)} %copy-done.10, s32[16]{0:T(128)S(1)} %fusion.2.req_ref, s32[16,2]{1,0:T(8,128)S(1)} %copy.24.exp_ref, bf16[1024,512]{1,0:T(8,128)(2,1)S(1)} %get-tuple-element.9.field_ref.h_ref, ...), custom_call_target="tpu_custom_call" | custom-call | flops 113246208 | bytes 3145728 | tf_op jit(solution)/shard_map/pallas_call | solution.py:315
  49.0 0.0 copy-start.5
  49.0 1.0 %copy-done.5 = bf16[16,64,512]{2,1,0:T(8,128)(2,1)} copy-done((bf16[16,64,512]{2,1,0:T(8,128)(2,1)}, bf16[16,64,512]{2,1,0:T(8,128)(2,1)S(1)}, u32[]{:S(2)}) %copy-start.5) | copy-done | bytes 1048600
  49.9 0.0 copy-done.3
  49.9 0.0 copy-done.6
  50.0 4.9 %all-to-all-start.2 = ((bf16[16,64,512]{2,1,0:T(8,128)(2,1)}), bf16[16,64,512]{2,1,0:T(8,128)(2,1)}, u32[]{:S(2)}, u32[]{:S(2)}) async-start(bf16[16,64,512]{2,1,0:T(8,128)(2,1)} %copy-done.5), calls=%async_computation.2 | async-start | bytes 2097152 | tf_op jit(solution)/shard_map/all_to_all | solution.py:417
  54.8 0.0 copy-done.18
  54.8 0.7 copy.27.mix_ref
  55.6 5.3 %shard_map.109 = bf16[1024,4096]{1,0:T(8,128)(2,1)} custom-call(bf16[1024,512]{1,0:T(8,128)(2,1)S(1)} %get-tuple-element.9.field_ref.h_ref, bf16[32,256]{1,0:T(8,128)(2,1)S(1)} %copy-done.8), custom_call_target="tpu_custom_call" | custom-call | flops 2147483648 | bytes 9437184 | tf_op jit(solution)/shard_map/pallas_call | solution.py:126
  60.9 2.3 %collective-permute-start.3 = (bf16[64,512]{1,0:T(8,128)(2,1)S(1)}, bf16[64,512]{1,0:T(8,128)(2,1)S(1)}, u32[]{:S(2)}, u32[]{:S(2)}) collective-permute-start(bf16[64,512]{1,0:T(8,128)(2,1)S(1)} %get-tuple-element.18), channel_id=1, source_target_pairs={{1,0},{2,1},{3,2},{4,3},{5,4},{6,5},{7,6},{8,7},{9,8},{10,9},{11,1... | collective-permute-start | bytes 196616 | tf_op jit(solution)/shard_map/ppermute | solution.py:384
  63.2 4.2 %collective-permute-start.2 = (bf16[64,512]{1,0:T(8,128)(2,1)S(1)}, bf16[64,512]{1,0:T(8,128)(2,1)S(1)}, u32[]{:S(2)}, u32[]{:S(2)}) collective-permute-start(bf16[64,512]{1,0:T(8,128)(2,1)S(1)} %get-tuple-element.19), channel_id=1, source_target_pairs={{0,1},{1,2},{2,3},{3,4},{4,5},{5,6},{6,7},{7,8},{8,9},{9,10},{10,1... | collective-permute-start | bytes 196616 | tf_op jit(solution)/shard_map/ppermute | solution.py:383
  67.4 8.4 %shard_map.107 = (bf16[1024,512]{1,0:T(8,128)(2,1)}, f32[1024,512]{1,0:T(8,128)}, f32[1024,512]{1,0:T(8,128)}, bf16[256,256]{1,0:T(8,128)(2,1)}) custom-call(s32[1,15]{1,0:T(1,128)} %col_ref.7, s32[1,17]{1,0:T(1,128)} %ptr_ref.7, bf16[1024,512]{1,0:T(8,128)(2,1)} %copy-done, bf16[64,512]{1,0:T(8,128)(2,1)} %copy-done.7, bf16[64,512]{1,0:T(8,128)(2,1)} %copy-done.6, ...), custom_call_target="tpu_custom_call" | custom-call | flops 1002438656 | bytes 10485760 | tf_op jit(solution)/shard_map/pallas_call | solution.py:335
  75.8 4.6 %collective-permute-done.3.hi_ref = bf16[64,512]{1,0:T(8,128)(2,1)S(1)} collective-permute-done((bf16[64,512]{1,0:T(8,128)(2,1)S(1)}, bf16[64,512]{1,0:T(8,128)(2,1)S(1)}, u32[]{:S(2)}, u32[]{:S(2)}) %collective-permute-start.3) | collective-permute-done | bytes 65568 | tf_op jit(solution)/shard_map/ppermute | solution.py:384
  80.4 0.0 collective-permute-done.2.lo_ref
  80.4 0.0 all-to-all-done.2.arr_ref
  80.4 0.6 copy-done.16
  81.0 0.0 copy-done.17
  81.0 5.8 %shard_map.108 = bf16[1024,512]{1,0:T(8,128)(2,1)} custom-call(s32[1,15]{1,0:T(1,128)} %col_ref.7, s32[1,17]{1,0:T(1,128)} %ptr_ref.7, bf16[64,512]{1,0:T(8,128)(2,1)} %copy-done.17, bf16[64,512]{1,0:T(8,128)(2,1)} %copy-done.16, bf16[16,64,512]{2,1,0:T(8,128)(2,1)} %all-to-all-done.2.arr_ref, bf16[1024,192]{1,0:T(8,128)(2,1)} %copy-done.2, ...), custom_call_target="tpu_custom_call" | custom-call | flops 339738624 | bytes 6291456 | tf_op jit(solution)/shard_map/pallas_call | solution.py:359
  (22 shorter events, 0.1 us)
Async XLA Ops:
  2.1 11.9 %all-to-all-start = ((s32[16,1,16]{2,1,0:T(1,128)}), s32[16,1,16]{2,1,0:T(1,128)S(1)}, u32[]{:S(2)}, u32[]{:S(2)}) async-start(s32[16,1,16]{2,1,0:T(1,128)} %bitcast.22), calls=%async_computation | async-start | bytes 16384 | tf_op jit(solution)/shard_map/all_to_all | solution.py:406
  8.6 1.6 %copy-start.4 = (bf16[1024,1024]{1,0:T(8,128)(2,1)S(1)}, bf16[1024,1024]{1,0:T(8,128)(2,1)}, u32[]{:S(2)}) copy-start(bf16[1024,1024]{1,0:T(8,128)(2,1)} %x_hbm.1) | copy-start | bytes 6291460
  10.2 0.7 copy-start.11
  10.9 0.7 copy-start.13
  13.9 41.6 %copy-start = (bf16[1024,512]{1,0:T(8,128)(2,1)}, bf16[1024,512]{1,0:T(8,128)(2,1)S(1)}, u32[]{:S(2)}) copy-start(bf16[1024,512]{1,0:T(8,128)(2,1)S(1)} %get-tuple-element.9.field_ref.h_ref) | copy-start | bytes 3145732
  14.0 14.2 %copy-start.12 = (s32[16,2]{0,1:T(2,128)S(1)}, s32[16,2]{0,1:T(2,128)}, u32[]{:S(2)}) copy-start(s32[16,2]{0,1:T(2,128)} %param.17) | copy-start | bytes 388
  14.0 14.3 %copy-start.15 = (bf16[64,960]{1,0:T(8,128)(2,1)S(1)}, bf16[64,960]{1,0:T(8,128)(2,1)}, u32[]{:S(2)}) copy-start(bf16[64,960]{1,0:T(8,128)(2,1)} %param.14) | copy-start | bytes 368644
  14.4 14.2 %copy-start.14 = (bf16[1024,192]{0,1:T(8,128)(2,1)S(1)}, bf16[1024,192]{0,1:T(8,128)(2,1)}, u32[]{:S(2)}) copy-start(bf16[1024,192]{0,1:T(8,128)(2,1)} %param.13) | copy-start | bytes 1179652
  15.5 31.7 %copy-start.9 = (s32[1,15]{1,0:T(1,128)S(1)}, s32[1,15]{1,0:T(1,128)}, u32[]{:S(2)}) copy-start(s32[1,15]{1,0:T(1,128)} %col_ref.7) | copy-start | bytes 184
  15.5 31.7 %copy-start.10 = (s32[1,17]{1,0:T(1,128)S(1)}, s32[1,17]{1,0:T(1,128)}, u32[]{:S(2)}) copy-start(s32[1,17]{1,0:T(1,128)} %ptr_ref.7) | copy-start | bytes 208
  15.5 31.7 %all-to-all-start.1 = ((bf16[16,64,512]{2,1,0:T(8,128)(2,1)}), bf16[16,64,512]{2,1,0:T(8,128)(2,1)S(1)}, u32[]{:S(2)}, u32[]{:S(2)}) async-start(bf16[16,64,512]{2,1,0:T(8,128)(2,1)} %broadcast_select_fusion), calls=%async_computation.1 | async-start | bytes 2097152 | tf_op jit(solution)/shard_map/all_to_all | solution.py:417
  21.7 25.5 %collective-permute-start.1 = (bf16[64,512]{1,0:T(8,128)(2,1)S(1)}, bf16[64,512]{1,0:T(8,128)(2,1)S(1)}, u32[]{:S(2)}, u32[]{:S(2)}) collective-permute-start(bf16[64,512]{1,0:T(8,128)(2,1)S(1)} %get-tuple-element.16), channel_id=1, source_target_pairs={{1,0},{2,1},{3,2},{4,3},{5,4},{6,5},{7,6},{8,7},{9,8},{10,9},{11,1... | collective-permute-start | bytes 196616 | tf_op jit(solution)/shard_map/ppermute | solution.py:384
  24.0 23.3 %collective-permute-start = (bf16[64,512]{1,0:T(8,128)(2,1)S(1)}, bf16[64,512]{1,0:T(8,128)(2,1)S(1)}, u32[]{:S(2)}, u32[]{:S(2)}) collective-permute-start(bf16[64,512]{1,0:T(8,128)(2,1)S(1)} %get-tuple-element.17), channel_id=1, source_target_pairs={{0,1},{1,2},{2,3},{3,4},{4,5},{5,6},{6,7},{7,8},{8,9},{9,10},{10,1... | collective-permute-start | bytes 196616 | tf_op jit(solution)/shard_map/ppermute | solution.py:383
  28.6 21.4 %copy-start.3 = (bf16[64,15,64]{2,0,1:T(8,128)(2,1)}, bf16[64,15,64]{2,0,1:T(8,128)(2,1)S(1)}, u32[]{:S(2)}) copy-start(bf16[64,15,64]{2,0,1:T(8,128)(2,1)S(1)} %copy.30) | copy-start | bytes 368644
  28.8 21.2 %copy-start.2 = (bf16[1024,192]{1,0:T(8,128)(2,1)}, bf16[1024,192]{1,0:T(8,128)(2,1)S(1)}, u32[]{:S(2)}) copy-start(bf16[1024,192]{1,0:T(8,128)(2,1)S(1)} %copy.25.band_ref) | copy-start | bytes 1179652
  47.2 2.7 %copy-start.6 = (bf16[64,512]{1,0:T(8,128)(2,1)}, bf16[64,512]{1,0:T(8,128)(2,1)S(1)}, u32[]{:S(2)}) copy-start(bf16[64,512]{1,0:T(8,128)(2,1)S(1)} %collective-permute-done.1.hi_ref) | copy-start | bytes 196612
  47.2 2.7 %copy-start.7 = (bf16[64,512]{1,0:T(8,128)(2,1)}, bf16[64,512]{1,0:T(8,128)(2,1)S(1)}, u32[]{:S(2)}) copy-start(bf16[64,512]{1,0:T(8,128)(2,1)S(1)} %collective-permute-done.lo_ref) | copy-start | bytes 196612
  47.2 2.7 %copy-start.1 = (bf16[16,64,512]{2,1,0:T(8,128)(2,1)}, bf16[16,64,512]{2,1,0:T(8,128)(2,1)S(1)}, u32[]{:S(2)}) copy-start(bf16[16,64,512]{2,1,0:T(8,128)(2,1)S(1)} %all-to-all-done.1.arr_ref) | copy-start | bytes 3145732
  47.3 7.6 %copy-start.18 = (bf16[96,32]{0,1:T(8,128)(2,1)S(1)}, bf16[96,32]{0,1:T(8,128)(2,1)}, u32[]{:S(2)}) copy-start(bf16[96,32]{0,1:T(8,128)(2,1)} %param.12) | copy-start | bytes 18436
  47.3 8.3 %copy-start.8 = (bf16[32,256]{1,0:T(8,128)(2,1)S(1)}, bf16[32,256]{1,0:T(8,128)(2,1)}, u32[]{:S(2)}) copy-start(bf16[32,256]{1,0:T(8,128)(2,1)} %sw_ref.1) | copy-start | bytes 49156
  49.0 1.0 %copy-start.5 = (bf16[16,64,512]{2,1,0:T(8,128)(2,1)}, bf16[16,64,512]{2,1,0:T(8,128)(2,1)S(1)}, u32[]{:S(2)}) copy-start(bf16[16,64,512]{2,1,0:T(8,128)(2,1)S(1)} %get-tuple-element.12) | copy-start | bytes 3145732
  50.0 30.4 %all-to-all-start.2 = ((bf16[16,64,512]{2,1,0:T(8,128)(2,1)}), bf16[16,64,512]{2,1,0:T(8,128)(2,1)}, u32[]{:S(2)}, u32[]{:S(2)}) async-start(bf16[16,64,512]{2,1,0:T(8,128)(2,1)} %copy-done.5), calls=%async_computation.2 | async-start | bytes 2097152 | tf_op jit(solution)/shard_map/all_to_all | solution.py:417
  60.9 19.5 %collective-permute-start.3 = (bf16[64,512]{1,0:T(8,128)(2,1)S(1)}, bf16[64,512]{1,0:T(8,128)(2,1)S(1)}, u32[]{:S(2)}, u32[]{:S(2)}) collective-permute-start(bf16[64,512]{1,0:T(8,128)(2,1)S(1)} %get-tuple-element.18), channel_id=1, source_target_pairs={{1,0},{2,1},{3,2},{4,3},{5,4},{6,5},{7,6},{8,7},{9,8},{10,9},{11,1... | collective-permute-start | bytes 196616 | tf_op jit(solution)/shard_map/ppermute | solution.py:384
  63.2 17.2 %collective-permute-start.2 = (bf16[64,512]{1,0:T(8,128)(2,1)S(1)}, bf16[64,512]{1,0:T(8,128)(2,1)S(1)}, u32[]{:S(2)}, u32[]{:S(2)}) collective-permute-start(bf16[64,512]{1,0:T(8,128)(2,1)S(1)} %get-tuple-element.19), channel_id=1, source_target_pairs={{0,1},{1,2},{2,3},{3,4},{4,5},{5,6},{6,7},{7,8},{8,9},{9,10},{10,1... | collective-permute-start | bytes 196616 | tf_op jit(solution)/shard_map/ppermute | solution.py:383
  80.4 0.6 copy-start.16
  80.4 0.6 copy-start.17
